TPU v7x, 256 devices: a whole 4x4x8 slice. The times are simulated.
256 devices in a mesh: slab: 64 (over z_hi, x, y), rep: 4 (over z_lo, core).
Axes of the slice: x: 4, y: 4, z: 8 (z_hi: 4, z_lo: 2; z = z_hi * 2 + z_lo), core: 2. Of those that a mesh axis runs over, the one named last changes fastest.
Arguments:
- volume: float32 [2048, 128, 1024], P('slab', 'rep'), may hold values from -6 to 6
- slices_x: bfloat16 [2048, 128, 128], P('slab', 'rep'), may hold values from -6 to 6
- slices_y: bfloat16 [2048, 16, 1024], P('slab'), may hold values from -6 to 6
- slices_z: bfloat16 [256, 128, 1024], P('slab', 'rep'), may hold values from -6 to 6
- profiles: float32 [4, 16, 128], replicated, may hold values from -1 to 2
- profile_index: int32 [25], replicated, may hold values from 0 to 3
- block_shift: int32 [25], replicated, may hold values from 0 to 7
Outputs:
- updated: float32 [2048, 128, 1024], P('slab', 'rep')
All inputs are finite; a program needn't handle non-finite values.
Results may differ from a plain program's by a relative error of at most 0.0044.
Values may be sent and summed in bfloat16 or wider, within the bound.
No kernel may reach another device: no remote copies, remote signals or barrier semaphores. Data moves between devices by JAX's collectives and lax.ppermute only.
A program may use at most 64 MiB of HBM per device.

v0:
```python
import jax
import jax.numpy as jnp
from jax import lax
from jax.sharding import PartitionSpec as P

BLOCK = 128
SLICES = 16


step_size = 0.5


def block_mats(profiles, profile_index, block_shift):
    kinds = profiles.shape[0]
    span = profiles.shape[2]
    onehot = (profile_index[:, None] == jnp.arange(kinds, dtype=jnp.int32)[None, :]).astype(
        jnp.float32
    )
    picked = jnp.einsum("bk,ksl->bsl", onehot, profiles, precision=lax.Precision.HIGHEST)
    columns = jnp.arange(span, dtype=jnp.int32)
    target = (columns[None, :] + block_shift[:, None]) % span
    moving = (target[:, :, None] == columns[None, None, :]).astype(jnp.float32)
    shifted = jnp.einsum("bsj,bjl->bsl", picked, moving, precision=lax.Precision.HIGHEST)
    return shifted.astype(jnp.bfloat16)


def banded_matrix(along):
    count = along.shape[0]
    identity = jnp.eye(count, dtype=jnp.bfloat16)
    return (along[:, :, None, :] * identity[:, None, :, None]).reshape(
        count * SLICES, count * BLOCK
    )


def zstack_work(gathered, observed, along_z):
    depth, middle, last = gathered.shape
    count_z = depth // BLOCK
    columns = middle * last
    fwd_z = jnp.einsum(
        "bsl,blp->bsp",
        along_z,
        gathered.reshape(count_z, BLOCK, columns),
        preferred_element_type=jnp.float32,
    )
    resid_z = (observed.reshape(count_z, SLICES, columns).astype(jnp.float32) - fwd_z).astype(
        jnp.bfloat16
    )
    corr_sheet = jnp.einsum("bsl,bsp->blp", along_z, resid_z, preferred_element_type=jnp.float32)
    return corr_sheet.reshape(depth, middle, last)


def shards(volume, slices_x, slices_y, slices_z, profiles, profile_index, block_shift):
    planes, rows_here, width = volume.shape
    count_x = width // BLOCK
    count_y = slices_y.shape[1] // SLICES
    mats = block_mats(profiles, profile_index, block_shift)
    along_x = mats[:count_x]
    along_y = mats[count_x : count_x + count_y]
    along_z = mats[count_x + count_y :]
    coarse = volume.astype(jnp.bfloat16)
    banded_x = banded_matrix(along_x)
    flat_coarse = coarse.reshape(planes * rows_here, width)
    fwd_x = lax.dot_general(
        flat_coarse, banded_x, (((1,), (1,)), ((), ())), preferred_element_type=jnp.float32
    )
    resid_x = (
        slices_x.reshape(planes * rows_here, count_x * SLICES).astype(jnp.float32) - fwd_x
    ).astype(jnp.bfloat16)
    corr_x = jnp.dot(resid_x, banded_x, preferred_element_type=jnp.float32).reshape(
        planes, rows_here, width
    )
    banded_y = banded_matrix(along_y)
    start_row = lax.axis_index("rep") * rows_here
    local_band = lax.dynamic_slice_in_dim(banded_y, start_row, rows_here, 1)
    plane_band = jnp.broadcast_to(local_band[None], (planes,) + local_band.shape)
    partial_y = jnp.einsum("zty,zyx->ztx", plane_band, coarse, preferred_element_type=jnp.float32)
    fwd_y = lax.psum(partial_y, "rep")
    resid_y = (slices_y.astype(jnp.float32) - fwd_y).astype(jnp.bfloat16)
    corr_y = jnp.einsum("zty,ztx->zyx", plane_band, resid_y, preferred_element_type=jnp.float32)
    groups = lax.axis_size("slab")
    piece_cols = rows_here * width // groups
    folded_coarse = coarse.reshape(planes, groups, piece_cols)
    folded_slices = slices_z.reshape(slices_z.shape[0], groups, piece_cols)
    corr_sheet = zstack_work(
        lax.all_to_all(folded_coarse, "slab", split_axis=1, concat_axis=0, tiled=True),
        lax.all_to_all(folded_slices, "slab", split_axis=1, concat_axis=0, tiled=True),
        along_z,
    )
    corr_z = lax.all_to_all(corr_sheet, "slab", split_axis=0, concat_axis=1, tiled=True).reshape(
        planes, rows_here, width
    )
    return volume + step_size * (corr_x + corr_y + corr_z)


def solution(mesh):
    return jax.shard_map(
        shards,
        mesh=mesh,
        in_specs=(
            P("slab", "rep", None),
            P("slab", "rep", None),
            P("slab", None, None),
            P("slab", "rep", None),
            P(),
            P(),
            P(),
        ),
        out_specs=P("slab", "rep", None),
        check_vma=False,
    )
```

profile of v0, /device:TPU:1, one launch (start us, length us, event | category | flops | bytes accessed | tf_op | source)
XLA Modules:
  0.0 273.9 jit_solution(10119166696304109315)
XLA Ops:
  6.5 1.0 reshape.93
  7.6 0.9 copy.26
  8.5 15.1 %all-to-all-start = ((bf16[4,64,512]{2,0,1:T(4,128)(2,1)}), bf16[4,64,512]{2,0,1:T(4,128)(2,1)S(1)}, u32[]{:S(2)}, u32[]{:S(2)}) async-start(bf16[4,64,512]{2,0,1:T(4,128)(2,1)} %copy.26), calls=%async_computation | async-start | bytes 524288 | tf_op jit(solution)/shard_map/all_to_all | solution.py:86
  23.6 2.5 convert_element_type.49
  26.1 2.1 reshape.94
  28.3 4.1 %copy.27 = bf16[32,64,512]{2,0,1:T(8,128)(2,1)} copy(bf16[32,64,512]{2,1,0:T(8,128)(2,1)} %reshape.94) | data formatting | bytes 4194304 | tf_op jit(solution)/shard_map/reshape | solution.py:82
  32.4 3.9 %all-to-all-done = bf16[4,64,512]{2,0,1:T(4,128)(2,1)S(1)} async-done(((bf16[4,64,512]{2,0,1:T(4,128)(2,1)}), bf16[4,64,512]{2,0,1:T(4,128)(2,1)S(1)}, u32[]{:S(2)}, u32[]{:S(2)}) %all-to-all-start) | async-done | bytes 262176 | tf_op jit(solution)/shard_map/all_to_all | solution.py:86
  36.3 8.7 %all-to-all-start.1 = ((bf16[32,64,512]{2,0,1:T(8,128)(2,1)}), bf16[32,64,512]{2,0,1:T(8,128)(2,1)}, u32[]{:S(2)}, u32[]{:S(2)}) async-start(bf16[32,64,512]{2,0,1:T(8,128)(2,1)} %copy.27), calls=%async_computation.1 | async-start | bytes 4194304 | tf_op jit(solution)/shard_map/all_to_all | solution.py:85
  45.1 0.3 fusion.13
  45.4 1.0 fusion.4
  46.7 44.6 %all-to-all-done.1 = bf16[32,64,512]{2,0,1:T(8,128)(2,1)} async-done(((bf16[32,64,512]{2,0,1:T(8,128)(2,1)}), bf16[32,64,512]{2,0,1:T(8,128)(2,1)}, u32[]{:S(2)}, u32[]{:S(2)}) %all-to-all-start.1) | async-done | bytes 2097184 | tf_op jit(solution)/shard_map/all_to_all | solution.py:85
  91.3 2.0 fusion.2
  93.2 0.8 fusion.23
  94.0 11.7 %copy.28 = f32[2048,1,512]{2,1,0:T(1,128)} copy(f32[2048,1,512]{2,0,1:T(8,128)S(1)} %bitcast.52) | data formatting | bytes 8388608 | tf_op jit(solution)/shard_map/reshape | solution.py:49
  105.7 12.0 %all-to-all-start.2 = ((f32[2048,1,512]{2,1,0:T(1,128)}), f32[2048,1,512]{2,1,0:T(1,128)}, u32[]{:S(2)}, u32[]{:S(2)}) async-start(f32[2048,1,512]{2,1,0:T(1,128)} %copy.28), calls=%async_computation.2 | async-start | bytes 8388608 | tf_op jit(solution)/shard_map/all_to_all | solution.py:89
  118.1 1.7 fusion.11
  119.9 0.9 copy-done.1
  121.3 0.8 fusion.3
  122.3 120.5 %all-reduce.2.cloned.1.call-done = f32[32,16,1024]{2,1,0:T(8,128)} async-done(((f32[32,16,1024]{2,1,0:T(8,128)}), f32[32,16,1024]{2,1,0:T(8,128)}) %all-reduce.2.cloned.1.call-update) | async-done | bytes 2097168 | tf_op jit(solution)/shard_map/psum | solution.py:77
  242.8 4.6 %fusion.5 = f32[32,32,1024]{2,1,0:T(8,128)} fusion(f32[32,16,1024]{2,1,0:T(8,128)} %all-reduce.2.cloned.1.call-done, bf16[32,16,1024]{2,1,0:T(8,128)(2,1)} %param.9, bf16[16,32]{1,0:T(8,128)(2,1)S(1)} %dynamic-slice_bitcast_fusion), kind=kOutput, calls=%fused_computation.10 | convolution fusion | flops 35127296 | bytes 7341056 | tf_op jit(solution)/shard_map/zty,ztx->zyx/dot_general | solution.py:79
  247.3 2.6 copy.30
  250.0 4.4 %copy.29 = f32[32,64,1,512]{3,1,0,2:T(8,128)} copy(f32[32,64,1,512]{3,0,1,2:T(8,128)S(1)} %bitcast.53) | data formatting | bytes 8388608 | tf_op jit(solution)/shard_map/all_to_all | solution.py:89
  254.4 5.2 %reshape.97 = f32[32,32,1024]{2,1,0:T(8,128)} reshape(f32[32,64,1,512]{3,1,0,2:T(8,128)} %copy.29) | data formatting | bytes 8388608 | tf_op jit(solution)/shard_map/reshape | solution.py:89
  259.7 7.4 %multiply_add_fusion = f32[32,32,1024]{2,1,0:T(8,128)} fusion(f32[32,32,1024]{2,1,0:T(8,128)} %param.7, f32[32,32,1024]{2,1,0:T(8,128)} %reshape.97, f32[32,32,1024]{2,1,0:T(8,128)} %fusion.5, bf16[32,32,128]{2,1,0:T(8,128)(2,1)S(1)} %bitcast.55, bf16[128,1024,1]{1,0,2:T(8,128)(2,1)S(1)} %reshape.102), kind=kOutput, calls=%fused_computation | convolution fusion | flops 272629760 | bytes 17301504 | tf_op jit(solution)/shard_map/dot_general | solution.py:69
  (22 shorter events, 1.3 us)
Async XLA Ops:
  6.5 38.5 %copy-start = (f32[4,16,128]{2,1,0:T(8,128)S(1)}, f32[4,16,128]{2,1,0:T(8,128)}, u32[]{:S(2)}) copy-start(f32[4,16,128]{2,1,0:T(8,128)} %param.11) | copy-start | bytes 98308
  8.5 27.8 %all-to-all-start = ((bf16[4,64,512]{2,0,1:T(4,128)(2,1)}), bf16[4,64,512]{2,0,1:T(4,128)(2,1)S(1)}, u32[]{:S(2)}, u32[]{:S(2)}) async-start(bf16[4,64,512]{2,0,1:T(4,128)(2,1)} %copy.26), calls=%async_computation | async-start | bytes 524288 | tf_op jit(solution)/shard_map/all_to_all | solution.py:86
  32.4 12.6 %copy-start.3 = (s32[25]{0:T(128)S(1)}, s32[25]{0:T(128)}, u32[]{:S(2)}) copy-start(s32[25]{0:T(128)} %param.13) | copy-start | bytes 304
  32.4 12.7 %copy-start.2 = (s32[25]{0:T(128)S(1)}, s32[25]{0:T(128)}, u32[]{:S(2)}) copy-start(s32[25]{0:T(128)} %param.12) | copy-start | bytes 304
  36.3 55.0 %all-to-all-start.1 = ((bf16[32,64,512]{2,0,1:T(8,128)(2,1)}), bf16[32,64,512]{2,0,1:T(8,128)(2,1)}, u32[]{:S(2)}, u32[]{:S(2)}) async-start(bf16[32,64,512]{2,0,1:T(8,128)(2,1)} %copy.27), calls=%async_computation.1 | async-start | bytes 4194304 | tf_op jit(solution)/shard_map/all_to_all | solution.py:85
  105.7 141.6 %all-to-all-start.2 = ((f32[2048,1,512]{2,1,0:T(1,128)}), f32[2048,1,512]{2,1,0:T(1,128)}, u32[]{:S(2)}, u32[]{:S(2)}) async-start(f32[2048,1,512]{2,1,0:T(1,128)} %copy.28), calls=%async_computation.2 | async-start | bytes 8388608 | tf_op jit(solution)/shard_map/all_to_all | solution.py:89
  117.7 125.0 %all-reduce.2.cloned.1.call-start = ((), (), s32[]{:S(2)}) async-start(), calls=%async_computation.3 | async-start | bytes 4194304 | tf_op jit(solution)/shard_map/psum | solution.py:77
  119.8 0.9 copy-start.1
Sparse Core Ops, SparseCore 0:
  121.2 121.4 all-reduce.1
where the time goes:
time: 275 us; the launch traced here: 274 us
  waiting for transfers between devices  169 us (61%)
  starting transfers between devices  36.1 us (13%)
  local copies, waits for them, and re-layouts  33.8 us (12%)
  matrix products  18.7 us (7%)
  between operations  13.6 us (5%)
  other arithmetic  2.79 us (1%)
    psum x1, waiting for transfers between devices, shards(): fwd_y = lax.psum(partial_y, 'rep')  120 us
    all_to_all x1, waiting for transfers between devices, shards(): lax.all_to_all(folded_coarse, 'slab', split_axis=1, concat_axis=0, tiled=...  44.6 us
    all_to_all x1, starting transfers between devices, shards(): lax.all_to_all(folded_slices, 'slab', split_axis=1, concat_axis=0, tiled=...  15.1 us
    all_to_all x1, starting transfers between devices, shards(): lax.all_to_all(corr_sheet, 'slab', split_axis=0, concat_axis=1, tiled=True)  12 us
    reshape x1, local copies, waits for them, and re-layouts, zstack_work(): return corr_sheet.reshape(depth, middle, last)  11.7 us
    all_to_all x1, starting transfers between devices, shards(): lax.all_to_all(folded_coarse, 'slab', split_axis=1, concat_axis=0, tiled=...  8.69 us
    dot_general x1, matrix products, shards(): jnp.dot(resid_x, banded_x, preferred_element_type=jnp.float32)  7.41 us
    reshape x2, local copies, waits for them, and re-layouts, shards(): folded_coarse = coarse.reshape(planes, groups, piece_cols)  6.22 us
  transfers between devices with their start and end apart: 4, of which 3 were waited for; matrix products, arithmetic and copies ran while one was open for 7% of the time, Pallas kernels for 0%

commit v1 on v0

v1 whole, which is shorter than its diff:
```python
import jax
import jax.numpy as jnp
from jax import lax
from jax.sharding import Mesh, PartitionSpec as P

BLOCK = 128
SLICES = 16


step_size = 0.5


def block_mats(profiles, profile_index, block_shift):
    kinds = profiles.shape[0]
    span = profiles.shape[2]
    onehot = (profile_index[:, None] == jnp.arange(kinds, dtype=jnp.int32)[None, :]).astype(
        jnp.float32
    )
    picked = jnp.einsum("bk,ksl->bsl", onehot, profiles, precision=lax.Precision.HIGHEST)
    columns = jnp.arange(span, dtype=jnp.int32)
    target = (columns[None, :] + block_shift[:, None]) % span
    moving = (target[:, :, None] == columns[None, None, :]).astype(jnp.float32)
    shifted = jnp.einsum("bsj,bjl->bsl", picked, moving, precision=lax.Precision.HIGHEST)
    return shifted.astype(jnp.bfloat16)


def banded_matrix(along):
    count = along.shape[0]
    identity = jnp.eye(count, dtype=jnp.bfloat16)
    return (along[:, :, None, :] * identity[:, None, :, None]).reshape(
        count * SLICES, count * BLOCK
    )


def shards(volume, slices_x, slices_y, slices_z, profiles, profile_index, block_shift):
    planes, rows_here, width = volume.shape
    count_x = width // BLOCK
    count_y = slices_y.shape[1] // SLICES
    mats = block_mats(profiles, profile_index, block_shift)
    along_x = mats[:count_x]
    along_y = mats[count_x : count_x + count_y]
    along_z = mats[count_x + count_y :]
    coarse = volume.astype(jnp.bfloat16)

    banded_x = banded_matrix(along_x)
    flat_coarse = coarse.reshape(planes * rows_here, width)
    fwd_x = lax.dot_general(
        flat_coarse, banded_x, (((1,), (1,)), ((), ())), preferred_element_type=jnp.float32
    )
    resid_x = (
        slices_x.reshape(planes * rows_here, count_x * SLICES).astype(jnp.float32) - fwd_x
    ).astype(jnp.bfloat16)
    corr_x = jnp.dot(resid_x, banded_x, preferred_element_type=jnp.float32).reshape(
        planes, rows_here, width
    )

    rep = lax.axis_index("rep")
    nrep = lax.axis_size("rep")
    band_y = lax.dynamic_slice_in_dim(along_y[0], rep * rows_here, rows_here, 1)
    partial_y = jnp.einsum("sl,zlx->zsx", band_y, coarse, preferred_element_type=jnp.float32)
    fwd_y = lax.psum_scatter(partial_y, "rep", scatter_dimension=0, tiled=True)
    part_z = planes // nrep
    obs_y = lax.dynamic_slice_in_dim(slices_y, rep * part_z, part_z, 0)
    resid_y = (obs_y.astype(jnp.float32) - fwd_y).astype(jnp.bfloat16)
    resid_y = lax.all_gather(resid_y, "rep", axis=0, tiled=True)
    corr_y = jnp.einsum("sl,zsx->zlx", band_y, resid_y, preferred_element_type=jnp.float32)

    zb = lax.axis_index("zb")
    zq = lax.axis_index("zq")
    mat_z = lax.dynamic_index_in_dim(along_z, zb, 0, keepdims=False)
    band_z = lax.dynamic_slice_in_dim(mat_z, zq * planes, planes, 1)
    partial_z = jnp.einsum("sl,lyx->syx", band_z, coarse, preferred_element_type=jnp.float32)
    fwd_z = lax.psum_scatter(partial_z, "zq", scatter_dimension=0, tiled=True)
    resid_z = (slices_z.astype(jnp.float32) - fwd_z).astype(jnp.bfloat16)
    resid_z = lax.all_gather(resid_z, "zq", axis=0, tiled=True)
    corr_z = jnp.einsum("sl,syx->lyx", band_z, resid_z, preferred_element_type=jnp.float32)

    return volume + step_size * (corr_x + corr_y + corr_z)


def solution(mesh):
    nslab, nrep = mesh.devices.shape
    slab = ("zb", "zq")

    def run(volume, *rest):
        group = BLOCK // (volume.shape[0] // nslab)
        inner = Mesh(mesh.devices.reshape(nslab // group, group, nrep), ("zb", "zq", "rep"))
        return jax.shard_map(
            shards,
            mesh=inner,
            in_specs=(
                P(slab, "rep", None),
                P(slab, "rep", None),
                P(slab, None, None),
                P(slab, "rep", None),
                P(),
                P(),
                P(),
            ),
            out_specs=P(slab, "rep", None),
            check_vma=False,
        )(volume, *rest)

    return run
```

time: 275 us -> 158 us (0.57)
  waiting for transfers between devices: 169 us -> 109 us
  starting transfers between devices: 36.1 us -> 0.31 us
  local copies, waits for them, and re-layouts: 33.8 us -> 3.76 us
  matrix products: 18.7 us -> 24.8 us
  other arithmetic: 2.79 us -> 7.08 us
    psum x1 -> x0, waiting for transfers between devices: 120 us -> none  [shards(): fwd_y = lax.psum(partial_y, 'rep')]
    reduce_scatter x0 -> x2, waiting for transfers between devices: none -> 65.6 us  [the longest x1 34.2 us: shards(): fwd_z = lax.psum_scatter(partial_z, 'zq', scatter_dimension=0, tiled=True)]
    all_to_all x3 -> x0, waiting for transfers between devices: 48.5 us -> none  [the longest x1 44.6 us: shards(): lax.all_to_all(folded_coarse, 'slab', split_axis=1, concat_axis=0, tiled=...]
    all_gather x0 -> x2, waiting for transfers between devices: none -> 43.4 us  [the longest x1 23.7 us: shards(): resid_y = lax.all_gather(resid_y, 'rep', axis=0, tiled=True)]
    all_to_all x3 -> x0, starting transfers between devices: 35.8 us -> none  [the longest x1 15.1 us: shards(): lax.all_to_all(folded_slices, 'slab', split_axis=1, concat_axis=0, tiled=...]
    reshape x6 -> x0, local copies, waits for them, and re-layouts: 25.1 us -> none  [the longest x1 11.7 us: zstack_work(): return corr_sheet.reshape(depth, middle, last)]
    dot_general x4, matrix products: 9.07 us -> 19.2 us  [the longest x1 10.9 us: shards(): jnp.einsum('sl,zsx->zlx', band_y, resid_y, preferred_element_type=jnp.flo...]
    dot_general x1, matrix products: 7.41 us -> 2.7 us  [shards(): jnp.dot(resid_x, banded_x, preferred_element_type=jnp.float32)]
  transfers between devices with their start and end apart: 4 -> 4, of which waited for: 3 -> 4; matrix products, arithmetic and copies ran while one was open for 7% -> 9% of each run, Pallas kernels for 0% -> 0%
where the time goes in v1:
time: 158 us
  waiting for transfers between devices  109 us (69%)
  matrix products  24.8 us (16%)
  between operations  13.3 us (8%)
  other arithmetic  7.08 us (4%)
  local copies, waits for them, and re-layouts  3.76 us (2%)
    reduce_scatter x1, waiting for transfers between devices, shards(): fwd_z = lax.psum_scatter(partial_z, 'zq', scatter_dimension=0, tiled=True)  34.2 us
    reduce_scatter x1, waiting for transfers between devices, shards(): fwd_y = lax.psum_scatter(partial_y, 'rep', scatter_dimension=0, tiled=True)  31.4 us
    all_gather x1, waiting for transfers between devices, shards(): resid_y = lax.all_gather(resid_y, 'rep', axis=0, tiled=True)  23.7 us
    all_gather x1, waiting for transfers between devices, shards(): resid_z = lax.all_gather(resid_z, 'zq', axis=0, tiled=True)  19.7 us
    dot_general x1, matrix products, shards(): jnp.einsum('sl,zsx->zlx', band_y, resid_y, preferred_element_type=jnp.flo...  10.9 us
    dot_general x1, matrix products, shards(): jnp.einsum('sl,syx->lyx', band_z, resid_z, preferred_element_type=jnp.flo...  4.13 us
  transfers between devices with their start and end apart: 4, of which 4 were waited for; matrix products, arithmetic and copies ran while one was open for 9% of the time, Pallas kernels for 0%

profile of v1, /device:TPU:1, one launch (start us, length us, event | category | flops | bytes accessed | tf_op | source)
XLA Modules:
  0.0 158.2 jit_solution(11104190824409723244)
XLA Ops:
  6.5 0.7 add_select_fusion
  7.3 1.0 fusion.15
  8.3 1.0 fusion.8
  9.3 2.5 %convert_element_type.40 = bf16[32,32,1024]{2,1,0:T(8,128)(2,1)S(1)} convert(f32[32,32,1024]{2,1,0:T(8,128)} %param.7) | non-fusion elementwise | flops 1048576 | bytes 6291456 | tf_op jit(solution)/shard_map/convert_element_type | solution.py:43
  11.9 2.4 %fusion.3 = f32[16,32,1024]{2,0,1:T(8,128)S(1)} fusion(bf16[32,32,1024]{2,1,0:T(8,128)(2,1)S(1)} %convert_element_type.40, bf16[16,16,128]{2,1,0:T(8,128)(2,1)S(1)} %slice.14, s32[]{:T(128)S(6)} %select_n.32, s32[]{:T(128)S(6)} %select_n.34), kind=kOutput, calls=%fused_computation.4 | convolution fusion | flops 33554432 | bytes 4198408 | tf_op jit(solution)/shard_map/sl,lyx->syx/dot_general | solution.py:72
  14.2 2.5 %copy.21 = f32[16,32,1024]{2,1,0:T(8,128)} copy(f32[16,32,1024]{2,0,1:T(8,128)S(1)} %fusion.3) | data formatting | bytes 4194304 | tf_op jit(solution)/shard_map/sl,lyx->syx/dot_general | solution.py:72
  16.8 0.0 reduce-scatter.3.cloned.1.call-start
  16.9 1.8 %convolution_bitcast_fusion = f32[32,16,1024]{2,1,0:T(8,128)} fusion(bf16[32,32,1024]{2,1,0:T(8,128)(2,1)S(1)} %convert_element_type.40, bf16[1,16,128]{2,1,0:T(8,128)(2,1)S(1)} %slice.13, s32[]{:T(128)S(6)} %select_n.30), kind=kOutput, calls=%fused_computation.8 | convolution fusion | flops 33554432 | bytes 4198404 | tf_op jit(solution)/shard_map/sl,zlx->zsx/dot_general | solution.py:60
  18.8 34.2 %reduce-scatter.5.cloned.1.call-done = f32[4,32,1024]{2,1,0:T(8,128)} async-done(((f32[16,32,1024]{2,1,0:T(8,128)}), f32[4,32,1024]{2,1,0:T(8,128)}) %reduce-scatter.5.cloned.1.call-update) | async-done | bytes 524304 | tf_op jit(solution)/shard_map/reduce_scatter | solution.py:73
  53.0 1.8 %subtract_convert_fusion = bf16[4,32,1024]{2,1,0:T(8,128)(2,1)} fusion(f32[4,32,1024]{2,1,0:T(8,128)} %reduce-scatter.5.cloned.1.call-done, bf16[4,32,1024]{2,1,0:T(8,128)(2,1)S(1)} %copy-done.3), kind=kLoop, calls=%fused_computation.16 | loop fusion | flops 393216 | bytes 1048576 | tf_op jit(solution)/shard_map/convert_element_type | solution.py:74
  54.8 0.2 all-gather.3.cloned.1.call-start
  55.1 31.4 %reduce-scatter.3.cloned.1.call-done = f32[8,16,1024]{2,1,0:T(8,128)} async-done(((f32[32,16,1024]{2,1,0:T(8,128)}), f32[8,16,1024]{2,1,0:T(8,128)}) %reduce-scatter.3.cloned.1.call-update) | async-done | bytes 524304 | tf_op jit(solution)/shard_map/reduce_scatter | solution.py:61
  86.4 1.9 %subtract_convert_fusion.1 = bf16[8,16,1024]{2,1,0:T(8,128)(2,1)} fusion(f32[8,16,1024]{2,1,0:T(8,128)} %reduce-scatter.3.cloned.1.call-done, bf16[32,16,1024]{2,1,0:T(8,128)(2,1)} %param.9, s32[]{:T(128)S(6)} %select_n.29), kind=kLoop, calls=%fused_computation.17 | loop fusion | flops 393216 | bytes 1048580 | tf_op jit(solution)/shard_map/convert_element_type | solution.py:64
  88.3 0.1 broadcast_multiply_fusion
  88.4 0.8 reshape.72
  89.2 0.1 bitcast_convert_fusion
  89.3 0.2 copy.18
  89.5 0.8 fusion.7
  90.4 0.2 copy.19
  90.5 2.7 %fusion.37 = f32[32,32,1024]{2,1,0:T(8,128)} fusion(bf16[32,32,128]{2,1,0:T(8,128)(2,1)S(1)} %bitcast.50, bf16[128,1024,1]{1,0,2:T(8,128)(2,1)S(1)} %copy-done.1), kind=kOutput, calls=%fused_computation.49 | convolution fusion | flops 268435456 | bytes 4718592 | tf_op jit(solution)/shard_map/dot_general | solution.py:53
  93.2 19.7 %all-gather.5.cloned.1.call-done = bf16[16,32,1024]{2,1,0:T(8,128)(2,1)} async-done(((bf16[4,32,1024]{2,1,0:T(8,128)(2,1)}), bf16[16,32,1024]{2,1,0:T(8,128)(2,1)}) %all-gather.5.cloned.1.call-update) | async-done | bytes 1048592 | tf_op jit(solution)/shard_map/all_gather | solution.py:75
  112.9 4.1 %fusion.9 = f32[32,32,1024]{2,0,1:T(8,128)} fusion(bf16[16,32,1024]{2,1,0:T(8,128)(2,1)} %all-gather.5.cloned.1.call-done, bf16[16,16,128]{2,1,0:T(8,128)(2,1)S(1)} %slice.14, s32[]{:T(128)S(6)} %select_n.32, s32[]{:T(128)S(6)} %select_n.34), kind=kOutput, calls=%fused_computation.13 | convolution fusion | flops 33554432 | bytes 5246984 | tf_op jit(solution)/shard_map/sl,syx->lyx/dot_general | solution.py:76
  117.1 23.7 %all-gather.3.cloned.1.call-done = bf16[32,16,1024]{2,1,0:T(8,128)(2,1)} async-done(((bf16[8,16,1024]{2,1,0:T(8,128)(2,1)}), bf16[32,16,1024]{2,1,0:T(8,128)(2,1)}) %all-gather.3.cloned.1.call-update) | async-done | bytes 1048592 | tf_op jit(solution)/shard_map/all_gather | solution.py:65
  140.8 10.9 %fusion.2 = f32[32,32,1024]{2,1,0:T(8,128)} fusion(f32[32,32,1024]{2,1,0:T(8,128)} %param.7, f32[32,32,1024]{2,1,0:T(8,128)} %fusion.37, f32[32,32,1024]{2,0,1:T(8,128)} %fusion.9, bf16[32,16,1024]{2,1,0:T(8,128)(2,1)} %all-gather.3.cloned.1.call-done, bf16[1,16,128]{2,1,0:T(8,128)(2,1)S(1)} %slice.13, s32[]{:T(128)S(6)} %select_n.30), kind=kOutput, calls=%fused_computation.3 | convolution fusion | flops 37748736 | bytes 17829892 | tf_op jit(solution)/shard_map/sl,zsx->zlx/dot_general | solution.py:66
  (18 shorter events, 0.2 us)
Async XLA Ops:
  6.5 0.8 copy-start
  6.5 46.4 %reduce-scatter.5.cloned.1.call-start = ((), (), s32[]{:S(2)}) async-start(), calls=%async_computation.4 | async-start | bytes 2621440 | tf_op jit(solution)/shard_map/reduce_scatter | solution.py:73
  16.8 69.6 %reduce-scatter.3.cloned.1.call-start = ((), (), s32[]{:S(2)}) async-start(), calls=%async_computation.2 | async-start | bytes 2621440 | tf_op jit(solution)/shard_map/reduce_scatter | solution.py:61
  18.7 34.3 %copy-start.3 = (bf16[4,32,1024]{2,1,0:T(8,128)(2,1)S(1)}, bf16[4,32,1024]{2,1,0:T(8,128)(2,1)}, u32[]{:S(2)}) copy-start(bf16[4,32,1024]{2,1,0:T(8,128)(2,1)} %param.10) | copy-start | bytes 786436
  18.7 70.5 %copy-start.2 = (bf16[32,32,128]{2,1,0:T(8,128)(2,1)S(1)}, bf16[32,32,128]{2,1,0:T(8,128)(2,1)}, u32[]{:S(2)}) copy-start(bf16[32,32,128]{2,1,0:T(8,128)(2,1)} %param.8) | copy-start | bytes 786436
  18.7 94.2 %all-gather.5.cloned.1.call-start = ((), (), s32[]{:S(2)}) async-start(), calls=%async_computation.5 | async-start | bytes 1310720 | tf_op jit(solution)/shard_map/all_gather | solution.py:75
  54.8 86.0 %all-gather.3.cloned.1.call-start = ((), (), s32[]{:S(2)}) async-start(), calls=%async_computation.3 | async-start | bytes 1310720 | tf_op jit(solution)/shard_map/all_gather | solution.py:65
  89.5 1.0 copy-start.1
Sparse Core Ops, SparseCore 0:
  16.9 36.0 reduce-scatter.4
  55.5 30.8 reduce-scatter.2
  88.2 24.6 all-gather.4
  114.6 26.1 all-gather.2

commit v2 on v1

--- a/solution.py
+++ b/solution.py
@@ -32,6 +32,20 @@
     )
 
 
+def halve(values, axis, me):
+    half = values.shape[0] // 2
+    keep = lax.dynamic_slice_in_dim(values, me * half, half, 0)
+    give = lax.dynamic_slice_in_dim(values, (1 - me) * half, half, 0)
+    return keep + lax.ppermute(give, axis, [(0, 1), (1, 0)])
+
+
+def double(values, axis, me):
+    other = lax.ppermute(values, axis, [(0, 1), (1, 0)])
+    low = jnp.where(me == 0, values, other)
+    high = jnp.where(me == 0, other, values)
+    return jnp.concatenate([low, high], 0)
+
+
 def shards(volume, slices_x, slices_y, slices_z, profiles, profile_index, block_shift):
     planes, rows_here, width = volume.shape
     count_x = width // BLOCK
@@ -54,26 +68,45 @@
         planes, rows_here, width
     )
 
-    rep = lax.axis_index("rep")
-    nrep = lax.axis_size("rep")
+    zl = lax.axis_index("zl")
+    co = lax.axis_index("co")
+    rep = zl * 2 + co
     band_y = lax.dynamic_slice_in_dim(along_y[0], rep * rows_here, rows_here, 1)
     partial_y = jnp.einsum("sl,zlx->zsx", band_y, coarse, preferred_element_type=jnp.float32)
-    fwd_y = lax.psum_scatter(partial_y, "rep", scatter_dimension=0, tiled=True)
-    part_z = planes // nrep
-    obs_y = lax.dynamic_slice_in_dim(slices_y, rep * part_z, part_z, 0)
+    fwd_y = halve(partial_y, "co", co)
+    fwd_y = halve(fwd_y, "zl", zl)
+    part_z = planes // 4
+    obs_y = lax.dynamic_slice_in_dim(slices_y, (co * 2 + zl) * part_z, part_z, 0)
     resid_y = (obs_y.astype(jnp.float32) - fwd_y).astype(jnp.bfloat16)
-    resid_y = lax.all_gather(resid_y, "rep", axis=0, tiled=True)
+    resid_y = double(resid_y, "zl", zl)
+    resid_y = double(resid_y, "co", co)
     corr_y = jnp.einsum("sl,zsx->zlx", band_y, resid_y, preferred_element_type=jnp.float32)
 
     zb = lax.axis_index("zb")
     zq = lax.axis_index("zq")
+    group = lax.axis_size("zq")
     mat_z = lax.dynamic_index_in_dim(along_z, zb, 0, keepdims=False)
     band_z = lax.dynamic_slice_in_dim(mat_z, zq * planes, planes, 1)
     partial_z = jnp.einsum("sl,lyx->syx", band_z, coarse, preferred_element_type=jnp.float32)
-    fwd_z = lax.psum_scatter(partial_z, "zq", scatter_dimension=0, tiled=True)
+    piece = SLICES // group
+    fwd_z = lax.dynamic_slice_in_dim(partial_z, zq * piece, piece, 0)
+    for k in range(1, group):
+        dest = (zq + k) % group
+        sent = lax.dynamic_slice_in_dim(partial_z, dest * piece, piece, 0)
+        fwd_z = fwd_z + lax.ppermute(sent, "zq", [(j, (j + k) % group) for j in range(group)])
     resid_z = (slices_z.astype(jnp.float32) - fwd_z).astype(jnp.bfloat16)
-    resid_z = lax.all_gather(resid_z, "zq", axis=0, tiled=True)
-    corr_z = jnp.einsum("sl,syx->lyx", band_z, resid_z, preferred_element_type=jnp.float32)
+    pieces = [resid_z]
+    rows = [lax.dynamic_slice_in_dim(band_z, zq * piece, piece, 0)]
+    for k in range(1, group):
+        pieces.append(lax.ppermute(resid_z, "zq", [(j, (j + k) % group) for j in range(group)]))
+        src = (zq - k + group) % group
+        rows.append(lax.dynamic_slice_in_dim(band_z, src * piece, piece, 0))
+    corr_z = jnp.einsum(
+        "sl,syx->lyx",
+        jnp.concatenate(rows, 0),
+        jnp.concatenate(pieces, 0),
+        preferred_element_type=jnp.float32,
+    )
 
     return volume + step_size * (corr_x + corr_y + corr_z)
 
@@ -81,23 +114,26 @@
 def solution(mesh):
     nslab, nrep = mesh.devices.shape
     slab = ("zb", "zq")
+    rep = ("zl", "co")
 
     def run(volume, *rest):
         group = BLOCK // (volume.shape[0] // nslab)
-        inner = Mesh(mesh.devices.reshape(nslab // group, group, nrep), ("zb", "zq", "rep"))
+        inner = Mesh(
+            mesh.devices.reshape(nslab // group, group, 2, nrep // 2), ("zb", "zq", "zl", "co")
+        )
         return jax.shard_map(
             shards,
             mesh=inner,
             in_specs=(
-                P(slab, "rep", None),
-                P(slab, "rep", None),
+                P(slab, rep, None),
+                P(slab, rep, None),
                 P(slab, None, None),
-                P(slab, "rep", None),
+                P(slab, rep, None),
                 P(),
                 P(),
                 P(),
             ),
-            out_specs=P(slab, "rep", None),
+            out_specs=P(slab, rep, None),
             check_vma=False,
         )(volume, *rest)
 

time: 158 us -> 70.6 us (0.45)
  waiting for transfers between devices: 109 us -> 19.2 us
  starting transfers between devices: 0.31 us -> 14.4 us
  between operations: 13.3 us -> 0.19 us
  matrix products: 24.8 us -> 14.8 us
  local copies, waits for them, and re-layouts: 3.76 us -> 11.9 us
  other arithmetic: 7.08 us -> 9.55 us
    reduce_scatter x2 -> x0, waiting for transfers between devices: 65.6 us -> none  [the longest x1 34.2 us: shards(): fwd_z = lax.psum_scatter(partial_z, 'zq', scatter_dimension=0, tiled=True)]
    all_gather x2 -> x0, waiting for transfers between devices: 43.4 us -> none  [the longest x1 23.7 us: shards(): resid_y = lax.all_gather(resid_y, 'rep', axis=0, tiled=True)]
    ppermute x0 -> x10, waiting for transfers between devices: none -> 19.2 us  [the longest x3 11.4 us: shards(): lax.ppermute(resid_z, 'zq', [(j, (j + k) % group) for j in range(group)])]
    ppermute x0 -> x10, starting transfers between devices: none -> 14.4 us  [the longest x2 4.9 us: halve(): return keep + lax.ppermute(give, axis, [(0, 1), (1, 0)])]
    dot_general x1, matrix products: 10.9 us -> 5.97 us  [shards(): jnp.einsum('sl,zsx->zlx', band_y, resid_y, preferred_element_type=jnp.flo...]
    unnamed x8 -> x18, local copies, waits for them, and re-layouts: 0.03 us -> 4.63 us
    dot_general x1, matrix products: 4.13 us -> 0.77 us  [shards(): jnp.einsum('sl,syx->lyx', jnp.concatenate(rows, 0), jnp.concatenate(piece...]
    dynamic_slice x0 -> x4, local copies, waits for them, and re-layouts: none -> 3.23 us  [the longest x1 1.4 us: shards(): sent = lax.dynamic_slice_in_dim(partial_z, dest * piece, piece, 0)]
  transfers between devices with their start and end apart: 4 -> 10, of which waited for: 4 -> 6; matrix products, arithmetic and copies ran while one was open for 9% -> 28% of each run, Pallas kernels for 0% -> 0%
where the time goes in v2:
time: 70.6 us; the launch traced here: 70.1 us
  waiting for transfers between devices  19.2 us (27%)
  matrix products  14.8 us (21%)
  starting transfers between devices  14.4 us (20%)
  local copies, waits for them, and re-layouts  11.9 us (17%)
  other arithmetic  9.55 us (14%)
    ppermute x3, waiting for transfers between devices, shards(): lax.ppermute(resid_z, 'zq', [(j, (j + k) % group) for j in range(group)])  11.4 us
    dot_general x1, matrix products, shards(): jnp.einsum('sl,zsx->zlx', band_y, resid_y, preferred_element_type=jnp.flo...  5.97 us
    ppermute x2, starting transfers between devices, halve(): return keep + lax.ppermute(give, axis, [(0, 1), (1, 0)])  4.9 us
    unnamed x18, local copies, waits for them, and re-layouts  4.63 us
    ppermute x2, waiting for transfers between devices, halve(): return keep + lax.ppermute(give, axis, [(0, 1), (1, 0)])  3.95 us
    ppermute x3, waiting for transfers between devices, shards(): lax.ppermute(sent, 'zq', [(j, (j + k) % group) for j in range(group)])  3.84 us
    ppermute x3, starting transfers between devices, shards(): lax.ppermute(resid_z, 'zq', [(j, (j + k) % group) for j in range(group)])  3.58 us
    ppermute x2, starting transfers between devices, double(): other = lax.ppermute(values, axis, [(0, 1), (1, 0)])  3.24 us
  transfers between devices with their start and end apart: 10, of which 6 were waited for; matrix products, arithmetic and copies ran while one was open for 28% of the time, Pallas kernels for 0%

profile of v2, /device:TPU:1, one launch (start us, length us, event | category | flops | bytes accessed | tf_op | source)
XLA Modules:
  0.0 70.1 jit_solution(2188314246178657320)
XLA Ops:
  2.8 2.6 %convert_element_type.40 = bf16[32,32,1024]{2,1,0:T(8,128)(2,1)S(1)} convert(f32[32,32,1024]{2,1,0:T(8,128)} %param.7) | non-fusion elementwise | flops 1048576 | bytes 6291456 | tf_op jit(solution)/shard_map/convert_element_type | solution.py:57
  5.9 1.3 %copy-done.2 = f32[16,32,1024]{2,0,1:T(8,128)} copy-done((f32[16,32,1024]{2,0,1:T(8,128)}, f32[16,32,1024]{2,0,1:T(8,128)S(1)}, u32[]{:S(2)}) %copy-start.2) | copy-done | bytes 2097176
  7.3 3.3 %collective-permute-start = (f32[16,16,1024]{2,1,0:T(8,128)S(1)}, f32[16,16,1024]{2,1,0:T(8,128)}, u32[]{:S(2)}, u32[]{:S(2)}) collective-permute-start(f32[16,16,1024]{2,1,0:T(8,128)S(1)} %dynamic-slice_bitcast_fusion), channel_id=1, source_target_pairs={{0,1},{1,0},{2,3},{3,2},{4,5},{5,4},{6,7},{7,6},{8,9},{9,8},{10,11... | collective-permute-start | bytes 3145736 | tf_op jit(solution)/shard_map/ppermute | solution.py:39
  11.2 2.4 %fusion.3 = f32[16,32,1024]{2,0,1:T(8,128)S(1)} fusion(bf16[32,32,1024]{2,1,0:T(8,128)(2,1)S(1)} %convert_element_type.40, bf16[16,16,128]{2,1,0:T(8,128)(2,1)S(1)} %slice.14, s32[]{:T(128)S(6)} %select_n.122, s32[]{:T(128)S(6)} %select_n.126), kind=kOutput, calls=%fused_computation.4 | convolution fusion | flops 33554432 | bytes 4198408 | tf_op jit(solution)/shard_map/sl,lyx->syx/dot_general | solution.py:90
  13.5 1.3 %copy-done.3 = f32[16,32,1024]{2,0,1:T(8,128)} copy-done((f32[16,32,1024]{2,0,1:T(8,128)}, f32[16,32,1024]{2,0,1:T(8,128)S(1)}, u32[]{:S(2)}) %copy-start.3) | copy-done | bytes 2097176
  14.9 1.4 %constant_dynamic-slice_fusion.1 = (f32[4,32,1024]{2,0,1:T(4,128)}, f32[4,32,1024]{2,0,1:T(4,128)}, f32[4,32,1024]{2,0,1:T(4,128)}) fusion(f32[16,32,1024]{2,0,1:T(8,128)S(1)} %fusion.3, s32[]{:T(128)S(6)} %select_n.134, s32[]{:T(128)S(6)} %select_n.128, s32[]{:T(128)S(6)} %select_n.131), kind=kLoop, calls=%fused_computation.68 | loop fusion | bytes 3145740 | tf_op jit(solution)/shard_map/dynamic_slice | solution.py:95
  16.3 2.7 %collective-permute-start.6 = (f32[4,32,1024]{2,0,1:T(4,128)}, f32[4,32,1024]{2,0,1:T(4,128)}, u32[]{:S(2)}, u32[]{:S(2)}) collective-permute-start(f32[4,32,1024]{2,0,1:T(4,128)} %get-tuple-element.6), channel_id=1, source_target_pairs={{0,12},{4,0},{8,4},{12,8},{1,13},{5,1},{9,5},{13,9},{2,14},{6,2},{... | collective-permute-start | bytes 1572872 | tf_op jit(solution)/shard_map/ppermute | solution.py:96
  19.8 1.7 %bitcast_add_fusion.1 = f32[16,16,1024]{2,1,0:T(8,128)S(1)} fusion(f32[16,16,1024]{2,1,0:T(8,128)} %collective-permute-done, f32[16,32,1024]{2,0,1:T(8,128)} %copy-done.2, s32[]{:T(128)S(6)} %select_n.113), kind=kLoop, calls=%fused_computation.23 | loop fusion | flops 262144 | bytes 3145732 | tf_op jit(solution)/shard_map/add | solution.py:39
  22.4 1.6 %collective-permute-start.1 = (f32[8,16,1024]{2,1,0:T(8,128)}, f32[8,16,1024]{2,1,0:T(8,128)}, u32[]{:S(2)}, u32[]{:S(2)}) collective-permute-start(f32[8,16,1024]{2,1,0:T(8,128)} %constant_dynamic-slice_fusion.2), channel_id=1, source_target_pairs={{0,2},{2,0},{1,3},{3,1},{4,6},{6,4},{5,7},{7,5},{8,10},{10,8},{9,1... | collective-permute-start | bytes 1572872 | tf_op jit(solution)/shard_map/ppermute | solution.py:39
  24.9 2.0 %copy.13 = f32[1024,128]{0,1:T(8,128)} copy(f32[1024,128]{1,0:T(8,128)} %bitcast_convert_fusion) | data formatting | bytes 1048576 | tf_op jit(solution)/shard_map/convert_element_type | solution.py:65
  27.0 2.6 %fusion.7 = bf16[1024,128]{0,1:T(8,128)(2,1)} fusion(f32[1024,128]{0,1:T(8,128)} %copy.13, bf16[1024,1024]{1,0:T(8,128)(2,1)S(1)} %bitcast.58, bf16[16,8,8,128]{3,2,1,0:T(8,128)(2,1)S(1)} %bitcast.59), kind=kOutput, calls=%fused_computation.10 | convolution fusion | flops 268697600 | bytes 3145728 | tf_op jit(solution)/shard_map/dot_general | solution.py:61
  29.5 1.2 %copy.14 = bf16[1024,128]{1,0:T(8,128)(2,1)S(1)} copy(bf16[1024,128]{0,1:T(8,128)(2,1)} %fusion.7) | data formatting | bytes 524288 | tf_op jit(solution)/shard_map/convert_element_type | solution.py:66
  31.6 3.9 %collective-permute-done.1 = f32[8,16,1024]{2,1,0:T(8,128)} collective-permute-done((f32[8,16,1024]{2,1,0:T(8,128)}, f32[8,16,1024]{2,1,0:T(8,128)}, u32[]{:S(2)}, u32[]{:S(2)}) %collective-permute-start.1) | collective-permute-done | bytes 524320 | tf_op jit(solution)/shard_map/ppermute | solution.py:39
  35.6 1.2 %subtract_convert_fusion.1 = bf16[8,16,1024]{2,1,0:T(8,128)(2,1)S(1)} fusion(f32[8,16,1024]{2,1,0:T(8,128)} %collective-permute-done.1, f32[16,16,1024]{2,1,0:T(8,128)S(1)} %bitcast_add_fusion.1, s32[]{:T(128)S(6)} %select_n.115, bf16[32,16,1024]{2,1,0:T(8,128)(2,1)} %param.9, s32[]{:T(128)S(6)} %select_n.111), kind=kLoop, calls=%fused_computation.28 | loop fusion | flops 524288 | bytes 1572872 | tf_op jit(solution)/shard_map/convert_element_type | solution.py:80
  36.8 1.4 %collective-permute-start.2 = (bf16[8,16,1024]{2,1,0:T(8,128)(2,1)S(1)}, bf16[8,16,1024]{2,1,0:T(8,128)(2,1)S(1)}, u32[]{:S(2)}, u32[]{:S(2)}) collective-permute-start(bf16[8,16,1024]{2,1,0:T(8,128)(2,1)S(1)} %subtract_convert_fusion.1), channel_id=1, source_target_pairs={{0,2},{2,0},{1,3},{3,1},{4,6},{6,4},{5,7},{7,5},{8,10},{10,8},{9,1... | collective-permute-start | bytes 786440 | tf_op jit(solution)/shard_map/ppermute | solution.py:43
  38.2 3.1 %collective-permute-done.6 = f32[4,32,1024]{2,0,1:T(4,128)} collective-permute-done((f32[4,32,1024]{2,0,1:T(4,128)}, f32[4,32,1024]{2,0,1:T(4,128)}, u32[]{:S(2)}, u32[]{:S(2)}) %collective-permute-start.6) | collective-permute-done | bytes 524320 | tf_op jit(solution)/shard_map/ppermute | solution.py:96
  42.0 2.2 %subtract_convert_fusion = bf16[4,32,1024]{2,0,1:T(4,128)(2,1)S(1)} fusion(f32[4,32,1024]{2,0,1:T(4,128)} %collective-permute-done.6, f32[4,32,1024]{2,0,1:T(4,128)} %collective-permute-done.5, f32[4,32,1024]{2,0,1:T(4,128)} %collective-permute-done.4, f32[16,32,1024]{2,0,1:T(8,128)} %copy-done.3, s32[]{:T(128)S(6)} %select_n.123, ...), kind=kLoop, calls=%fused_computation.27 | loop fusion | flops 786432 | bytes 2621444 | tf_op jit(solution)/shard_map/convert_element_type | solution.py:97
  44.3 2.9 %collective-permute-start.9 = (bf16[4,32,1024]{2,0,1:T(4,128)(2,1)S(1)}, bf16[4,32,1024]{2,0,1:T(4,128)(2,1)S(1)}, u32[]{:S(2)}, u32[]{:S(2)}) collective-permute-start(bf16[4,32,1024]{2,0,1:T(4,128)(2,1)S(1)} %subtract_convert_fusion), channel_id=1, source_target_pairs={{0,12},{4,0},{8,4},{12,8},{1,13},{5,1},{9,5},{13,9},{2,14},{6,2},{... | collective-permute-start | bytes 786440 | tf_op jit(solution)/shard_map/ppermute | solution.py:101
  47.9 1.9 %collective-permute-start.3 = (bf16[16,16,1024]{2,1,0:T(8,128)(2,1)S(1)}, bf16[16,16,1024]{2,1,0:T(8,128)(2,1)S(1)}, u32[]{:S(2)}, u32[]{:S(2)}) collective-permute-start(bf16[16,16,1024]{2,1,0:T(8,128)(2,1)S(1)} %pad_maximum_fusion), channel_id=1, source_target_pairs={{0,1},{1,0},{2,3},{3,2},{4,5},{5,4},{6,7},{7,6},{8,9},{9,8},{10,11... | collective-permute-start | bytes 1572872 | tf_op jit(solution)/shard_map/ppermute | solution.py:43
  50.5 2.4 %collective-permute-done.9 = bf16[4,32,1024]{2,0,1:T(4,128)(2,1)S(1)} collective-permute-done((bf16[4,32,1024]{2,0,1:T(4,128)(2,1)S(1)}, bf16[4,32,1024]{2,0,1:T(4,128)(2,1)S(1)}, u32[]{:S(2)}, u32[]{:S(2)}) %collective-permute-start.9) | collective-permute-done | bytes 262176 | tf_op jit(solution)/shard_map/ppermute | solution.py:101
  52.9 2.2 %collective-permute-done.8 = bf16[4,32,1024]{2,0,1:T(4,128)(2,1)S(1)} collective-permute-done((bf16[4,32,1024]{2,0,1:T(4,128)(2,1)S(1)}, bf16[4,32,1024]{2,0,1:T(4,128)(2,1)S(1)}, u32[]{:S(2)}, u32[]{:S(2)}) %collective-permute-start.8) | collective-permute-done | bytes 262176 | tf_op jit(solution)/shard_map/ppermute | solution.py:101
  55.1 6.8 %collective-permute-done.7 = bf16[4,32,1024]{2,0,1:T(4,128)(2,1)S(1)} collective-permute-done((bf16[4,32,1024]{2,0,1:T(4,128)(2,1)S(1)}, bf16[4,32,1024]{2,0,1:T(4,128)(2,1)S(1)}, u32[]{:S(2)}, u32[]{:S(2)}) %collective-permute-start.7) | collective-permute-done | bytes 262176 | tf_op jit(solution)/shard_map/ppermute | solution.py:101
  62.8 1.3 %copy-done.1 = f32[32,32,1024]{2,1,0:T(8,128)S(1)} copy-done((f32[32,32,1024]{2,1,0:T(8,128)S(1)}, f32[32,32,1024]{2,1,0:T(8,128)}, u32[]{:S(2)}) %copy-start.1) | copy-done | bytes 4194328
  64.1 6.0 %fusion.2 = f32[32,32,1024]{2,1,0:T(8,128)} fusion(f32[32,32,1024]{2,1,0:T(8,128)S(1)} %copy-done.1, f32[32,32,1024]{2,1,0:T(8,128)S(1)} %fusion.52, f32[32,32,1024]{2,0,1:T(8,128)S(1)} %fusion.12, bf16[16,16,1024]{2,1,0:T(8,128)(2,1)S(1)} %get-tuple-element.9, bf16[16,16,1024]{2,1,0:T(8,128)(2,1)S(1)} %get-tuple-element.8, ...), kind=kOutput, calls=%fused_computation.3 | convolution fusion | flops 38273024 | bytes 17829892 | tf_op jit(solution)/shard_map/sl,zsx->zlx/dot_general | solution.py:83
  (44 shorter events, 10.6 us)
Async XLA Ops:
  0.0 0.8 %copy-start = (f32[4,16,128]{2,1,0:T(8,128)S(1)}, f32[4,16,128]{2,1,0:T(8,128)}, u32[]{:S(2)}) copy-start(f32[4,16,128]{2,1,0:T(8,128)} %param.11) | copy-start | bytes 98308
  2.8 16.2 %copy-start.7 = (bf16[25,16,128]{2,1,0:T(8,128)(2,1)}, bf16[25,16,128]{2,1,0:T(8,128)(2,1)S(1)}, u32[]{:S(2)}) copy-start(bf16[25,16,128]{2,1,0:T(8,128)(2,1)S(1)} %fusion.8) | copy-start | bytes 307204
  5.8 1.3 %copy-start.2 = (f32[16,32,1024]{2,0,1:T(8,128)}, f32[16,32,1024]{2,0,1:T(8,128)S(1)}, u32[]{:S(2)}) copy-start(f32[16,32,1024]{2,0,1:T(8,128)S(1)} %fusion.41) | copy-start | bytes 6291460
  7.3 12.6 %collective-permute-start = (f32[16,16,1024]{2,1,0:T(8,128)S(1)}, f32[16,16,1024]{2,1,0:T(8,128)}, u32[]{:S(2)}, u32[]{:S(2)}) collective-permute-start(f32[16,16,1024]{2,1,0:T(8,128)S(1)} %dynamic-slice_bitcast_fusion), channel_id=1, source_target_pairs={{0,1},{1,0},{2,3},{3,2},{4,5},{5,4},{6,7},{7,6},{8,9},{9,8},{10,11... | collective-permute-start | bytes 3145736 | tf_op jit(solution)/shard_map/ppermute | solution.py:39
  10.6 0.6 copy-start.8
  13.5 1.3 %copy-start.3 = (f32[16,32,1024]{2,0,1:T(8,128)}, f32[16,32,1024]{2,0,1:T(8,128)S(1)}, u32[]{:S(2)}) copy-start(f32[16,32,1024]{2,0,1:T(8,128)S(1)} %fusion.3) | copy-start | bytes 6291460
  14.9 4.1 %copy-start.5 = (bf16[32,32,128]{2,1,0:T(8,128)(2,1)S(1)}, bf16[32,32,128]{2,1,0:T(8,128)(2,1)}, u32[]{:S(2)}) copy-start(bf16[32,32,128]{2,1,0:T(8,128)(2,1)} %param.8) | copy-start | bytes 786436
  16.3 21.9 %collective-permute-start.4 = (f32[4,32,1024]{2,0,1:T(4,128)}, f32[4,32,1024]{2,0,1:T(4,128)}, u32[]{:S(2)}, u32[]{:S(2)}) collective-permute-start(f32[4,32,1024]{2,0,1:T(4,128)} %get-tuple-element.5), channel_id=1, source_target_pairs={{0,4},{4,8},{8,12},{12,0},{1,5},{5,9},{9,13},{13,1},{2,6},{6,10},{... | collective-permute-start | bytes 1572872 | tf_op jit(solution)/shard_map/ppermute | solution.py:96
  16.3 25.0 %collective-permute-start.6 = (f32[4,32,1024]{2,0,1:T(4,128)}, f32[4,32,1024]{2,0,1:T(4,128)}, u32[]{:S(2)}, u32[]{:S(2)}) collective-permute-start(f32[4,32,1024]{2,0,1:T(4,128)} %get-tuple-element.6), channel_id=1, source_target_pairs={{0,12},{4,0},{8,4},{12,8},{1,13},{5,1},{9,5},{13,9},{2,14},{6,2},{... | collective-permute-start | bytes 1572872 | tf_op jit(solution)/shard_map/ppermute | solution.py:96
  18.9 23.1 %collective-permute-start.5 = (f32[4,32,1024]{2,0,1:T(4,128)}, f32[4,32,1024]{2,0,1:T(4,128)}, u32[]{:S(2)}, u32[]{:S(2)}) collective-permute-start(f32[4,32,1024]{2,0,1:T(4,128)} %get-tuple-element.7), channel_id=1, source_target_pairs={{0,8},{4,12},{8,0},{12,4},{1,9},{5,13},{9,1},{13,5},{2,10},{6,14},... | collective-permute-start | bytes 1572872 | tf_op jit(solution)/shard_map/ppermute | solution.py:96
  19.8 4.2 %slice-start = ((bf16[25,16,128]{2,1,0:T(8,128)(2,1)}), bf16[8,16,128]{2,1,0:T(8,128)(2,1)S(1)}, s32[]{:S(2)}) async-start(bf16[25,16,128]{2,1,0:T(8,128)(2,1)} %copy-done.7), calls=%async_computation | async-start | bytes 65536 | tf_op jit(solution)/shard_map/slice | solution.py:54
  22.4 13.2 %collective-permute-start.1 = (f32[8,16,1024]{2,1,0:T(8,128)}, f32[8,16,1024]{2,1,0:T(8,128)}, u32[]{:S(2)}, u32[]{:S(2)}) collective-permute-start(f32[8,16,1024]{2,1,0:T(8,128)} %constant_dynamic-slice_fusion.2), channel_id=1, source_target_pairs={{0,2},{2,0},{1,3},{3,1},{4,6},{6,4},{5,7},{7,5},{8,10},{10,8},{9,1... | collective-permute-start | bytes 1572872 | tf_op jit(solution)/shard_map/ppermute | solution.py:39
  29.5 12.5 %copy-start.6 = (bf16[4,32,1024]{2,1,0:T(8,128)(2,1)S(1)}, bf16[4,32,1024]{2,1,0:T(8,128)(2,1)}, u32[]{:S(2)}) copy-start(bf16[4,32,1024]{2,1,0:T(8,128)(2,1)} %param.10) | copy-start | bytes 786436
  36.8 13.0 %copy-start.4 = (bf16[128,1024,1]{1,0,2:T(8,128)(2,1)S(1)}, bf16[128,1024,1]{1,0,2:T(8,128)(2,1)}, u32[]{:S(2)}) copy-start(bf16[128,1024,1]{1,0,2:T(8,128)(2,1)} %reshape.76) | copy-start | bytes 786436
  36.8 11.1 %collective-permute-start.2 = (bf16[8,16,1024]{2,1,0:T(8,128)(2,1)S(1)}, bf16[8,16,1024]{2,1,0:T(8,128)(2,1)S(1)}, u32[]{:S(2)}, u32[]{:S(2)}) collective-permute-start(bf16[8,16,1024]{2,1,0:T(8,128)(2,1)S(1)} %subtract_convert_fusion.1), channel_id=1, source_target_pairs={{0,2},{2,0},{1,3},{3,1},{4,6},{6,4},{5,7},{7,5},{8,10},{10,8},{9,1... | collective-permute-start | bytes 786440 | tf_op jit(solution)/shard_map/ppermute | solution.py:43
  44.3 8.7 %collective-permute-start.9 = (bf16[4,32,1024]{2,0,1:T(4,128)(2,1)S(1)}, bf16[4,32,1024]{2,0,1:T(4,128)(2,1)S(1)}, u32[]{:S(2)}, u32[]{:S(2)}) collective-permute-start(bf16[4,32,1024]{2,0,1:T(4,128)(2,1)S(1)} %subtract_convert_fusion), channel_id=1, source_target_pairs={{0,12},{4,0},{8,4},{12,8},{1,13},{5,1},{9,5},{13,9},{2,14},{6,2},{... | collective-permute-start | bytes 786440 | tf_op jit(solution)/shard_map/ppermute | solution.py:101
  47.2 8.0 %collective-permute-start.8 = (bf16[4,32,1024]{2,0,1:T(4,128)(2,1)S(1)}, bf16[4,32,1024]{2,0,1:T(4,128)(2,1)S(1)}, u32[]{:S(2)}, u32[]{:S(2)}) collective-permute-start(bf16[4,32,1024]{2,0,1:T(4,128)(2,1)S(1)} %subtract_convert_fusion), channel_id=1, source_target_pairs={{0,8},{4,12},{8,0},{12,4},{1,9},{5,13},{9,1},{13,5},{2,10},{6,14},... | collective-permute-start | bytes 786440 | tf_op jit(solution)/shard_map/ppermute | solution.py:101
  47.2 14.8 %collective-permute-start.7 = (bf16[4,32,1024]{2,0,1:T(4,128)(2,1)S(1)}, bf16[4,32,1024]{2,0,1:T(4,128)(2,1)S(1)}, u32[]{:S(2)}, u32[]{:S(2)}) collective-permute-start(bf16[4,32,1024]{2,0,1:T(4,128)(2,1)S(1)} %subtract_convert_fusion), channel_id=1, source_target_pairs={{0,4},{4,8},{8,12},{12,0},{1,5},{5,9},{9,13},{13,1},{2,6},{6,10},{... | collective-permute-start | bytes 786440 | tf_op jit(solution)/shard_map/ppermute | solution.py:101
  47.9 14.8 %collective-permute-start.3 = (bf16[16,16,1024]{2,1,0:T(8,128)(2,1)S(1)}, bf16[16,16,1024]{2,1,0:T(8,128)(2,1)S(1)}, u32[]{:S(2)}, u32[]{:S(2)}) collective-permute-start(bf16[16,16,1024]{2,1,0:T(8,128)(2,1)S(1)} %pad_maximum_fusion), channel_id=1, source_target_pairs={{0,1},{1,0},{2,3},{3,2},{4,5},{5,4},{6,7},{7,6},{8,9},{9,8},{10,11... | collective-permute-start | bytes 1572872 | tf_op jit(solution)/shard_map/ppermute | solution.py:43
  61.9 2.2 %copy-start.1 = (f32[32,32,1024]{2,1,0:T(8,128)S(1)}, f32[32,32,1024]{2,1,0:T(8,128)}, u32[]{:S(2)}) copy-start(f32[32,32,1024]{2,1,0:T(8,128)} %param.7) | copy-start | bytes 12582916

commit v3 on v2

--- a/solution.py
+++ b/solution.py
@@ -36,7 +36,8 @@
     half = values.shape[0] // 2
     keep = lax.dynamic_slice_in_dim(values, me * half, half, 0)
     give = lax.dynamic_slice_in_dim(values, (1 - me) * half, half, 0)
-    return keep + lax.ppermute(give, axis, [(0, 1), (1, 0)])
+    got = lax.ppermute(give.astype(jnp.bfloat16), axis, [(0, 1), (1, 0)])
+    return keep + got.astype(jnp.float32)
 
 
 def double(values, axis, me):
@@ -92,8 +93,9 @@
     fwd_z = lax.dynamic_slice_in_dim(partial_z, zq * piece, piece, 0)
     for k in range(1, group):
         dest = (zq + k) % group
-        sent = lax.dynamic_slice_in_dim(partial_z, dest * piece, piece, 0)
-        fwd_z = fwd_z + lax.ppermute(sent, "zq", [(j, (j + k) % group) for j in range(group)])
+        sent = lax.dynamic_slice_in_dim(partial_z, dest * piece, piece, 0).astype(jnp.bfloat16)
+        got = lax.ppermute(sent, "zq", [(j, (j + k) % group) for j in range(group)])
+        fwd_z = fwd_z + got.astype(jnp.float32)
     resid_z = (slices_z.astype(jnp.float32) - fwd_z).astype(jnp.bfloat16)
     pieces = [resid_z]
     rows = [lax.dynamic_slice_in_dim(band_z, zq * piece, piece, 0)]

time: 70.6 us -> 58.7 us (0.83)
  local copies, waits for them, and re-layouts: 11.9 us -> 6.7 us
  waiting for transfers between devices: 19.2 us -> 16.2 us
  matrix products: 14.8 us -> 13.1 us
  other arithmetic: 9.55 us -> 8.07 us
    ppermute x5, waiting for transfers between devices: 7.79 us -> 4.96 us  [the longest x2 4.95 us: halve(): got = lax.ppermute(give.astype(jnp.bfloat16), axis, [(0, 1), (1, 0)])]
    dynamic_slice x3 -> x0, local copies, waits for them, and re-layouts: 2.32 us -> none  [the longest x1 1.4 us: shards(): sent = lax.dynamic_slice_in_dim(partial_z, dest * piece, piece, 0)]
    convert_element_type x0 -> x3, local copies, waits for them, and re-layouts: none -> 2.11 us  [the longest x1 1.2 us: shards(): lax.dynamic_slice_in_dim(partial_z, dest * piece, piece, 0)]
    convert_element_type x1, local copies, waits for them, and re-layouts: 2.03 us -> 0.2 us  [shards(): slices_x.reshape(planes * rows_here, count_x * SLICES).astype(jnp.float32)]
    dot_general x1, matrix products: 2.57 us -> 0.83 us  [shards(): lax.dot_general(flat_coarse, banded_x, (((1,), (1,)), ((), ())), preferre...]
    convert_element_type x1, local copies, waits for them, and re-layouts: 1.16 us -> 0.17 us  [shards(): resid_x = (slices_x.reshape(planes * rows_here, count_x * SLICES).astype(...]
    dynamic_slice x1, local copies, waits for them, and re-layouts: 0.91 us -> 0.09 us  [shards(): rows = [lax.dynamic_slice_in_dim(band_z, zq * piece, piece, 0)]]
    convert_element_type x1, other arithmetic: 0.86 us -> 0.05 us  [shards(): slices_x.reshape(planes * rows_here, count_x * SLICES).astype(jnp.float32)]
  transfers between devices with their start and end apart: 10 -> 10, of which waited for: 6 -> 4; matrix products, arithmetic and copies ran while one was open for 28% -> 19% of each run, Pallas kernels for 0% -> 0%
where the time goes in v3:
time: 58.7 us; the launch traced here: 58.4 us
  waiting for transfers between devices  16.2 us (28%)
  starting transfers between devices  14.1 us (24%)
  matrix products  13.1 us (22%)
  other arithmetic  8.07 us (14%)
  local copies, waits for them, and re-layouts  6.7 us (11%)
    ppermute x3, waiting for transfers between devices, shards(): lax.ppermute(resid_z, 'zq', [(j, (j + k) % group) for j in range(group)])  11.2 us
    dot_general x1, matrix products, shards(): jnp.einsum('sl,zsx->zlx', band_y, resid_y, preferred_element_type=jnp.flo...  5.97 us
    ppermute x2, waiting for transfers between devices, halve(): got = lax.ppermute(give.astype(jnp.bfloat16), axis, [(0, 1), (1, 0)])  4.95 us
    ppermute x2, starting transfers between devices, halve(): got = lax.ppermute(give.astype(jnp.bfloat16), axis, [(0, 1), (1, 0)])  4.9 us
    unnamed x12, local copies, waits for them, and re-layouts  4.01 us
    ppermute x2, starting transfers between devices, double(): other = lax.ppermute(values, axis, [(0, 1), (1, 0)])  3.45 us
    ppermute x3, starting transfers between devices, shards(): lax.ppermute(resid_z, 'zq', [(j, (j + k) % group) for j in range(group)])  3.1 us
    ppermute x3, starting transfers between devices, shards(): got = lax.ppermute(sent, 'zq', [(j, (j + k) % group) for j in range(group)])  2.68 us
  transfers between devices with their start and end apart: 10, of which 4 were waited for; matrix products, arithmetic and copies ran while one was open for 19% of the time, Pallas kernels for 0%

profile of v3, /device:TPU:1, one launch (start us, length us, event | category | flops | bytes accessed | tf_op | source)
XLA Modules:
  0.0 58.4 jit_solution(4374899732835325557)
XLA Ops:
  0.8 1.0 %fusion.25 = f32[25,16,128]{2,0,1:T(8,128)S(1)} fusion(f32[4,16,128]{2,1,0:T(8,128)S(1)} %copy-done, s32[25]{0:T(128)} %param.12), kind=kOutput, calls=%fused_computation.43 | convolution fusion | flops 2457700 | bytes 237668 | tf_op jit(solution)/shard_map/bk,ksl->bsl/dot_general | solution.py:19
  1.7 1.0 %fusion.8 = bf16[25,16,128]{2,1,0:T(8,128)(2,1)S(1)} fusion(s32[25,128]{1,0:T(8,128)S(1)} %add_select_fusion, f32[25,16,128]{2,0,1:T(8,128)S(1)} %fusion.25), kind=kOutput, calls=%fused_computation.11 | convolution fusion | flops 79104000 | bytes 320000 | tf_op jit(solution)/shard_map/bsj,bjl->bsl/dot_general | solution.py:23
  2.8 2.5 %convert_element_type.73 = bf16[32,32,1024]{2,1,0:T(8,128)(2,1)S(1)} convert(f32[32,32,1024]{2,1,0:T(8,128)} %param.7) | non-fusion elementwise | flops 1048576 | bytes 6291456 | tf_op jit(solution)/shard_map/convert_element_type | solution.py:58
  5.8 1.3 %copy-done.2 = f32[16,32,1024]{2,0,1:T(8,128)} copy-done((f32[16,32,1024]{2,0,1:T(8,128)}, f32[16,32,1024]{2,0,1:T(8,128)S(1)}, u32[]{:S(2)}) %copy-start.2) | copy-done | bytes 2097176
  7.1 0.9 %fusion.21 = bf16[16,16,1024]{2,1,0:T(8,128)(2,1)} fusion(f32[16,32,1024]{2,0,1:T(8,128)S(1)} %fusion.42, s32[]{:T(128)S(6)} %select_n.114), kind=kLoop, calls=%fused_computation.26 | loop fusion | bytes 1048580 | tf_op jit(solution)/shard_map/convert_element_type | solution.py:39
  8.0 3.2 %collective-permute-start = (bf16[16,16,1024]{2,1,0:T(8,128)(2,1)}, bf16[16,16,1024]{2,1,0:T(8,128)(2,1)}, u32[]{:S(2)}, u32[]{:S(2)}) collective-permute-start(bf16[16,16,1024]{2,1,0:T(8,128)(2,1)} %fusion.21), channel_id=1, source_target_pairs={{0,1},{1,0},{2,3},{3,2},{4,5},{5,4},{6,7},{7,6},{8,9},{9,8},{10,11... | collective-permute-start | bytes 1572872 | tf_op jit(solution)/shard_map/ppermute | solution.py:39
  11.2 2.4 %fusion.3 = f32[16,32,1024]{2,0,1:T(8,128)S(1)} fusion(bf16[32,32,1024]{2,1,0:T(8,128)(2,1)S(1)} %convert_element_type.73, bf16[16,16,128]{2,1,0:T(8,128)(2,1)S(1)} %slice.14, s32[]{:T(128)S(6)} %select_n.122, s32[]{:T(128)S(6)} %select_n.126), kind=kOutput, calls=%fused_computation.4 | convolution fusion | flops 33554432 | bytes 4198408 | tf_op jit(solution)/shard_map/sl,lyx->syx/dot_general | solution.py:91
  13.6 1.3 %copy-done.3 = f32[16,32,1024]{2,0,1:T(8,128)} copy-done((f32[16,32,1024]{2,0,1:T(8,128)}, f32[16,32,1024]{2,0,1:T(8,128)S(1)}, u32[]{:S(2)}) %copy-start.3) | copy-done | bytes 2097176
  14.9 1.2 %dynamic-slice_convert_fusion.3 = (bf16[4,32,1024]{2,0,1:T(4,128)(2,1)}, bf16[4,32,1024]{2,0,1:T(4,128)(2,1)}, bf16[4,32,1024]{2,0,1:T(4,128)(2,1)S(1)}) fusion(f32[16,32,1024]{2,0,1:T(8,128)S(1)} %fusion.3, s32[]{:T(128)S(6)} %select_n.134, s32[]{:T(128)S(6)} %select_n.128, s32[]{:T(128)S(6)} %select_n.131), kind=kLoop, calls=%fused_computation.31 | loop fusion | bytes 1572876 | tf_op jit(solution)/shard_map/convert_element_type | solution.py:96
  16.1 2.7 %collective-permute-start.6 = (bf16[4,32,1024]{2,0,1:T(4,128)(2,1)}, bf16[4,32,1024]{2,0,1:T(4,128)(2,1)}, u32[]{:S(2)}, u32[]{:S(2)}) collective-permute-start(bf16[4,32,1024]{2,0,1:T(4,128)(2,1)} %get-tuple-element.6), channel_id=1, source_target_pairs={{0,12},{4,0},{8,4},{12,8},{1,13},{5,1},{9,5},{13,9},{2,14},{6,2},{... | collective-permute-start | bytes 786440 | tf_op jit(solution)/shard_map/ppermute | solution.py:97
  19.2 1.5 %bitcast_add_fusion.1 = f32[16,16,1024]{2,1,0:T(8,128)S(1)} fusion(bf16[16,16,1024]{2,1,0:T(8,128)(2,1)} %collective-permute-done, f32[16,32,1024]{2,0,1:T(8,128)} %copy-done.2, s32[]{:T(128)S(6)} %select_n.113), kind=kLoop, calls=%fused_computation.23 | loop fusion | flops 524288 | bytes 2621444 | tf_op jit(solution)/shard_map/add | solution.py:40
  20.8 1.7 %collective-permute-start.1 = (bf16[8,16,1024]{2,1,0:T(8,128)(2,1)S(1)}, bf16[8,16,1024]{2,1,0:T(8,128)(2,1)S(1)}, u32[]{:S(2)}, u32[]{:S(2)}) collective-permute-start(bf16[8,16,1024]{2,1,0:T(8,128)(2,1)S(1)} %dynamic-slice_convert_fusion.4), channel_id=1, source_target_pairs={{0,2},{2,0},{1,3},{3,1},{4,6},{6,4},{5,7},{7,5},{8,10},{10,8},{9,1... | collective-permute-start | bytes 786440 | tf_op jit(solution)/shard_map/ppermute | solution.py:39
  22.5 0.8 %fusion.7 = bf16[1024,128]{0,1:T(8,128)(2,1)S(1)} fusion(f32[1024,128]{0,1:T(8,128)S(1)} %copy.13, bf16[1024,1024]{1,0:T(8,128)(2,1)S(1)} %bitcast.58, bf16[16,8,8,128]{3,2,1,0:T(8,128)(2,1)S(1)} %bitcast.59), kind=kOutput, calls=%fused_computation.10 | convolution fusion | flops 268697600 | bytes 3145728 | tf_op jit(solution)/shard_map/dot_general | solution.py:62
  23.3 4.9 %collective-permute-done.1 = bf16[8,16,1024]{2,1,0:T(8,128)(2,1)S(1)} collective-permute-done((bf16[8,16,1024]{2,1,0:T(8,128)(2,1)S(1)}, bf16[8,16,1024]{2,1,0:T(8,128)(2,1)S(1)}, u32[]{:S(2)}, u32[]{:S(2)}) %collective-permute-start.1) | collective-permute-done | bytes 262176 | tf_op jit(solution)/shard_map/ppermute | solution.py:39
  28.3 1.1 %subtract_convert_fusion.1 = bf16[8,16,1024]{2,1,0:T(8,128)(2,1)S(1)} fusion(bf16[8,16,1024]{2,1,0:T(8,128)(2,1)S(1)} %collective-permute-done.1, f32[16,16,1024]{2,1,0:T(8,128)S(1)} %bitcast_add_fusion.1, s32[]{:T(128)S(6)} %select_n.115, bf16[32,16,1024]{2,1,0:T(8,128)(2,1)} %param.9, s32[]{:T(128)S(6)} %select_n.111), kind=kLoop, calls=%fused_computation.32 | loop fusion | flops 655360 | bytes 1310728 | tf_op jit(solution)/shard_map/convert_element_type | solution.py:81
  29.3 1.4 %collective-permute-start.2 = (bf16[8,16,1024]{2,1,0:T(8,128)(2,1)S(1)}, bf16[8,16,1024]{2,1,0:T(8,128)(2,1)S(1)}, u32[]{:S(2)}, u32[]{:S(2)}) collective-permute-start(bf16[8,16,1024]{2,1,0:T(8,128)(2,1)S(1)} %subtract_convert_fusion.1), channel_id=1, source_target_pairs={{0,2},{2,0},{1,3},{3,1},{4,6},{6,4},{5,7},{7,5},{8,10},{10,8},{9,1... | collective-permute-start | bytes 786440 | tf_op jit(solution)/shard_map/ppermute | solution.py:44
  31.1 1.9 %subtract_convert_fusion = bf16[4,32,1024]{2,0,1:T(4,128)(2,1)S(1)} fusion(bf16[4,32,1024]{2,0,1:T(4,128)(2,1)} %collective-permute-done.6, bf16[4,32,1024]{2,0,1:T(4,128)(2,1)} %collective-permute-done.5, bf16[4,32,1024]{2,0,1:T(4,128)(2,1)} %collective-permute-done.4, f32[16,32,1024]{2,0,1:T(8,128)} %copy-done.3, s32[]{:T(128)S(6)} %select_n.123, ...), kind=kLoop, calls=%fused_computation.28 | loop fusion | flops 1179648 | bytes 1835012 | tf_op jit(solution)/shard_map/convert_element_type | solution.py:99
  33.0 2.4 %collective-permute-start.9 = (bf16[4,32,1024]{2,0,1:T(4,128)(2,1)S(1)}, bf16[4,32,1024]{2,0,1:T(4,128)(2,1)S(1)}, u32[]{:S(2)}, u32[]{:S(2)}) collective-permute-start(bf16[4,32,1024]{2,0,1:T(4,128)(2,1)S(1)} %subtract_convert_fusion), channel_id=1, source_target_pairs={{0,12},{4,0},{8,4},{12,8},{1,13},{5,1},{9,5},{13,9},{2,14},{6,2},{... | collective-permute-start | bytes 786440 | tf_op jit(solution)/shard_map/ppermute | solution.py:103
  36.2 2.1 %collective-permute-start.3 = (bf16[16,16,1024]{2,1,0:T(8,128)(2,1)S(1)}, bf16[16,16,1024]{2,1,0:T(8,128)(2,1)S(1)}, u32[]{:S(2)}, u32[]{:S(2)}) collective-permute-start(bf16[16,16,1024]{2,1,0:T(8,128)(2,1)S(1)} %pad_maximum_fusion), channel_id=1, source_target_pairs={{0,1},{1,0},{2,3},{3,2},{4,5},{5,4},{6,7},{7,6},{8,9},{9,8},{10,11... | collective-permute-start | bytes 1572872 | tf_op jit(solution)/shard_map/ppermute | solution.py:44
  39.0 2.3 %collective-permute-done.9 = bf16[4,32,1024]{2,0,1:T(4,128)(2,1)S(1)} collective-permute-done((bf16[4,32,1024]{2,0,1:T(4,128)(2,1)S(1)}, bf16[4,32,1024]{2,0,1:T(4,128)(2,1)S(1)}, u32[]{:S(2)}, u32[]{:S(2)}) %collective-permute-start.9) | collective-permute-done | bytes 262176 | tf_op jit(solution)/shard_map/ppermute | solution.py:103
  41.3 2.1 %collective-permute-done.8 = bf16[4,32,1024]{2,0,1:T(4,128)(2,1)S(1)} collective-permute-done((bf16[4,32,1024]{2,0,1:T(4,128)(2,1)S(1)}, bf16[4,32,1024]{2,0,1:T(4,128)(2,1)S(1)}, u32[]{:S(2)}, u32[]{:S(2)}) %collective-permute-start.8) | collective-permute-done | bytes 262176 | tf_op jit(solution)/shard_map/ppermute | solution.py:103
  43.5 6.8 %collective-permute-done.7 = bf16[4,32,1024]{2,0,1:T(4,128)(2,1)S(1)} collective-permute-done((bf16[4,32,1024]{2,0,1:T(4,128)(2,1)S(1)}, bf16[4,32,1024]{2,0,1:T(4,128)(2,1)S(1)}, u32[]{:S(2)}, u32[]{:S(2)}) %collective-permute-start.7) | collective-permute-done | bytes 262176 | tf_op jit(solution)/shard_map/ppermute | solution.py:103
  51.1 1.3 %copy-done.1 = f32[32,32,1024]{2,1,0:T(8,128)S(1)} copy-done((f32[32,32,1024]{2,1,0:T(8,128)S(1)}, f32[32,32,1024]{2,1,0:T(8,128)}, u32[]{:S(2)}) %copy-start.1) | copy-done | bytes 4194328
  52.4 6.0 %fusion.2 = f32[32,32,1024]{2,1,0:T(8,128)} fusion(f32[32,32,1024]{2,1,0:T(8,128)S(1)} %copy-done.1, f32[32,32,1024]{2,1,0:T(8,128)S(1)} %fusion.53, f32[32,32,1024]{2,0,1:T(8,128)S(1)} %fusion.12, bf16[16,16,1024]{2,1,0:T(8,128)(2,1)S(1)} %get-tuple-element.9, bf16[16,16,1024]{2,1,0:T(8,128)(2,1)S(1)} %get-tuple-element.8, ...), kind=kOutput, calls=%fused_computation.3 | convolution fusion | flops 38273024 | bytes 17829892 | tf_op jit(solution)/shard_map/sl,zsx->zlx/dot_general | solution.py:84
  (37 shorter events, 4.4 us)
Async XLA Ops:
  0.0 0.8 %copy-start = (f32[4,16,128]{2,1,0:T(8,128)S(1)}, f32[4,16,128]{2,1,0:T(8,128)}, u32[]{:S(2)}) copy-start(f32[4,16,128]{2,1,0:T(8,128)} %param.11) | copy-start | bytes 98308
  5.8 1.3 %copy-start.2 = (f32[16,32,1024]{2,0,1:T(8,128)}, f32[16,32,1024]{2,0,1:T(8,128)S(1)}, u32[]{:S(2)}) copy-start(f32[16,32,1024]{2,0,1:T(8,128)S(1)} %fusion.42) | copy-start | bytes 6291460
  8.0 11.2 %collective-permute-start = (bf16[16,16,1024]{2,1,0:T(8,128)(2,1)}, bf16[16,16,1024]{2,1,0:T(8,128)(2,1)}, u32[]{:S(2)}, u32[]{:S(2)}) collective-permute-start(bf16[16,16,1024]{2,1,0:T(8,128)(2,1)} %fusion.21), channel_id=1, source_target_pairs={{0,1},{1,0},{2,3},{3,2},{4,5},{5,4},{6,7},{7,6},{8,9},{9,8},{10,11... | collective-permute-start | bytes 1572872 | tf_op jit(solution)/shard_map/ppermute | solution.py:39
  11.2 7.6 %copy-start.4 = (bf16[32,32,128]{2,1,0:T(8,128)(2,1)S(1)}, bf16[32,32,128]{2,1,0:T(8,128)(2,1)}, u32[]{:S(2)}) copy-start(bf16[32,32,128]{2,1,0:T(8,128)(2,1)} %param.8) | copy-start | bytes 786436
  13.6 1.3 %copy-start.3 = (f32[16,32,1024]{2,0,1:T(8,128)}, f32[16,32,1024]{2,0,1:T(8,128)S(1)}, u32[]{:S(2)}) copy-start(f32[16,32,1024]{2,0,1:T(8,128)S(1)} %fusion.3) | copy-start | bytes 6291460
  16.1 15.0 %collective-permute-start.4 = (bf16[4,32,1024]{2,0,1:T(4,128)(2,1)}, bf16[4,32,1024]{2,0,1:T(4,128)(2,1)}, u32[]{:S(2)}, u32[]{:S(2)}) collective-permute-start(bf16[4,32,1024]{2,0,1:T(4,128)(2,1)} %get-tuple-element.5), channel_id=1, source_target_pairs={{0,4},{4,8},{8,12},{12,0},{1,5},{5,9},{9,13},{13,1},{2,6},{6,10},{... | collective-permute-start | bytes 786440 | tf_op jit(solution)/shard_map/ppermute | solution.py:97
  16.1 15.0 %collective-permute-start.6 = (bf16[4,32,1024]{2,0,1:T(4,128)(2,1)}, bf16[4,32,1024]{2,0,1:T(4,128)(2,1)}, u32[]{:S(2)}, u32[]{:S(2)}) collective-permute-start(bf16[4,32,1024]{2,0,1:T(4,128)(2,1)} %get-tuple-element.6), channel_id=1, source_target_pairs={{0,12},{4,0},{8,4},{12,8},{1,13},{5,1},{9,5},{13,9},{2,14},{6,2},{... | collective-permute-start | bytes 786440 | tf_op jit(solution)/shard_map/ppermute | solution.py:97
  18.8 12.3 %collective-permute-start.5 = (bf16[4,32,1024]{2,0,1:T(4,128)(2,1)S(1)}, bf16[4,32,1024]{2,0,1:T(4,128)(2,1)}, u32[]{:S(2)}, u32[]{:S(2)}) collective-permute-start(bf16[4,32,1024]{2,0,1:T(4,128)(2,1)S(1)} %get-tuple-element.7), channel_id=1, source_target_pairs={{0,8},{4,12},{8,0},{12,4},{1,9},{5,13},{9,1},{13,5},{2,10},{6,14},... | collective-permute-start | bytes 786440 | tf_op jit(solution)/shard_map/ppermute | solution.py:97
  20.8 7.5 %collective-permute-start.1 = (bf16[8,16,1024]{2,1,0:T(8,128)(2,1)S(1)}, bf16[8,16,1024]{2,1,0:T(8,128)(2,1)S(1)}, u32[]{:S(2)}, u32[]{:S(2)}) collective-permute-start(bf16[8,16,1024]{2,1,0:T(8,128)(2,1)S(1)} %dynamic-slice_convert_fusion.4), channel_id=1, source_target_pairs={{0,2},{2,0},{1,3},{3,1},{4,6},{6,4},{5,7},{7,5},{8,10},{10,8},{9,1... | collective-permute-start | bytes 786440 | tf_op jit(solution)/shard_map/ppermute | solution.py:39
  23.3 7.8 %copy-start.5 = (bf16[4,32,1024]{2,1,0:T(8,128)(2,1)S(1)}, bf16[4,32,1024]{2,1,0:T(8,128)(2,1)}, u32[]{:S(2)}) copy-start(bf16[4,32,1024]{2,1,0:T(8,128)(2,1)} %param.10) | copy-start | bytes 786436
  29.3 6.8 %collective-permute-start.2 = (bf16[8,16,1024]{2,1,0:T(8,128)(2,1)S(1)}, bf16[8,16,1024]{2,1,0:T(8,128)(2,1)S(1)}, u32[]{:S(2)}, u32[]{:S(2)}) collective-permute-start(bf16[8,16,1024]{2,1,0:T(8,128)(2,1)S(1)} %subtract_convert_fusion.1), channel_id=1, source_target_pairs={{0,2},{2,0},{1,3},{3,1},{4,6},{6,4},{5,7},{7,5},{8,10},{10,8},{9,1... | collective-permute-start | bytes 786440 | tf_op jit(solution)/shard_map/ppermute | solution.py:44
  33.0 8.3 %collective-permute-start.9 = (bf16[4,32,1024]{2,0,1:T(4,128)(2,1)S(1)}, bf16[4,32,1024]{2,0,1:T(4,128)(2,1)S(1)}, u32[]{:S(2)}, u32[]{:S(2)}) collective-permute-start(bf16[4,32,1024]{2,0,1:T(4,128)(2,1)S(1)} %subtract_convert_fusion), channel_id=1, source_target_pairs={{0,12},{4,0},{8,4},{12,8},{1,13},{5,1},{9,5},{13,9},{2,14},{6,2},{... | collective-permute-start | bytes 786440 | tf_op jit(solution)/shard_map/ppermute | solution.py:103
  35.5 8.0 %collective-permute-start.8 = (bf16[4,32,1024]{2,0,1:T(4,128)(2,1)S(1)}, bf16[4,32,1024]{2,0,1:T(4,128)(2,1)S(1)}, u32[]{:S(2)}, u32[]{:S(2)}) collective-permute-start(bf16[4,32,1024]{2,0,1:T(4,128)(2,1)S(1)} %subtract_convert_fusion), channel_id=1, source_target_pairs={{0,8},{4,12},{8,0},{12,4},{1,9},{5,13},{9,1},{13,5},{2,10},{6,14},... | collective-permute-start | bytes 786440 | tf_op jit(solution)/shard_map/ppermute | solution.py:103
  35.5 14.8 %collective-permute-start.7 = (bf16[4,32,1024]{2,0,1:T(4,128)(2,1)S(1)}, bf16[4,32,1024]{2,0,1:T(4,128)(2,1)S(1)}, u32[]{:S(2)}, u32[]{:S(2)}) collective-permute-start(bf16[4,32,1024]{2,0,1:T(4,128)(2,1)S(1)} %subtract_convert_fusion), channel_id=1, source_target_pairs={{0,4},{4,8},{8,12},{12,0},{1,5},{5,9},{9,13},{13,1},{2,6},{6,10},{... | collective-permute-start | bytes 786440 | tf_op jit(solution)/shard_map/ppermute | solution.py:103
  36.2 14.8 %collective-permute-start.3 = (bf16[16,16,1024]{2,1,0:T(8,128)(2,1)S(1)}, bf16[16,16,1024]{2,1,0:T(8,128)(2,1)S(1)}, u32[]{:S(2)}, u32[]{:S(2)}) collective-permute-start(bf16[16,16,1024]{2,1,0:T(8,128)(2,1)S(1)} %pad_maximum_fusion), channel_id=1, source_target_pairs={{0,1},{1,0},{2,3},{3,2},{4,5},{5,4},{6,7},{7,6},{8,9},{9,8},{10,11... | collective-permute-start | bytes 1572872 | tf_op jit(solution)/shard_map/ppermute | solution.py:44
  50.2 2.2 %copy-start.1 = (f32[32,32,1024]{2,1,0:T(8,128)S(1)}, f32[32,32,1024]{2,1,0:T(8,128)}, u32[]{:S(2)}) copy-start(f32[32,32,1024]{2,1,0:T(8,128)} %param.7) | copy-start | bytes 12582916

commit v4 on v3

--- a/solution.py
+++ b/solution.py
@@ -30,6 +30,52 @@
     return (along[:, :, None, :] * identity[:, None, :, None]).reshape(
         count * SLICES, count * BLOCK
     )
+
+
+RING = 4
+PLUS = [(j, (j + 1) % RING) for j in range(RING)]
+MINUS = [(j, (j - 1) % RING) for j in range(RING)]
+
+
+def ring_send(values, pairs):
+    return lax.ppermute(values, "zq", pairs)
+
+
+def ring_reduce(partial, me, piece):
+    cut = partial.shape[1] // 2
+
+    def chunk(d):
+        return lax.dynamic_slice_in_dim(partial, ((me + d) % RING) * piece, piece, 0)
+
+    def lo(v):
+        return v[:, :cut]
+
+    def hi(v):
+        return v[:, cut:]
+
+    def wire(v):
+        return v.astype(jnp.bfloat16)
+
+    own, nxt, far, prv = chunk(0), chunk(1), chunk(2), chunk(3)
+    got_p_far = ring_send(wire(lo(far)), PLUS).astype(jnp.float32)
+    got_p_own = ring_send(wire(hi(nxt)), PLUS).astype(jnp.float32)
+    got_m_far = ring_send(wire(hi(far)), MINUS).astype(jnp.float32)
+    got_m_own = ring_send(wire(lo(prv)), MINUS).astype(jnp.float32)
+    got2_p = ring_send(wire(got_p_far + lo(nxt)), PLUS).astype(jnp.float32)
+    got2_m = ring_send(wire(got_m_far + hi(prv)), MINUS).astype(jnp.float32)
+    low = lo(own) + got_m_own + got2_p
+    high = hi(own) + got_p_own + got2_m
+    return jnp.concatenate([low, high], 1)
+
+
+def ring_gather(values):
+    cut = values.shape[1] // 2
+    from_prev = ring_send(values, PLUS)
+    from_next = ring_send(values, MINUS)
+    far_lo = ring_send(from_prev[:, :cut], PLUS)
+    far_hi = ring_send(from_next[:, cut:], MINUS)
+    far = jnp.concatenate([far_lo, far_hi], 1)
+    return [values, from_prev, from_next, far], [0, RING - 1, 1, 2]
 
 
 def halve(values, axis, me):
@@ -90,19 +136,10 @@
     band_z = lax.dynamic_slice_in_dim(mat_z, zq * planes, planes, 1)
     partial_z = jnp.einsum("sl,lyx->syx", band_z, coarse, preferred_element_type=jnp.float32)
     piece = SLICES // group
-    fwd_z = lax.dynamic_slice_in_dim(partial_z, zq * piece, piece, 0)
-    for k in range(1, group):
-        dest = (zq + k) % group
-        sent = lax.dynamic_slice_in_dim(partial_z, dest * piece, piece, 0).astype(jnp.bfloat16)
-        got = lax.ppermute(sent, "zq", [(j, (j + k) % group) for j in range(group)])
-        fwd_z = fwd_z + got.astype(jnp.float32)
+    fwd_z = ring_reduce(partial_z, zq, piece)
     resid_z = (slices_z.astype(jnp.float32) - fwd_z).astype(jnp.bfloat16)
-    pieces = [resid_z]
-    rows = [lax.dynamic_slice_in_dim(band_z, zq * piece, piece, 0)]
-    for k in range(1, group):
-        pieces.append(lax.ppermute(resid_z, "zq", [(j, (j + k) % group) for j in range(group)]))
-        src = (zq - k + group) % group
-        rows.append(lax.dynamic_slice_in_dim(band_z, src * piece, piece, 0))
+    pieces, sources = ring_gather(resid_z)
+    rows = [lax.dynamic_slice_in_dim(band_z, ((zq + d) % group) * piece, piece, 0) for d in sources]
     corr_z = jnp.einsum(
         "sl,syx->lyx",
         jnp.concatenate(rows, 0),

time: 58.7 us -> 68.9 us (1.17)
  waiting for transfers between devices: 16.2 us -> 8.61 us
  matrix products: 13.1 us -> 18.5 us
  other arithmetic: 8.07 us -> 12.6 us
  starting transfers between devices: 14.1 us -> 18.3 us
  local copies, waits for them, and re-layouts: 6.7 us -> 9.94 us
    ppermute x6 -> x10, waiting for transfers between devices: 11.2 us -> 7.39 us  [ring_send(): return lax.ppermute(values, 'zq', pairs)]
    ppermute x2, waiting for transfers between devices: 4.95 us -> 1.22 us  [halve(): got = lax.ppermute(give.astype(jnp.bfloat16), axis, [(0, 1), (1, 0)])]
    ppermute x6 -> x10, starting transfers between devices: 5.78 us -> 9.37 us  [ring_send(): return lax.ppermute(values, 'zq', pairs)]
    add x0 -> x2, other arithmetic: none -> 2.67 us  [the longest x1 1.5 us: ring_reduce(): low = lo(own) + got_m_own + got2_p]
    slice x0 -> x3, local copies, waits for them, and re-layouts: none -> 2.64 us  [the longest x1 0.95 us: ring_gather(): far_hi = ring_send(from_next[:, cut:], MINUS)]
    dot_general x1, matrix products: 5.97 us -> 8.14 us  [shards(): jnp.einsum('sl,zsx->zlx', band_y, resid_y, preferred_element_type=jnp.flo...]
    another operation x0 -> x2, local copies, waits for them, and re-layouts: none -> 2.13 us  [run(): jax.shard_map(shards, mesh=inner, in_specs=(P(slab, rep, None), P(slab, r...]
    dot_general x1, matrix products: 0.69 us -> 2.7 us  [shards(): jnp.dot(resid_x, banded_x, preferred_element_type=jnp.float32)]
  transfers between devices with their start and end apart: 10 -> 14, of which waited for: 4 -> 3; matrix products, arithmetic and copies ran while one was open for 19% -> 31% of each run, Pallas kernels for 0% -> 0%
where the time goes in v4:
time: 68.9 us; the launch traced here: 68.2 us
  matrix products  18.5 us (27%)
  starting transfers between devices  18.3 us (27%)
  other arithmetic  12.6 us (18%)
  local copies, waits for them, and re-layouts  9.94 us (14%)
  waiting for transfers between devices  8.61 us (12%)
    ppermute x10, starting transfers between devices, ring_send(): return lax.ppermute(values, 'zq', pairs)  9.37 us
    dot_general x1, matrix products, shards(): jnp.einsum('sl,zsx->zlx', band_y, resid_y, preferred_element_type=jnp.flo...  8.14 us
    ppermute x10, waiting for transfers between devices, ring_send(): return lax.ppermute(values, 'zq', pairs)  7.39 us
    ppermute x2, starting transfers between devices, halve(): got = lax.ppermute(give.astype(jnp.bfloat16), axis, [(0, 1), (1, 0)])  4.94 us
    ppermute x2, starting transfers between devices, double(): other = lax.ppermute(values, axis, [(0, 1), (1, 0)])  3.96 us
    unnamed x14, local copies, waits for them, and re-layouts  2.97 us
    dot_general x1, matrix products, shards(): jnp.dot(resid_x, banded_x, preferred_element_type=jnp.float32)  2.7 us
    convert_element_type x1, other arithmetic, shards(): coarse = volume.astype(jnp.bfloat16)  2.52 us
  transfers between devices with their start and end apart: 14, of which 3 were waited for; matrix products, arithmetic and copies ran while one was open for 31% of the time, Pallas kernels for 0%

profile of v4, /device:TPU:1, one launch (start us, length us, event | category | flops | bytes accessed | tf_op | source)
XLA Modules:
  0.0 68.2 jit_solution(2756687750229063797)
XLA Ops:
  2.8 2.5 %convert_element_type.83 = bf16[32,32,1024]{2,1,0:T(8,128)(2,1)S(1)} convert(f32[32,32,1024]{2,1,0:T(8,128)} %param.7) | non-fusion elementwise | flops 1048576 | bytes 6291456 | tf_op jit(solution)/shard_map/convert_element_type | solution.py:104
  5.3 2.4 %fusion.3 = f32[16,32,1024]{2,0,1:T(8,128)S(1)} fusion(bf16[32,32,1024]{2,1,0:T(8,128)(2,1)S(1)} %convert_element_type.83, bf16[16,16,128]{2,1,0:T(8,128)(2,1)S(1)} %slice.58, s32[]{:T(128)S(6)} %select_n.128, s32[]{:T(128)S(6)} %select_n.133), kind=kOutput, calls=%fused_computation.4 | convolution fusion | flops 33554432 | bytes 4198408 | tf_op jit(solution)/shard_map/sl,lyx->syx/dot_general | solution.py:137
  7.7 1.3 %copy-done.2 = f32[16,32,1024]{2,0,1:T(8,128)} copy-done((f32[16,32,1024]{2,0,1:T(8,128)}, f32[16,32,1024]{2,0,1:T(8,128)S(1)}, u32[]{:S(2)}) %copy-start.2) | copy-done | bytes 2097176
  9.9 2.1 %collective-permute-start.5 = (bf16[4,16,1024]{2,0,1:T(4,128)(2,1)S(1)}, bf16[4,16,1024]{2,0,1:T(4,128)(2,1)S(1)}, u32[]{:S(2)}, u32[]{:S(2)}) collective-permute-start(bf16[4,16,1024]{2,0,1:T(4,128)(2,1)S(1)} %get-tuple-element.13), channel_id=1, source_target_pairs={{0,4},{4,8},{8,12},{12,0},{1,5},{5,9},{9,13},{13,1},{2,6},{6,10},{... | collective-permute-start | bytes 393224 | tf_op jit(solution)/shard_map/ppermute | solution.py:41
  12.0 1.4 %collective-permute-start.8 = (bf16[4,16,1024]{2,0,1:T(4,128)(2,1)}, bf16[4,16,1024]{2,0,1:T(4,128)(2,1)}, u32[]{:S(2)}, u32[]{:S(2)}) collective-permute-start(bf16[4,16,1024]{2,0,1:T(4,128)(2,1)} %get-tuple-element.14), channel_id=1, source_target_pairs={{0,12},{4,0},{8,4},{12,8},{1,13},{5,1},{9,5},{13,9},{2,14},{6,2},{... | collective-permute-start | bytes 393224 | tf_op jit(solution)/shard_map/ppermute | solution.py:41
  13.4 2.0 %dynamic-slice_convert_fusion.4 = (bf16[4,16,1024]{2,0,1:T(4,128)(2,1)}, bf16[4,16,1024]{2,0,1:T(4,128)(2,1)}) fusion(f32[16,32,1024]{2,0,1:T(8,128)} %copy-done.2, s32[]{:T(128)S(6)} %select_n.135, s32[]{:T(128)S(6)} %select_n.138, s32[]{:T(128)S(6)} %add.187), kind=kLoop, calls=%fused_computation.46 | loop fusion | bytes 524300 | tf_op jit(solution)/shard_map/convert.4 | solution.py:163
  15.4 1.5 %collective-permute-start.4 = (bf16[4,16,1024]{2,0,1:T(4,128)(2,1)}, bf16[4,16,1024]{2,0,1:T(4,128)(2,1)}, u32[]{:S(2)}, u32[]{:S(2)}) collective-permute-start(bf16[4,16,1024]{2,0,1:T(4,128)(2,1)} %get-tuple-element.7), channel_id=1, source_target_pairs={{0,12},{4,0},{8,4},{12,8},{1,13},{5,1},{9,5},{13,9},{2,14},{6,2},{... | collective-permute-start | bytes 393224 | tf_op jit(solution)/shard_map/ppermute | solution.py:41
  17.4 1.3 %copy-done.3 = f32[16,32,1024]{2,0,1:T(8,128)} copy-done((f32[16,32,1024]{2,0,1:T(8,128)}, f32[16,32,1024]{2,0,1:T(8,128)S(1)}, u32[]{:S(2)}) %copy-start.3) | copy-done | bytes 2097176
  19.6 3.4 %collective-permute-start = (bf16[16,16,1024]{2,1,0:T(8,128)(2,1)}, bf16[16,16,1024]{2,1,0:T(8,128)(2,1)}, u32[]{:S(2)}, u32[]{:S(2)}) collective-permute-start(bf16[16,16,1024]{2,1,0:T(8,128)(2,1)} %fusion.23), channel_id=1, source_target_pairs={{0,1},{1,0},{2,3},{3,2},{4,5},{5,4},{6,7},{7,6},{8,9},{9,8},{10,11... | collective-permute-start | bytes 1572872 | tf_op jit(solution)/shard_map/ppermute | solution.py:85
  24.0 1.8 %fusion.29 = bf16[4,16,1024]{2,0,1:T(4,128)(2,1)} fusion(f32[16,32,1024]{2,0,1:T(8,128)} %copy-done.2, s32[]{:T(128)S(6)} %select_n.138, bf16[4,16,1024]{2,0,1:T(4,128)(2,1)S(1)} %collective-permute-done.5), kind=kLoop, calls=%fused_computation.45 | loop fusion | flops 196608 | bytes 524292 | tf_op jit(solution)/shard_map/convert_element_type | solution.py:57
  26.1 6.3 %collective-permute-done.6 = bf16[4,16,1024]{2,0,1:T(4,128)(2,1)} collective-permute-done((bf16[4,16,1024]{2,0,1:T(4,128)(2,1)}, bf16[4,16,1024]{2,0,1:T(4,128)(2,1)}, u32[]{:S(2)}, u32[]{:S(2)}) %collective-permute-start.6) | collective-permute-done | bytes 131104 | tf_op jit(solution)/shard_map/ppermute | solution.py:41
  32.3 1.5 %fusion.30 = (f32[4,16,1024]{2,0,1:T(4,128)S(1)}, bf16[4,16,1024]{2,0,1:T(4,128)(2,1)S(1)}) fusion(f32[16,32,1024]{2,0,1:T(8,128)} %copy-done.2, s32[]{:T(128)S(6)} %select_n.130, bf16[4,16,1024]{2,0,1:T(4,128)(2,1)} %collective-permute-done.6, bf16[4,16,1024]{2,0,1:T(4,128)(2,1)} %collective-permute-done.4, s32[]{:T(128)S(6)} %select_n.135, s32[]{:T(128)S(6)} %add.187, ...), kind=kLoop, calls=%fused_computation.48 | loop fusion | flops 458752 | bytes 1310732 | tf_op jit(solution)/shard_map/add | solution.py:66
  34.0 1.5 %bitcast_add_fusion.1 = f32[16,16,1024]{2,1,0:T(8,128)S(1)} fusion(bf16[16,16,1024]{2,1,0:T(8,128)(2,1)} %collective-permute-done, f32[16,32,1024]{2,0,1:T(8,128)} %copy-done.3, s32[]{:T(128)S(6)} %select_n.119), kind=kLoop, calls=%fused_computation.25 | loop fusion | flops 524288 | bytes 2621444 | tf_op jit(solution)/shard_map/add | solution.py:86
  35.5 1.5 %collective-permute-start.1 = (bf16[8,16,1024]{2,1,0:T(8,128)(2,1)S(1)}, bf16[8,16,1024]{2,1,0:T(8,128)(2,1)S(1)}, u32[]{:S(2)}, u32[]{:S(2)}) collective-permute-start(bf16[8,16,1024]{2,1,0:T(8,128)(2,1)S(1)} %dynamic-slice_convert_fusion.2), channel_id=1, source_target_pairs={{0,2},{2,0},{1,3},{3,1},{4,6},{6,4},{5,7},{7,5},{8,10},{10,8},{9,1... | collective-permute-start | bytes 786440 | tf_op jit(solution)/shard_map/ppermute | solution.py:85
  38.1 1.2 %fusion.28 = f32[4,16,1024]{2,0,1:T(4,128)S(1)} fusion(f32[16,32,1024]{2,0,1:T(8,128)} %copy-done.2, s32[]{:T(128)S(6)} %select_n.130, s32[]{:T(128)S(6)} %add.187, bf16[4,16,1024]{2,0,1:T(4,128)(2,1)S(1)} %collective-permute-done.9, bf16[4,16,1024]{2,0,1:T(4,128)(2,1)} %collective-permute-done.7), kind=kLoop, calls=%fused_computation.43 | loop fusion | flops 262144 | bytes 786440 | tf_op jit(solution)/shard_map/add | solution.py:67
  39.6 1.7 %collective-permute-start.11 = (bf16[4,32,1024]{2,0,1:T(4,128)(2,1)S(1)}, bf16[4,32,1024]{2,0,1:T(4,128)(2,1)}, u32[]{:S(2)}, u32[]{:S(2)}) collective-permute-start(bf16[4,32,1024]{2,0,1:T(4,128)(2,1)S(1)} %fusion.24), channel_id=1, source_target_pairs={{0,12},{4,0},{8,4},{12,8},{1,13},{5,1},{9,5},{13,9},{2,14},{6,2},{... | collective-permute-start | bytes 786440 | tf_op jit(solution)/shard_map/ppermute | solution.py:41
  41.3 1.2 %collective-permute-done.1 = bf16[8,16,1024]{2,1,0:T(8,128)(2,1)S(1)} collective-permute-done((bf16[8,16,1024]{2,1,0:T(8,128)(2,1)S(1)}, bf16[8,16,1024]{2,1,0:T(8,128)(2,1)S(1)}, u32[]{:S(2)}, u32[]{:S(2)}) %collective-permute-start.1) | collective-permute-done | bytes 262176 | tf_op jit(solution)/shard_map/ppermute | solution.py:85
  42.6 1.8 %subtract_convert_fusion = bf16[8,16,1024]{2,1,0:T(8,128)(2,1)} fusion(bf16[8,16,1024]{2,1,0:T(8,128)(2,1)S(1)} %collective-permute-done.1, f32[16,16,1024]{2,1,0:T(8,128)S(1)} %bitcast_add_fusion.1, s32[]{:T(128)S(6)} %select_n.121, bf16[32,16,1024]{2,1,0:T(8,128)(2,1)} %param.9, s32[]{:T(128)S(6)} %select_n.117), kind=kLoop, calls=%fused_computation.33 | loop fusion | flops 655360 | bytes 1310728 | tf_op jit(solution)/shard_map/convert_element_type | solution.py:127
  44.3 1.2 %collective-permute-start.2 = (bf16[8,16,1024]{2,1,0:T(8,128)(2,1)}, bf16[8,16,1024]{2,1,0:T(8,128)(2,1)}, u32[]{:S(2)}, u32[]{:S(2)}) collective-permute-start(bf16[8,16,1024]{2,1,0:T(8,128)(2,1)} %subtract_convert_fusion), channel_id=1, source_target_pairs={{0,2},{2,0},{1,3},{3,1},{4,6},{6,4},{5,7},{7,5},{8,10},{10,8},{9,1... | collective-permute-start | bytes 786440 | tf_op jit(solution)/shard_map/ppermute | solution.py:90
  47.5 2.5 %collective-permute-start.13 = (bf16[4,16,1024]{2,0,1:T(4,128)(2,1)S(1)}, bf16[4,16,1024]{2,0,1:T(4,128)(2,1)S(1)}, u32[]{:S(2)}, u32[]{:S(2)}) collective-permute-start(bf16[4,16,1024]{2,0,1:T(4,128)(2,1)S(1)} %slice.62), channel_id=1, source_target_pairs={{0,12},{4,0},{8,4},{12,8},{1,13},{5,1},{9,5},{13,9},{2,14},{6,2},{... | collective-permute-start | bytes 393224 | tf_op jit(solution)/shard_map/ppermute | solution.py:41
  52.1 2.8 %collective-permute-start.3 = (bf16[16,16,1024]{2,1,0:T(8,128)(2,1)S(1)}, bf16[16,16,1024]{2,1,0:T(8,128)(2,1)S(1)}, u32[]{:S(2)}, u32[]{:S(2)}) collective-permute-start(bf16[16,16,1024]{2,1,0:T(8,128)(2,1)S(1)} %pad_maximum_fusion), channel_id=1, source_target_pairs={{0,1},{1,0},{2,3},{3,2},{4,5},{5,4},{6,7},{7,6},{8,9},{9,8},{10,11... | collective-permute-start | bytes 1572872 | tf_op jit(solution)/shard_map/ppermute | solution.py:90
  54.9 2.7 %fusion.57 = f32[32,32,1024]{2,1,0:T(8,128)} fusion(bf16[32,32,128]{2,1,0:T(8,128)(2,1)S(1)} %bitcast.60, bf16[128,1024,1]{1,0,2:T(8,128)(2,1)S(1)} %copy-done.4), kind=kOutput, calls=%fused_computation.89 | convolution fusion | flops 268435456 | bytes 4718592 | tf_op jit(solution)/shard_map/dot_general | solution.py:114
  57.7 2.0 %fusion.12 = f32[32,32,1024]{2,0,1:T(8,128)S(1)} fusion(bf16[4,16,1024]{2,0,1:T(4,128)(2,1)S(1)} %collective-permute-done.13, bf16[4,16,1024]{2,0,1:T(4,128)(2,1)S(1)} %collective-permute-done.12, bf16[4,32,1024]{2,0,1:T(4,128)(2,1)} %collective-permute-done.11, bf16[4,32,1024]{2,0,1:T(4,128)(2,1)} %collective-permute-done.10, ...), kind=kOutput, calls=%fused_computation.15 | convolution fusion | flops 38801408 | bytes 5243904 | tf_op jit(solution)/shard_map/sl,syx->lyx/dot_general | solution.py:143
  60.0 8.1 %fusion.2 = f32[32,32,1024]{2,1,0:T(8,128)} fusion(f32[32,32,1024]{2,1,0:T(8,128)S(1)} %copy-done.1, f32[32,32,1024]{2,1,0:T(8,128)} %fusion.57, f32[32,32,1024]{2,0,1:T(8,128)S(1)} %fusion.12, bf16[16,16,1024]{2,1,0:T(8,128)(2,1)S(1)} %get-tuple-element.10, bf16[16,16,1024]{2,1,0:T(8,128)(2,1)S(1)} %get-tuple-element.9, bf16[1,16,128]{2,1,0:T(8,128)(2,1)S(1)} %slice.57, ...), kind=kOutput, calls=%fused_computation.3 | convolution fusion | flops 38273024 | bytes 17829892 | tf_op jit(solution)/shard_map/sl,zsx->zlx/dot_general | solution.py:130
  (54 shorter events, 12.3 us)
Async XLA Ops:
  0.0 0.8 %copy-start = (f32[4,16,128]{2,1,0:T(8,128)S(1)}, f32[4,16,128]{2,1,0:T(8,128)}, u32[]{:S(2)}) copy-start(f32[4,16,128]{2,1,0:T(8,128)} %param.11) | copy-start | bytes 98308
  7.7 1.3 %copy-start.2 = (f32[16,32,1024]{2,0,1:T(8,128)}, f32[16,32,1024]{2,0,1:T(8,128)S(1)}, u32[]{:S(2)}) copy-start(f32[16,32,1024]{2,0,1:T(8,128)S(1)} %fusion.3) | copy-start | bytes 6291460
  9.9 14.1 %collective-permute-start.5 = (bf16[4,16,1024]{2,0,1:T(4,128)(2,1)S(1)}, bf16[4,16,1024]{2,0,1:T(4,128)(2,1)S(1)}, u32[]{:S(2)}, u32[]{:S(2)}) collective-permute-start(bf16[4,16,1024]{2,0,1:T(4,128)(2,1)S(1)} %get-tuple-element.13), channel_id=1, source_target_pairs={{0,4},{4,8},{8,12},{12,0},{1,5},{5,9},{9,13},{13,1},{2,6},{6,10},{... | collective-permute-start | bytes 393224 | tf_op jit(solution)/shard_map/ppermute | solution.py:41
  12.0 14.1 %collective-permute-start.8 = (bf16[4,16,1024]{2,0,1:T(4,128)(2,1)}, bf16[4,16,1024]{2,0,1:T(4,128)(2,1)}, u32[]{:S(2)}, u32[]{:S(2)}) collective-permute-start(bf16[4,16,1024]{2,0,1:T(4,128)(2,1)} %get-tuple-element.14), channel_id=1, source_target_pairs={{0,12},{4,0},{8,4},{12,8},{1,13},{5,1},{9,5},{13,9},{2,14},{6,2},{... | collective-permute-start | bytes 393224 | tf_op jit(solution)/shard_map/ppermute | solution.py:41
  15.4 10.6 %collective-permute-start.4 = (bf16[4,16,1024]{2,0,1:T(4,128)(2,1)}, bf16[4,16,1024]{2,0,1:T(4,128)(2,1)}, u32[]{:S(2)}, u32[]{:S(2)}) collective-permute-start(bf16[4,16,1024]{2,0,1:T(4,128)(2,1)} %get-tuple-element.7), channel_id=1, source_target_pairs={{0,12},{4,0},{8,4},{12,8},{1,13},{5,1},{9,5},{13,9},{2,14},{6,2},{... | collective-permute-start | bytes 393224 | tf_op jit(solution)/shard_map/ppermute | solution.py:41
  16.9 20.1 %collective-permute-start.7 = (bf16[4,16,1024]{2,0,1:T(4,128)(2,1)}, bf16[4,16,1024]{2,0,1:T(4,128)(2,1)}, u32[]{:S(2)}, u32[]{:S(2)}) collective-permute-start(bf16[4,16,1024]{2,0,1:T(4,128)(2,1)} %get-tuple-element.8), channel_id=1, source_target_pairs={{0,4},{4,8},{8,12},{12,0},{1,5},{5,9},{9,13},{13,1},{2,6},{6,10},{... | collective-permute-start | bytes 393224 | tf_op jit(solution)/shard_map/ppermute | solution.py:41
  17.4 1.3 %copy-start.3 = (f32[16,32,1024]{2,0,1:T(8,128)}, f32[16,32,1024]{2,0,1:T(8,128)S(1)}, u32[]{:S(2)}) copy-start(f32[16,32,1024]{2,0,1:T(8,128)S(1)} %fusion.49) | copy-start | bytes 6291460
  18.7 7.0 %copy-start.5 = (bf16[32,32,128]{2,1,0:T(8,128)(2,1)S(1)}, bf16[32,32,128]{2,1,0:T(8,128)(2,1)}, u32[]{:S(2)}) copy-start(bf16[32,32,128]{2,1,0:T(8,128)(2,1)} %param.8) | copy-start | bytes 786436
  19.6 14.3 %collective-permute-start = (bf16[16,16,1024]{2,1,0:T(8,128)(2,1)}, bf16[16,16,1024]{2,1,0:T(8,128)(2,1)}, u32[]{:S(2)}, u32[]{:S(2)}) collective-permute-start(bf16[16,16,1024]{2,1,0:T(8,128)(2,1)} %fusion.23), channel_id=1, source_target_pairs={{0,1},{1,0},{2,3},{3,2},{4,5},{5,4},{6,7},{7,6},{8,9},{9,8},{10,11... | collective-permute-start | bytes 1572872 | tf_op jit(solution)/shard_map/ppermute | solution.py:85
  25.8 6.6 %collective-permute-start.6 = (bf16[4,16,1024]{2,0,1:T(4,128)(2,1)}, bf16[4,16,1024]{2,0,1:T(4,128)(2,1)}, u32[]{:S(2)}, u32[]{:S(2)}) collective-permute-start(bf16[4,16,1024]{2,0,1:T(4,128)(2,1)} %fusion.29), channel_id=1, source_target_pairs={{0,4},{4,8},{8,12},{12,0},{1,5},{5,9},{9,13},{13,1},{2,6},{6,10},{... | collective-permute-start | bytes 393224 | tf_op jit(solution)/shard_map/ppermute | solution.py:41
  33.8 5.5 %copy-start.6 = (bf16[4,32,1024]{2,1,0:T(8,128)(2,1)S(1)}, bf16[4,32,1024]{2,1,0:T(8,128)(2,1)}, u32[]{:S(2)}) copy-start(bf16[4,32,1024]{2,1,0:T(8,128)(2,1)} %param.10) | copy-start | bytes 786436
  33.9 4.3 %collective-permute-start.9 = (bf16[4,16,1024]{2,0,1:T(4,128)(2,1)S(1)}, bf16[4,16,1024]{2,0,1:T(4,128)(2,1)S(1)}, u32[]{:S(2)}, u32[]{:S(2)}) collective-permute-start(bf16[4,16,1024]{2,0,1:T(4,128)(2,1)S(1)} %get-tuple-element.6), channel_id=1, source_target_pairs={{0,12},{4,0},{8,4},{12,8},{1,13},{5,1},{9,5},{13,9},{2,14},{6,2},{... | collective-permute-start | bytes 393224 | tf_op jit(solution)/shard_map/ppermute | solution.py:41
  35.5 7.0 %collective-permute-start.1 = (bf16[8,16,1024]{2,1,0:T(8,128)(2,1)S(1)}, bf16[8,16,1024]{2,1,0:T(8,128)(2,1)S(1)}, u32[]{:S(2)}, u32[]{:S(2)}) collective-permute-start(bf16[8,16,1024]{2,1,0:T(8,128)(2,1)S(1)} %dynamic-slice_convert_fusion.2), channel_id=1, source_target_pairs={{0,2},{2,0},{1,3},{3,1},{4,6},{6,4},{5,7},{7,5},{8,10},{10,8},{9,1... | collective-permute-start | bytes 786440 | tf_op jit(solution)/shard_map/ppermute | solution.py:85
  39.6 6.9 %collective-permute-start.11 = (bf16[4,32,1024]{2,0,1:T(4,128)(2,1)S(1)}, bf16[4,32,1024]{2,0,1:T(4,128)(2,1)}, u32[]{:S(2)}, u32[]{:S(2)}) collective-permute-start(bf16[4,32,1024]{2,0,1:T(4,128)(2,1)S(1)} %fusion.24), channel_id=1, source_target_pairs={{0,12},{4,0},{8,4},{12,8},{1,13},{5,1},{9,5},{13,9},{2,14},{6,2},{... | collective-permute-start | bytes 786440 | tf_op jit(solution)/shard_map/ppermute | solution.py:41
  41.3 8.7 %collective-permute-start.10 = (bf16[4,32,1024]{2,0,1:T(4,128)(2,1)S(1)}, bf16[4,32,1024]{2,0,1:T(4,128)(2,1)}, u32[]{:S(2)}, u32[]{:S(2)}) collective-permute-start(bf16[4,32,1024]{2,0,1:T(4,128)(2,1)S(1)} %fusion.24), channel_id=1, source_target_pairs={{0,4},{4,8},{8,12},{12,0},{1,5},{5,9},{9,13},{13,1},{2,6},{6,10},{... | collective-permute-start | bytes 786440 | tf_op jit(solution)/shard_map/ppermute | solution.py:41
  44.3 6.7 %collective-permute-start.2 = (bf16[8,16,1024]{2,1,0:T(8,128)(2,1)}, bf16[8,16,1024]{2,1,0:T(8,128)(2,1)}, u32[]{:S(2)}, u32[]{:S(2)}) collective-permute-start(bf16[8,16,1024]{2,1,0:T(8,128)(2,1)} %subtract_convert_fusion), channel_id=1, source_target_pairs={{0,2},{2,0},{1,3},{3,1},{4,6},{6,4},{5,7},{7,5},{8,10},{10,8},{9,1... | collective-permute-start | bytes 786440 | tf_op jit(solution)/shard_map/ppermute | solution.py:90
  46.3 8.6 %copy-start.4 = (bf16[128,1024,1]{1,0,2:T(8,128)(2,1)S(1)}, bf16[128,1024,1]{1,0,2:T(8,128)(2,1)}, u32[]{:S(2)}) copy-start(bf16[128,1024,1]{1,0,2:T(8,128)(2,1)} %reshape.76) | copy-start | bytes 786436
  47.5 10.2 %collective-permute-start.13 = (bf16[4,16,1024]{2,0,1:T(4,128)(2,1)S(1)}, bf16[4,16,1024]{2,0,1:T(4,128)(2,1)S(1)}, u32[]{:S(2)}, u32[]{:S(2)}) collective-permute-start(bf16[4,16,1024]{2,0,1:T(4,128)(2,1)S(1)} %slice.62), channel_id=1, source_target_pairs={{0,12},{4,0},{8,4},{12,8},{1,13},{5,1},{9,5},{13,9},{2,14},{6,2},{... | collective-permute-start | bytes 393224 | tf_op jit(solution)/shard_map/ppermute | solution.py:41
  50.9 6.8 %collective-permute-start.12 = (bf16[4,16,1024]{2,0,1:T(4,128)(2,1)S(1)}, bf16[4,16,1024]{2,0,1:T(4,128)(2,1)S(1)}, u32[]{:S(2)}, u32[]{:S(2)}) collective-permute-start(bf16[4,16,1024]{2,0,1:T(4,128)(2,1)S(1)} %slice.61), channel_id=1, source_target_pairs={{0,4},{4,8},{8,12},{12,0},{1,5},{5,9},{9,13},{13,1},{2,6},{6,10},{... | collective-permute-start | bytes 393224 | tf_op jit(solution)/shard_map/ppermute | solution.py:41
  52.1 7.5 %collective-permute-start.3 = (bf16[16,16,1024]{2,1,0:T(8,128)(2,1)S(1)}, bf16[16,16,1024]{2,1,0:T(8,128)(2,1)S(1)}, u32[]{:S(2)}, u32[]{:S(2)}) collective-permute-start(bf16[16,16,1024]{2,1,0:T(8,128)(2,1)S(1)} %pad_maximum_fusion), channel_id=1, source_target_pairs={{0,1},{1,0},{2,3},{3,2},{4,5},{5,4},{6,7},{7,6},{8,9},{9,8},{10,11... | collective-permute-start | bytes 1572872 | tf_op jit(solution)/shard_map/ppermute | solution.py:90
  57.7 2.3 %copy-start.1 = (f32[32,32,1024]{2,1,0:T(8,128)S(1)}, f32[32,32,1024]{2,1,0:T(8,128)}, u32[]{:S(2)}) copy-start(f32[32,32,1024]{2,1,0:T(8,128)} %param.7) | copy-start | bytes 12582916

commit v5 on v3

--- a/solution.py
+++ b/solution.py
@@ -73,8 +73,20 @@
     co = lax.axis_index("co")
     rep = zl * 2 + co
     band_y = lax.dynamic_slice_in_dim(along_y[0], rep * rows_here, rows_here, 1)
-    partial_y = jnp.einsum("sl,zlx->zsx", band_y, coarse, preferred_element_type=jnp.float32)
-    fwd_y = halve(partial_y, "co", co)
+    half = planes // 2
+    keep_y = jnp.einsum(
+        "sl,zlx->zsx",
+        band_y,
+        lax.dynamic_slice_in_dim(coarse, co * half, half, 0),
+        preferred_element_type=jnp.float32,
+    )
+    give_y = jnp.einsum(
+        "sl,zlx->zsx",
+        band_y,
+        lax.dynamic_slice_in_dim(coarse, (1 - co) * half, half, 0),
+        preferred_element_type=jnp.float32,
+    ).astype(jnp.bfloat16)
+    fwd_y = keep_y + lax.ppermute(give_y, "co", [(0, 1), (1, 0)]).astype(jnp.float32)
     fwd_y = halve(fwd_y, "zl", zl)
     part_z = planes // 4
     obs_y = lax.dynamic_slice_in_dim(slices_y, (co * 2 + zl) * part_z, part_z, 0)
@@ -88,14 +100,21 @@
     group = lax.axis_size("zq")
     mat_z = lax.dynamic_index_in_dim(along_z, zb, 0, keepdims=False)
     band_z = lax.dynamic_slice_in_dim(mat_z, zq * planes, planes, 1)
-    partial_z = jnp.einsum("sl,lyx->syx", band_z, coarse, preferred_element_type=jnp.float32)
     piece = SLICES // group
-    fwd_z = lax.dynamic_slice_in_dim(partial_z, zq * piece, piece, 0)
+    own_rows = lax.dynamic_slice_in_dim(band_z, zq * piece, piece, 0)
+    fwd_z = jnp.einsum("sl,lyx->syx", own_rows, coarse, preferred_element_type=jnp.float32)
+    far_rows = jnp.concatenate(
+        [lax.dynamic_slice_in_dim(band_z, ((zq + k) % group) * piece, piece, 0) for k in range(1, group)],
+        0,
+    )
+    far_z = jnp.einsum(
+        "sl,lyx->syx", far_rows, coarse, preferred_element_type=jnp.float32
+    ).astype(jnp.bfloat16)
     for k in range(1, group):
-        dest = (zq + k) % group
-        sent = lax.dynamic_slice_in_dim(partial_z, dest * piece, piece, 0).astype(jnp.bfloat16)
+        sent = far_z[(k - 1) * piece : k * piece]
         got = lax.ppermute(sent, "zq", [(j, (j + k) % group) for j in range(group)])
         fwd_z = fwd_z + got.astype(jnp.float32)
+    base, fwd_z = lax.optimization_barrier((volume + step_size * corr_x, fwd_z))
     resid_z = (slices_z.astype(jnp.float32) - fwd_z).astype(jnp.bfloat16)
     pieces = [resid_z]
     rows = [lax.dynamic_slice_in_dim(band_z, zq * piece, piece, 0)]
@@ -110,7 +129,7 @@
         preferred_element_type=jnp.float32,
     )
 
-    return volume + step_size * (corr_x + corr_y + corr_z)
+    return base + step_size * (corr_y + corr_z)
 
 
 def solution(mesh):

time: 58.7 us -> 63.8 us (1.087)
  matrix products: 13.1 us -> 22.6 us
  other arithmetic: 8.07 us -> 4.95 us
  local copies, waits for them, and re-layouts: 6.7 us -> 5.13 us
  starting transfers between devices: 14.1 us -> 15.2 us
  waiting for transfers between devices: 16.2 us -> 15.5 us
    dot_general x2 -> x4, matrix products: 2.85 us -> 8.46 us  [the longest x1 3.54 us: shards(): jnp.einsum('sl,lyx->syx', own_rows, coarse, preferred_element_type=jnp.fl...]
    dot_general x1, matrix products: 0.69 us -> 4.9 us  [shards(): jnp.dot(resid_x, banded_x, preferred_element_type=jnp.float32)]
    ppermute x2 -> x1, waiting for transfers between devices: 4.95 us -> 1.08 us  [halve(): got = lax.ppermute(give.astype(jnp.bfloat16), axis, [(0, 1), (1, 0)])]
    ppermute x2 -> x1, starting transfers between devices: 4.9 us -> 1.63 us  [halve(): got = lax.ppermute(give.astype(jnp.bfloat16), axis, [(0, 1), (1, 0)])]
    ppermute x0 -> x1, starting transfers between devices: none -> 3.2 us  [shards(): lax.ppermute(give_y, 'co', [(0, 1), (1, 0)]).astype(jnp.float32)]
    unnamed x12, local copies, waits for them, and re-layouts: 4.01 us -> 1.36 us
    ppermute x3, waiting for transfers between devices: 11.2 us -> 13 us  [shards(): lax.ppermute(resid_z, 'zq', [(j, (j + k) % group) for j in range(group)])]
    convert_element_type x1, other arithmetic: 1.92 us -> 0.27 us  [shards(): resid_z = (slices_z.astype(jnp.float32) - fwd_z).astype(jnp.bfloat16)]
  transfers between devices with their start and end apart: 10 -> 10, of which waited for: 4 -> 5; matrix products, arithmetic and copies ran while one was open for 19% -> 30% of each run, Pallas kernels for 0% -> 0%
where the time goes in v5:
time: 63.8 us; the launch traced here: 63.5 us
  matrix products  22.6 us (35%)
  waiting for transfers between devices  15.5 us (24%)
  starting transfers between devices  15.2 us (24%)
  local copies, waits for them, and re-layouts  5.13 us (8%)
  other arithmetic  4.95 us (8%)
    ppermute x3, waiting for transfers between devices, shards(): lax.ppermute(resid_z, 'zq', [(j, (j + k) % group) for j in range(group)])  13 us
    dot_general x1, matrix products, shards(): jnp.einsum('sl,zsx->zlx', band_y, resid_y, preferred_element_type=jnp.flo...  5.61 us
    dot_general x1, matrix products, shards(): jnp.dot(resid_x, banded_x, preferred_element_type=jnp.float32)  4.9 us
    ppermute x2, starting transfers between devices, double(): other = lax.ppermute(values, axis, [(0, 1), (1, 0)])  4.08 us
    ppermute x3, starting transfers between devices, shards(): lax.ppermute(resid_z, 'zq', [(j, (j + k) % group) for j in range(group)])  3.57 us
    dot_general x1, matrix products, shards(): jnp.einsum('sl,lyx->syx', own_rows, coarse, preferred_element_type=jnp.fl...  3.54 us
    ppermute x1, starting transfers between devices, shards(): lax.ppermute(give_y, 'co', [(0, 1), (1, 0)]).astype(jnp.float32)  3.2 us
    ppermute x3, starting transfers between devices, shards(): got = lax.ppermute(sent, 'zq', [(j, (j + k) % group) for j in range(group)])  2.68 us
  transfers between devices with their start and end apart: 10, of which 5 were waited for; matrix products, arithmetic and copies ran while one was open for 30% of the time, Pallas kernels for 0%

profile of v5, /device:TPU:1, one launch (start us, length us, event | category | flops | bytes accessed | tf_op | source)
XLA Modules:
  0.0 63.5 jit_solution(11489925040670034291)
XLA Ops:
  0.8 1.0 %fusion.34 = f32[25,16,128]{2,0,1:T(8,128)S(1)} fusion(f32[4,16,128]{2,1,0:T(8,128)S(1)} %copy-done, s32[25]{0:T(128)} %param.12), kind=kOutput, calls=%fused_computation.48 | convolution fusion | flops 2457700 | bytes 237668 | tf_op jit(solution)/shard_map/bk,ksl->bsl/dot_general | solution.py:19
  1.7 1.0 %fusion.13 = bf16[25,16,128]{2,1,0:T(8,128)(2,1)S(1)} fusion(s32[25,128]{1,0:T(8,128)S(1)} %add_select_fusion, f32[25,16,128]{2,0,1:T(8,128)S(1)} %fusion.34), kind=kOutput, calls=%fused_computation.17 | convolution fusion | flops 79104000 | bytes 320000 | tf_op jit(solution)/shard_map/bsj,bjl->bsl/dot_general | solution.py:23
  2.8 2.5 %convert_element_type.67 = bf16[32,32,1024]{2,1,0:T(8,128)(2,1)S(1)} convert(f32[32,32,1024]{2,1,0:T(8,128)} %param.7) | non-fusion elementwise | flops 1048576 | bytes 6291456 | tf_op jit(solution)/shard_map/convert_element_type | solution.py:58
  5.3 1.2 %fusion.11 = bf16[16,16,1024]{2,1,0:T(8,128)(2,1)} fusion(bf16[32,32,1024]{2,1,0:T(8,128)(2,1)S(1)} %convert_element_type.67, s32[]{:T(128)S(6)} %select_n.129, bf16[1,16,128]{2,1,0:T(8,128)(2,1)S(1)} %slice.29, s32[]{:T(128)S(6)} %select_n.128), kind=kOutput, calls=%fused_computation.15 | convolution fusion | flops 17039360 | bytes 1576968 | tf_op jit(solution)/shard_map/sl,zlx->zsx/dot_general | solution.py:83
  6.4 3.2 %collective-permute-start.3 = (bf16[16,16,1024]{2,1,0:T(8,128)(2,1)}, bf16[16,16,1024]{2,1,0:T(8,128)(2,1)}, u32[]{:S(2)}, u32[]{:S(2)}) collective-permute-start(bf16[16,16,1024]{2,1,0:T(8,128)(2,1)} %fusion.11), channel_id=1, source_target_pairs={{0,1},{1,0},{2,3},{3,2},{4,5},{5,4},{6,7},{7,6},{8,9},{9,8},{10,11... | collective-permute-start | bytes 1572872 | tf_op jit(solution)/shard_map/ppermute | solution.py:89
  9.7 2.3 %fusion.7 = bf16[12,32,1024]{2,0,1:T(8,128)(2,1)S(1)} fusion(bf16[32,32,1024]{2,1,0:T(8,128)(2,1)S(1)} %convert_element_type.67, bf16[4,32]{1,0:T(4,128)(2,1)S(1)} %get-tuple-element.17, bf16[4,32]{1,0:T(4,128)(2,1)S(1)} %get-tuple-element.18, bf16[4,32]{1,0:T(4,128)(2,1)S(1)} %get-tuple-element.19), kind=kOutput, calls=%fused_computation.10 | convolution fusion | flops 25561344 | bytes 2884352 | tf_op jit(solution)/shard_map/sl,lyx->syx/dot_general | solution.py:110
  12.1 1.1 %fusion.76 = (bf16[4,32,1024]{2,0,1:T(4,128)(2,1)}, bf16[4,32,1024]{2,0,1:T(4,128)(2,1)}, bf16[4,32,1024]{2,0,1:T(4,128)(2,1)}) fusion(bf16[12,32,1024]{2,0,1:T(8,128)(2,1)S(1)} %fusion.7), kind=kLoop, calls=%fused_computation.92 | loop fusion | bytes 1572864 | tf_op jit(solution)/shard_map/slice | solution.py:114
  13.2 2.7 %collective-permute-start.2 = (bf16[4,32,1024]{2,0,1:T(4,128)(2,1)}, bf16[4,32,1024]{2,0,1:T(4,128)(2,1)}, u32[]{:S(2)}, u32[]{:S(2)}) collective-permute-start(bf16[4,32,1024]{2,0,1:T(4,128)(2,1)} %get-tuple-element.12), channel_id=1, source_target_pairs={{0,12},{4,0},{8,4},{12,8},{1,13},{5,1},{9,5},{13,9},{2,14},{6,2},{... | collective-permute-start | bytes 786440 | tf_op jit(solution)/shard_map/ppermute | solution.py:115
  18.7 1.4 %convert_add_fusion = f32[16,16,1024]{2,1,0:T(8,128)S(1)} fusion(bf16[16,16,1024]{2,1,0:T(8,128)(2,1)} %collective-permute-done.3, bf16[32,32,1024]{2,1,0:T(8,128)(2,1)S(1)} %convert_element_type.67, s32[]{:T(128)S(6)} %select_n.127, bf16[1,16,128]{2,1,0:T(8,128)(2,1)S(1)} %slice.29, s32[]{:T(128)S(6)} %select_n.128), kind=kOutput, calls=%fused_computation.30 | convolution fusion | flops 17301504 | bytes 2625544 | tf_op jit(solution)/shard_map/sl,zlx->zsx/dot_general | solution.py:77
  20.9 1.6 %collective-permute-start.4 = (bf16[8,16,1024]{2,1,0:T(8,128)(2,1)}, bf16[8,16,1024]{2,1,0:T(8,128)(2,1)}, u32[]{:S(2)}, u32[]{:S(2)}) collective-permute-start(bf16[8,16,1024]{2,1,0:T(8,128)(2,1)} %dynamic-slice_convert_fusion), channel_id=1, source_target_pairs={{0,2},{2,0},{1,3},{3,1},{4,6},{6,4},{5,7},{7,5},{8,10},{10,8},{9,1... | collective-permute-start | bytes 786440 | tf_op jit(solution)/shard_map/ppermute | solution.py:39
  22.5 4.9 %multiply_add_fusion = f32[32,32,1024]{2,1,0:T(8,128)} fusion(f32[32,32,1024]{2,1,0:T(8,128)} %param.7, bf16[32,32,128]{2,1,0:T(8,128)(2,1)S(1)} %bitcast.67, bf16[128,1024,1]{1,0,2:T(8,128)(2,1)S(1)} %copy-done.2), kind=kOutput, calls=%fused_computation.3 | convolution fusion | flops 270532608 | bytes 8912896 | tf_op jit(solution)/shard_map/dot_general | solution.py:68
  27.4 1.1 %collective-permute-done.4 = bf16[8,16,1024]{2,1,0:T(8,128)(2,1)} collective-permute-done((bf16[8,16,1024]{2,1,0:T(8,128)(2,1)}, bf16[8,16,1024]{2,1,0:T(8,128)(2,1)}, u32[]{:S(2)}, u32[]{:S(2)}) %collective-permute-start.4) | collective-permute-done | bytes 262176 | tf_op jit(solution)/shard_map/ppermute | solution.py:39
  28.5 1.1 %subtract_convert_fusion.1 = bf16[8,16,1024]{2,1,0:T(8,128)(2,1)S(1)} fusion(bf16[8,16,1024]{2,1,0:T(8,128)(2,1)} %collective-permute-done.4, f32[16,16,1024]{2,1,0:T(8,128)S(1)} %convert_add_fusion, s32[]{:T(128)S(6)} %select_n.130, bf16[32,16,1024]{2,1,0:T(8,128)(2,1)} %param.9, s32[]{:T(128)S(6)} %select_n.126), kind=kLoop, calls=%fused_computation.36 | loop fusion | flops 655360 | bytes 1310728 | tf_op jit(solution)/shard_map/convert_element_type | solution.py:93
  29.6 1.6 %collective-permute-start.5 = (bf16[8,16,1024]{2,1,0:T(8,128)(2,1)S(1)}, bf16[8,16,1024]{2,1,0:T(8,128)(2,1)S(1)}, u32[]{:S(2)}, u32[]{:S(2)}) collective-permute-start(bf16[8,16,1024]{2,1,0:T(8,128)(2,1)S(1)} %subtract_convert_fusion.1), channel_id=1, source_target_pairs={{0,2},{2,0},{1,3},{3,1},{4,6},{6,4},{5,7},{7,5},{8,10},{10,8},{9,1... | collective-permute-start | bytes 786440 | tf_op jit(solution)/shard_map/ppermute | solution.py:44
  31.2 3.5 %convert_add_fusion.1 = f32[4,32,1024]{2,0,1:T(4,128)S(1)} fusion(bf16[4,32,1024]{2,0,1:T(4,128)(2,1)} %collective-permute-done.2, bf16[4,32,1024]{2,0,1:T(4,128)(2,1)} %collective-permute-done.1, bf16[4,32,1024]{2,0,1:T(4,128)(2,1)} %collective-permute-done, bf16[32,32,1024]{2,1,0:T(8,128)(2,1)S(1)} %convert_element_type.67, ...), kind=kOutput, calls=%fused_computation.38 | convolution fusion | flops 9175040 | bytes 3408908 | tf_op jit(solution)/shard_map/sl,lyx->syx/dot_general | solution.py:105
  34.8 1.4 %collective-permute-done.5 = bf16[8,16,1024]{2,1,0:T(8,128)(2,1)S(1)} collective-permute-done((bf16[8,16,1024]{2,1,0:T(8,128)(2,1)S(1)}, bf16[8,16,1024]{2,1,0:T(8,128)(2,1)S(1)}, u32[]{:S(2)}, u32[]{:S(2)}) %collective-permute-start.5) | collective-permute-done | bytes 262176 | tf_op jit(solution)/shard_map/ppermute | solution.py:44
  36.3 2.5 %collective-permute-start.6 = (bf16[16,16,1024]{2,1,0:T(8,128)(2,1)S(1)}, bf16[16,16,1024]{2,1,0:T(8,128)(2,1)S(1)}, u32[]{:S(2)}, u32[]{:S(2)}) collective-permute-start(bf16[16,16,1024]{2,1,0:T(8,128)(2,1)S(1)} %pad_maximum_fusion), channel_id=1, source_target_pairs={{0,1},{1,0},{2,3},{3,2},{4,5},{5,4},{6,7},{7,6},{8,9},{9,8},{10,11... | collective-permute-start | bytes 1572872 | tf_op jit(solution)/shard_map/ppermute | solution.py:44
  39.1 1.2 %collective-permute-start.9 = (bf16[4,32,1024]{2,0,1:T(4,128)(2,1)S(1)}, bf16[4,32,1024]{2,0,1:T(4,128)(2,1)S(1)}, u32[]{:S(2)}, u32[]{:S(2)}) collective-permute-start(bf16[4,32,1024]{2,0,1:T(4,128)(2,1)S(1)} %subtract_convert_fusion), channel_id=1, source_target_pairs={{0,12},{4,0},{8,4},{12,8},{1,13},{5,1},{9,5},{13,9},{2,14},{6,2},{... | collective-permute-start | bytes 786440 | tf_op jit(solution)/shard_map/ppermute | solution.py:122
  40.3 1.6 %collective-permute-start.8 = (bf16[4,32,1024]{2,0,1:T(4,128)(2,1)S(1)}, bf16[4,32,1024]{2,0,1:T(4,128)(2,1)S(1)}, u32[]{:S(2)}, u32[]{:S(2)}) collective-permute-start(bf16[4,32,1024]{2,0,1:T(4,128)(2,1)S(1)} %subtract_convert_fusion), channel_id=1, source_target_pairs={{0,8},{4,12},{8,0},{12,4},{1,9},{5,13},{9,1},{13,5},{2,10},{6,14},... | collective-permute-start | bytes 786440 | tf_op jit(solution)/shard_map/ppermute | solution.py:122
  42.7 4.3 %collective-permute-done.9 = bf16[4,32,1024]{2,0,1:T(4,128)(2,1)S(1)} collective-permute-done((bf16[4,32,1024]{2,0,1:T(4,128)(2,1)S(1)}, bf16[4,32,1024]{2,0,1:T(4,128)(2,1)S(1)}, u32[]{:S(2)}, u32[]{:S(2)}) %collective-permute-start.9) | collective-permute-done | bytes 262176 | tf_op jit(solution)/shard_map/ppermute | solution.py:122
  47.0 2.4 %collective-permute-done.8 = bf16[4,32,1024]{2,0,1:T(4,128)(2,1)S(1)} collective-permute-done((bf16[4,32,1024]{2,0,1:T(4,128)(2,1)S(1)}, bf16[4,32,1024]{2,0,1:T(4,128)(2,1)S(1)}, u32[]{:S(2)}, u32[]{:S(2)}) %collective-permute-start.8) | collective-permute-done | bytes 262176 | tf_op jit(solution)/shard_map/ppermute | solution.py:122
  49.4 6.3 %collective-permute-done.7 = bf16[4,32,1024]{2,0,1:T(4,128)(2,1)S(1)} collective-permute-done((bf16[4,32,1024]{2,0,1:T(4,128)(2,1)S(1)}, bf16[4,32,1024]{2,0,1:T(4,128)(2,1)S(1)}, u32[]{:S(2)}, u32[]{:S(2)}) %collective-permute-start.7) | collective-permute-done | bytes 262176 | tf_op jit(solution)/shard_map/ppermute | solution.py:122
  56.5 1.3 %copy-done.1 = f32[32,32,1024]{2,1,0:T(8,128)S(1)} copy-done((f32[32,32,1024]{2,1,0:T(8,128)S(1)}, f32[32,32,1024]{2,1,0:T(8,128)}, u32[]{:S(2)}) %copy-start.1) | copy-done | bytes 4194328
  57.9 5.6 %fusion.1 = f32[32,32,1024]{2,1,0:T(8,128)} fusion(f32[32,32,1024]{2,1,0:T(8,128)S(1)} %copy-done.1, f32[32,32,1024]{2,0,1:T(8,128)S(1)} %fusion.18, bf16[1,16,128]{2,1,0:T(8,128)(2,1)S(1)} %slice.29, s32[]{:T(128)S(6)} %select_n.128, bf16[16,16,1024]{2,1,0:T(8,128)(2,1)S(1)} %get-tuple-element.10, bf16[16,16,1024]{2,1,0:T(8,128)(2,1)S(1)} %get-tuple-element.9), kind=kOutput, calls=%fused_computation.2 | convolution fusion | flops 37224448 | bytes 13635588 | tf_op jit(solution)/shard_map/sl,zsx->zlx/dot_general | solution.py:96
  (37 shorter events, 6.4 us)
Async XLA Ops:
  0.0 0.8 %copy-start = (f32[4,16,128]{2,1,0:T(8,128)S(1)}, f32[4,16,128]{2,1,0:T(8,128)}, u32[]{:S(2)}) copy-start(f32[4,16,128]{2,1,0:T(8,128)} %param.11) | copy-start | bytes 98308
  6.4 12.3 %collective-permute-start.3 = (bf16[16,16,1024]{2,1,0:T(8,128)(2,1)}, bf16[16,16,1024]{2,1,0:T(8,128)(2,1)}, u32[]{:S(2)}, u32[]{:S(2)}) collective-permute-start(bf16[16,16,1024]{2,1,0:T(8,128)(2,1)} %fusion.11), channel_id=1, source_target_pairs={{0,1},{1,0},{2,3},{3,2},{4,5},{5,4},{6,7},{7,6},{8,9},{9,8},{10,11... | collective-permute-start | bytes 1572872 | tf_op jit(solution)/shard_map/ppermute | solution.py:89
  9.7 7.0 %copy-start.4 = (bf16[32,32,128]{2,1,0:T(8,128)(2,1)S(1)}, bf16[32,32,128]{2,1,0:T(8,128)(2,1)}, u32[]{:S(2)}) copy-start(bf16[32,32,128]{2,1,0:T(8,128)(2,1)} %param.8) | copy-start | bytes 786436
  13.2 18.0 %collective-permute-start = (bf16[4,32,1024]{2,0,1:T(4,128)(2,1)}, bf16[4,32,1024]{2,0,1:T(4,128)(2,1)}, u32[]{:S(2)}, u32[]{:S(2)}) collective-permute-start(bf16[4,32,1024]{2,0,1:T(4,128)(2,1)} %get-tuple-element.11), channel_id=1, source_target_pairs={{0,4},{4,8},{8,12},{12,0},{1,5},{5,9},{9,13},{13,1},{2,6},{6,10},{... | collective-permute-start | bytes 786440 | tf_op jit(solution)/shard_map/ppermute | solution.py:115
  13.2 18.0 %collective-permute-start.2 = (bf16[4,32,1024]{2,0,1:T(4,128)(2,1)}, bf16[4,32,1024]{2,0,1:T(4,128)(2,1)}, u32[]{:S(2)}, u32[]{:S(2)}) collective-permute-start(bf16[4,32,1024]{2,0,1:T(4,128)(2,1)} %get-tuple-element.12), channel_id=1, source_target_pairs={{0,12},{4,0},{8,4},{12,8},{1,13},{5,1},{9,5},{13,9},{2,14},{6,2},{... | collective-permute-start | bytes 786440 | tf_op jit(solution)/shard_map/ppermute | solution.py:115
  15.8 15.4 %collective-permute-start.1 = (bf16[4,32,1024]{2,0,1:T(4,128)(2,1)}, bf16[4,32,1024]{2,0,1:T(4,128)(2,1)}, u32[]{:S(2)}, u32[]{:S(2)}) collective-permute-start(bf16[4,32,1024]{2,0,1:T(4,128)(2,1)} %get-tuple-element.13), channel_id=1, source_target_pairs={{0,8},{4,12},{8,0},{12,4},{1,9},{5,13},{9,1},{13,5},{2,10},{6,14},... | collective-permute-start | bytes 786440 | tf_op jit(solution)/shard_map/ppermute | solution.py:115
  17.8 4.7 %copy-start.2 = (bf16[128,1024,1]{1,0,2:T(8,128)(2,1)S(1)}, bf16[128,1024,1]{1,0,2:T(8,128)(2,1)}, u32[]{:S(2)}) copy-start(bf16[128,1024,1]{1,0,2:T(8,128)(2,1)} %reshape.79) | copy-start | bytes 786436
  18.7 3.8 %copy-start.3 = (bf16[1024,128]{1,0:T(8,128)(2,1)S(1)}, bf16[1024,128]{1,0:T(8,128)(2,1)}, u32[]{:S(2)}) copy-start(bf16[1024,128]{1,0:T(8,128)(2,1)} %copy.15) | copy-start | bytes 786436
  20.9 7.6 %collective-permute-start.4 = (bf16[8,16,1024]{2,1,0:T(8,128)(2,1)}, bf16[8,16,1024]{2,1,0:T(8,128)(2,1)}, u32[]{:S(2)}, u32[]{:S(2)}) collective-permute-start(bf16[8,16,1024]{2,1,0:T(8,128)(2,1)} %dynamic-slice_convert_fusion), channel_id=1, source_target_pairs={{0,2},{2,0},{1,3},{3,1},{4,6},{6,4},{5,7},{7,5},{8,10},{10,8},{9,1... | collective-permute-start | bytes 786440 | tf_op jit(solution)/shard_map/ppermute | solution.py:39
  29.6 9.2 %copy-start.5 = (bf16[4,32,1024]{2,1,0:T(8,128)(2,1)S(1)}, bf16[4,32,1024]{2,1,0:T(8,128)(2,1)}, u32[]{:S(2)}) copy-start(bf16[4,32,1024]{2,1,0:T(8,128)(2,1)} %param.10) | copy-start | bytes 786436
  29.6 6.5 %collective-permute-start.5 = (bf16[8,16,1024]{2,1,0:T(8,128)(2,1)S(1)}, bf16[8,16,1024]{2,1,0:T(8,128)(2,1)S(1)}, u32[]{:S(2)}, u32[]{:S(2)}) collective-permute-start(bf16[8,16,1024]{2,1,0:T(8,128)(2,1)S(1)} %subtract_convert_fusion.1), channel_id=1, source_target_pairs={{0,2},{2,0},{1,3},{3,1},{4,6},{6,4},{5,7},{7,5},{8,10},{10,8},{9,1... | collective-permute-start | bytes 786440 | tf_op jit(solution)/shard_map/ppermute | solution.py:44
  36.3 20.2 %collective-permute-start.6 = (bf16[16,16,1024]{2,1,0:T(8,128)(2,1)S(1)}, bf16[16,16,1024]{2,1,0:T(8,128)(2,1)S(1)}, u32[]{:S(2)}, u32[]{:S(2)}) collective-permute-start(bf16[16,16,1024]{2,1,0:T(8,128)(2,1)S(1)} %pad_maximum_fusion), channel_id=1, source_target_pairs={{0,1},{1,0},{2,3},{3,2},{4,5},{5,4},{6,7},{7,6},{8,9},{9,8},{10,11... | collective-permute-start | bytes 1572872 | tf_op jit(solution)/shard_map/ppermute | solution.py:44
  39.1 7.9 %collective-permute-start.9 = (bf16[4,32,1024]{2,0,1:T(4,128)(2,1)S(1)}, bf16[4,32,1024]{2,0,1:T(4,128)(2,1)S(1)}, u32[]{:S(2)}, u32[]{:S(2)}) collective-permute-start(bf16[4,32,1024]{2,0,1:T(4,128)(2,1)S(1)} %subtract_convert_fusion), channel_id=1, source_target_pairs={{0,12},{4,0},{8,4},{12,8},{1,13},{5,1},{9,5},{13,9},{2,14},{6,2},{... | collective-permute-start | bytes 786440 | tf_op jit(solution)/shard_map/ppermute | solution.py:122
  40.3 9.1 %collective-permute-start.8 = (bf16[4,32,1024]{2,0,1:T(4,128)(2,1)S(1)}, bf16[4,32,1024]{2,0,1:T(4,128)(2,1)S(1)}, u32[]{:S(2)}, u32[]{:S(2)}) collective-permute-start(bf16[4,32,1024]{2,0,1:T(4,128)(2,1)S(1)} %subtract_convert_fusion), channel_id=1, source_target_pairs={{0,8},{4,12},{8,0},{12,4},{1,9},{5,13},{9,1},{13,5},{2,10},{6,14},... | collective-permute-start | bytes 786440 | tf_op jit(solution)/shard_map/ppermute | solution.py:122
  41.9 13.8 %collective-permute-start.7 = (bf16[4,32,1024]{2,0,1:T(4,128)(2,1)S(1)}, bf16[4,32,1024]{2,0,1:T(4,128)(2,1)S(1)}, u32[]{:S(2)}, u32[]{:S(2)}) collective-permute-start(bf16[4,32,1024]{2,0,1:T(4,128)(2,1)S(1)} %subtract_convert_fusion), channel_id=1, source_target_pairs={{0,4},{4,8},{8,12},{12,0},{1,5},{5,9},{9,13},{13,1},{2,6},{6,10},{... | collective-permute-start | bytes 786440 | tf_op jit(solution)/shard_map/ppermute | solution.py:122
  55.7 2.2 %copy-start.1 = (f32[32,32,1024]{2,1,0:T(8,128)S(1)}, f32[32,32,1024]{2,1,0:T(8,128)}, u32[]{:S(2)}) copy-start(f32[32,32,1024]{2,1,0:T(8,128)} %multiply_add_fusion) | copy-start | bytes 12582916

commit v6 on v5

--- a/solution.py
+++ b/solution.py
@@ -114,7 +114,6 @@
         sent = far_z[(k - 1) * piece : k * piece]
         got = lax.ppermute(sent, "zq", [(j, (j + k) % group) for j in range(group)])
         fwd_z = fwd_z + got.astype(jnp.float32)
-    base, fwd_z = lax.optimization_barrier((volume + step_size * corr_x, fwd_z))
     resid_z = (slices_z.astype(jnp.float32) - fwd_z).astype(jnp.bfloat16)
     pieces = [resid_z]
     rows = [lax.dynamic_slice_in_dim(band_z, zq * piece, piece, 0)]
@@ -129,7 +128,7 @@
         preferred_element_type=jnp.float32,
     )
 
-    return base + step_size * (corr_y + corr_z)
+    return volume + step_size * (corr_x + corr_y + corr_z)
 
 
 def solution(mesh):

time: 63.8 us -> 57.6 us (0.903)
  matrix products: 22.6 us -> 18.9 us
  waiting for transfers between devices: 15.5 us -> 12.3 us
  local copies, waits for them, and re-layouts: 5.13 us -> 6.77 us
  starting transfers between devices: 15.2 us -> 14.5 us
    dot_general x1, matrix products: 4.9 us -> 0.69 us  [shards(): jnp.dot(resid_x, banded_x, preferred_element_type=jnp.float32)]
    ppermute x3, waiting for transfers between devices: 13 us -> 9.86 us  [shards(): lax.ppermute(resid_z, 'zq', [(j, (j + k) % group) for j in range(group)])]
    ppermute x2, waiting for transfers between devices: 1.44 us -> 0.01 us  [double(): other = lax.ppermute(values, axis, [(0, 1), (1, 0)])]
    ppermute x1, waiting for transfers between devices: 1.08 us -> 2.45 us  [halve(): got = lax.ppermute(give.astype(jnp.bfloat16), axis, [(0, 1), (1, 0)])]
    ppermute x3, starting transfers between devices: 3.57 us -> 2.34 us  [shards(): lax.ppermute(resid_z, 'zq', [(j, (j + k) % group) for j in range(group)])]
    convert_element_type x1, local copies, waits for them, and re-layouts: 0.2 us -> 1 us  [shards(): slices_x.reshape(planes * rows_here, count_x * SLICES).astype(jnp.float32)]
    dot_general x1, matrix products: 1.15 us -> 0.35 us  [shards(): jnp.einsum('sl,zlx->zsx', band_y, lax.dynamic_slice_in_dim(coarse, (1 - c...]
    dot_general x1, matrix products: 0.83 us -> 1.54 us  [shards(): lax.dot_general(flat_coarse, banded_x, (((1,), (1,)), ((), ())), preferre...]
  transfers between devices with their start and end apart: 10 -> 10, of which waited for: 5 -> 3; matrix products, arithmetic and copies ran while one was open for 30% -> 30% of each run, Pallas kernels for 0% -> 0%
where the time goes in v6:
time: 57.6 us; the launch traced here: 57.3 us
  matrix products  18.9 us (33%)
  starting transfers between devices  14.5 us (25%)
  waiting for transfers between devices  12.3 us (21%)
  local copies, waits for them, and re-layouts  6.77 us (12%)
  other arithmetic  4.7 us (8%)
    ppermute x3, waiting for transfers between devices, shards(): lax.ppermute(resid_z, 'zq', [(j, (j + k) % group) for j in range(group)])  9.86 us
    dot_general x1, matrix products, shards(): jnp.einsum('sl,zsx->zlx', band_y, resid_y, preferred_element_type=jnp.flo...  5.96 us
    ppermute x2, starting transfers between devices, double(): other = lax.ppermute(values, axis, [(0, 1), (1, 0)])  4.52 us
    dot_general x1, matrix products, shards(): jnp.einsum('sl,lyx->syx', own_rows, coarse, preferred_element_type=jnp.fl...  3.82 us
    ppermute x1, starting transfers between devices, shards(): lax.ppermute(give_y, 'co', [(0, 1), (1, 0)]).astype(jnp.float32)  3.29 us
    ppermute x3, starting transfers between devices, shards(): got = lax.ppermute(sent, 'zq', [(j, (j + k) % group) for j in range(group)])  2.68 us
    convert_element_type x1, other arithmetic, shards(): coarse = volume.astype(jnp.bfloat16)  2.52 us
    ppermute x1, waiting for transfers between devices, halve(): got = lax.ppermute(give.astype(jnp.bfloat16), axis, [(0, 1), (1, 0)])  2.45 us
  transfers between devices with their start and end apart: 10, of which 3 were waited for; matrix products, arithmetic and copies ran while one was open for 30% of the time, Pallas kernels for 0%

profile of v6, /device:TPU:1, one launch (start us, length us, event | category | flops | bytes accessed | tf_op | source)
XLA Modules:
  0.0 57.3 jit_solution(8655194808759616922)
XLA Ops:
  0.8 1.0 %fusion.34 = f32[25,16,128]{2,0,1:T(8,128)S(1)} fusion(f32[4,16,128]{2,1,0:T(8,128)S(1)} %copy-done, s32[25]{0:T(128)} %param.12), kind=kOutput, calls=%fused_computation.46 | convolution fusion | flops 2457700 | bytes 237668 | tf_op jit(solution)/shard_map/bk,ksl->bsl/dot_general | solution.py:19
  1.7 1.0 %fusion.14 = bf16[25,16,128]{2,1,0:T(8,128)(2,1)S(1)} fusion(s32[25,128]{1,0:T(8,128)S(1)} %add_select_fusion, f32[25,16,128]{2,0,1:T(8,128)S(1)} %fusion.34), kind=kOutput, calls=%fused_computation.17 | convolution fusion | flops 79104000 | bytes 320000 | tf_op jit(solution)/shard_map/bsj,bjl->bsl/dot_general | solution.py:23
  2.8 2.5 %convert_element_type.67 = bf16[32,32,1024]{2,1,0:T(8,128)(2,1)S(1)} convert(f32[32,32,1024]{2,1,0:T(8,128)} %param.7) | non-fusion elementwise | flops 1048576 | bytes 6291456 | tf_op jit(solution)/shard_map/convert_element_type | solution.py:58
  5.7 3.3 %collective-permute-start = (bf16[16,16,1024]{2,1,0:T(8,128)(2,1)S(1)}, bf16[16,16,1024]{2,1,0:T(8,128)(2,1)}, u32[]{:S(2)}, u32[]{:S(2)}) collective-permute-start(bf16[16,16,1024]{2,1,0:T(8,128)(2,1)S(1)} %fusion.12), channel_id=1, source_target_pairs={{0,1},{1,0},{2,3},{3,2},{4,5},{5,4},{6,7},{7,6},{8,9},{9,8},{10,11... | collective-permute-start | bytes 1572872 | tf_op jit(solution)/shard_map/ppermute | solution.py:89
  9.6 2.3 %fusion.8 = bf16[12,32,1024]{2,0,1:T(8,128)(2,1)S(1)} fusion(bf16[32,32,1024]{2,1,0:T(8,128)(2,1)S(1)} %convert_element_type.67, bf16[4,32]{1,0:T(4,128)(2,1)S(1)} %get-tuple-element.15, bf16[4,32]{1,0:T(4,128)(2,1)S(1)} %get-tuple-element.14, bf16[4,32]{1,0:T(4,128)(2,1)S(1)} %get-tuple-element.13), kind=kOutput, calls=%fused_computation.10 | convolution fusion | flops 25561344 | bytes 2884352 | tf_op jit(solution)/shard_map/sl,lyx->syx/dot_general | solution.py:110
  12.0 1.1 %fusion.72 = (bf16[4,32,1024]{2,0,1:T(4,128)(2,1)}, bf16[4,32,1024]{2,0,1:T(4,128)(2,1)}, bf16[4,32,1024]{2,0,1:T(4,128)(2,1)}) fusion(bf16[12,32,1024]{2,0,1:T(8,128)(2,1)S(1)} %fusion.8), kind=kLoop, calls=%fused_computation.90 | loop fusion | bytes 1572864 | tf_op jit(solution)/shard_map/slice | solution.py:114
  13.0 2.7 %collective-permute-start.6 = (bf16[4,32,1024]{2,0,1:T(4,128)(2,1)}, bf16[4,32,1024]{2,0,1:T(4,128)(2,1)}, u32[]{:S(2)}, u32[]{:S(2)}) collective-permute-start(bf16[4,32,1024]{2,0,1:T(4,128)(2,1)} %get-tuple-element.8), channel_id=1, source_target_pairs={{0,12},{4,0},{8,4},{12,8},{1,13},{5,1},{9,5},{13,9},{2,14},{6,2},{... | collective-permute-start | bytes 786440 | tf_op jit(solution)/shard_map/ppermute | solution.py:115
  15.8 1.0 %copy.14 = f32[1024,128]{0,1:T(8,128)} copy(f32[1024,128]{1,0:T(8,128)S(1)} %bitcast_convert_fusion) | data formatting | bytes 1048576 | tf_op jit(solution)/shard_map/convert_element_type | solution.py:66
  16.9 1.4 %convert_add_fusion = f32[16,16,1024]{2,1,0:T(8,128)S(1)} fusion(bf16[16,16,1024]{2,1,0:T(8,128)(2,1)} %collective-permute-done, bf16[32,32,1024]{2,1,0:T(8,128)(2,1)S(1)} %convert_element_type.67, s32[]{:T(128)S(6)} %select_n.112, bf16[1,16,128]{2,1,0:T(8,128)(2,1)S(1)} %slice.25, s32[]{:T(128)S(6)} %select_n.113), kind=kOutput, calls=%fused_computation.29 | convolution fusion | flops 17301504 | bytes 2625544 | tf_op jit(solution)/shard_map/sl,zlx->zsx/dot_general | solution.py:77
  19.1 1.6 %collective-permute-start.1 = (bf16[8,16,1024]{2,1,0:T(8,128)(2,1)}, bf16[8,16,1024]{2,1,0:T(8,128)(2,1)}, u32[]{:S(2)}, u32[]{:S(2)}) collective-permute-start(bf16[8,16,1024]{2,1,0:T(8,128)(2,1)} %dynamic-slice_convert_fusion), channel_id=1, source_target_pairs={{0,2},{2,0},{1,3},{3,1},{4,6},{6,4},{5,7},{7,5},{8,10},{10,8},{9,1... | collective-permute-start | bytes 786440 | tf_op jit(solution)/shard_map/ppermute | solution.py:39
  20.7 1.5 %fusion.13 = bf16[1024,128]{0,1:T(8,128)(2,1)} fusion(f32[1024,128]{0,1:T(8,128)S(1)} %copy-done.2, bf16[1024,1024]{1,0:T(8,128)(2,1)S(1)} %bitcast.65, bf16[16,8,8,128]{3,2,1,0:T(8,128)(2,1)S(1)} %bitcast.66), kind=kOutput, calls=%fused_computation.16 | convolution fusion | flops 268697600 | bytes 3145728 | tf_op jit(solution)/shard_map/dot_general | solution.py:62
  22.2 0.8 %reshape.79 = bf16[128,1024,1]{1,0,2:T(8,128)(2,1)} reshape(bf16[8,16,8,128]{3,2,1,0:T(8,128)(2,1)S(1)} %broadcast_multiply_fusion) | data formatting | bytes 524288 | tf_op jit(solution)/shard_map/mul | solution.py:30
  23.0 1.1 %copy.15 = bf16[1024,128]{1,0:T(8,128)(2,1)S(1)} copy(bf16[1024,128]{0,1:T(8,128)(2,1)} %fusion.13) | data formatting | bytes 524288 | tf_op jit(solution)/shard_map/convert_element_type | solution.py:67
  24.2 2.5 %collective-permute-done.1 = bf16[8,16,1024]{2,1,0:T(8,128)(2,1)} collective-permute-done((bf16[8,16,1024]{2,1,0:T(8,128)(2,1)}, bf16[8,16,1024]{2,1,0:T(8,128)(2,1)}, u32[]{:S(2)}, u32[]{:S(2)}) %collective-permute-start.1) | collective-permute-done | bytes 262176 | tf_op jit(solution)/shard_map/ppermute | solution.py:39
  26.6 1.1 %subtract_convert_fusion.1 = bf16[8,16,1024]{2,1,0:T(8,128)(2,1)S(1)} fusion(bf16[8,16,1024]{2,1,0:T(8,128)(2,1)} %collective-permute-done.1, f32[16,16,1024]{2,1,0:T(8,128)S(1)} %convert_add_fusion, s32[]{:T(128)S(6)} %select_n.115, bf16[32,16,1024]{2,1,0:T(8,128)(2,1)} %param.9, s32[]{:T(128)S(6)} %select_n.111), kind=kLoop, calls=%fused_computation.35 | loop fusion | flops 655360 | bytes 1310728 | tf_op jit(solution)/shard_map/convert_element_type | solution.py:93
  27.8 1.6 %collective-permute-start.2 = (bf16[8,16,1024]{2,1,0:T(8,128)(2,1)S(1)}, bf16[8,16,1024]{2,1,0:T(8,128)(2,1)S(1)}, u32[]{:S(2)}, u32[]{:S(2)}) collective-permute-start(bf16[8,16,1024]{2,1,0:T(8,128)(2,1)S(1)} %subtract_convert_fusion.1), channel_id=1, source_target_pairs={{0,2},{2,0},{1,3},{3,1},{4,6},{6,4},{5,7},{7,5},{8,10},{10,8},{9,1... | collective-permute-start | bytes 786440 | tf_op jit(solution)/shard_map/ppermute | solution.py:44
  29.3 3.8 %subtract_convert_fusion = bf16[4,32,1024]{2,0,1:T(4,128)(2,1)S(1)} fusion(bf16[4,32,1024]{2,0,1:T(4,128)(2,1)} %collective-permute-done.6, bf16[4,32,1024]{2,0,1:T(4,128)(2,1)} %collective-permute-done.5, bf16[4,32,1024]{2,0,1:T(4,128)(2,1)} %collective-permute-done.4, bf16[4,32,1024]{2,1,0:T(8,128)(2,1)} %param.10, ...), kind=kOutput, calls=%fused_computation.34 | convolution fusion | flops 9568256 | bytes 3408908 | tf_op jit(solution)/shard_map/sl,lyx->syx/dot_general | solution.py:105
  33.2 1.1 %collective-permute-start.9 = (bf16[4,32,1024]{2,0,1:T(4,128)(2,1)S(1)}, bf16[4,32,1024]{2,0,1:T(4,128)(2,1)S(1)}, u32[]{:S(2)}, u32[]{:S(2)}) collective-permute-start(bf16[4,32,1024]{2,0,1:T(4,128)(2,1)S(1)} %subtract_convert_fusion), channel_id=1, source_target_pairs={{0,12},{4,0},{8,4},{12,8},{1,13},{5,1},{9,5},{13,9},{2,14},{6,2},{... | collective-permute-start | bytes 786440 | tf_op jit(solution)/shard_map/ppermute | solution.py:121
  34.2 1.2 %collective-permute-start.8 = (bf16[4,32,1024]{2,0,1:T(4,128)(2,1)S(1)}, bf16[4,32,1024]{2,0,1:T(4,128)(2,1)S(1)}, u32[]{:S(2)}, u32[]{:S(2)}) collective-permute-start(bf16[4,32,1024]{2,0,1:T(4,128)(2,1)S(1)} %subtract_convert_fusion), channel_id=1, source_target_pairs={{0,8},{4,12},{8,0},{12,4},{1,9},{5,13},{9,1},{13,5},{2,10},{6,14},... | collective-permute-start | bytes 786440 | tf_op jit(solution)/shard_map/ppermute | solution.py:121
  35.6 3.0 %collective-permute-start.3 = (bf16[16,16,1024]{2,1,0:T(8,128)(2,1)S(1)}, bf16[16,16,1024]{2,1,0:T(8,128)(2,1)S(1)}, u32[]{:S(2)}, u32[]{:S(2)}) collective-permute-start(bf16[16,16,1024]{2,1,0:T(8,128)(2,1)S(1)} %pad_maximum_fusion), channel_id=1, source_target_pairs={{0,1},{1,0},{2,3},{3,2},{4,5},{5,4},{6,7},{7,6},{8,9},{9,8},{10,11... | collective-permute-start | bytes 1572872 | tf_op jit(solution)/shard_map/ppermute | solution.py:44
  39.3 2.2 %collective-permute-done.8 = bf16[4,32,1024]{2,0,1:T(4,128)(2,1)S(1)} collective-permute-done((bf16[4,32,1024]{2,0,1:T(4,128)(2,1)S(1)}, bf16[4,32,1024]{2,0,1:T(4,128)(2,1)S(1)}, u32[]{:S(2)}, u32[]{:S(2)}) %collective-permute-start.8) | collective-permute-done | bytes 262176 | tf_op jit(solution)/shard_map/ppermute | solution.py:121
  41.5 7.7 %collective-permute-done.7 = bf16[4,32,1024]{2,0,1:T(4,128)(2,1)S(1)} collective-permute-done((bf16[4,32,1024]{2,0,1:T(4,128)(2,1)S(1)}, bf16[4,32,1024]{2,0,1:T(4,128)(2,1)S(1)}, u32[]{:S(2)}, u32[]{:S(2)}) %collective-permute-start.7) | collective-permute-done | bytes 262176 | tf_op jit(solution)/shard_map/ppermute | solution.py:121
  50.0 1.3 %copy-done.1 = f32[32,32,1024]{2,1,0:T(8,128)S(1)} copy-done((f32[32,32,1024]{2,1,0:T(8,128)S(1)}, f32[32,32,1024]{2,1,0:T(8,128)}, u32[]{:S(2)}) %copy-start.1) | copy-done | bytes 4194328
  51.3 6.0 %fusion.2 = f32[32,32,1024]{2,1,0:T(8,128)} fusion(f32[32,32,1024]{2,1,0:T(8,128)S(1)} %copy-done.1, f32[32,32,1024]{2,1,0:T(8,128)S(1)} %fusion.73, f32[32,32,1024]{2,0,1:T(8,128)S(1)} %fusion.18, bf16[16,16,1024]{2,1,0:T(8,128)(2,1)S(1)} %get-tuple-element.6, bf16[16,16,1024]{2,1,0:T(8,128)(2,1)S(1)} %get-tuple-element.5, ...), kind=kOutput, calls=%fused_computation.3 | convolution fusion | flops 38273024 | bytes 17829892 | tf_op jit(solution)/shard_map/sl,zsx->zlx/dot_general | solution.py:96
  (36 shorter events, 4.4 us)
Async XLA Ops:
  0.0 0.8 %copy-start = (f32[4,16,128]{2,1,0:T(8,128)S(1)}, f32[4,16,128]{2,1,0:T(8,128)}, u32[]{:S(2)}) copy-start(f32[4,16,128]{2,1,0:T(8,128)} %param.11) | copy-start | bytes 98308
  5.7 11.2 %collective-permute-start = (bf16[16,16,1024]{2,1,0:T(8,128)(2,1)S(1)}, bf16[16,16,1024]{2,1,0:T(8,128)(2,1)}, u32[]{:S(2)}, u32[]{:S(2)}) collective-permute-start(bf16[16,16,1024]{2,1,0:T(8,128)(2,1)S(1)} %fusion.12), channel_id=1, source_target_pairs={{0,1},{1,0},{2,3},{3,2},{4,5},{5,4},{6,7},{7,6},{8,9},{9,8},{10,11... | collective-permute-start | bytes 1572872 | tf_op jit(solution)/shard_map/ppermute | solution.py:89
  9.6 6.1 %copy-start.4 = (bf16[32,32,128]{2,1,0:T(8,128)(2,1)S(1)}, bf16[32,32,128]{2,1,0:T(8,128)(2,1)}, u32[]{:S(2)}) copy-start(bf16[32,32,128]{2,1,0:T(8,128)(2,1)} %param.8) | copy-start | bytes 786436
  13.0 16.3 %collective-permute-start.4 = (bf16[4,32,1024]{2,0,1:T(4,128)(2,1)}, bf16[4,32,1024]{2,0,1:T(4,128)(2,1)}, u32[]{:S(2)}, u32[]{:S(2)}) collective-permute-start(bf16[4,32,1024]{2,0,1:T(4,128)(2,1)} %get-tuple-element.7), channel_id=1, source_target_pairs={{0,4},{4,8},{8,12},{12,0},{1,5},{5,9},{9,13},{13,1},{2,6},{6,10},{... | collective-permute-start | bytes 786440 | tf_op jit(solution)/shard_map/ppermute | solution.py:115
  13.0 16.3 %collective-permute-start.6 = (bf16[4,32,1024]{2,0,1:T(4,128)(2,1)}, bf16[4,32,1024]{2,0,1:T(4,128)(2,1)}, u32[]{:S(2)}, u32[]{:S(2)}) collective-permute-start(bf16[4,32,1024]{2,0,1:T(4,128)(2,1)} %get-tuple-element.8), channel_id=1, source_target_pairs={{0,12},{4,0},{8,4},{12,8},{1,13},{5,1},{9,5},{13,9},{2,14},{6,2},{... | collective-permute-start | bytes 786440 | tf_op jit(solution)/shard_map/ppermute | solution.py:115
  15.7 13.6 %collective-permute-start.5 = (bf16[4,32,1024]{2,0,1:T(4,128)(2,1)}, bf16[4,32,1024]{2,0,1:T(4,128)(2,1)}, u32[]{:S(2)}, u32[]{:S(2)}) collective-permute-start(bf16[4,32,1024]{2,0,1:T(4,128)(2,1)} %get-tuple-element.9), channel_id=1, source_target_pairs={{0,8},{4,12},{8,0},{12,4},{1,9},{5,13},{9,1},{13,5},{2,10},{6,14},... | collective-permute-start | bytes 786440 | tf_op jit(solution)/shard_map/ppermute | solution.py:115
  16.8 3.9 %copy-start.2 = (f32[1024,128]{0,1:T(8,128)S(1)}, f32[1024,128]{0,1:T(8,128)}, u32[]{:S(2)}) copy-start(f32[1024,128]{0,1:T(8,128)} %copy.14) | copy-start | bytes 1572868
  19.1 7.5 %collective-permute-start.1 = (bf16[8,16,1024]{2,1,0:T(8,128)(2,1)}, bf16[8,16,1024]{2,1,0:T(8,128)(2,1)}, u32[]{:S(2)}, u32[]{:S(2)}) collective-permute-start(bf16[8,16,1024]{2,1,0:T(8,128)(2,1)} %dynamic-slice_convert_fusion), channel_id=1, source_target_pairs={{0,2},{2,0},{1,3},{3,1},{4,6},{6,4},{5,7},{7,5},{8,10},{10,8},{9,1... | collective-permute-start | bytes 786440 | tf_op jit(solution)/shard_map/ppermute | solution.py:39
  27.8 7.8 %collective-permute-start.2 = (bf16[8,16,1024]{2,1,0:T(8,128)(2,1)S(1)}, bf16[8,16,1024]{2,1,0:T(8,128)(2,1)S(1)}, u32[]{:S(2)}, u32[]{:S(2)}) collective-permute-start(bf16[8,16,1024]{2,1,0:T(8,128)(2,1)S(1)} %subtract_convert_fusion.1), channel_id=1, source_target_pairs={{0,2},{2,0},{1,3},{3,1},{4,6},{6,4},{5,7},{7,5},{8,10},{10,8},{9,1... | collective-permute-start | bytes 786440 | tf_op jit(solution)/shard_map/ppermute | solution.py:44
  33.2 5.4 %copy-start.3 = (bf16[128,1024,1]{1,0,2:T(8,128)(2,1)S(1)}, bf16[128,1024,1]{1,0,2:T(8,128)(2,1)}, u32[]{:S(2)}) copy-start(bf16[128,1024,1]{1,0,2:T(8,128)(2,1)} %reshape.79) | copy-start | bytes 786436
  33.2 6.1 %collective-permute-start.9 = (bf16[4,32,1024]{2,0,1:T(4,128)(2,1)S(1)}, bf16[4,32,1024]{2,0,1:T(4,128)(2,1)S(1)}, u32[]{:S(2)}, u32[]{:S(2)}) collective-permute-start(bf16[4,32,1024]{2,0,1:T(4,128)(2,1)S(1)} %subtract_convert_fusion), channel_id=1, source_target_pairs={{0,12},{4,0},{8,4},{12,8},{1,13},{5,1},{9,5},{13,9},{2,14},{6,2},{... | collective-permute-start | bytes 786440 | tf_op jit(solution)/shard_map/ppermute | solution.py:121
  34.2 7.3 %collective-permute-start.8 = (bf16[4,32,1024]{2,0,1:T(4,128)(2,1)S(1)}, bf16[4,32,1024]{2,0,1:T(4,128)(2,1)S(1)}, u32[]{:S(2)}, u32[]{:S(2)}) collective-permute-start(bf16[4,32,1024]{2,0,1:T(4,128)(2,1)S(1)} %subtract_convert_fusion), channel_id=1, source_target_pairs={{0,8},{4,12},{8,0},{12,4},{1,9},{5,13},{9,1},{13,5},{2,10},{6,14},... | collective-permute-start | bytes 786440 | tf_op jit(solution)/shard_map/ppermute | solution.py:121
  35.4 13.7 %collective-permute-start.7 = (bf16[4,32,1024]{2,0,1:T(4,128)(2,1)S(1)}, bf16[4,32,1024]{2,0,1:T(4,128)(2,1)S(1)}, u32[]{:S(2)}, u32[]{:S(2)}) collective-permute-start(bf16[4,32,1024]{2,0,1:T(4,128)(2,1)S(1)} %subtract_convert_fusion), channel_id=1, source_target_pairs={{0,4},{4,8},{8,12},{12,0},{1,5},{5,9},{9,13},{13,1},{2,6},{6,10},{... | collective-permute-start | bytes 786440 | tf_op jit(solution)/shard_map/ppermute | solution.py:121
  35.6 14.3 %collective-permute-start.3 = (bf16[16,16,1024]{2,1,0:T(8,128)(2,1)S(1)}, bf16[16,16,1024]{2,1,0:T(8,128)(2,1)S(1)}, u32[]{:S(2)}, u32[]{:S(2)}) collective-permute-start(bf16[16,16,1024]{2,1,0:T(8,128)(2,1)S(1)} %pad_maximum_fusion), channel_id=1, source_target_pairs={{0,1},{1,0},{2,3},{3,2},{4,5},{5,4},{6,7},{7,6},{8,9},{9,8},{10,11... | collective-permute-start | bytes 1572872 | tf_op jit(solution)/shard_map/ppermute | solution.py:44
  38.6 10.6 %copy-start.5 = (bf16[4,32]{1,0:T(4,128)(2,1)S(1)}, bf16[4,32]{1,0:T(4,128)(2,1)}, u32[]{:S(2)}) copy-start(bf16[4,32]{1,0:T(4,128)(2,1)} %get-tuple-element.12) | copy-start | bytes 772
  49.1 2.2 %copy-start.1 = (f32[32,32,1024]{2,1,0:T(8,128)S(1)}, f32[32,32,1024]{2,1,0:T(8,128)}, u32[]{:S(2)}) copy-start(f32[32,32,1024]{2,1,0:T(8,128)} %param.7) | copy-start | bytes 12582916

commit v7 on v6

--- a/solution.py
+++ b/solution.py
@@ -69,6 +69,15 @@
         planes, rows_here, width
     )
 
+    zb = lax.axis_index("zb")
+    zq = lax.axis_index("zq")
+    group = lax.axis_size("zq")
+    mat_z = lax.dynamic_index_in_dim(along_z, zb, 0, keepdims=False)
+    band_z = lax.dynamic_slice_in_dim(mat_z, zq * planes, planes, 1)
+    piece = SLICES // group
+    own_rows = lax.dynamic_slice_in_dim(band_z, zq * piece, piece, 0)
+    own_z = jnp.einsum("sl,lyx->syx", own_rows, coarse, preferred_element_type=jnp.float32)
+
     zl = lax.axis_index("zl")
     co = lax.axis_index("co")
     rep = zl * 2 + co
@@ -86,8 +95,9 @@
         lax.dynamic_slice_in_dim(coarse, (1 - co) * half, half, 0),
         preferred_element_type=jnp.float32,
     ).astype(jnp.bfloat16)
-    fwd_y = keep_y + lax.ppermute(give_y, "co", [(0, 1), (1, 0)]).astype(jnp.float32)
-    fwd_y = halve(fwd_y, "zl", zl)
+    got_y = lax.ppermute(give_y, "co", [(0, 1), (1, 0)])
+    own_z, got_y = lax.optimization_barrier((own_z, got_y))
+    fwd_y = halve(keep_y + got_y.astype(jnp.float32), "zl", zl)
     part_z = planes // 4
     obs_y = lax.dynamic_slice_in_dim(slices_y, (co * 2 + zl) * part_z, part_z, 0)
     resid_y = (obs_y.astype(jnp.float32) - fwd_y).astype(jnp.bfloat16)
@@ -95,14 +105,6 @@
     resid_y = double(resid_y, "co", co)
     corr_y = jnp.einsum("sl,zsx->zlx", band_y, resid_y, preferred_element_type=jnp.float32)
 
-    zb = lax.axis_index("zb")
-    zq = lax.axis_index("zq")
-    group = lax.axis_size("zq")
-    mat_z = lax.dynamic_index_in_dim(along_z, zb, 0, keepdims=False)
-    band_z = lax.dynamic_slice_in_dim(mat_z, zq * planes, planes, 1)
-    piece = SLICES // group
-    own_rows = lax.dynamic_slice_in_dim(band_z, zq * piece, piece, 0)
-    fwd_z = jnp.einsum("sl,lyx->syx", own_rows, coarse, preferred_element_type=jnp.float32)
     far_rows = jnp.concatenate(
         [lax.dynamic_slice_in_dim(band_z, ((zq + k) % group) * piece, piece, 0) for k in range(1, group)],
         0,
@@ -110,6 +112,7 @@
     far_z = jnp.einsum(
         "sl,lyx->syx", far_rows, coarse, preferred_element_type=jnp.float32
     ).astype(jnp.bfloat16)
+    fwd_z = own_z
     for k in range(1, group):
         sent = far_z[(k - 1) * piece : k * piece]
         got = lax.ppermute(sent, "zq", [(j, (j + k) % group) for j in range(group)])

time: 57.6 us -> 64.2 us (1.11)
  other arithmetic: 4.7 us -> 9.61 us
  local copies, waits for them, and re-layouts: 6.77 us -> 8.88 us
  matrix products: 18.9 us -> 17.9 us
  waiting for transfers between devices: 12.3 us -> 13.2 us
    convert_element_type x0 -> x1, other arithmetic: none -> 1.53 us  [shards(): resid_z = (slices_z.astype(jnp.float32) - fwd_z).astype(jnp.bfloat16)]
    add x0 -> x1, other arithmetic: none -> 1.28 us  [shards(): fwd_y = halve(keep_y + got_y.astype(jnp.float32), 'zl', zl)]
    ppermute x2, waiting for transfers between devices: 0.01 us -> 1.11 us  [double(): other = lax.ppermute(values, axis, [(0, 1), (1, 0)])]
    dot_general x1, matrix products: 1.43 us -> 0.35 us  [shards(): jnp.einsum('sl,zlx->zsx', band_y, lax.dynamic_slice_in_dim(coarse, co * h...]
    convert_element_type x1, local copies, waits for them, and re-layouts: 1 us -> 2.05 us  [shards(): slices_x.reshape(planes * rows_here, count_x * SLICES).astype(jnp.float32)]
    unnamed x12 -> x20, local copies, waits for them, and re-layouts: 1.36 us -> 2.33 us
    ppermute x3, waiting for transfers between devices: 9.86 us -> 8.92 us  [shards(): lax.ppermute(resid_z, 'zq', [(j, (j + k) % group) for j in range(group)])]
    dot_general x1, matrix products: 0.35 us -> 1.16 us  [shards(): jnp.einsum('sl,zlx->zsx', band_y, lax.dynamic_slice_in_dim(coarse, (1 - c...]
  transfers between devices with their start and end apart: 10 -> 10, of which waited for: 3 -> 4; matrix products, arithmetic and copies ran while one was open for 30% -> 34% of each run, Pallas kernels for 0% -> 0%
where the time goes in v7:
time: 64.2 us; the launch traced here: 63.8 us
  matrix products  17.9 us (28%)
  starting transfers between devices  13.9 us (22%)
  waiting for transfers between devices  13.2 us (21%)
  other arithmetic  9.61 us (15%)
  local copies, waits for them, and re-layouts  8.88 us (14%)
    ppermute x3, waiting for transfers between devices, shards(): lax.ppermute(resid_z, 'zq', [(j, (j + k) % group) for j in range(group)])  8.92 us
    dot_general x1, matrix products, shards(): jnp.einsum('sl,zsx->zlx', band_y, resid_y, preferred_element_type=jnp.flo...  5.96 us
    ppermute x2, starting transfers between devices, double(): other = lax.ppermute(values, axis, [(0, 1), (1, 0)])  4.04 us
    ppermute x1, starting transfers between devices, shards(): got_y = lax.ppermute(give_y, 'co', [(0, 1), (1, 0)])  3.2 us
    ppermute x1, waiting for transfers between devices, halve(): got = lax.ppermute(give.astype(jnp.bfloat16), axis, [(0, 1), (1, 0)])  3.2 us
    dot_general x1, matrix products, shards(): jnp.einsum('sl,lyx->syx', own_rows, coarse, preferred_element_type=jnp.fl...  3.14 us
    ppermute x3, starting transfers between devices, shards(): got = lax.ppermute(sent, 'zq', [(j, (j + k) % group) for j in range(group)])  2.68 us
    convert_element_type x1, other arithmetic, shards(): coarse = volume.astype(jnp.bfloat16)  2.56 us
  transfers between devices with their start and end apart: 10, of which 4 were waited for; matrix products, arithmetic and copies ran while one was open for 34% of the time, Pallas kernels for 0%

profile of v7, /device:TPU:1, one launch (start us, length us, event | category | flops | bytes accessed | tf_op | source)
XLA Modules:
  0.0 63.8 jit_solution(14414593702761459422)
XLA Ops:
  1.7 1.0 %fusion.14 = bf16[25,16,128]{2,1,0:T(8,128)(2,1)S(1)} fusion(s32[25,128]{1,0:T(8,128)S(1)} %add_select_fusion, f32[25,16,128]{2,0,1:T(8,128)S(1)} %fusion.32), kind=kOutput, calls=%fused_computation.17 | convolution fusion | flops 79104000 | bytes 320000 | tf_op jit(solution)/shard_map/bsj,bjl->bsl/dot_general | solution.py:23
  2.8 2.6 %convert_element_type.67 = bf16[32,32,1024]{2,1,0:T(8,128)(2,1)S(1)} convert(f32[32,32,1024]{2,1,0:T(8,128)} %param.7) | non-fusion elementwise | flops 1048576 | bytes 6291456 | tf_op jit(solution)/shard_map/convert_element_type | solution.py:58
  5.3 1.2 %fusion.12 = bf16[16,16,1024]{2,1,0:T(8,128)(2,1)} fusion(bf16[32,32,1024]{2,1,0:T(8,128)(2,1)S(1)} %convert_element_type.67, s32[]{:T(128)S(6)} %select_n.120, bf16[1,16,128]{2,1,0:T(8,128)(2,1)S(1)} %slice.25, s32[]{:T(128)S(6)} %select_n.113), kind=kOutput, calls=%fused_computation.15 | convolution fusion | flops 17039360 | bytes 1576968 | tf_op jit(solution)/shard_map/sl,zlx->zsx/dot_general | solution.py:92
  6.5 3.2 %collective-permute-start = (bf16[16,16,1024]{2,1,0:T(8,128)(2,1)}, bf16[16,16,1024]{2,1,0:T(8,128)(2,1)}, u32[]{:S(2)}, u32[]{:S(2)}) collective-permute-start(bf16[16,16,1024]{2,1,0:T(8,128)(2,1)} %fusion.12), channel_id=1, source_target_pairs={{0,1},{1,0},{2,3},{3,2},{4,5},{5,4},{6,7},{7,6},{8,9},{9,8},{10,11... | collective-permute-start | bytes 1572872 | tf_op jit(solution)/shard_map/ppermute | solution.py:98
  10.4 2.3 %fusion.8 = bf16[12,32,1024]{2,0,1:T(8,128)(2,1)S(1)} fusion(bf16[32,32,1024]{2,1,0:T(8,128)(2,1)S(1)} %convert_element_type.67, bf16[4,32]{1,0:T(4,128)(2,1)S(1)} %get-tuple-element.19, bf16[4,32]{1,0:T(4,128)(2,1)S(1)} %get-tuple-element.18, bf16[4,32]{1,0:T(4,128)(2,1)S(1)} %get-tuple-element.17), kind=kOutput, calls=%fused_computation.10 | convolution fusion | flops 25561344 | bytes 2884352 | tf_op jit(solution)/shard_map/sl,lyx->syx/dot_general | solution.py:112
  12.8 1.0 %fusion.66 = (bf16[4,32,1024]{2,0,1:T(4,128)(2,1)}, bf16[4,32,1024]{2,0,1:T(4,128)(2,1)}, bf16[4,32,1024]{2,0,1:T(4,128)(2,1)}) fusion(bf16[12,32,1024]{2,0,1:T(8,128)(2,1)S(1)} %fusion.8), kind=kLoop, calls=%fused_computation.90 | loop fusion | bytes 1572864 | tf_op jit(solution)/shard_map/slice | solution.py:117
  13.8 2.7 %collective-permute-start.6 = (bf16[4,32,1024]{2,0,1:T(4,128)(2,1)}, bf16[4,32,1024]{2,0,1:T(4,128)(2,1)}, u32[]{:S(2)}, u32[]{:S(2)}) collective-permute-start(bf16[4,32,1024]{2,0,1:T(4,128)(2,1)} %get-tuple-element.12), channel_id=1, source_target_pairs={{0,12},{4,0},{8,4},{12,8},{1,13},{5,1},{9,5},{13,9},{2,14},{6,2},{... | collective-permute-start | bytes 786440 | tf_op jit(solution)/shard_map/ppermute | solution.py:118
  19.0 2.1 %copy.14 = f32[1024,128]{0,1:T(8,128)} copy(f32[1024,128]{1,0:T(8,128)} %bitcast_convert_fusion) | data formatting | bytes 1048576 | tf_op jit(solution)/shard_map/convert_element_type | solution.py:66
  21.9 3.1 %fusion.5 = f32[4,32,1024]{2,0,1:T(4,128)} fusion(bf16[32,32,1024]{2,1,0:T(8,128)(2,1)S(1)} %convert_element_type.67, bf16[16,16,128]{2,1,0:T(8,128)(2,1)S(1)} %slice.26, s32[]{:T(128)S(6)} %select_n.115, s32[]{:T(128)S(6)} %select_n.117, s32[]{:T(128)S(6)} %select_n.119), kind=kOutput, calls=%fused_computation.6 | convolution fusion | flops 8388608 | bytes 2622476 | tf_op jit(solution)/shard_map/sl,lyx->syx/dot_general | solution.py:79
  25.0 1.3 %convert_add_fusion = f32[16,16,1024]{2,1,0:T(8,128)S(1)} fusion(f32[16,16,1024]{2,1,0:T(8,128)S(1)} %convolution_bitcast_fusion, bf16[16,16,1024]{2,1,0:T(8,128)(2,1)} %collective-permute-done), kind=kLoop, calls=%fused_computation.29 | loop fusion | flops 524288 | bytes 2621440 | tf_op jit(solution)/shard_map/add | solution.py:100
  28.0 1.6 %collective-permute-start.1 = (bf16[8,16,1024]{2,1,0:T(8,128)(2,1)}, bf16[8,16,1024]{2,1,0:T(8,128)(2,1)}, u32[]{:S(2)}, u32[]{:S(2)}) collective-permute-start(bf16[8,16,1024]{2,1,0:T(8,128)(2,1)} %dynamic-slice_convert_fusion), channel_id=1, source_target_pairs={{0,2},{2,0},{1,3},{3,1},{4,6},{6,4},{5,7},{7,5},{8,10},{10,8},{9,1... | collective-permute-start | bytes 786440 | tf_op jit(solution)/shard_map/ppermute | solution.py:39
  29.6 1.5 %fusion.13 = bf16[1024,128]{0,1:T(8,128)(2,1)} fusion(f32[1024,128]{0,1:T(8,128)S(1)} %copy-done.5, bf16[1024,1024]{1,0:T(8,128)(2,1)S(1)} %bitcast.61, bf16[16,8,8,128]{3,2,1,0:T(8,128)(2,1)S(1)} %bitcast.62), kind=kOutput, calls=%fused_computation.16 | convolution fusion | flops 268697600 | bytes 3145728 | tf_op jit(solution)/shard_map/dot_general | solution.py:62
  31.3 1.2 %copy.15 = bf16[1024,128]{1,0:T(8,128)(2,1)S(1)} copy(bf16[1024,128]{0,1:T(8,128)(2,1)} %fusion.13) | data formatting | bytes 524288 | tf_op jit(solution)/shard_map/convert_element_type | solution.py:67
  32.5 3.2 %collective-permute-done.1 = bf16[8,16,1024]{2,1,0:T(8,128)(2,1)} collective-permute-done((bf16[8,16,1024]{2,1,0:T(8,128)(2,1)}, bf16[8,16,1024]{2,1,0:T(8,128)(2,1)}, u32[]{:S(2)}, u32[]{:S(2)}) %collective-permute-start.1) | collective-permute-done | bytes 262176 | tf_op jit(solution)/shard_map/ppermute | solution.py:39
  35.7 1.1 %subtract_convert_fusion.1 = bf16[8,16,1024]{2,1,0:T(8,128)(2,1)S(1)} fusion(bf16[8,16,1024]{2,1,0:T(8,128)(2,1)} %collective-permute-done.1, f32[16,16,1024]{2,1,0:T(8,128)S(1)} %copy-done.3, s32[]{:T(128)S(6)} %select_n.121, bf16[32,16,1024]{2,1,0:T(8,128)(2,1)} %param.9, s32[]{:T(128)S(6)} %select_n.111), kind=kLoop, calls=%fused_computation.35 | loop fusion | flops 655360 | bytes 1310728 | tf_op jit(solution)/shard_map/convert_element_type | solution.py:103
  36.8 1.6 %collective-permute-start.2 = (bf16[8,16,1024]{2,1,0:T(8,128)(2,1)S(1)}, bf16[8,16,1024]{2,1,0:T(8,128)(2,1)S(1)}, u32[]{:S(2)}, u32[]{:S(2)}) collective-permute-start(bf16[8,16,1024]{2,1,0:T(8,128)(2,1)S(1)} %subtract_convert_fusion.1), channel_id=1, source_target_pairs={{0,2},{2,0},{1,3},{3,1},{4,6},{6,4},{5,7},{7,5},{8,10},{10,8},{9,1... | collective-permute-start | bytes 786440 | tf_op jit(solution)/shard_map/ppermute | solution.py:44
  38.4 1.5 %subtract_convert_fusion = bf16[4,32,1024]{2,0,1:T(4,128)(2,1)S(1)} fusion(bf16[4,32,1024]{2,0,1:T(4,128)(2,1)} %collective-permute-done.6, bf16[4,32,1024]{2,0,1:T(4,128)(2,1)} %collective-permute-done.5, f32[4,32,1024]{2,0,1:T(4,128)S(1)} %copy-done.4, bf16[4,32,1024]{2,0,1:T(4,128)(2,1)} %collective-permute-done.4, bf16[4,32,1024]{2,1,0:T(8,128)(2,1)S(1)} %copy-done.7), kind=kLoop, calls=%fused_computation.34 | loop fusion | flops 1179648 | bytes 1835008 | tf_op jit(solution)/shard_map/convert_element_type | solution.py:120
  40.8 1.4 %collective-permute-start.8 = (bf16[4,32,1024]{2,0,1:T(4,128)(2,1)S(1)}, bf16[4,32,1024]{2,0,1:T(4,128)(2,1)S(1)}, u32[]{:S(2)}, u32[]{:S(2)}) collective-permute-start(bf16[4,32,1024]{2,0,1:T(4,128)(2,1)S(1)} %subtract_convert_fusion), channel_id=1, source_target_pairs={{0,8},{4,12},{8,0},{12,4},{1,9},{5,13},{9,1},{13,5},{2,10},{6,14},... | collective-permute-start | bytes 786440 | tf_op jit(solution)/shard_map/ppermute | solution.py:124
  42.3 1.1 %collective-permute-done.2 = bf16[8,16,1024]{2,1,0:T(8,128)(2,1)S(1)} collective-permute-done((bf16[8,16,1024]{2,1,0:T(8,128)(2,1)S(1)}, bf16[8,16,1024]{2,1,0:T(8,128)(2,1)S(1)}, u32[]{:S(2)}, u32[]{:S(2)}) %collective-permute-start.2) | collective-permute-done | bytes 262176 | tf_op jit(solution)/shard_map/ppermute | solution.py:44
  43.5 2.5 %collective-permute-start.3 = (bf16[16,16,1024]{2,1,0:T(8,128)(2,1)S(1)}, bf16[16,16,1024]{2,1,0:T(8,128)(2,1)S(1)}, u32[]{:S(2)}, u32[]{:S(2)}) collective-permute-start(bf16[16,16,1024]{2,1,0:T(8,128)(2,1)S(1)} %pad_maximum_fusion), channel_id=1, source_target_pairs={{0,1},{1,0},{2,3},{3,2},{4,5},{5,4},{6,7},{7,6},{8,9},{9,8},{10,11... | collective-permute-start | bytes 1572872 | tf_op jit(solution)/shard_map/ppermute | solution.py:44
  46.7 1.2 %collective-permute-done.8 = bf16[4,32,1024]{2,0,1:T(4,128)(2,1)S(1)} collective-permute-done((bf16[4,32,1024]{2,0,1:T(4,128)(2,1)S(1)}, bf16[4,32,1024]{2,0,1:T(4,128)(2,1)S(1)}, u32[]{:S(2)}, u32[]{:S(2)}) %collective-permute-start.8) | collective-permute-done | bytes 262176 | tf_op jit(solution)/shard_map/ppermute | solution.py:124
  47.9 7.7 %collective-permute-done.7 = bf16[4,32,1024]{2,0,1:T(4,128)(2,1)S(1)} collective-permute-done((bf16[4,32,1024]{2,0,1:T(4,128)(2,1)S(1)}, bf16[4,32,1024]{2,0,1:T(4,128)(2,1)S(1)}, u32[]{:S(2)}, u32[]{:S(2)}) %collective-permute-start.7) | collective-permute-done | bytes 262176 | tf_op jit(solution)/shard_map/ppermute | solution.py:124
  56.5 1.3 %copy-done.1 = f32[32,32,1024]{2,1,0:T(8,128)S(1)} copy-done((f32[32,32,1024]{2,1,0:T(8,128)S(1)}, f32[32,32,1024]{2,1,0:T(8,128)}, u32[]{:S(2)}) %copy-start.1) | copy-done | bytes 4194328
  57.8 6.0 %fusion.2 = f32[32,32,1024]{2,1,0:T(8,128)} fusion(f32[32,32,1024]{2,1,0:T(8,128)S(1)} %copy-done.1, f32[32,32,1024]{2,1,0:T(8,128)S(1)} %fusion.67, f32[32,32,1024]{2,0,1:T(8,128)S(1)} %fusion.18, bf16[16,16,1024]{2,1,0:T(8,128)(2,1)S(1)} %get-tuple-element.10, bf16[16,16,1024]{2,1,0:T(8,128)(2,1)S(1)} %get-tuple-element.9, ...), kind=kOutput, calls=%fused_computation.3 | convolution fusion | flops 38273024 | bytes 17829892 | tf_op jit(solution)/shard_map/sl,zsx->zlx/dot_general | solution.py:106
  (46 shorter events, 10.2 us)
Async XLA Ops:
  0.0 0.8 %copy-start = (f32[4,16,128]{2,1,0:T(8,128)S(1)}, f32[4,16,128]{2,1,0:T(8,128)}, u32[]{:S(2)}) copy-start(f32[4,16,128]{2,1,0:T(8,128)} %param.11) | copy-start | bytes 98308
  2.8 7.0 %copy-start.8 = (bf16[25,16,128]{2,1,0:T(8,128)(2,1)}, bf16[25,16,128]{2,1,0:T(8,128)(2,1)S(1)}, u32[]{:S(2)}) copy-start(bf16[25,16,128]{2,1,0:T(8,128)(2,1)S(1)} %fusion.14) | copy-start | bytes 307204
  6.5 18.5 %collective-permute-start = (bf16[16,16,1024]{2,1,0:T(8,128)(2,1)}, bf16[16,16,1024]{2,1,0:T(8,128)(2,1)}, u32[]{:S(2)}, u32[]{:S(2)}) collective-permute-start(bf16[16,16,1024]{2,1,0:T(8,128)(2,1)} %fusion.12), channel_id=1, source_target_pairs={{0,1},{1,0},{2,3},{3,2},{4,5},{5,4},{6,7},{7,6},{8,9},{9,8},{10,11... | collective-permute-start | bytes 1572872 | tf_op jit(solution)/shard_map/ppermute | solution.py:98
  10.4 6.0 %copy-start.6 = (bf16[32,32,128]{2,1,0:T(8,128)(2,1)S(1)}, bf16[32,32,128]{2,1,0:T(8,128)(2,1)}, u32[]{:S(2)}) copy-start(bf16[32,32,128]{2,1,0:T(8,128)(2,1)} %param.8) | copy-start | bytes 786436
  13.8 24.6 %collective-permute-start.4 = (bf16[4,32,1024]{2,0,1:T(4,128)(2,1)}, bf16[4,32,1024]{2,0,1:T(4,128)(2,1)}, u32[]{:S(2)}, u32[]{:S(2)}) collective-permute-start(bf16[4,32,1024]{2,0,1:T(4,128)(2,1)} %get-tuple-element.11), channel_id=1, source_target_pairs={{0,4},{4,8},{8,12},{12,0},{1,5},{5,9},{9,13},{13,1},{2,6},{6,10},{... | collective-permute-start | bytes 786440 | tf_op jit(solution)/shard_map/ppermute | solution.py:118
  13.8 24.6 %collective-permute-start.6 = (bf16[4,32,1024]{2,0,1:T(4,128)(2,1)}, bf16[4,32,1024]{2,0,1:T(4,128)(2,1)}, u32[]{:S(2)}, u32[]{:S(2)}) collective-permute-start(bf16[4,32,1024]{2,0,1:T(4,128)(2,1)} %get-tuple-element.12), channel_id=1, source_target_pairs={{0,12},{4,0},{8,4},{12,8},{1,13},{5,1},{9,5},{13,9},{2,14},{6,2},{... | collective-permute-start | bytes 786440 | tf_op jit(solution)/shard_map/ppermute | solution.py:118
  16.5 21.9 %collective-permute-start.5 = (bf16[4,32,1024]{2,0,1:T(4,128)(2,1)}, bf16[4,32,1024]{2,0,1:T(4,128)(2,1)}, u32[]{:S(2)}, u32[]{:S(2)}) collective-permute-start(bf16[4,32,1024]{2,0,1:T(4,128)(2,1)} %get-tuple-element.13), channel_id=1, source_target_pairs={{0,8},{4,12},{8,0},{12,4},{1,9},{5,13},{9,1},{13,5},{2,10},{6,14},... | collective-permute-start | bytes 786440 | tf_op jit(solution)/shard_map/ppermute | solution.py:118
  25.0 4.6 %copy-start.5 = (f32[1024,128]{0,1:T(8,128)S(1)}, f32[1024,128]{0,1:T(8,128)}, u32[]{:S(2)}) copy-start(f32[1024,128]{0,1:T(8,128)} %copy.14) | copy-start | bytes 1572868
  26.3 1.0 %copy-start.2 = (f32[16,16,1024]{2,1,0:T(8,128)}, f32[16,16,1024]{2,1,0:T(8,128)S(1)}, u32[]{:S(2)}) copy-start(f32[16,16,1024]{2,1,0:T(8,128)S(1)} %convert_add_fusion) | copy-start | bytes 3145732
  28.0 7.7 %collective-permute-start.1 = (bf16[8,16,1024]{2,1,0:T(8,128)(2,1)}, bf16[8,16,1024]{2,1,0:T(8,128)(2,1)}, u32[]{:S(2)}, u32[]{:S(2)}) collective-permute-start(bf16[8,16,1024]{2,1,0:T(8,128)(2,1)} %dynamic-slice_convert_fusion), channel_id=1, source_target_pairs={{0,2},{2,0},{1,3},{3,1},{4,6},{6,4},{5,7},{7,5},{8,10},{10,8},{9,1... | collective-permute-start | bytes 786440 | tf_op jit(solution)/shard_map/ppermute | solution.py:39
  29.6 6.0 %copy-start.3 = (f32[16,16,1024]{2,1,0:T(8,128)S(1)}, f32[16,16,1024]{2,1,0:T(8,128)}, u32[]{:S(2)}) copy-start(f32[16,16,1024]{2,1,0:T(8,128)} %copy-done.2) | copy-start | bytes 3145732
  31.2 7.2 %copy-start.4 = (f32[4,32,1024]{2,0,1:T(4,128)S(1)}, f32[4,32,1024]{2,0,1:T(4,128)}, u32[]{:S(2)}) copy-start(f32[4,32,1024]{2,0,1:T(4,128)} %fusion.5) | copy-start | bytes 1572868
  31.2 7.2 %copy-start.7 = (bf16[4,32,1024]{2,1,0:T(8,128)(2,1)S(1)}, bf16[4,32,1024]{2,1,0:T(8,128)(2,1)}, u32[]{:S(2)}) copy-start(bf16[4,32,1024]{2,1,0:T(8,128)(2,1)} %param.10) | copy-start | bytes 786436
  36.8 6.6 %collective-permute-start.2 = (bf16[8,16,1024]{2,1,0:T(8,128)(2,1)S(1)}, bf16[8,16,1024]{2,1,0:T(8,128)(2,1)S(1)}, u32[]{:S(2)}, u32[]{:S(2)}) collective-permute-start(bf16[8,16,1024]{2,1,0:T(8,128)(2,1)S(1)} %subtract_convert_fusion.1), channel_id=1, source_target_pairs={{0,2},{2,0},{1,3},{3,1},{4,6},{6,4},{5,7},{7,5},{8,10},{10,8},{9,1... | collective-permute-start | bytes 786440 | tf_op jit(solution)/shard_map/ppermute | solution.py:44
  39.9 6.7 %collective-permute-start.9 = (bf16[4,32,1024]{2,0,1:T(4,128)(2,1)S(1)}, bf16[4,32,1024]{2,0,1:T(4,128)(2,1)S(1)}, u32[]{:S(2)}, u32[]{:S(2)}) collective-permute-start(bf16[4,32,1024]{2,0,1:T(4,128)(2,1)S(1)} %subtract_convert_fusion), channel_id=1, source_target_pairs={{0,12},{4,0},{8,4},{12,8},{1,13},{5,1},{9,5},{13,9},{2,14},{6,2},{... | collective-permute-start | bytes 786440 | tf_op jit(solution)/shard_map/ppermute | solution.py:124
  40.8 7.1 %collective-permute-start.8 = (bf16[4,32,1024]{2,0,1:T(4,128)(2,1)S(1)}, bf16[4,32,1024]{2,0,1:T(4,128)(2,1)S(1)}, u32[]{:S(2)}, u32[]{:S(2)}) collective-permute-start(bf16[4,32,1024]{2,0,1:T(4,128)(2,1)S(1)} %subtract_convert_fusion), channel_id=1, source_target_pairs={{0,8},{4,12},{8,0},{12,4},{1,9},{5,13},{9,1},{13,5},{2,10},{6,14},... | collective-permute-start | bytes 786440 | tf_op jit(solution)/shard_map/ppermute | solution.py:124
  42.2 13.4 %collective-permute-start.7 = (bf16[4,32,1024]{2,0,1:T(4,128)(2,1)S(1)}, bf16[4,32,1024]{2,0,1:T(4,128)(2,1)S(1)}, u32[]{:S(2)}, u32[]{:S(2)}) collective-permute-start(bf16[4,32,1024]{2,0,1:T(4,128)(2,1)S(1)} %subtract_convert_fusion), channel_id=1, source_target_pairs={{0,4},{4,8},{8,12},{12,0},{1,5},{5,9},{9,13},{13,1},{2,6},{6,10},{... | collective-permute-start | bytes 786440 | tf_op jit(solution)/shard_map/ppermute | solution.py:124
  43.5 12.9 %collective-permute-start.3 = (bf16[16,16,1024]{2,1,0:T(8,128)(2,1)S(1)}, bf16[16,16,1024]{2,1,0:T(8,128)(2,1)S(1)}, u32[]{:S(2)}, u32[]{:S(2)}) collective-permute-start(bf16[16,16,1024]{2,1,0:T(8,128)(2,1)S(1)} %pad_maximum_fusion), channel_id=1, source_target_pairs={{0,1},{1,0},{2,3},{3,2},{4,5},{5,4},{6,7},{7,6},{8,9},{9,8},{10,11... | collective-permute-start | bytes 1572872 | tf_op jit(solution)/shard_map/ppermute | solution.py:44
  46.0 9.6 %copy-start.9 = (bf16[4,32]{1,0:T(4,128)(2,1)S(1)}, bf16[4,32]{1,0:T(4,128)(2,1)}, u32[]{:S(2)}) copy-start(bf16[4,32]{1,0:T(4,128)(2,1)} %get-tuple-element.16) | copy-start | bytes 772
  55.6 2.2 %copy-start.1 = (f32[32,32,1024]{2,1,0:T(8,128)S(1)}, f32[32,32,1024]{2,1,0:T(8,128)}, u32[]{:S(2)}) copy-start(f32[32,32,1024]{2,1,0:T(8,128)} %param.7) | copy-start | bytes 12582916

commit v8 on v6

--- a/solution.py
+++ b/solution.py
@@ -121,6 +121,9 @@
         pieces.append(lax.ppermute(resid_z, "zq", [(j, (j + k) % group) for j in range(group)]))
         src = (zq - k + group) % group
         rows.append(lax.dynamic_slice_in_dim(band_z, src * piece, piece, 0))
+    base, pieces[1] = lax.optimization_barrier(
+        (volume + step_size * (corr_x + corr_y), pieces[1])
+    )
     corr_z = jnp.einsum(
         "sl,syx->lyx",
         jnp.concatenate(rows, 0),
@@ -128,7 +131,7 @@
         preferred_element_type=jnp.float32,
     )
 
-    return volume + step_size * (corr_x + corr_y + corr_z)
+    return base + step_size * corr_z
 
 
 def solution(mesh):

time: 57.6 us -> 65.2 us (1.13)
  other arithmetic: 4.7 us -> 13.1 us
  matrix products: 18.9 us -> 14.7 us
  waiting for transfers between devices: 12.3 us -> 15.8 us
  local copies, waits for them, and re-layouts: 6.77 us -> 5.76 us
  starting transfers between devices: 14.5 us -> 15.3 us
    add x0 -> x1, other arithmetic: none -> 4.97 us  [shards(): return base + step_size * corr_z]
    dot_general x1, matrix products: 5.96 us -> 1.38 us  [shards(): jnp.einsum('sl,zsx->zlx', band_y, resid_y, preferred_element_type=jnp.flo...]
    ppermute x2, waiting for transfers between devices: 0.01 us -> 3.07 us  [double(): other = lax.ppermute(values, axis, [(0, 1), (1, 0)])]
    ppermute x3, waiting for transfers between devices: 9.86 us -> 11.6 us  [shards(): lax.ppermute(resid_z, 'zq', [(j, (j + k) % group) for j in range(group)])]
    convert_element_type x1, other arithmetic: 0.05 us -> 1.78 us  [shards(): slices_x.reshape(planes * rows_here, count_x * SLICES).astype(jnp.float32)]
    ppermute x1, waiting for transfers between devices: 2.45 us -> 1.17 us  [halve(): got = lax.ppermute(give.astype(jnp.bfloat16), axis, [(0, 1), (1, 0)])]
    ppermute x3, starting transfers between devices: 2.34 us -> 3.59 us  [shards(): lax.ppermute(resid_z, 'zq', [(j, (j + k) % group) for j in range(group)])]
    unnamed x12 -> x18, local copies, waits for them, and re-layouts: 1.36 us -> 0.28 us
  transfers between devices with their start and end apart: 10 -> 10, of which waited for: 3 -> 3; matrix products, arithmetic and copies ran while one was open for 30% -> 34% of each run, Pallas kernels for 0% -> 0%
where the time goes in v8:
time: 65.2 us; the launch traced here: 64.8 us
  waiting for transfers between devices  15.8 us (24%)
  starting transfers between devices  15.3 us (23%)
  matrix products  14.7 us (23%)
  other arithmetic  13.1 us (20%)
  local copies, waits for them, and re-layouts  5.76 us (9%)
    ppermute x3, waiting for transfers between devices, shards(): lax.ppermute(resid_z, 'zq', [(j, (j + k) % group) for j in range(group)])  11.6 us
    add x1, other arithmetic, shards(): return base + step_size * corr_z  4.97 us
    ppermute x2, starting transfers between devices, double(): other = lax.ppermute(values, axis, [(0, 1), (1, 0)])  4.08 us
    dot_general x1, matrix products, shards(): jnp.einsum('sl,lyx->syx', own_rows, coarse, preferred_element_type=jnp.fl...  3.88 us
    ppermute x3, starting transfers between devices, shards(): lax.ppermute(resid_z, 'zq', [(j, (j + k) % group) for j in range(group)])  3.59 us
    ppermute x1, starting transfers between devices, shards(): lax.ppermute(give_y, 'co', [(0, 1), (1, 0)]).astype(jnp.float32)  3.29 us
    ppermute x2, waiting for transfers between devices, double(): other = lax.ppermute(values, axis, [(0, 1), (1, 0)])  3.07 us
    ppermute x3, starting transfers between devices, shards(): got = lax.ppermute(sent, 'zq', [(j, (j + k) % group) for j in range(group)])  2.68 us
  transfers between devices with their start and end apart: 10, of which 3 were waited for; matrix products, arithmetic and copies ran while one was open for 34% of the time, Pallas kernels for 0%

profile of v8, /device:TPU:1, one launch (start us, length us, event | category | flops | bytes accessed | tf_op | source)
XLA Modules:
  0.0 64.8 jit_solution(3693332875438821768)
XLA Ops:
  0.8 1.0 %fusion.34 = f32[25,16,128]{2,0,1:T(8,128)S(1)} fusion(f32[4,16,128]{2,1,0:T(8,128)S(1)} %copy-done, s32[25]{0:T(128)} %param.12), kind=kOutput, calls=%fused_computation.47 | convolution fusion | flops 2457700 | bytes 237668 | tf_op jit(solution)/shard_map/bk,ksl->bsl/dot_general | solution.py:19
  1.7 1.0 %fusion.14 = bf16[25,16,128]{2,1,0:T(8,128)(2,1)S(1)} fusion(s32[25,128]{1,0:T(8,128)S(1)} %add_select_fusion, f32[25,16,128]{2,0,1:T(8,128)S(1)} %fusion.34), kind=kOutput, calls=%fused_computation.18 | convolution fusion | flops 79104000 | bytes 320000 | tf_op jit(solution)/shard_map/bsj,bjl->bsl/dot_general | solution.py:23
  2.8 2.6 %convert_element_type.67 = bf16[32,32,1024]{2,1,0:T(8,128)(2,1)S(1)} convert(f32[32,32,1024]{2,1,0:T(8,128)} %param.7) | non-fusion elementwise | flops 1048576 | bytes 6291456 | tf_op jit(solution)/shard_map/convert_element_type | solution.py:58
  5.7 3.3 %collective-permute-start = (bf16[16,16,1024]{2,1,0:T(8,128)(2,1)S(1)}, bf16[16,16,1024]{2,1,0:T(8,128)(2,1)}, u32[]{:S(2)}, u32[]{:S(2)}) collective-permute-start(bf16[16,16,1024]{2,1,0:T(8,128)(2,1)S(1)} %fusion.12), channel_id=1, source_target_pairs={{0,1},{1,0},{2,3},{3,2},{4,5},{5,4},{6,7},{7,6},{8,9},{9,8},{10,11... | collective-permute-start | bytes 1572872 | tf_op jit(solution)/shard_map/ppermute | solution.py:89
  9.7 2.3 %fusion.8 = bf16[12,32,1024]{2,0,1:T(8,128)(2,1)S(1)} fusion(bf16[32,32,1024]{2,1,0:T(8,128)(2,1)S(1)} %convert_element_type.67, bf16[4,32]{1,0:T(4,128)(2,1)S(1)} %get-tuple-element.17, bf16[4,32]{1,0:T(4,128)(2,1)S(1)} %get-tuple-element.18, bf16[4,32]{1,0:T(4,128)(2,1)S(1)} %get-tuple-element.19), kind=kOutput, calls=%fused_computation.11 | convolution fusion | flops 25561344 | bytes 2884352 | tf_op jit(solution)/shard_map/sl,lyx->syx/dot_general | solution.py:110
  12.0 1.0 %fusion.72 = (bf16[4,32,1024]{2,0,1:T(4,128)(2,1)}, bf16[4,32,1024]{2,0,1:T(4,128)(2,1)}, bf16[4,32,1024]{2,0,1:T(4,128)(2,1)}) fusion(bf16[12,32,1024]{2,0,1:T(8,128)(2,1)S(1)} %fusion.8), kind=kLoop, calls=%fused_computation.91 | loop fusion | bytes 1572864 | tf_op jit(solution)/shard_map/slice | solution.py:114
  13.0 2.7 %collective-permute-start.6 = (bf16[4,32,1024]{2,0,1:T(4,128)(2,1)}, bf16[4,32,1024]{2,0,1:T(4,128)(2,1)}, u32[]{:S(2)}, u32[]{:S(2)}) collective-permute-start(bf16[4,32,1024]{2,0,1:T(4,128)(2,1)} %get-tuple-element.10), channel_id=1, source_target_pairs={{0,12},{4,0},{8,4},{12,8},{1,13},{5,1},{9,5},{13,9},{2,14},{6,2},{... | collective-permute-start | bytes 786440 | tf_op jit(solution)/shard_map/ppermute | solution.py:115
  15.7 1.4 %convert_add_fusion = f32[16,16,1024]{2,1,0:T(8,128)S(1)} fusion(bf16[16,16,1024]{2,1,0:T(8,128)(2,1)} %collective-permute-done, bf16[32,32,1024]{2,1,0:T(8,128)(2,1)S(1)} %convert_element_type.67, s32[]{:T(128)S(6)} %select_n.112, bf16[1,16,128]{2,1,0:T(8,128)(2,1)S(1)} %slice.25, s32[]{:T(128)S(6)} %select_n.113), kind=kOutput, calls=%fused_computation.30 | convolution fusion | flops 17301504 | bytes 2625544 | tf_op jit(solution)/shard_map/sl,zlx->zsx/dot_general | solution.py:77
  17.9 1.6 %collective-permute-start.1 = (bf16[8,16,1024]{2,1,0:T(8,128)(2,1)}, bf16[8,16,1024]{2,1,0:T(8,128)(2,1)}, u32[]{:S(2)}, u32[]{:S(2)}) collective-permute-start(bf16[8,16,1024]{2,1,0:T(8,128)(2,1)} %dynamic-slice_convert_fusion), channel_id=1, source_target_pairs={{0,2},{2,0},{1,3},{3,1},{4,6},{6,4},{5,7},{7,5},{8,10},{10,8},{9,1... | collective-permute-start | bytes 786440 | tf_op jit(solution)/shard_map/ppermute | solution.py:39
  20.4 1.8 %bitcast_convert_fusion = f32[1024,128]{1,0:T(8,128)} fusion(bf16[32,32,128]{2,1,0:T(8,128)(2,1)} %param.8), kind=kLoop, calls=%fused_computation.42 | loop fusion | flops 131072 | bytes 786432 | tf_op jit(solution)/shard_map/convert_element_type | solution.py:66
  22.2 2.1 %copy.14 = f32[1024,128]{0,1:T(8,128)} copy(f32[1024,128]{1,0:T(8,128)} %bitcast_convert_fusion) | data formatting | bytes 1048576 | tf_op jit(solution)/shard_map/convert_element_type | solution.py:66
  24.3 1.2 %collective-permute-done.1 = bf16[8,16,1024]{2,1,0:T(8,128)(2,1)} collective-permute-done((bf16[8,16,1024]{2,1,0:T(8,128)(2,1)}, bf16[8,16,1024]{2,1,0:T(8,128)(2,1)}, u32[]{:S(2)}, u32[]{:S(2)}) %collective-permute-start.1) | collective-permute-done | bytes 262176 | tf_op jit(solution)/shard_map/ppermute | solution.py:39
  25.4 1.8 %subtract_convert_fusion.1 = bf16[8,16,1024]{2,1,0:T(8,128)(2,1)} fusion(bf16[8,16,1024]{2,1,0:T(8,128)(2,1)} %collective-permute-done.1, f32[16,16,1024]{2,1,0:T(8,128)S(1)} %convert_add_fusion, s32[]{:T(128)S(6)} %select_n.115, bf16[32,16,1024]{2,1,0:T(8,128)(2,1)} %param.9, s32[]{:T(128)S(6)} %select_n.111), kind=kLoop, calls=%fused_computation.36 | loop fusion | flops 655360 | bytes 1310728 | tf_op jit(solution)/shard_map/convert_element_type | solution.py:93
  27.3 1.3 %collective-permute-start.2 = (bf16[8,16,1024]{2,1,0:T(8,128)(2,1)}, bf16[8,16,1024]{2,1,0:T(8,128)(2,1)S(1)}, u32[]{:S(2)}, u32[]{:S(2)}) collective-permute-start(bf16[8,16,1024]{2,1,0:T(8,128)(2,1)} %subtract_convert_fusion.1), channel_id=1, source_target_pairs={{0,2},{2,0},{1,3},{3,1},{4,6},{6,4},{5,7},{7,5},{8,10},{10,8},{9,1... | collective-permute-start | bytes 786440 | tf_op jit(solution)/shard_map/ppermute | solution.py:44
  28.6 1.9 %fusion.13 = bf16[1024,128]{0,1:T(8,128)(2,1)S(1)} fusion(f32[1024,128]{0,1:T(8,128)} %copy.14, bf16[1024,1024]{1,0:T(8,128)(2,1)S(1)} %bitcast.63, bf16[16,8,8,128]{3,2,1,0:T(8,128)(2,1)S(1)} %bitcast.64), kind=kOutput, calls=%fused_computation.17 | convolution fusion | flops 268697600 | bytes 3145728 | tf_op jit(solution)/shard_map/dot_general | solution.py:62
  30.6 3.1 %collective-permute-done.2 = bf16[8,16,1024]{2,1,0:T(8,128)(2,1)S(1)} collective-permute-done((bf16[8,16,1024]{2,1,0:T(8,128)(2,1)}, bf16[8,16,1024]{2,1,0:T(8,128)(2,1)S(1)}, u32[]{:S(2)}, u32[]{:S(2)}) %collective-permute-start.2) | collective-permute-done | bytes 262176 | tf_op jit(solution)/shard_map/ppermute | solution.py:44
  33.7 1.0 %broadcast_select_fusion.3 = (bf16[8,16,1024]{2,1,0:T(8,128)(2,1)S(1)}, bf16[8,16,1024]{2,1,0:T(8,128)(2,1)S(1)}) fusion(bf16[8,16,1024]{2,1,0:T(8,128)(2,1)} %subtract_convert_fusion.1, bf16[8,16,1024]{2,1,0:T(8,128)(2,1)S(1)} %collective-permute-done.2, pred[]{:T(512)S(6)} %eq.58), kind=kLoop, calls=%fused_computation.44 | loop fusion | flops 262144 | bytes 1048577 | tf_op jit(solution)/shard_map/jit(_where)/select_n | solution.py:45
  34.7 2.8 %collective-permute-start.3 = (bf16[16,16,1024]{2,1,0:T(8,128)(2,1)S(1)}, bf16[16,16,1024]{2,1,0:T(8,128)(2,1)S(1)}, u32[]{:S(2)}, u32[]{:S(2)}) collective-permute-start(bf16[16,16,1024]{2,1,0:T(8,128)(2,1)S(1)} %pad_maximum_fusion), channel_id=1, source_target_pairs={{0,1},{1,0},{2,3},{3,2},{4,5},{5,4},{6,7},{7,6},{8,9},{9,8},{10,11... | collective-permute-start | bytes 1572872 | tf_op jit(solution)/shard_map/ppermute | solution.py:44
  38.5 3.9 %subtract_convert_fusion = bf16[4,32,1024]{2,0,1:T(4,128)(2,1)S(1)} fusion(bf16[4,32,1024]{2,0,1:T(4,128)(2,1)} %collective-permute-done.6, bf16[4,32,1024]{2,0,1:T(4,128)(2,1)} %collective-permute-done.5, bf16[4,32,1024]{2,0,1:T(4,128)(2,1)} %collective-permute-done.4, bf16[4,32,1024]{2,1,0:T(8,128)(2,1)S(1)} %copy-done.8, ...), kind=kOutput, calls=%fused_computation.35 | convolution fusion | flops 9568256 | bytes 3408908 | tf_op jit(solution)/shard_map/sl,lyx->syx/dot_general | solution.py:105
  42.4 1.3 %collective-permute-start.9 = (bf16[4,32,1024]{2,0,1:T(4,128)(2,1)S(1)}, bf16[4,32,1024]{2,0,1:T(4,128)(2,1)S(1)}, u32[]{:S(2)}, u32[]{:S(2)}) collective-permute-start(bf16[4,32,1024]{2,0,1:T(4,128)(2,1)S(1)} %subtract_convert_fusion), channel_id=1, source_target_pairs={{0,12},{4,0},{8,4},{12,8},{1,13},{5,1},{9,5},{13,9},{2,14},{6,2},{... | collective-permute-start | bytes 786440 | tf_op jit(solution)/shard_map/ppermute | solution.py:121
  43.6 1.5 %collective-permute-start.8 = (bf16[4,32,1024]{2,0,1:T(4,128)(2,1)S(1)}, bf16[4,32,1024]{2,0,1:T(4,128)(2,1)S(1)}, u32[]{:S(2)}, u32[]{:S(2)}) collective-permute-start(bf16[4,32,1024]{2,0,1:T(4,128)(2,1)S(1)} %subtract_convert_fusion), channel_id=1, source_target_pairs={{0,8},{4,12},{8,0},{12,4},{1,9},{5,13},{9,1},{13,5},{2,10},{6,14},... | collective-permute-start | bytes 786440 | tf_op jit(solution)/shard_map/ppermute | solution.py:121
  46.0 1.4 %fusion.1 = f32[32,32,1024]{2,1,0:T(8,128)S(1)} fusion(f32[32,32,1024]{2,1,0:T(8,128)S(1)} %copy-done.1, f32[32,32,1024]{2,1,0:T(8,128)S(1)} %fusion.73, bf16[16,16,1024]{2,1,0:T(8,128)(2,1)S(1)} %get-tuple-element.13, bf16[16,16,1024]{2,1,0:T(8,128)(2,1)S(1)} %get-tuple-element.12, bf16[1,16,128]{2,1,0:T(8,128)(2,1)S(1)} %slice.25, s32[]{:T(128)S(6)} %select_n.113), kind=kOutput, calls=%fused_computation.2 | convolution fusion | flops 37224448 | bytes 13635588 | tf_op jit(solution)/shard_map/sl,zsx->zlx/dot_general | solution.py:96
  47.4 11.6 %collective-permute-done.7 = bf16[4,32,1024]{2,0,1:T(4,128)(2,1)S(1)} collective-permute-done((bf16[4,32,1024]{2,0,1:T(4,128)(2,1)S(1)}, bf16[4,32,1024]{2,0,1:T(4,128)(2,1)S(1)}, u32[]{:S(2)}, u32[]{:S(2)}) %collective-permute-start.7) | collective-permute-done | bytes 262176 | tf_op jit(solution)/shard_map/ppermute | solution.py:121
  59.8 5.0 %fusion.2 = f32[32,32,1024]{2,1,0:T(8,128)} fusion(f32[32,32,1024]{2,1,0:T(8,128)S(1)} %fusion.1, f32[32,32,1024]{2,0,1:T(8,128)S(1)} %fusion.18), kind=kLoop, calls=%fused_computation.4 | loop fusion | flops 2097152 | bytes 12582912 | tf_op jit(solution)/shard_map/add | solution.py:134
  (44 shorter events, 6.2 us)
Async XLA Ops:
  0.0 0.8 %copy-start = (f32[4,16,128]{2,1,0:T(8,128)S(1)}, f32[4,16,128]{2,1,0:T(8,128)}, u32[]{:S(2)}) copy-start(f32[4,16,128]{2,1,0:T(8,128)} %param.11) | copy-start | bytes 98308
  2.8 12.9 %copy-start.3 = (bf16[25,16,128]{2,1,0:T(8,128)(2,1)}, bf16[25,16,128]{2,1,0:T(8,128)(2,1)S(1)}, u32[]{:S(2)}) copy-start(bf16[25,16,128]{2,1,0:T(8,128)(2,1)S(1)} %fusion.14) | copy-start | bytes 307204
  5.7 10.0 %collective-permute-start = (bf16[16,16,1024]{2,1,0:T(8,128)(2,1)S(1)}, bf16[16,16,1024]{2,1,0:T(8,128)(2,1)}, u32[]{:S(2)}, u32[]{:S(2)}) collective-permute-start(bf16[16,16,1024]{2,1,0:T(8,128)(2,1)S(1)} %fusion.12), channel_id=1, source_target_pairs={{0,1},{1,0},{2,3},{3,2},{4,5},{5,4},{6,7},{7,6},{8,9},{9,8},{10,11... | collective-permute-start | bytes 1572872 | tf_op jit(solution)/shard_map/ppermute | solution.py:89
  9.0 4.0 %copy-start.4 = (bf16[16,16,128]{2,1,0:T(8,128)(2,1)}, bf16[16,16,128]{2,1,0:T(8,128)(2,1)S(1)}, u32[]{:S(2)}) copy-start(bf16[16,16,128]{2,1,0:T(8,128)(2,1)S(1)} %slice.26) | copy-start | bytes 196612
  9.7 3.4 %copy-start.5 = (bf16[4,32]{1,0:T(4,128)(2,1)}, bf16[4,32]{1,0:T(4,128)(2,1)S(1)}, u32[]{:S(2)}) copy-start(bf16[4,32]{1,0:T(4,128)(2,1)S(1)} %get-tuple-element.19) | copy-start | bytes 772
  13.0 25.2 %collective-permute-start.4 = (bf16[4,32,1024]{2,0,1:T(4,128)(2,1)}, bf16[4,32,1024]{2,0,1:T(4,128)(2,1)}, u32[]{:S(2)}, u32[]{:S(2)}) collective-permute-start(bf16[4,32,1024]{2,0,1:T(4,128)(2,1)} %get-tuple-element.9), channel_id=1, source_target_pairs={{0,4},{4,8},{8,12},{12,0},{1,5},{5,9},{9,13},{13,1},{2,6},{6,10},{... | collective-permute-start | bytes 786440 | tf_op jit(solution)/shard_map/ppermute | solution.py:115
  13.0 25.2 %collective-permute-start.6 = (bf16[4,32,1024]{2,0,1:T(4,128)(2,1)}, bf16[4,32,1024]{2,0,1:T(4,128)(2,1)}, u32[]{:S(2)}, u32[]{:S(2)}) collective-permute-start(bf16[4,32,1024]{2,0,1:T(4,128)(2,1)} %get-tuple-element.10), channel_id=1, source_target_pairs={{0,12},{4,0},{8,4},{12,8},{1,13},{5,1},{9,5},{13,9},{2,14},{6,2},{... | collective-permute-start | bytes 786440 | tf_op jit(solution)/shard_map/ppermute | solution.py:115
  15.7 22.5 %collective-permute-start.5 = (bf16[4,32,1024]{2,0,1:T(4,128)(2,1)}, bf16[4,32,1024]{2,0,1:T(4,128)(2,1)}, u32[]{:S(2)}, u32[]{:S(2)}) collective-permute-start(bf16[4,32,1024]{2,0,1:T(4,128)(2,1)} %get-tuple-element.11), channel_id=1, source_target_pairs={{0,8},{4,12},{8,0},{12,4},{1,9},{5,13},{9,1},{13,5},{2,10},{6,14},... | collective-permute-start | bytes 786440 | tf_op jit(solution)/shard_map/ppermute | solution.py:115
  15.7 3.8 %slice-start = ((bf16[25,16,128]{2,1,0:T(8,128)(2,1)}), bf16[8,16,128]{2,1,0:T(8,128)(2,1)S(1)}, s32[]{:S(2)}) async-start(bf16[25,16,128]{2,1,0:T(8,128)(2,1)} %copy-done.3), calls=%async_computation | async-start | bytes 65536 | tf_op jit(solution)/shard_map/slice | solution.py:55
  17.9 7.5 %collective-permute-start.1 = (bf16[8,16,1024]{2,1,0:T(8,128)(2,1)}, bf16[8,16,1024]{2,1,0:T(8,128)(2,1)}, u32[]{:S(2)}, u32[]{:S(2)}) collective-permute-start(bf16[8,16,1024]{2,1,0:T(8,128)(2,1)} %dynamic-slice_convert_fusion), channel_id=1, source_target_pairs={{0,2},{2,0},{1,3},{3,1},{4,6},{6,4},{5,7},{7,5},{8,10},{10,8},{9,1... | collective-permute-start | bytes 786440 | tf_op jit(solution)/shard_map/ppermute | solution.py:39
  27.3 6.4 %collective-permute-start.2 = (bf16[8,16,1024]{2,1,0:T(8,128)(2,1)}, bf16[8,16,1024]{2,1,0:T(8,128)(2,1)S(1)}, u32[]{:S(2)}, u32[]{:S(2)}) collective-permute-start(bf16[8,16,1024]{2,1,0:T(8,128)(2,1)} %subtract_convert_fusion.1), channel_id=1, source_target_pairs={{0,2},{2,0},{1,3},{3,1},{4,6},{6,4},{5,7},{7,5},{8,10},{10,8},{9,1... | collective-permute-start | bytes 786440 | tf_op jit(solution)/shard_map/ppermute | solution.py:44
  30.4 7.1 %copy-start.2 = (bf16[128,1024,1]{1,0,2:T(8,128)(2,1)S(1)}, bf16[128,1024,1]{1,0,2:T(8,128)(2,1)}, u32[]{:S(2)}) copy-start(bf16[128,1024,1]{1,0,2:T(8,128)(2,1)} %reshape.79) | copy-start | bytes 786436
  34.7 11.2 %collective-permute-start.3 = (bf16[16,16,1024]{2,1,0:T(8,128)(2,1)S(1)}, bf16[16,16,1024]{2,1,0:T(8,128)(2,1)S(1)}, u32[]{:S(2)}, u32[]{:S(2)}) collective-permute-start(bf16[16,16,1024]{2,1,0:T(8,128)(2,1)S(1)} %pad_maximum_fusion), channel_id=1, source_target_pairs={{0,1},{1,0},{2,3},{3,2},{4,5},{5,4},{6,7},{7,6},{8,9},{9,8},{10,11... | collective-permute-start | bytes 1572872 | tf_op jit(solution)/shard_map/ppermute | solution.py:44
  37.5 1.0 %copy-start.8 = (bf16[4,32,1024]{2,1,0:T(8,128)(2,1)S(1)}, bf16[4,32,1024]{2,1,0:T(8,128)(2,1)}, u32[]{:S(2)}) copy-start(bf16[4,32,1024]{2,1,0:T(8,128)(2,1)} %param.10) | copy-start | bytes 786436
  38.5 7.6 %copy-start.1 = (f32[32,32,1024]{2,1,0:T(8,128)S(1)}, f32[32,32,1024]{2,1,0:T(8,128)}, u32[]{:S(2)}) copy-start(f32[32,32,1024]{2,1,0:T(8,128)} %param.7) | copy-start | bytes 12582916
  42.4 16.7 %collective-permute-start.9 = (bf16[4,32,1024]{2,0,1:T(4,128)(2,1)S(1)}, bf16[4,32,1024]{2,0,1:T(4,128)(2,1)S(1)}, u32[]{:S(2)}, u32[]{:S(2)}) collective-permute-start(bf16[4,32,1024]{2,0,1:T(4,128)(2,1)S(1)} %subtract_convert_fusion), channel_id=1, source_target_pairs={{0,12},{4,0},{8,4},{12,8},{1,13},{5,1},{9,5},{13,9},{2,14},{6,2},{... | collective-permute-start | bytes 786440 | tf_op jit(solution)/shard_map/ppermute | solution.py:121
  43.6 15.4 %collective-permute-start.8 = (bf16[4,32,1024]{2,0,1:T(4,128)(2,1)S(1)}, bf16[4,32,1024]{2,0,1:T(4,128)(2,1)S(1)}, u32[]{:S(2)}, u32[]{:S(2)}) collective-permute-start(bf16[4,32,1024]{2,0,1:T(4,128)(2,1)S(1)} %subtract_convert_fusion), channel_id=1, source_target_pairs={{0,8},{4,12},{8,0},{12,4},{1,9},{5,13},{9,1},{13,5},{2,10},{6,14},... | collective-permute-start | bytes 786440 | tf_op jit(solution)/shard_map/ppermute | solution.py:121
  45.2 13.8 %collective-permute-start.7 = (bf16[4,32,1024]{2,0,1:T(4,128)(2,1)S(1)}, bf16[4,32,1024]{2,0,1:T(4,128)(2,1)S(1)}, u32[]{:S(2)}, u32[]{:S(2)}) collective-permute-start(bf16[4,32,1024]{2,0,1:T(4,128)(2,1)S(1)} %subtract_convert_fusion), channel_id=1, source_target_pairs={{0,4},{4,8},{8,12},{12,0},{1,5},{5,9},{9,13},{13,1},{2,6},{6,10},{... | collective-permute-start | bytes 786440 | tf_op jit(solution)/shard_map/ppermute | solution.py:121
  46.0 13.0 %copy-start.6 = (bf16[4,32]{1,0:T(4,128)(2,1)S(1)}, bf16[4,32]{1,0:T(4,128)(2,1)}, u32[]{:S(2)}) copy-start(bf16[4,32]{1,0:T(4,128)(2,1)} %copy-done.5) | copy-start | bytes 772
  46.0 13.0 %copy-start.7 = (bf16[4,32]{1,0:T(4,128)(2,1)S(1)}, bf16[4,32]{1,0:T(4,128)(2,1)}, u32[]{:S(2)}) copy-start(bf16[4,32]{1,0:T(4,128)(2,1)} %get-tuple-element.16) | copy-start | bytes 772

commit v9 on v6

--- a/solution.py
+++ b/solution.py
@@ -73,26 +73,27 @@
     co = lax.axis_index("co")
     rep = zl * 2 + co
     band_y = lax.dynamic_slice_in_dim(along_y[0], rep * rows_here, rows_here, 1)
-    half = planes // 2
-    keep_y = jnp.einsum(
-        "sl,zlx->zsx",
-        band_y,
-        lax.dynamic_slice_in_dim(coarse, co * half, half, 0),
-        preferred_element_type=jnp.float32,
+    nrep = 4
+    part_z = planes // nrep
+    axes = ("zl", "co")
+    chunks = jnp.einsum(
+        "sl,zlx->zsx", band_y, coarse, preferred_element_type=jnp.float32
+    ).reshape(nrep, part_z, SLICES, width)
+    fwd_y = lax.dynamic_index_in_dim(chunks, rep, 0, keepdims=False)
+    for k in range(1, nrep):
+        sent = lax.dynamic_index_in_dim(chunks, (rep + k) % nrep, 0, keepdims=False)
+        got = lax.ppermute(sent.astype(jnp.bfloat16), axes, [(j, (j + k) % nrep) for j in range(nrep)])
+        fwd_y = fwd_y + got.astype(jnp.float32)
+    obs_y = lax.dynamic_slice_in_dim(slices_y, rep * part_z, part_z, 0)
+    resid_y = (obs_y.astype(jnp.float32) - fwd_y).astype(jnp.bfloat16)
+    placed = [resid_y]
+    for k in range(1, nrep):
+        placed.append(lax.ppermute(resid_y, axes, [(j, (j + k) % nrep) for j in range(nrep)]))
+    order = [(nrep - ((t - rep) % nrep)) % nrep for t in range(nrep)]
+    stacked = jnp.stack(placed, 0)
+    resid_y = jnp.concatenate(
+        [lax.dynamic_index_in_dim(stacked, order[t], 0, keepdims=False) for t in range(nrep)], 0
     )
-    give_y = jnp.einsum(
-        "sl,zlx->zsx",
-        band_y,
-        lax.dynamic_slice_in_dim(coarse, (1 - co) * half, half, 0),
-        preferred_element_type=jnp.float32,
-    ).astype(jnp.bfloat16)
-    fwd_y = keep_y + lax.ppermute(give_y, "co", [(0, 1), (1, 0)]).astype(jnp.float32)
-    fwd_y = halve(fwd_y, "zl", zl)
-    part_z = planes // 4
-    obs_y = lax.dynamic_slice_in_dim(slices_y, (co * 2 + zl) * part_z, part_z, 0)
-    resid_y = (obs_y.astype(jnp.float32) - fwd_y).astype(jnp.bfloat16)
-    resid_y = double(resid_y, "zl", zl)
-    resid_y = double(resid_y, "co", co)
     corr_y = jnp.einsum("sl,zsx->zlx", band_y, resid_y, preferred_element_type=jnp.float32)
 
     zb = lax.axis_index("zb")

time: 57.6 us -> 66.3 us (1.15)
  waiting for transfers between devices: 12.3 us -> 21.5 us
    ppermute x4 -> x6, waiting for transfers between devices: 2.46 us -> 12.2 us  [the longest x3 8.33 us: shards(): lax.ppermute(sent.astype(jnp.bfloat16), axes, [(j, (j + k) % nrep) for j...]
    ppermute x4 -> x6, starting transfers between devices: 9.43 us -> 6.74 us  [the longest x3 3.7 us: shards(): lax.ppermute(resid_y, axes, [(j, (j + k) % nrep) for j in range(nrep)])]
    ppermute x3, starting transfers between devices: 2.68 us -> 5.2 us  [shards(): got = lax.ppermute(sent, 'zq', [(j, (j + k) % group) for j in range(group)])]
    dot_general x1, matrix products: 0.69 us -> 2.7 us  [shards(): jnp.dot(resid_x, banded_x, preferred_element_type=jnp.float32)]
    unnamed x12 -> x14, local copies, waits for them, and re-layouts: 1.36 us -> 2.75 us
    dot_general x2 -> x1, matrix products: 1.79 us -> 0.49 us  [shards(): jnp.einsum('sl,zlx->zsx', band_y, coarse, preferred_element_type=jnp.floa...]
    convert_element_type x1, local copies, waits for them, and re-layouts: 1.12 us -> 0.17 us  [shards(): resid_x = (slices_x.reshape(planes * rows_here, count_x * SLICES).astype(...]
    convert_element_type x1, local copies, waits for them, and re-layouts: 1 us -> 0.2 us  [shards(): slices_x.reshape(planes * rows_here, count_x * SLICES).astype(jnp.float32)]
  transfers between devices with their start and end apart: 10 -> 12, of which waited for: 3 -> 7; matrix products, arithmetic and copies ran while one was open for 30% -> 18% of each run, Pallas kernels for 0% -> 0%
where the time goes in v9:
time: 66.3 us; the launch traced here: 66 us
  waiting for transfers between devices  21.5 us (32%)
  matrix products  18.8 us (28%)
  starting transfers between devices  14.4 us (22%)
  local copies, waits for them, and re-layouts  6.16 us (9%)
  other arithmetic  5 us (8%)
    ppermute x3, waiting for transfers between devices, shards(): lax.ppermute(resid_z, 'zq', [(j, (j + k) % group) for j in range(group)])  9.25 us
    ppermute x3, waiting for transfers between devices, shards(): lax.ppermute(sent.astype(jnp.bfloat16), axes, [(j, (j + k) % nrep) for j...  8.33 us
    dot_general x1, matrix products, shards(): jnp.einsum('sl,zsx->zlx', band_y, resid_y, preferred_element_type=jnp.flo...  5.99 us
    ppermute x3, starting transfers between devices, shards(): got = lax.ppermute(sent, 'zq', [(j, (j + k) % group) for j in range(group)])  5.2 us
    ppermute x3, waiting for transfers between devices, shards(): lax.ppermute(resid_y, axes, [(j, (j + k) % nrep) for j in range(nrep)])  3.89 us
    dot_general x1, matrix products, shards(): jnp.einsum('sl,lyx->syx', own_rows, coarse, preferred_element_type=jnp.fl...  3.74 us
    ppermute x3, starting transfers between devices, shards(): lax.ppermute(resid_y, axes, [(j, (j + k) % nrep) for j in range(nrep)])  3.7 us
    ppermute x3, starting transfers between devices, shards(): lax.ppermute(sent.astype(jnp.bfloat16), axes, [(j, (j + k) % nrep) for j...  3.04 us
  transfers between devices with their start and end apart: 12, of which 7 were waited for; matrix products, arithmetic and copies ran while one was open for 18% of the time, Pallas kernels for 0%

profile of v9, /device:TPU:1, one launch (start us, length us, event | category | flops | bytes accessed | tf_op | source)
XLA Modules:
  0.0 66.0 jit_solution(1880197834139188984)
XLA Ops:
  0.8 1.0 %fusion.40 = f32[25,16,128]{2,0,1:T(8,128)S(1)} fusion(f32[4,16,128]{2,1,0:T(8,128)S(1)} %copy-done, s32[25]{0:T(128)} %param.12), kind=kOutput, calls=%fused_computation.53 | convolution fusion | flops 2457700 | bytes 237668 | tf_op jit(solution)/shard_map/bk,ksl->bsl/dot_general | solution.py:19
  1.7 1.0 %fusion.13 = bf16[25,16,128]{2,1,0:T(8,128)(2,1)S(1)} fusion(s32[25,128]{1,0:T(8,128)S(1)} %add_select_fusion, f32[25,16,128]{2,0,1:T(8,128)S(1)} %fusion.40), kind=kOutput, calls=%fused_computation.14 | convolution fusion | flops 79104000 | bytes 320000 | tf_op jit(solution)/shard_map/bsj,bjl->bsl/dot_general | solution.py:23
  2.8 2.5 %convert_element_type.79 = bf16[32,32,1024]{2,1,0:T(8,128)(2,1)S(1)} convert(f32[32,32,1024]{2,1,0:T(8,128)} %param.7) | non-fusion elementwise | flops 1048576 | bytes 6291456 | tf_op jit(solution)/shard_map/convert_element_type | solution.py:58
  5.4 2.3 %fusion.8 = bf16[12,32,1024]{2,0,1:T(8,128)(2,1)S(1)} fusion(bf16[32,32,1024]{2,1,0:T(8,128)(2,1)S(1)} %convert_element_type.79, bf16[4,32]{1,0:T(4,128)(2,1)S(1)} %get-tuple-element.18, bf16[4,32]{1,0:T(4,128)(2,1)S(1)} %get-tuple-element.17, bf16[4,32]{1,0:T(4,128)(2,1)S(1)} %get-tuple-element.16), kind=kOutput, calls=%fused_computation.10 | convolution fusion | flops 25561344 | bytes 2884352 | tf_op jit(solution)/shard_map/sl,lyx->syx/dot_general | solution.py:111
  7.8 1.1 %fusion.76 = (bf16[4,32,1024]{2,0,1:T(4,128)(2,1)}, bf16[4,32,1024]{2,0,1:T(4,128)(2,1)}, bf16[4,32,1024]{2,0,1:T(4,128)(2,1)}) fusion(bf16[12,32,1024]{2,0,1:T(8,128)(2,1)S(1)} %fusion.8), kind=kLoop, calls=%fused_computation.95 | loop fusion | bytes 1572864 | tf_op jit(solution)/shard_map/slice | solution.py:115
  8.8 2.1 %collective-permute-start.6 = (bf16[4,32,1024]{2,0,1:T(4,128)(2,1)}, bf16[4,32,1024]{2,0,1:T(4,128)(2,1)}, u32[]{:S(2)}, u32[]{:S(2)}) collective-permute-start(bf16[4,32,1024]{2,0,1:T(4,128)(2,1)} %get-tuple-element.12), channel_id=1, source_target_pairs={{0,4},{4,8},{8,12},{12,0},{1,5},{5,9},{9,13},{13,1},{2,6},{6,10},{... | collective-permute-start | bytes 786440 | tf_op jit(solution)/shard_map/ppermute | solution.py:116
  10.9 1.4 %collective-permute-start.8 = (bf16[4,32,1024]{2,0,1:T(4,128)(2,1)}, bf16[4,32,1024]{2,0,1:T(4,128)(2,1)}, u32[]{:S(2)}, u32[]{:S(2)}) collective-permute-start(bf16[4,32,1024]{2,0,1:T(4,128)(2,1)} %get-tuple-element.13), channel_id=1, source_target_pairs={{0,12},{4,0},{8,4},{12,8},{1,13},{5,1},{9,5},{13,9},{2,14},{6,2},{... | collective-permute-start | bytes 786440 | tf_op jit(solution)/shard_map/ppermute | solution.py:116
  12.4 1.6 %collective-permute-start.7 = (bf16[4,32,1024]{2,0,1:T(4,128)(2,1)}, bf16[4,32,1024]{2,0,1:T(4,128)(2,1)}, u32[]{:S(2)}, u32[]{:S(2)}) collective-permute-start(bf16[4,32,1024]{2,0,1:T(4,128)(2,1)} %get-tuple-element.14), channel_id=1, source_target_pairs={{0,8},{4,12},{8,0},{12,4},{1,9},{5,13},{9,1},{13,5},{2,10},{6,14},... | collective-permute-start | bytes 786440 | tf_op jit(solution)/shard_map/ppermute | solution.py:116
  14.5 1.3 %copy-done.3 = f32[16,32,1024]{2,0,1:T(8,128)} copy-done((f32[16,32,1024]{2,0,1:T(8,128)}, f32[16,32,1024]{2,0,1:T(8,128)S(1)}, u32[]{:S(2)}) %copy-start.3) | copy-done | bytes 2097176
  16.8 3.0 %collective-permute-start = (bf16[8,16,1024]{2,1,0:T(8,128)(2,1)}, bf16[8,16,1024]{2,1,0:T(8,128)(2,1)}, u32[]{:S(2)}, u32[]{:S(2)}) collective-permute-start(bf16[8,16,1024]{2,1,0:T(8,128)(2,1)} %get-tuple-element.5), channel_id=1, source_target_pairs={{0,1},{1,2},{2,3},{3,0},{4,5},{5,6},{6,7},{7,4},{8,9},{9,10},{10,1... | collective-permute-start | bytes 786440 | tf_op jit(solution)/shard_map/ppermute | solution.py:85
  22.0 3.8 %collective-permute-done = bf16[8,16,1024]{2,1,0:T(8,128)(2,1)} collective-permute-done((bf16[8,16,1024]{2,1,0:T(8,128)(2,1)}, bf16[8,16,1024]{2,1,0:T(8,128)(2,1)}, u32[]{:S(2)}, u32[]{:S(2)}) %collective-permute-start) | collective-permute-done | bytes 262176 | tf_op jit(solution)/shard_map/ppermute | solution.py:85
  25.8 2.7 %fusion.77 = f32[32,32,1024]{2,1,0:T(8,128)} fusion(bf16[32,32,128]{2,1,0:T(8,128)(2,1)S(1)} %bitcast.93, bf16[128,1024,1]{1,0,2:T(8,128)(2,1)S(1)} %copy-done.4), kind=kOutput, calls=%fused_computation.96 | convolution fusion | flops 268435456 | bytes 4718592 | tf_op jit(solution)/shard_map/dot_general | solution.py:68
  28.6 4.5 %collective-permute-done.1 = bf16[8,16,1024]{2,1,0:T(8,128)(2,1)S(1)} collective-permute-done((bf16[8,16,1024]{2,1,0:T(8,128)(2,1)}, bf16[8,16,1024]{2,1,0:T(8,128)(2,1)S(1)}, u32[]{:S(2)}, u32[]{:S(2)}) %collective-permute-start.1) | collective-permute-done | bytes 262176 | tf_op jit(solution)/shard_map/ppermute | solution.py:85
  33.1 1.5 %fusion.33 = bf16[8,16,1024]{2,1,0:T(8,128)(2,1)S(1)} fusion(bf16[8,16,1024]{2,1,0:T(8,128)(2,1)} %collective-permute-done.2, bf16[8,16,1024]{2,1,0:T(8,128)(2,1)S(1)} %collective-permute-done.1, bf16[8,16,1024]{2,1,0:T(8,128)(2,1)} %collective-permute-done, f32[4,8,16,1024]{3,2,1,0:T(8,128)} %bitcast.91, s32[]{:T(128)S(6)} %select_n.145, ...), kind=kLoop, calls=%fused_computation.36 | loop fusion | flops 1179648 | bytes 1835016 | tf_op jit(solution)/shard_map/convert_element_type | solution.py:88
  34.5 1.8 %collective-permute-start.5 = (bf16[8,16,1024]{2,1,0:T(8,128)(2,1)S(1)}, bf16[8,16,1024]{2,1,0:T(8,128)(2,1)S(1)}, u32[]{:S(2)}, u32[]{:S(2)}) collective-permute-start(bf16[8,16,1024]{2,1,0:T(8,128)(2,1)S(1)} %fusion.33), channel_id=1, source_target_pairs={{0,3},{1,0},{2,1},{3,2},{4,7},{5,4},{6,5},{7,6},{8,11},{9,8},{10,9... | collective-permute-start | bytes 786440 | tf_op jit(solution)/shard_map/ppermute | solution.py:91
  36.6 1.7 %collective-permute-start.3 = (bf16[8,16,1024]{2,1,0:T(8,128)(2,1)S(1)}, bf16[8,16,1024]{2,1,0:T(8,128)(2,1)S(1)}, u32[]{:S(2)}, u32[]{:S(2)}) collective-permute-start(bf16[8,16,1024]{2,1,0:T(8,128)(2,1)S(1)} %fusion.33), channel_id=1, source_target_pairs={{0,1},{1,2},{2,3},{3,0},{4,5},{5,6},{6,7},{7,4},{8,9},{9,10},{10,1... | collective-permute-start | bytes 786440 | tf_op jit(solution)/shard_map/ppermute | solution.py:91
  38.2 3.7 %subtract_convert_fusion = bf16[4,32,1024]{2,0,1:T(4,128)(2,1)S(1)} fusion(bf16[4,32,1024]{2,0,1:T(4,128)(2,1)} %collective-permute-done.8, bf16[4,32,1024]{2,0,1:T(4,128)(2,1)} %collective-permute-done.7, bf16[4,32,1024]{2,0,1:T(4,128)(2,1)} %collective-permute-done.6, bf16[4,32,1024]{2,1,0:T(8,128)(2,1)S(1)} %copy-done.6, ...), kind=kOutput, calls=%fused_computation.37 | convolution fusion | flops 9568256 | bytes 3408908 | tf_op jit(solution)/shard_map/sl,lyx->syx/dot_general | solution.py:106
  42.7 1.5 %collective-permute-start.10 = (bf16[4,32,1024]{2,0,1:T(4,128)(2,1)S(1)}, bf16[4,32,1024]{2,0,1:T(4,128)(2,1)S(1)}, u32[]{:S(2)}, u32[]{:S(2)}) collective-permute-start(bf16[4,32,1024]{2,0,1:T(4,128)(2,1)S(1)} %subtract_convert_fusion), channel_id=1, source_target_pairs={{0,8},{4,12},{8,0},{12,4},{1,9},{5,13},{9,1},{13,5},{2,10},{6,14},... | collective-permute-start | bytes 786440 | tf_op jit(solution)/shard_map/ppermute | solution.py:122
  44.6 3.7 %collective-permute-done.3 = bf16[8,16,1024]{2,1,0:T(8,128)(2,1)S(1)} collective-permute-done((bf16[8,16,1024]{2,1,0:T(8,128)(2,1)S(1)}, bf16[8,16,1024]{2,1,0:T(8,128)(2,1)S(1)}, u32[]{:S(2)}, u32[]{:S(2)}) %collective-permute-start.3) | collective-permute-done | bytes 262176 | tf_op jit(solution)/shard_map/ppermute | solution.py:91
  48.6 1.8 %collective-permute-done.11 = bf16[4,32,1024]{2,0,1:T(4,128)(2,1)S(1)} collective-permute-done((bf16[4,32,1024]{2,0,1:T(4,128)(2,1)S(1)}, bf16[4,32,1024]{2,0,1:T(4,128)(2,1)S(1)}, u32[]{:S(2)}, u32[]{:S(2)}) %collective-permute-start.11) | collective-permute-done | bytes 262176 | tf_op jit(solution)/shard_map/ppermute | solution.py:122
  50.4 1.9 %collective-permute-done.10 = bf16[4,32,1024]{2,0,1:T(4,128)(2,1)S(1)} collective-permute-done((bf16[4,32,1024]{2,0,1:T(4,128)(2,1)S(1)}, bf16[4,32,1024]{2,0,1:T(4,128)(2,1)S(1)}, u32[]{:S(2)}, u32[]{:S(2)}) %collective-permute-start.10) | collective-permute-done | bytes 262176 | tf_op jit(solution)/shard_map/ppermute | solution.py:122
  52.3 5.5 %collective-permute-done.9 = bf16[4,32,1024]{2,0,1:T(4,128)(2,1)S(1)} collective-permute-done((bf16[4,32,1024]{2,0,1:T(4,128)(2,1)S(1)}, bf16[4,32,1024]{2,0,1:T(4,128)(2,1)S(1)}, u32[]{:S(2)}, u32[]{:S(2)}) %collective-permute-start.9) | collective-permute-done | bytes 262176 | tf_op jit(solution)/shard_map/ppermute | solution.py:122
  58.6 1.4 %copy-done.1 = f32[32,32,1024]{2,1,0:T(8,128)S(1)} copy-done((f32[32,32,1024]{2,1,0:T(8,128)S(1)}, f32[32,32,1024]{2,1,0:T(8,128)}, u32[]{:S(2)}) %copy-start.1) | copy-done | bytes 4194328
  60.0 6.0 %fusion.2 = f32[32,32,1024]{2,1,0:T(8,128)} fusion(f32[32,32,1024]{2,1,0:T(8,128)S(1)} %copy-done.1, f32[32,32,1024]{2,1,0:T(8,128)S(1)} %copy-done.2, f32[32,32,1024]{2,0,1:T(8,128)S(1)} %fusion.21, bf16[8,16,1024]{2,1,0:T(8,128)(2,1)S(1)} %get-tuple-element.9, bf16[8,16,1024]{2,1,0:T(8,128)(2,1)S(1)} %get-tuple-element.10, ...), kind=kOutput, calls=%fused_computation.3 | convolution fusion | flops 39321600 | bytes 17829892 | tf_op jit(solution)/shard_map/sl,zsx->zlx/dot_general | solution.py:97
  (40 shorter events, 6.9 us)
Async XLA Ops:
  0.0 0.8 %copy-start = (f32[4,16,128]{2,1,0:T(8,128)S(1)}, f32[4,16,128]{2,1,0:T(8,128)}, u32[]{:S(2)}) copy-start(f32[4,16,128]{2,1,0:T(8,128)} %param.11) | copy-start | bytes 98308
  8.8 27.7 %collective-permute-start.6 = (bf16[4,32,1024]{2,0,1:T(4,128)(2,1)}, bf16[4,32,1024]{2,0,1:T(4,128)(2,1)}, u32[]{:S(2)}, u32[]{:S(2)}) collective-permute-start(bf16[4,32,1024]{2,0,1:T(4,128)(2,1)} %get-tuple-element.12), channel_id=1, source_target_pairs={{0,4},{4,8},{8,12},{12,0},{1,5},{5,9},{9,13},{13,1},{2,6},{6,10},{... | collective-permute-start | bytes 786440 | tf_op jit(solution)/shard_map/ppermute | solution.py:116
  10.9 27.3 %collective-permute-start.8 = (bf16[4,32,1024]{2,0,1:T(4,128)(2,1)}, bf16[4,32,1024]{2,0,1:T(4,128)(2,1)}, u32[]{:S(2)}, u32[]{:S(2)}) collective-permute-start(bf16[4,32,1024]{2,0,1:T(4,128)(2,1)} %get-tuple-element.13), channel_id=1, source_target_pairs={{0,12},{4,0},{8,4},{12,8},{1,13},{5,1},{9,5},{13,9},{2,14},{6,2},{... | collective-permute-start | bytes 786440 | tf_op jit(solution)/shard_map/ppermute | solution.py:116
  12.4 25.9 %collective-permute-start.7 = (bf16[4,32,1024]{2,0,1:T(4,128)(2,1)}, bf16[4,32,1024]{2,0,1:T(4,128)(2,1)}, u32[]{:S(2)}, u32[]{:S(2)}) collective-permute-start(bf16[4,32,1024]{2,0,1:T(4,128)(2,1)} %get-tuple-element.14), channel_id=1, source_target_pairs={{0,8},{4,12},{8,0},{12,4},{1,9},{5,13},{9,1},{13,5},{2,10},{6,14},... | collective-permute-start | bytes 786440 | tf_op jit(solution)/shard_map/ppermute | solution.py:116
  14.5 1.3 %copy-start.3 = (f32[16,32,1024]{2,0,1:T(8,128)}, f32[16,32,1024]{2,0,1:T(8,128)S(1)}, u32[]{:S(2)}) copy-start(f32[16,32,1024]{2,0,1:T(8,128)S(1)} %fusion.60) | copy-start | bytes 6291460
  14.5 6.2 %copy-start.5 = (bf16[32,32,128]{2,1,0:T(8,128)(2,1)S(1)}, bf16[32,32,128]{2,1,0:T(8,128)(2,1)}, u32[]{:S(2)}) copy-start(bf16[32,32,128]{2,1,0:T(8,128)(2,1)} %param.8) | copy-start | bytes 786436
  16.8 9.1 %collective-permute-start = (bf16[8,16,1024]{2,1,0:T(8,128)(2,1)}, bf16[8,16,1024]{2,1,0:T(8,128)(2,1)}, u32[]{:S(2)}, u32[]{:S(2)}) collective-permute-start(bf16[8,16,1024]{2,1,0:T(8,128)(2,1)} %get-tuple-element.5), channel_id=1, source_target_pairs={{0,1},{1,2},{2,3},{3,0},{4,5},{5,6},{6,7},{7,4},{8,9},{9,10},{10,1... | collective-permute-start | bytes 786440 | tf_op jit(solution)/shard_map/ppermute | solution.py:85
  19.8 8.7 %collective-permute-start.2 = (bf16[8,16,1024]{2,1,0:T(8,128)(2,1)}, bf16[8,16,1024]{2,1,0:T(8,128)(2,1)}, u32[]{:S(2)}, u32[]{:S(2)}) collective-permute-start(bf16[8,16,1024]{2,1,0:T(8,128)(2,1)} %get-tuple-element.6), channel_id=1, source_target_pairs={{0,3},{1,0},{2,1},{3,2},{4,7},{5,4},{6,5},{7,6},{8,11},{9,8},{10,9... | collective-permute-start | bytes 786440 | tf_op jit(solution)/shard_map/ppermute | solution.py:85
  21.0 4.8 %copy-start.4 = (bf16[128,1024,1]{1,0,2:T(8,128)(2,1)S(1)}, bf16[128,1024,1]{1,0,2:T(8,128)(2,1)}, u32[]{:S(2)}) copy-start(bf16[128,1024,1]{1,0,2:T(8,128)(2,1)} %reshape.86) | copy-start | bytes 786436
  25.8 7.2 %collective-permute-start.1 = (bf16[8,16,1024]{2,1,0:T(8,128)(2,1)}, bf16[8,16,1024]{2,1,0:T(8,128)(2,1)S(1)}, u32[]{:S(2)}, u32[]{:S(2)}) collective-permute-start(bf16[8,16,1024]{2,1,0:T(8,128)(2,1)} %get-tuple-element.7), channel_id=1, source_target_pairs={{0,2},{1,3},{2,0},{3,1},{4,6},{5,7},{6,4},{7,5},{8,10},{9,11},{10,... | collective-permute-start | bytes 786440 | tf_op jit(solution)/shard_map/ppermute | solution.py:85
  25.8 12.4 %copy-start.6 = (bf16[4,32,1024]{2,1,0:T(8,128)(2,1)S(1)}, bf16[4,32,1024]{2,1,0:T(8,128)(2,1)}, u32[]{:S(2)}) copy-start(bf16[4,32,1024]{2,1,0:T(8,128)(2,1)} %param.10) | copy-start | bytes 786436
  34.5 9.7 %collective-permute-start.5 = (bf16[8,16,1024]{2,1,0:T(8,128)(2,1)S(1)}, bf16[8,16,1024]{2,1,0:T(8,128)(2,1)S(1)}, u32[]{:S(2)}, u32[]{:S(2)}) collective-permute-start(bf16[8,16,1024]{2,1,0:T(8,128)(2,1)S(1)} %fusion.33), channel_id=1, source_target_pairs={{0,3},{1,0},{2,1},{3,2},{4,7},{5,4},{6,5},{7,6},{8,11},{9,8},{10,9... | collective-permute-start | bytes 786440 | tf_op jit(solution)/shard_map/ppermute | solution.py:91
  36.3 8.3 %collective-permute-start.4 = (bf16[8,16,1024]{2,1,0:T(8,128)(2,1)S(1)}, bf16[8,16,1024]{2,1,0:T(8,128)(2,1)S(1)}, u32[]{:S(2)}, u32[]{:S(2)}) collective-permute-start(bf16[8,16,1024]{2,1,0:T(8,128)(2,1)S(1)} %fusion.33), channel_id=1, source_target_pairs={{0,2},{1,3},{2,0},{3,1},{4,6},{5,7},{6,4},{7,5},{8,10},{9,11},{10,... | collective-permute-start | bytes 786440 | tf_op jit(solution)/shard_map/ppermute | solution.py:91
  36.6 11.7 %collective-permute-start.3 = (bf16[8,16,1024]{2,1,0:T(8,128)(2,1)S(1)}, bf16[8,16,1024]{2,1,0:T(8,128)(2,1)S(1)}, u32[]{:S(2)}, u32[]{:S(2)}) collective-permute-start(bf16[8,16,1024]{2,1,0:T(8,128)(2,1)S(1)} %fusion.33), channel_id=1, source_target_pairs={{0,1},{1,2},{2,3},{3,0},{4,5},{5,6},{6,7},{7,4},{8,9},{9,10},{10,1... | collective-permute-start | bytes 786440 | tf_op jit(solution)/shard_map/ppermute | solution.py:91
  42.0 8.4 %collective-permute-start.11 = (bf16[4,32,1024]{2,0,1:T(4,128)(2,1)S(1)}, bf16[4,32,1024]{2,0,1:T(4,128)(2,1)S(1)}, u32[]{:S(2)}, u32[]{:S(2)}) collective-permute-start(bf16[4,32,1024]{2,0,1:T(4,128)(2,1)S(1)} %subtract_convert_fusion), channel_id=1, source_target_pairs={{0,12},{4,0},{8,4},{12,8},{1,13},{5,1},{9,5},{13,9},{2,14},{6,2},{... | collective-permute-start | bytes 786440 | tf_op jit(solution)/shard_map/ppermute | solution.py:122
  42.7 9.6 %collective-permute-start.10 = (bf16[4,32,1024]{2,0,1:T(4,128)(2,1)S(1)}, bf16[4,32,1024]{2,0,1:T(4,128)(2,1)S(1)}, u32[]{:S(2)}, u32[]{:S(2)}) collective-permute-start(bf16[4,32,1024]{2,0,1:T(4,128)(2,1)S(1)} %subtract_convert_fusion), channel_id=1, source_target_pairs={{0,8},{4,12},{8,0},{12,4},{1,9},{5,13},{9,1},{13,5},{2,10},{6,14},... | collective-permute-start | bytes 786440 | tf_op jit(solution)/shard_map/ppermute | solution.py:122
  44.2 13.6 %collective-permute-start.9 = (bf16[4,32,1024]{2,0,1:T(4,128)(2,1)S(1)}, bf16[4,32,1024]{2,0,1:T(4,128)(2,1)S(1)}, u32[]{:S(2)}, u32[]{:S(2)}) collective-permute-start(bf16[4,32,1024]{2,0,1:T(4,128)(2,1)S(1)} %subtract_convert_fusion), channel_id=1, source_target_pairs={{0,4},{4,8},{8,12},{12,0},{1,5},{5,9},{9,13},{13,1},{2,6},{6,10},{... | collective-permute-start | bytes 786440 | tf_op jit(solution)/shard_map/ppermute | solution.py:122
  48.3 10.3 %copy-start.2 = (f32[32,32,1024]{2,1,0:T(8,128)S(1)}, f32[32,32,1024]{2,1,0:T(8,128)}, u32[]{:S(2)}) copy-start(f32[32,32,1024]{2,1,0:T(8,128)} %fusion.77) | copy-start | bytes 12582916
  57.8 2.2 %copy-start.1 = (f32[32,32,1024]{2,1,0:T(8,128)S(1)}, f32[32,32,1024]{2,1,0:T(8,128)}, u32[]{:S(2)}) copy-start(f32[32,32,1024]{2,1,0:T(8,128)} %param.7) | copy-start | bytes 12582916

commit v10 on v6

--- a/solution.py
+++ b/solution.py
@@ -101,32 +101,19 @@
     mat_z = lax.dynamic_index_in_dim(along_z, zb, 0, keepdims=False)
     band_z = lax.dynamic_slice_in_dim(mat_z, zq * planes, planes, 1)
     piece = SLICES // group
-    own_rows = lax.dynamic_slice_in_dim(band_z, zq * piece, piece, 0)
-    fwd_z = jnp.einsum("sl,lyx->syx", own_rows, coarse, preferred_element_type=jnp.float32)
-    far_rows = jnp.concatenate(
-        [lax.dynamic_slice_in_dim(band_z, ((zq + k) % group) * piece, piece, 0) for k in range(1, group)],
-        0,
+    full_z = jnp.einsum(
+        "sl,lyx->syx", band_z, coarse, preferred_element_type=jnp.float32
+    ).reshape((group, piece) + coarse.shape[1:])
+    came = lax.all_to_all(full_z.astype(jnp.bfloat16), "zq", 0, 0, tiled=True)
+    others = (jnp.arange(group) != zq)[:, None, None, None]
+    fwd_z = jnp.sum(jnp.where(others, came.astype(jnp.float32), 0.0), 0)
+    fwd_z = fwd_z + lax.dynamic_index_in_dim(full_z, zq, 0, keepdims=False)
+    resid_z = (slices_z.astype(jnp.float32) - fwd_z).astype(jnp.bfloat16)
+    every = jnp.broadcast_to(resid_z[None], (group,) + resid_z.shape)
+    gathered = lax.all_to_all(every, "zq", 0, 0, tiled=True).reshape(
+        (SLICES,) + resid_z.shape[1:]
     )
-    far_z = jnp.einsum(
-        "sl,lyx->syx", far_rows, coarse, preferred_element_type=jnp.float32
-    ).astype(jnp.bfloat16)
-    for k in range(1, group):
-        sent = far_z[(k - 1) * piece : k * piece]
-        got = lax.ppermute(sent, "zq", [(j, (j + k) % group) for j in range(group)])
-        fwd_z = fwd_z + got.astype(jnp.float32)
-    resid_z = (slices_z.astype(jnp.float32) - fwd_z).astype(jnp.bfloat16)
-    pieces = [resid_z]
-    rows = [lax.dynamic_slice_in_dim(band_z, zq * piece, piece, 0)]
-    for k in range(1, group):
-        pieces.append(lax.ppermute(resid_z, "zq", [(j, (j + k) % group) for j in range(group)]))
-        src = (zq - k + group) % group
-        rows.append(lax.dynamic_slice_in_dim(band_z, src * piece, piece, 0))
-    corr_z = jnp.einsum(
-        "sl,syx->lyx",
-        jnp.concatenate(rows, 0),
-        jnp.concatenate(pieces, 0),
-        preferred_element_type=jnp.float32,
-    )
+    corr_z = jnp.einsum("sl,syx->lyx", band_z, gathered, preferred_element_type=jnp.float32)
 
     return volume + step_size * (corr_x + corr_y + corr_z)
 

time: 57.6 us -> 67 us (1.16)
  the two profiles are of different devices: /device:TPU:1 before, /device:TPU:4 now
where the time goes in v10:
time: 67 us; the launch traced here: 66.3 us
  matrix products  23.1 us (34%)
  starting transfers between devices  12.8 us (19%)
  other arithmetic  12.7 us (19%)
  local copies, waits for them, and re-layouts  12.4 us (19%)
  waiting for transfers between devices  5.04 us (8%)
    dot_general x1, matrix products, shards(): jnp.einsum('sl,zsx->zlx', band_y, resid_y, preferred_element_type=jnp.flo...  8.14 us
    all_to_all x1, starting transfers between devices, shards(): came = lax.all_to_all(full_z.astype(jnp.bfloat16), 'zq', 0, 0, tiled=True)  4.6 us
    all_to_all x1, starting transfers between devices, shards(): lax.all_to_all(every, 'zq', 0, 0, tiled=True)  4.52 us
    dot_general x1, matrix products, shards(): jnp.einsum('sl,lyx->syx', band_z, coarse, preferred_element_type=jnp.floa...  4.42 us
    dot_general x1, matrix products, shards(): jnp.dot(resid_x, banded_x, preferred_element_type=jnp.float32)  3.72 us
    unnamed x24, local copies, waits for them, and re-layouts  3.42 us
    select_n x2, other arithmetic, double(): low = jnp.where(me == 0, values, other)  3.21 us
    all_to_all x1, waiting for transfers between devices, shards(): lax.all_to_all(every, 'zq', 0, 0, tiled=True)  2.85 us
  transfers between devices with their start and end apart: 6, of which 2 were waited for; matrix products, arithmetic and copies ran while one was open for 43% of the time, Pallas kernels for 0%

profile of v10, /device:TPU:4, one launch (start us, length us, event | category | flops | bytes accessed | tf_op | source)
XLA Modules:
  0.0 66.3 jit_solution(18090311512090456253)
XLA Ops:
  0.8 1.0 %fusion.24 = f32[25,16,128]{2,0,1:T(8,128)S(1)} fusion(f32[4,16,128]{2,1,0:T(8,128)S(1)} %copy-done, s32[25]{0:T(128)} %param.12), kind=kOutput, calls=%fused_computation.39 | convolution fusion | flops 2457700 | bytes 237668 | tf_op jit(solution)/shard_map/bk,ksl->bsl/dot_general | solution.py:19
  1.8 1.0 %fusion.10 = bf16[25,16,128]{2,1,0:T(8,128)(2,1)S(1)} fusion(s32[25,128]{1,0:T(8,128)S(1)} %add_select_fusion, f32[25,16,128]{2,0,1:T(8,128)S(1)} %fusion.24), kind=kOutput, calls=%fused_computation.16 | convolution fusion | flops 79104000 | bytes 320000 | tf_op jit(solution)/shard_map/bsj,bjl->bsl/dot_general | solution.py:23
  2.8 2.6 %convert_element_type.61 = bf16[32,32,1024]{2,1,0:T(8,128)(2,1)S(1)} convert(f32[32,32,1024]{2,1,0:T(8,128)} %param.7) | non-fusion elementwise | flops 1048576 | bytes 6291456 | tf_op jit(solution)/shard_map/convert_element_type | solution.py:58
  5.4 1.2 %fusion.8 = bf16[16,16,1024]{2,1,0:T(8,128)(2,1)} fusion(bf16[32,32,1024]{2,1,0:T(8,128)(2,1)S(1)} %convert_element_type.61, s32[]{:T(128)S(6)} %select_n.78, bf16[1,16,128]{2,1,0:T(8,128)(2,1)S(1)} %slice.13, s32[]{:T(128)S(6)} %select_n.77), kind=kOutput, calls=%fused_computation.14 | convolution fusion | flops 17039360 | bytes 1576968 | tf_op jit(solution)/shard_map/sl,zlx->zsx/dot_general | solution.py:83
  6.6 4.4 %fusion.46 = (bf16[4,4,32,1024]{3,1,2,0:T(4,128)(2,1)}, f32[4,4,32,1024]{3,1,2,0:T(4,128)}) fusion(bf16[4,4,32,1]{2,1,3,0:T(4,128)(2,1)S(1)} %bitcast.73, bf16[32,32,1024]{2,1,0:T(8,128)(2,1)S(1)} %convert_element_type.61), kind=kOutput, calls=%fused_computation.68 | convolution fusion | flops 34078720 | bytes 5243904 | tf_op jit(solution)/shard_map/sl,lyx->syx/dot_general | solution.py:104
  11.1 4.6 %all-to-all-start = ((bf16[4,4,32,1024]{3,1,2,0:T(4,128)(2,1)}), bf16[4,4,32,1024]{3,1,2,0:T(4,128)(2,1)S(1)}, u32[]{:S(2)}, u32[]{:S(2)}) async-start(bf16[4,4,32,1024]{3,1,2,0:T(4,128)(2,1)} %get-tuple-element.9), calls=%async_computation | async-start | bytes 2097152 | tf_op jit(solution)/shard_map/all_to_all | solution.py:107
  16.5 1.4 %convert_add_fusion = f32[16,16,1024]{2,1,0:T(8,128)S(1)} fusion(bf16[16,16,1024]{2,1,0:T(8,128)(2,1)} %collective-permute-done, bf16[32,32,1024]{2,1,0:T(8,128)(2,1)S(1)} %convert_element_type.61, s32[]{:T(128)S(6)} %select_n.76, bf16[1,16,128]{2,1,0:T(8,128)(2,1)S(1)} %slice.13, s32[]{:T(128)S(6)} %select_n.77), kind=kOutput, calls=%fused_computation.20 | convolution fusion | flops 17301504 | bytes 2625544 | tf_op jit(solution)/shard_map/sl,zlx->zsx/dot_general | solution.py:77
  19.6 1.9 %collective-permute-start.1 = (bf16[8,16,1024]{2,1,0:T(8,128)(2,1)}, bf16[8,16,1024]{2,1,0:T(8,128)(2,1)}, u32[]{:S(2)}, u32[]{:S(2)}) collective-permute-start(bf16[8,16,1024]{2,1,0:T(8,128)(2,1)} %dynamic-slice_convert_fusion), channel_id=1, source_target_pairs={{0,2},{2,0},{1,3},{3,1},{4,6},{6,4},{5,7},{7,5},{8,10},{10,8},{9,1... | collective-permute-start | bytes 786440 | tf_op jit(solution)/shard_map/ppermute | solution.py:39
  22.5 2.0 %copy.31 = f32[1024,128]{0,1:T(8,128)} copy(f32[1024,128]{1,0:T(8,128)} %bitcast_convert_fusion) | data formatting | bytes 1048576 | tf_op jit(solution)/shard_map/convert_element_type | solution.py:66
  24.5 1.9 %constant_dynamic-slice_fusion.1 = f32[1,4,32,1024]{3,1,2,0:T(4,128)} fusion(f32[4,4,32,1024]{3,1,2,0:T(4,128)} %get-tuple-element.10, s32[]{:T(128)S(6)} %select_n.90), kind=kLoop, calls=%fused_computation.62 | loop fusion | bytes 1048580 | tf_op jit(solution)/shard_map/jit(dynamic_index_in_dim)/dynamic_slice | solution.py:110
  26.4 2.2 %collective-permute-done.1 = bf16[8,16,1024]{2,1,0:T(8,128)(2,1)} collective-permute-done((bf16[8,16,1024]{2,1,0:T(8,128)(2,1)}, bf16[8,16,1024]{2,1,0:T(8,128)(2,1)}, u32[]{:S(2)}, u32[]{:S(2)}) %collective-permute-start.1) | collective-permute-done | bytes 262176 | tf_op jit(solution)/shard_map/ppermute | solution.py:39
  28.6 2.0 %subtract_convert_fusion = bf16[8,16,1024]{2,1,0:T(8,128)(2,1)} fusion(bf16[8,16,1024]{2,1,0:T(8,128)(2,1)} %collective-permute-done.1, f32[16,16,1024]{2,1,0:T(8,128)} %copy-done.2, s32[]{:T(128)S(6)} %select_n.79, bf16[32,16,1024]{2,1,0:T(8,128)(2,1)} %param.9, s32[]{:T(128)S(6)} %select_n.75), kind=kLoop, calls=%fused_computation.28 | loop fusion | flops 655360 | bytes 1310728 | tf_op jit(solution)/shard_map/convert_element_type | solution.py:93
  30.5 1.7 %collective-permute-start.2 = (bf16[8,16,1024]{2,1,0:T(8,128)(2,1)}, bf16[8,16,1024]{2,1,0:T(8,128)(2,1)}, u32[]{:S(2)}, u32[]{:S(2)}) collective-permute-start(bf16[8,16,1024]{2,1,0:T(8,128)(2,1)} %subtract_convert_fusion), channel_id=1, source_target_pairs={{0,2},{2,0},{1,3},{3,1},{4,6},{6,4},{5,7},{7,5},{8,10},{10,8},{9,1... | collective-permute-start | bytes 786440 | tf_op jit(solution)/shard_map/ppermute | solution.py:44
  33.0 1.7 %fusion.20 = bf16[4,32,1024]{2,1,0:T(8,128)(2,1)S(1)} fusion(f32[4,32,1024]{2,0,1:T(4,128)S(1)} %select_reduce_fusion, f32[1,4,32,1024]{3,1,2,0:T(4,128)} %constant_dynamic-slice_fusion.1, bf16[4,32,1024]{2,1,0:T(8,128)(2,1)} %param.10), kind=kLoop, calls=%fused_computation.27 | loop fusion | flops 524288 | bytes 1572864 | tf_op jit(solution)/shard_map/convert_element_type | solution.py:111
  34.9 1.3 %broadcast_in_dim.12 = bf16[4,4,32,1024]{3,1,2,0:T(4,128)(2,1)} broadcast(bf16[4,32,1024]{2,0,1:T(4,128)(2,1)S(1)} %copy.36), dimensions={1,2,3} | broadcast | bytes 1310720 | tf_op jit(solution)/shard_map/broadcast_in_dim | solution.py:112
  36.2 4.5 %all-to-all-start.1 = ((bf16[4,4,32,1024]{3,1,2,0:T(4,128)(2,1)}), bf16[4,4,32,1024]{3,1,2,0:T(4,128)(2,1)S(1)}, u32[]{:S(2)}, u32[]{:S(2)}) async-start(bf16[4,4,32,1024]{3,1,2,0:T(4,128)(2,1)} %broadcast_in_dim.12), calls=%async_computation.1 | async-start | bytes 2097152 | tf_op jit(solution)/shard_map/all_to_all | solution.py:113
  40.8 1.1 %broadcast_select_fusion.3 = (bf16[8,16,1024]{2,1,0:T(8,128)(2,1)S(1)}, bf16[8,16,1024]{2,1,0:T(8,128)(2,1)S(1)}) fusion(bf16[8,16,1024]{2,1,0:T(8,128)(2,1)} %subtract_convert_fusion, bf16[8,16,1024]{2,1,0:T(8,128)(2,1)} %collective-permute-done.2, pred[]{:T(512)S(6)} %eq.51), kind=kLoop, calls=%fused_computation.36 | loop fusion | flops 262144 | bytes 1048577 | tf_op jit(solution)/shard_map/jit(_where)/select_n | solution.py:45
  43.5 1.5 %fusion.9 = bf16[1024,128]{0,1:T(8,128)(2,1)} fusion(f32[1024,128]{0,1:T(8,128)S(1)} %copy-done.9, bf16[1024,1024]{1,0:T(8,128)(2,1)S(1)} %bitcast.70, bf16[16,8,8,128]{3,2,1,0:T(8,128)(2,1)S(1)} %bitcast.71), kind=kOutput, calls=%fused_computation.15 | convolution fusion | flops 268697600 | bytes 3145728 | tf_op jit(solution)/shard_map/dot_general | solution.py:62
  45.0 1.1 %copy.32 = bf16[1024,128]{1,0:T(8,128)(2,1)S(1)} copy(bf16[1024,128]{0,1:T(8,128)(2,1)} %fusion.9) | data formatting | bytes 524288 | tf_op jit(solution)/shard_map/convert_element_type | solution.py:67
  46.2 3.7 %fusion.47 = f32[32,32,1024]{2,1,0:T(8,128)} fusion(bf16[32,32,128]{2,1,0:T(8,128)(2,1)S(1)} %bitcast.72, bf16[128,1024,1]{1,0,2:T(8,128)(2,1)} %reshape.84), kind=kOutput, calls=%fused_computation.69 | convolution fusion | flops 268435456 | bytes 4718592 | tf_op jit(solution)/shard_map/dot_general | solution.py:68
  49.9 2.1 %broadcast_select_fusion.1 = (bf16[16,16,1024]{2,1,0:T(8,128)(2,1)}, bf16[16,16,1024]{2,1,0:T(8,128)(2,1)}) fusion(bf16[16,16,1024]{2,1,0:T(8,128)(2,1)} %collective-permute-done.3, pred[]{:T(512)S(6)} %eq.50, bf16[8,16,1024]{2,1,0:T(8,128)(2,1)S(1)} %copy-done.6, bf16[8,16,1024]{2,1,0:T(8,128)(2,1)S(1)} %copy-done.4), kind=kLoop, calls=%fused_computation.31 | loop fusion | flops 786432 | bytes 2097153 | tf_op jit(solution)/shard_map/jit(_where)/select_n | solution.py:45
  52.0 2.9 %all-to-all-done.1 = bf16[4,4,32,1024]{3,1,2,0:T(4,128)(2,1)S(1)} async-done(((bf16[4,4,32,1024]{3,1,2,0:T(4,128)(2,1)}), bf16[4,4,32,1024]{3,1,2,0:T(4,128)(2,1)S(1)}, u32[]{:S(2)}, u32[]{:S(2)}) %all-to-all-start.1) | async-done | bytes 1048608 | tf_op jit(solution)/shard_map/all_to_all | solution.py:113
  56.4 1.4 %copy-done.1 = f32[32,32,1024]{2,1,0:T(8,128)S(1)} copy-done((f32[32,32,1024]{2,1,0:T(8,128)S(1)}, f32[32,32,1024]{2,1,0:T(8,128)}, u32[]{:S(2)}) %copy-start.1) | copy-done | bytes 4194328
  58.1 8.1 %fusion.2 = f32[32,32,1024]{2,1,0:T(8,128)} fusion(f32[32,32,1024]{2,1,0:T(8,128)S(1)} %copy-done.1, f32[32,32,1024]{2,1,0:T(8,128)} %fusion.47, f32[32,32,1024]{2,0,1:T(8,128)S(1)} %fusion.30, bf16[16,16,1024]{2,1,0:T(8,128)(2,1)S(1)} %copy-done.8, bf16[16,16,1024]{2,1,0:T(8,128)(2,1)S(1)} %copy-done.7, bf16[1,16,128]{2,1,0:T(8,128)(2,1)S(1)} %slice.13, ...), kind=kOutput, calls=%fused_computation.3 | convolution fusion | flops 38273024 | bytes 17829892 | tf_op jit(solution)/shard_map/sl,zsx->zlx/dot_general | solution.py:96
  (47 shorter events, 8.6 us)
Async XLA Ops:
  0.0 0.8 %copy-start = (f32[4,16,128]{2,1,0:T(8,128)S(1)}, f32[4,16,128]{2,1,0:T(8,128)}, u32[]{:S(2)}) copy-start(f32[4,16,128]{2,1,0:T(8,128)} %param.11) | copy-start | bytes 98308
  2.8 12.9 %copy-start.11 = (bf16[25,16,128]{2,1,0:T(8,128)(2,1)}, bf16[25,16,128]{2,1,0:T(8,128)(2,1)S(1)}, u32[]{:S(2)}) copy-start(bf16[25,16,128]{2,1,0:T(8,128)(2,1)S(1)} %fusion.10) | copy-start | bytes 307204
  6.5 10.0 %collective-permute-start = (bf16[16,16,1024]{2,1,0:T(8,128)(2,1)}, bf16[16,16,1024]{2,1,0:T(8,128)(2,1)}, u32[]{:S(2)}, u32[]{:S(2)}) collective-permute-start(bf16[16,16,1024]{2,1,0:T(8,128)(2,1)} %fusion.8), channel_id=1, source_target_pairs={{0,1},{1,0},{2,3},{3,2},{4,5},{5,4},{6,7},{7,6},{8,9},{9,8},{10,11... | collective-permute-start | bytes 1572872 | tf_op jit(solution)/shard_map/ppermute | solution.py:89
  11.1 4.6 %copy-start.10 = (bf16[32,32,128]{2,1,0:T(8,128)(2,1)S(1)}, bf16[32,32,128]{2,1,0:T(8,128)(2,1)}, u32[]{:S(2)}) copy-start(bf16[32,32,128]{2,1,0:T(8,128)(2,1)} %param.8) | copy-start | bytes 786436
  11.1 21.2 %all-to-all-start = ((bf16[4,4,32,1024]{3,1,2,0:T(4,128)(2,1)}), bf16[4,4,32,1024]{3,1,2,0:T(4,128)(2,1)S(1)}, u32[]{:S(2)}, u32[]{:S(2)}) async-start(bf16[4,4,32,1024]{3,1,2,0:T(4,128)(2,1)} %get-tuple-element.9), calls=%async_computation | async-start | bytes 2097152 | tf_op jit(solution)/shard_map/all_to_all | solution.py:107
  15.7 5.9 %slice-start = ((bf16[25,16,128]{2,1,0:T(8,128)(2,1)}), bf16[8,16,128]{2,1,0:T(8,128)(2,1)S(1)}, s32[]{:S(2)}) async-start(bf16[25,16,128]{2,1,0:T(8,128)(2,1)} %copy-done.11), calls=%async_computation.2 | async-start | bytes 65536 | tf_op jit(solution)/shard_map/slice | solution.py:55
  18.0 1.0 %copy-start.2 = (f32[16,16,1024]{2,1,0:T(8,128)}, f32[16,16,1024]{2,1,0:T(8,128)S(1)}, u32[]{:S(2)}) copy-start(f32[16,16,1024]{2,1,0:T(8,128)S(1)} %convert_add_fusion) | copy-start | bytes 3145732
  19.6 8.9 %collective-permute-start.1 = (bf16[8,16,1024]{2,1,0:T(8,128)(2,1)}, bf16[8,16,1024]{2,1,0:T(8,128)(2,1)}, u32[]{:S(2)}, u32[]{:S(2)}) collective-permute-start(bf16[8,16,1024]{2,1,0:T(8,128)(2,1)} %dynamic-slice_convert_fusion), channel_id=1, source_target_pairs={{0,2},{2,0},{1,3},{3,1},{4,6},{6,4},{5,7},{7,5},{8,10},{10,8},{9,1... | collective-permute-start | bytes 786440 | tf_op jit(solution)/shard_map/ppermute | solution.py:39
  30.5 10.2 %collective-permute-start.2 = (bf16[8,16,1024]{2,1,0:T(8,128)(2,1)}, bf16[8,16,1024]{2,1,0:T(8,128)(2,1)}, u32[]{:S(2)}, u32[]{:S(2)}) collective-permute-start(bf16[8,16,1024]{2,1,0:T(8,128)(2,1)} %subtract_convert_fusion), channel_id=1, source_target_pairs={{0,2},{2,0},{1,3},{3,1},{4,6},{6,4},{5,7},{7,5},{8,10},{10,8},{9,1... | collective-permute-start | bytes 786440 | tf_op jit(solution)/shard_map/ppermute | solution.py:44
  36.2 18.6 %all-to-all-start.1 = ((bf16[4,4,32,1024]{3,1,2,0:T(4,128)(2,1)}), bf16[4,4,32,1024]{3,1,2,0:T(4,128)(2,1)S(1)}, u32[]{:S(2)}, u32[]{:S(2)}) async-start(bf16[4,4,32,1024]{3,1,2,0:T(4,128)(2,1)} %broadcast_in_dim.12), calls=%async_computation.1 | async-start | bytes 2097152 | tf_op jit(solution)/shard_map/all_to_all | solution.py:113
  40.8 2.7 %copy-start.9 = (f32[1024,128]{0,1:T(8,128)S(1)}, f32[1024,128]{0,1:T(8,128)}, u32[]{:S(2)}) copy-start(f32[1024,128]{0,1:T(8,128)} %copy.31) | copy-start | bytes 1572868
  41.9 0.7 %copy-start.3 = (bf16[8,16,1024]{2,1,0:T(8,128)(2,1)}, bf16[8,16,1024]{2,1,0:T(8,128)(2,1)S(1)}, u32[]{:S(2)}) copy-start(bf16[8,16,1024]{2,1,0:T(8,128)(2,1)S(1)} %get-tuple-element.7) | copy-start | bytes 786436
  41.9 1.6 %copy-start.5 = (bf16[8,16,1024]{2,1,0:T(8,128)(2,1)}, bf16[8,16,1024]{2,1,0:T(8,128)(2,1)S(1)}, u32[]{:S(2)}) copy-start(bf16[8,16,1024]{2,1,0:T(8,128)(2,1)S(1)} %get-tuple-element.8) | copy-start | bytes 786436
  43.5 6.4 %collective-permute-start.3 = (bf16[16,16,1024]{2,1,0:T(8,128)(2,1)}, bf16[16,16,1024]{2,1,0:T(8,128)(2,1)}, u32[]{:S(2)}, u32[]{:S(2)}) collective-permute-start(bf16[16,16,1024]{2,1,0:T(8,128)(2,1)} %pad_maximum_fusion), channel_id=1, source_target_pairs={{0,1},{1,0},{2,3},{3,2},{4,5},{5,4},{6,7},{7,6},{8,9},{9,8},{10,11... | collective-permute-start | bytes 1572872 | tf_op jit(solution)/shard_map/ppermute | solution.py:44
  46.1 3.7 %copy-start.4 = (bf16[8,16,1024]{2,1,0:T(8,128)(2,1)S(1)}, bf16[8,16,1024]{2,1,0:T(8,128)(2,1)}, u32[]{:S(2)}) copy-start(bf16[8,16,1024]{2,1,0:T(8,128)(2,1)} %copy-done.3) | copy-start | bytes 786436
  46.1 3.7 %copy-start.6 = (bf16[8,16,1024]{2,1,0:T(8,128)(2,1)S(1)}, bf16[8,16,1024]{2,1,0:T(8,128)(2,1)}, u32[]{:S(2)}) copy-start(bf16[8,16,1024]{2,1,0:T(8,128)(2,1)} %copy-done.5) | copy-start | bytes 786436
  55.7 2.2 %copy-start.1 = (f32[32,32,1024]{2,1,0:T(8,128)S(1)}, f32[32,32,1024]{2,1,0:T(8,128)}, u32[]{:S(2)}) copy-start(f32[32,32,1024]{2,1,0:T(8,128)} %param.7) | copy-start | bytes 12582916
  55.7 2.3 %copy-start.7 = (bf16[16,16,1024]{2,1,0:T(8,128)(2,1)S(1)}, bf16[16,16,1024]{2,1,0:T(8,128)(2,1)}, u32[]{:S(2)}) copy-start(bf16[16,16,1024]{2,1,0:T(8,128)(2,1)} %get-tuple-element.5) | copy-start | bytes 1572868
  55.7 2.4 %copy-start.8 = (bf16[16,16,1024]{2,1,0:T(8,128)(2,1)S(1)}, bf16[16,16,1024]{2,1,0:T(8,128)(2,1)}, u32[]{:S(2)}) copy-start(bf16[16,16,1024]{2,1,0:T(8,128)(2,1)} %get-tuple-element.6) | copy-start | bytes 1572868

commit v11 on v6

--- a/solution.py
+++ b/solution.py
@@ -101,32 +101,32 @@
     mat_z = lax.dynamic_index_in_dim(along_z, zb, 0, keepdims=False)
     band_z = lax.dynamic_slice_in_dim(mat_z, zq * planes, planes, 1)
     piece = SLICES // group
+    sheet = coarse.reshape(planes, rows_here * width)
     own_rows = lax.dynamic_slice_in_dim(band_z, zq * piece, piece, 0)
-    fwd_z = jnp.einsum("sl,lyx->syx", own_rows, coarse, preferred_element_type=jnp.float32)
+    fwd_z = jnp.dot(own_rows, sheet, preferred_element_type=jnp.float32)
     far_rows = jnp.concatenate(
         [lax.dynamic_slice_in_dim(band_z, ((zq + k) % group) * piece, piece, 0) for k in range(1, group)],
         0,
     )
-    far_z = jnp.einsum(
-        "sl,lyx->syx", far_rows, coarse, preferred_element_type=jnp.float32
-    ).astype(jnp.bfloat16)
+    far_z = jnp.dot(far_rows, sheet, preferred_element_type=jnp.float32).astype(jnp.bfloat16)
     for k in range(1, group):
         sent = far_z[(k - 1) * piece : k * piece]
         got = lax.ppermute(sent, "zq", [(j, (j + k) % group) for j in range(group)])
         fwd_z = fwd_z + got.astype(jnp.float32)
-    resid_z = (slices_z.astype(jnp.float32) - fwd_z).astype(jnp.bfloat16)
+    observed = slices_z.reshape(piece, rows_here * width).astype(jnp.float32)
+    resid_z = (observed - fwd_z).astype(jnp.bfloat16)
     pieces = [resid_z]
-    rows = [lax.dynamic_slice_in_dim(band_z, zq * piece, piece, 0)]
+    rows = [own_rows]
     for k in range(1, group):
         pieces.append(lax.ppermute(resid_z, "zq", [(j, (j + k) % group) for j in range(group)]))
         src = (zq - k + group) % group
         rows.append(lax.dynamic_slice_in_dim(band_z, src * piece, piece, 0))
-    corr_z = jnp.einsum(
-        "sl,syx->lyx",
+    corr_z = lax.dot_general(
         jnp.concatenate(rows, 0),
         jnp.concatenate(pieces, 0),
+        (((0,), (0,)), ((), ())),
         preferred_element_type=jnp.float32,
-    )
+    ).reshape(planes, rows_here, width)
 
     return volume + step_size * (corr_x + corr_y + corr_z)
 

time: 57.6 us -> 57 us (0.990)
  local copies, waits for them, and re-layouts: 6.77 us -> 12 us
  matrix products: 18.9 us -> 14.9 us
  waiting for transfers between devices: 12.3 us -> 10.3 us
  starting transfers between devices: 14.5 us -> 13.6 us
  other arithmetic: 4.7 us -> 5.59 us
    unnamed x12 -> x19, local copies, waits for them, and re-layouts: 1.36 us -> 7.16 us
    ppermute x1, waiting for transfers between devices: 2.45 us -> 0.01 us  [halve(): got = lax.ppermute(give.astype(jnp.bfloat16), axis, [(0, 1), (1, 0)])]
    dot_general x3, matrix products: 6.93 us -> 4.69 us  [the longest x1 2.06 us: shards(): jnp.dot(far_rows, sheet, preferred_element_type=jnp.float32)]
    dot_general x1, matrix products: 5.96 us -> 4.25 us  [shards(): jnp.einsum('sl,zsx->zlx', band_y, resid_y, preferred_element_type=jnp.flo...]
    ppermute x2, starting transfers between devices: 4.52 us -> 2.94 us  [double(): other = lax.ppermute(values, axis, [(0, 1), (1, 0)])]
    ppermute x2, waiting for transfers between devices: 0.01 us -> 1.01 us  [double(): other = lax.ppermute(values, axis, [(0, 1), (1, 0)])]
    unnamed x0 -> x1, other arithmetic: none -> 0.85 us
    ppermute x3, starting transfers between devices: 2.34 us -> 3.06 us  [shards(): lax.ppermute(resid_z, 'zq', [(j, (j + k) % group) for j in range(group)])]
  transfers between devices with their start and end apart: 10 -> 10, of which waited for: 3 -> 3; matrix products, arithmetic and copies ran while one was open for 30% -> 40% of each run, Pallas kernels for 0% -> 0%
where the time goes in v11:
time: 57 us; the launch traced here: 56.6 us
  matrix products  14.9 us (26%)
  starting transfers between devices  13.6 us (24%)
  local copies, waits for them, and re-layouts  12 us (21%)
  waiting for transfers between devices  10.3 us (18%)
  other arithmetic  5.59 us (10%)
    ppermute x3, waiting for transfers between devices, shards(): lax.ppermute(resid_z, 'zq', [(j, (j + k) % group) for j in range(group)])  9.3 us
    unnamed x19, local copies, waits for them, and re-layouts  7.16 us
    dot_general x1, matrix products, shards(): jnp.einsum('sl,zsx->zlx', band_y, resid_y, preferred_element_type=jnp.flo...  4.25 us
    ppermute x1, starting transfers between devices, shards(): lax.ppermute(give_y, 'co', [(0, 1), (1, 0)]).astype(jnp.float32)  3.29 us
    ppermute x3, starting transfers between devices, shards(): lax.ppermute(resid_z, 'zq', [(j, (j + k) % group) for j in range(group)])  3.06 us
    ppermute x2, starting transfers between devices, double(): other = lax.ppermute(values, axis, [(0, 1), (1, 0)])  2.94 us
    ppermute x3, starting transfers between devices, shards(): got = lax.ppermute(sent, 'zq', [(j, (j + k) % group) for j in range(group)])  2.68 us
    convert_element_type x1, other arithmetic, shards(): coarse = volume.astype(jnp.bfloat16)  2.56 us
  transfers between devices with their start and end apart: 10, of which 3 were waited for; matrix products, arithmetic and copies ran while one was open for 40% of the time, Pallas kernels for 0%

profile of v11, /device:TPU:1, one launch (start us, length us, event | category | flops | bytes accessed | tf_op | source)
XLA Modules:
  0.0 56.6 jit_solution(14277449324865357815)
XLA Ops:
  0.8 1.0 %fusion.26 = f32[25,16,128]{2,0,1:T(8,128)S(1)} fusion(f32[4,16,128]{2,1,0:T(8,128)S(1)} %copy-done, s32[25]{0:T(128)} %param.12), kind=kOutput, calls=%fused_computation.43 | convolution fusion | flops 2457700 | bytes 237668 | tf_op jit(solution)/shard_map/bk,ksl->bsl/dot_general | solution.py:19
  1.7 1.0 %fusion.6 = bf16[25,16,128]{2,1,0:T(8,128)(2,1)S(1)} fusion(s32[25,128]{1,0:T(8,128)S(1)} %add_select_fusion, f32[25,16,128]{2,0,1:T(8,128)S(1)} %fusion.26), kind=kOutput, calls=%fused_computation.13 | convolution fusion | flops 79104000 | bytes 320000 | tf_op jit(solution)/shard_map/bsj,bjl->bsl/dot_general | solution.py:23
  2.8 2.6 %convert_element_type.70 = bf16[32,32,1024]{2,1,0:T(8,128)(2,1)S(1)} convert(f32[32,32,1024]{2,1,0:T(8,128)} %param.7) | non-fusion elementwise | flops 1048576 | bytes 6291456 | tf_op jit(solution)/shard_map/convert_element_type | solution.py:58
  5.7 3.3 %collective-permute-start = (bf16[16,16,1024]{2,1,0:T(8,128)(2,1)S(1)}, bf16[16,16,1024]{2,1,0:T(8,128)(2,1)}, u32[]{:S(2)}, u32[]{:S(2)}) collective-permute-start(bf16[16,16,1024]{2,1,0:T(8,128)(2,1)S(1)} %fusion.4), channel_id=1, source_target_pairs={{0,1},{1,0},{2,3},{3,2},{4,5},{5,4},{6,7},{7,6},{8,9},{9,8},{10,11... | collective-permute-start | bytes 1572872 | tf_op jit(solution)/shard_map/ppermute | solution.py:89
  9.0 2.5 %copy.16 = bf16[4,8,32,1024]{3,1,2,0:T(8,128)(2,1)} copy(bf16[4,8,32,1024]{3,2,1,0:T(8,128)(2,1)S(1)} %bitcast.65) | data formatting | bytes 4194304
  11.6 2.1 %convolution_convert_fusion = bf16[12,32768]{1,0:T(8,128)(2,1)S(1)} fusion(bf16[32,32768]{1,0:T(8,128)(2,1)} %bitcast.68, bf16[4,32]{1,0:T(4,128)(2,1)S(1)} %get-tuple-element.15, bf16[4,32]{1,0:T(4,128)(2,1)S(1)} %get-tuple-element.14, bf16[4,32]{1,0:T(4,128)(2,1)S(1)} %get-tuple-element.13), kind=kOutput, calls=%fused_computation | convolution fusion | flops 25561344 | bytes 2884352 | tf_op jit(solution)/shard_map/dot_general | solution.py:111
  13.7 1.0 %fusion.60 = (bf16[4,32768]{1,0:T(4,128)(2,1)}, bf16[4,32768]{1,0:T(4,128)(2,1)}, bf16[4,32768]{1,0:T(4,128)(2,1)}) fusion(bf16[12,32768]{1,0:T(8,128)(2,1)S(1)} %convolution_convert_fusion), kind=kLoop, calls=%fused_computation.85 | loop fusion | bytes 1572864 | tf_op jit(solution)/shard_map/slice | solution.py:113
  14.7 2.7 %collective-permute-start.6 = (bf16[4,32768]{1,0:T(4,128)(2,1)}, bf16[4,32768]{1,0:T(4,128)(2,1)}, u32[]{:S(2)}, u32[]{:S(2)}) collective-permute-start(bf16[4,32768]{1,0:T(4,128)(2,1)} %get-tuple-element.8), channel_id=1, source_target_pairs={{0,12},{4,0},{8,4},{12,8},{1,13},{5,1},{9,5},{13,9},{2,14},{6,2},{... | collective-permute-start | bytes 786440 | tf_op jit(solution)/shard_map/ppermute | solution.py:114
  17.4 1.0 %copy.10 = f32[1024,128]{0,1:T(8,128)} copy(f32[1024,128]{1,0:T(8,128)S(1)} %bitcast_convert_fusion) | data formatting | bytes 1048576 | tf_op jit(solution)/shard_map/convert_element_type | solution.py:66
  18.5 1.4 %convert_add_fusion = f32[16,16,1024]{2,1,0:T(8,128)S(1)} fusion(bf16[16,16,1024]{2,1,0:T(8,128)(2,1)} %collective-permute-done, bf16[32,32,1024]{2,1,0:T(8,128)(2,1)S(1)} %convert_element_type.70, s32[]{:T(128)S(6)} %select_n.111, bf16[1,16,128]{2,1,0:T(8,128)(2,1)S(1)} %slice.25, s32[]{:T(128)S(6)} %select_n.112), kind=kOutput, calls=%fused_computation.25 | convolution fusion | flops 17301504 | bytes 2625544 | tf_op jit(solution)/shard_map/sl,zlx->zsx/dot_general | solution.py:77
  20.8 1.6 %collective-permute-start.1 = (bf16[8,16,1024]{2,1,0:T(8,128)(2,1)}, bf16[8,16,1024]{2,1,0:T(8,128)(2,1)}, u32[]{:S(2)}, u32[]{:S(2)}) collective-permute-start(bf16[8,16,1024]{2,1,0:T(8,128)(2,1)} %dynamic-slice_convert_fusion), channel_id=1, source_target_pairs={{0,2},{2,0},{1,3},{3,1},{4,6},{6,4},{5,7},{7,5},{8,10},{10,8},{9,1... | collective-permute-start | bytes 786440 | tf_op jit(solution)/shard_map/ppermute | solution.py:39
  22.4 1.5 %fusion.5 = bf16[1024,128]{0,1:T(8,128)(2,1)} fusion(f32[1024,128]{0,1:T(8,128)S(1)} %copy-done.3, bf16[1024,1024]{1,0:T(8,128)(2,1)S(1)} %bitcast.66, bf16[16,8,8,128]{3,2,1,0:T(8,128)(2,1)S(1)} %bitcast.70), kind=kOutput, calls=%fused_computation.12 | convolution fusion | flops 268697600 | bytes 3145728 | tf_op jit(solution)/shard_map/dot_general | solution.py:62
  25.6 2.2 %copy.15 = f32[1,4,32,1024]{3,1,2,0:T(4,128)} copy(f32[1,4,32,1024]{3,2,1,0:T(8,128)} %convert_bitcast_fusion) | data formatting | bytes 1048576
  27.8 1.1 %copy.11 = bf16[1024,128]{1,0:T(8,128)(2,1)S(1)} copy(bf16[1024,128]{0,1:T(8,128)(2,1)} %fusion.5) | data formatting | bytes 524288 | tf_op jit(solution)/shard_map/convert_element_type | solution.py:67
  28.9 1.1 %subtract_convert_fusion.1 = bf16[8,16,1024]{2,1,0:T(8,128)(2,1)S(1)} fusion(bf16[8,16,1024]{2,1,0:T(8,128)(2,1)} %collective-permute-done.1, f32[16,16,1024]{2,1,0:T(8,128)S(1)} %convert_add_fusion, s32[]{:T(128)S(6)} %select_n.114, bf16[32,16,1024]{2,1,0:T(8,128)(2,1)} %param.9, s32[]{:T(128)S(6)} %select_n.110), kind=kLoop, calls=%fused_computation.32 | loop fusion | flops 655360 | bytes 1310728 | tf_op jit(solution)/shard_map/convert_element_type | solution.py:93
  30.9 1.9 %subtract_convert_fusion = bf16[4,32768]{1,0:T(4,128)(2,1)S(1)} fusion(f32[4,32768]{1,0:T(4,128)} %bitcast.72, bf16[4,32768]{1,0:T(4,128)(2,1)} %collective-permute-done.6, bf16[4,32768]{1,0:T(4,128)(2,1)} %collective-permute-done.5, bf16[4,32768]{1,0:T(4,128)(2,1)} %collective-permute-done.4, bf16[4,32]{1,0:T(4,128)(2,1)S(1)} %get-tuple-element.12, ...), kind=kOutput, calls=%fused_computation.31 | convolution fusion | flops 9437184 | bytes 3670272 | tf_op jit(solution)/shard_map/dot_general | solution.py:106
  32.7 1.2 %collective-permute-start.9 = (bf16[4,32768]{1,0:T(4,128)(2,1)S(1)}, bf16[4,32768]{1,0:T(4,128)(2,1)S(1)}, u32[]{:S(2)}, u32[]{:S(2)}) collective-permute-start(bf16[4,32768]{1,0:T(4,128)(2,1)S(1)} %subtract_convert_fusion), channel_id=1, source_target_pairs={{0,12},{4,0},{8,4},{12,8},{1,13},{5,1},{9,5},{13,9},{2,14},{6,2},{... | collective-permute-start | bytes 786440 | tf_op jit(solution)/shard_map/ppermute | solution.py:121
  34.0 1.1 %collective-permute-start.8 = (bf16[4,32768]{1,0:T(4,128)(2,1)S(1)}, bf16[4,32768]{1,0:T(4,128)(2,1)S(1)}, u32[]{:S(2)}, u32[]{:S(2)}) collective-permute-start(bf16[4,32768]{1,0:T(4,128)(2,1)S(1)} %subtract_convert_fusion), channel_id=1, source_target_pairs={{0,8},{4,12},{8,0},{12,4},{1,9},{5,13},{9,1},{13,5},{2,10},{6,14},... | collective-permute-start | bytes 786440 | tf_op jit(solution)/shard_map/ppermute | solution.py:121
  35.8 1.0 %collective-permute-done.2 = bf16[8,16,1024]{2,1,0:T(8,128)(2,1)S(1)} collective-permute-done((bf16[8,16,1024]{2,1,0:T(8,128)(2,1)S(1)}, bf16[8,16,1024]{2,1,0:T(8,128)(2,1)S(1)}, u32[]{:S(2)}, u32[]{:S(2)}) %collective-permute-start.2) | collective-permute-done | bytes 262176 | tf_op jit(solution)/shard_map/ppermute | solution.py:44
  36.9 2.2 %collective-permute-start.3 = (bf16[16,16,1024]{2,1,0:T(8,128)(2,1)S(1)}, bf16[16,16,1024]{2,1,0:T(8,128)(2,1)S(1)}, u32[]{:S(2)}, u32[]{:S(2)}) collective-permute-start(bf16[16,16,1024]{2,1,0:T(8,128)(2,1)S(1)} %pad_maximum_fusion), channel_id=1, source_target_pairs={{0,1},{1,0},{2,3},{3,2},{4,5},{5,4},{6,7},{7,6},{8,9},{9,8},{10,11... | collective-permute-start | bytes 1572872 | tf_op jit(solution)/shard_map/ppermute | solution.py:44
  39.8 1.6 %collective-permute-done.8 = bf16[4,32768]{1,0:T(4,128)(2,1)S(1)} collective-permute-done((bf16[4,32768]{1,0:T(4,128)(2,1)S(1)}, bf16[4,32768]{1,0:T(4,128)(2,1)S(1)}, u32[]{:S(2)}, u32[]{:S(2)}) %collective-permute-start.8) | collective-permute-done | bytes 262176 | tf_op jit(solution)/shard_map/ppermute | solution.py:121
  41.4 7.7 %collective-permute-done.7 = bf16[4,32768]{1,0:T(4,128)(2,1)S(1)} collective-permute-done((bf16[4,32768]{1,0:T(4,128)(2,1)S(1)}, bf16[4,32768]{1,0:T(4,128)(2,1)S(1)}, u32[]{:S(2)}, u32[]{:S(2)}) %collective-permute-start.7) | collective-permute-done | bytes 262176 | tf_op jit(solution)/shard_map/ppermute | solution.py:121
  49.9 2.4 %copy.17 = f32[4,8,32,1024]{3,2,1,0:T(8,128)S(1)} copy(f32[4,8,32,1024]{3,1,2,0:T(8,128)S(1)} %bitcast.67) | data formatting | bytes 8388608
  52.4 4.2 %fusion.1 = f32[32,32,1024]{2,1,0:T(8,128)} fusion(f32[32,32,1024]{2,1,0:T(8,128)S(1)} %copy-done.1, f32[4,8,32,1024]{3,2,1,0:T(8,128)S(1)} %copy.17, f32[32,32,1024]{2,1,0:T(8,128)S(1)} %fusion.61, bf16[16,16,1024]{2,1,0:T(8,128)(2,1)S(1)} %get-tuple-element.6, bf16[16,16,1024]{2,1,0:T(8,128)(2,1)S(1)} %get-tuple-element.5, ...), kind=kOutput, calls=%fused_computation.3 | convolution fusion | flops 38273024 | bytes 17829892 | tf_op jit(solution)/shard_map/sl,zsx->zlx/dot_general | solution.py:96
  (46 shorter events, 7.0 us)
Async XLA Ops:
  0.0 0.8 %copy-start = (f32[4,16,128]{2,1,0:T(8,128)S(1)}, f32[4,16,128]{2,1,0:T(8,128)}, u32[]{:S(2)}) copy-start(f32[4,16,128]{2,1,0:T(8,128)} %param.11) | copy-start | bytes 98308
  2.8 6.2 %copy-start.7 = (bf16[25,16,128]{2,1,0:T(8,128)(2,1)}, bf16[25,16,128]{2,1,0:T(8,128)(2,1)S(1)}, u32[]{:S(2)}) copy-start(bf16[25,16,128]{2,1,0:T(8,128)(2,1)S(1)} %fusion.6) | copy-start | bytes 307204
  5.7 12.8 %collective-permute-start = (bf16[16,16,1024]{2,1,0:T(8,128)(2,1)S(1)}, bf16[16,16,1024]{2,1,0:T(8,128)(2,1)}, u32[]{:S(2)}, u32[]{:S(2)}) collective-permute-start(bf16[16,16,1024]{2,1,0:T(8,128)(2,1)S(1)} %fusion.4), channel_id=1, source_target_pairs={{0,1},{1,0},{2,3},{3,2},{4,5},{5,4},{6,7},{7,6},{8,9},{9,8},{10,11... | collective-permute-start | bytes 1572872 | tf_op jit(solution)/shard_map/ppermute | solution.py:89
  9.0 2.5 %slice-start = ((bf16[25,16,128]{2,1,0:T(8,128)(2,1)}), bf16[16,16,128]{2,1,0:T(8,128)(2,1)S(1)}, s32[]{:S(2)}) async-start(bf16[25,16,128]{2,1,0:T(8,128)(2,1)} %copy-done.7), calls=%async_computation | async-start | bytes 131072 | tf_op jit(solution)/shard_map/slice | solution.py:57
  11.6 5.8 %copy-start.5 = (bf16[32,32,128]{2,1,0:T(8,128)(2,1)S(1)}, bf16[32,32,128]{2,1,0:T(8,128)(2,1)}, u32[]{:S(2)}) copy-start(bf16[32,32,128]{2,1,0:T(8,128)(2,1)} %param.8) | copy-start | bytes 786436
  13.7 4.8 %slice-start.1 = ((bf16[25,16,128]{2,1,0:T(8,128)(2,1)}), bf16[8,16,128]{2,1,0:T(8,128)(2,1)S(1)}, s32[]{:S(2)}) async-start(bf16[25,16,128]{2,1,0:T(8,128)(2,1)} %copy-done.7), calls=%async_computation.1 | async-start | bytes 65536 | tf_op jit(solution)/shard_map/slice | solution.py:55
  14.7 16.2 %collective-permute-start.4 = (bf16[4,32768]{1,0:T(4,128)(2,1)}, bf16[4,32768]{1,0:T(4,128)(2,1)}, u32[]{:S(2)}, u32[]{:S(2)}) collective-permute-start(bf16[4,32768]{1,0:T(4,128)(2,1)} %get-tuple-element.7), channel_id=1, source_target_pairs={{0,4},{4,8},{8,12},{12,0},{1,5},{5,9},{9,13},{13,1},{2,6},{6,10},{... | collective-permute-start | bytes 786440 | tf_op jit(solution)/shard_map/ppermute | solution.py:114
  14.7 16.2 %collective-permute-start.6 = (bf16[4,32768]{1,0:T(4,128)(2,1)}, bf16[4,32768]{1,0:T(4,128)(2,1)}, u32[]{:S(2)}, u32[]{:S(2)}) collective-permute-start(bf16[4,32768]{1,0:T(4,128)(2,1)} %get-tuple-element.8), channel_id=1, source_target_pairs={{0,12},{4,0},{8,4},{12,8},{1,13},{5,1},{9,5},{13,9},{2,14},{6,2},{... | collective-permute-start | bytes 786440 | tf_op jit(solution)/shard_map/ppermute | solution.py:114
  17.4 13.5 %collective-permute-start.5 = (bf16[4,32768]{1,0:T(4,128)(2,1)}, bf16[4,32768]{1,0:T(4,128)(2,1)}, u32[]{:S(2)}, u32[]{:S(2)}) collective-permute-start(bf16[4,32768]{1,0:T(4,128)(2,1)} %get-tuple-element.9), channel_id=1, source_target_pairs={{0,8},{4,12},{8,0},{12,4},{1,9},{5,13},{9,1},{13,5},{2,10},{6,14},... | collective-permute-start | bytes 786440 | tf_op jit(solution)/shard_map/ppermute | solution.py:114
  18.4 3.9 %copy-start.3 = (f32[1024,128]{0,1:T(8,128)S(1)}, f32[1024,128]{0,1:T(8,128)}, u32[]{:S(2)}) copy-start(f32[1024,128]{0,1:T(8,128)} %copy.10) | copy-start | bytes 1572868
  20.0 3.9 %copy-start.6 = (bf16[4,32,1024]{2,1,0:T(8,128)(2,1)S(1)}, bf16[4,32,1024]{2,1,0:T(8,128)(2,1)}, u32[]{:S(2)}) copy-start(bf16[4,32,1024]{2,1,0:T(8,128)(2,1)} %param.10) | copy-start | bytes 786436
  20.8 8.2 %collective-permute-start.1 = (bf16[8,16,1024]{2,1,0:T(8,128)(2,1)}, bf16[8,16,1024]{2,1,0:T(8,128)(2,1)}, u32[]{:S(2)}, u32[]{:S(2)}) collective-permute-start(bf16[8,16,1024]{2,1,0:T(8,128)(2,1)} %dynamic-slice_convert_fusion), channel_id=1, source_target_pairs={{0,2},{2,0},{1,3},{3,1},{4,6},{6,4},{5,7},{7,5},{8,10},{10,8},{9,1... | collective-permute-start | bytes 786440 | tf_op jit(solution)/shard_map/ppermute | solution.py:39
  23.9 6.9 %copy-start.2 = (bf16[4,8,32,1024]{3,1,2,0:T(8,128)(2,1)S(1)}, bf16[4,8,32,1024]{3,1,2,0:T(8,128)(2,1)}, u32[]{:S(2)}) copy-start(bf16[4,8,32,1024]{3,1,2,0:T(8,128)(2,1)} %copy.16) | copy-start | bytes 6291460
  30.1 6.7 %collective-permute-start.2 = (bf16[8,16,1024]{2,1,0:T(8,128)(2,1)S(1)}, bf16[8,16,1024]{2,1,0:T(8,128)(2,1)S(1)}, u32[]{:S(2)}, u32[]{:S(2)}) collective-permute-start(bf16[8,16,1024]{2,1,0:T(8,128)(2,1)S(1)} %subtract_convert_fusion.1), channel_id=1, source_target_pairs={{0,2},{2,0},{1,3},{3,1},{4,6},{6,4},{5,7},{7,5},{8,10},{10,8},{9,1... | collective-permute-start | bytes 786440 | tf_op jit(solution)/shard_map/ppermute | solution.py:44
  30.9 8.2 %copy-start.4 = (bf16[128,1024,1]{1,0,2:T(8,128)(2,1)S(1)}, bf16[128,1024,1]{1,0,2:T(8,128)(2,1)}, u32[]{:S(2)}) copy-start(bf16[128,1024,1]{1,0,2:T(8,128)(2,1)} %reshape.91) | copy-start | bytes 786436
  32.7 7.0 %collective-permute-start.9 = (bf16[4,32768]{1,0:T(4,128)(2,1)S(1)}, bf16[4,32768]{1,0:T(4,128)(2,1)S(1)}, u32[]{:S(2)}, u32[]{:S(2)}) collective-permute-start(bf16[4,32768]{1,0:T(4,128)(2,1)S(1)} %subtract_convert_fusion), channel_id=1, source_target_pairs={{0,12},{4,0},{8,4},{12,8},{1,13},{5,1},{9,5},{13,9},{2,14},{6,2},{... | collective-permute-start | bytes 786440 | tf_op jit(solution)/shard_map/ppermute | solution.py:121
  34.0 7.4 %collective-permute-start.8 = (bf16[4,32768]{1,0:T(4,128)(2,1)S(1)}, bf16[4,32768]{1,0:T(4,128)(2,1)S(1)}, u32[]{:S(2)}, u32[]{:S(2)}) collective-permute-start(bf16[4,32768]{1,0:T(4,128)(2,1)S(1)} %subtract_convert_fusion), channel_id=1, source_target_pairs={{0,8},{4,12},{8,0},{12,4},{1,9},{5,13},{9,1},{13,5},{2,10},{6,14},... | collective-permute-start | bytes 786440 | tf_op jit(solution)/shard_map/ppermute | solution.py:121
  35.0 14.0 %collective-permute-start.7 = (bf16[4,32768]{1,0:T(4,128)(2,1)S(1)}, bf16[4,32768]{1,0:T(4,128)(2,1)S(1)}, u32[]{:S(2)}, u32[]{:S(2)}) collective-permute-start(bf16[4,32768]{1,0:T(4,128)(2,1)S(1)} %subtract_convert_fusion), channel_id=1, source_target_pairs={{0,4},{4,8},{8,12},{12,0},{1,5},{5,9},{9,13},{13,1},{2,6},{6,10},{... | collective-permute-start | bytes 786440 | tf_op jit(solution)/shard_map/ppermute | solution.py:121
  36.9 15.4 %collective-permute-start.3 = (bf16[16,16,1024]{2,1,0:T(8,128)(2,1)S(1)}, bf16[16,16,1024]{2,1,0:T(8,128)(2,1)S(1)}, u32[]{:S(2)}, u32[]{:S(2)}) collective-permute-start(bf16[16,16,1024]{2,1,0:T(8,128)(2,1)S(1)} %pad_maximum_fusion), channel_id=1, source_target_pairs={{0,1},{1,0},{2,3},{3,2},{4,5},{5,4},{6,7},{7,6},{8,9},{9,8},{10,11... | collective-permute-start | bytes 1572872 | tf_op jit(solution)/shard_map/ppermute | solution.py:44
  49.8 2.5 %copy-start.1 = (f32[32,32,1024]{2,1,0:T(8,128)S(1)}, f32[32,32,1024]{2,1,0:T(8,128)}, u32[]{:S(2)}) copy-start(f32[32,32,1024]{2,1,0:T(8,128)} %param.7) | copy-start | bytes 12582916

commit v12 on v11

--- a/solution.py
+++ b/solution.py
@@ -22,6 +22,14 @@
     moving = (target[:, :, None] == columns[None, None, :]).astype(jnp.float32)
     shifted = jnp.einsum("bsj,bjl->bsl", picked, moving, precision=lax.Precision.HIGHEST)
     return shifted.astype(jnp.bfloat16)
+
+
+def one_band(profiles, profile_index, block_shift, block):
+    span = profiles.shape[2]
+    picked = lax.dynamic_index_in_dim(profiles, profile_index[block], 0, keepdims=False)
+    doubled = jnp.concatenate([picked, picked], 1)
+    shift = block_shift[block] % span
+    return lax.dynamic_slice_in_dim(doubled, span - shift, span, 1).astype(jnp.bfloat16)
 
 
 def banded_matrix(along):
@@ -53,8 +61,6 @@
     count_y = slices_y.shape[1] // SLICES
     mats = block_mats(profiles, profile_index, block_shift)
     along_x = mats[:count_x]
-    along_y = mats[count_x : count_x + count_y]
-    along_z = mats[count_x + count_y :]
     coarse = volume.astype(jnp.bfloat16)
 
     banded_x = banded_matrix(along_x)
@@ -72,7 +78,8 @@
     zl = lax.axis_index("zl")
     co = lax.axis_index("co")
     rep = zl * 2 + co
-    band_y = lax.dynamic_slice_in_dim(along_y[0], rep * rows_here, rows_here, 1)
+    mat_y = one_band(profiles, profile_index, block_shift, count_x)
+    band_y = lax.dynamic_slice_in_dim(mat_y, rep * rows_here, rows_here, 1)
     half = planes // 2
     keep_y = jnp.einsum(
         "sl,zlx->zsx",
@@ -98,7 +105,7 @@
     zb = lax.axis_index("zb")
     zq = lax.axis_index("zq")
     group = lax.axis_size("zq")
-    mat_z = lax.dynamic_index_in_dim(along_z, zb, 0, keepdims=False)
+    mat_z = one_band(profiles, profile_index, block_shift, count_x + count_y + zb)
     band_z = lax.dynamic_slice_in_dim(mat_z, zq * planes, planes, 1)
     piece = SLICES // group
     sheet = coarse.reshape(planes, rows_here * width)

time: 57 us -> 64.4 us (1.13)
  between operations: 0.23 us -> 8.23 us
  local copies, waits for them, and re-layouts: 12 us -> 13.4 us
  matrix products: 14.9 us -> 14.1 us
    slice x3 -> x1, local copies, waits for them, and re-layouts: 0.01 us -> 1.42 us  [one_band(): profile_index[block]]
    select_n x1, other arithmetic: 0.74 us -> 0.08 us  [block_mats(): target = (columns[None, :] + block_shift[:, None]) % span]
    dot_general x1, matrix products: 0.95 us -> 0.3 us  [block_mats(): jnp.einsum('bk,ksl->bsl', onehot, profiles, precision=lax.Precision.HIGHEST)]
    ppermute x3, waiting for transfers between devices: 9.3 us -> 8.65 us  [shards(): lax.ppermute(resid_z, 'zq', [(j, (j + k) % group) for j in range(group)])]
    unnamed x19 -> x21, local copies, waits for them, and re-layouts: 7.16 us -> 7.15 us
  transfers between devices with their start and end apart: 10 -> 10, of which waited for: 3 -> 3; matrix products, arithmetic and copies ran while one was open for 40% -> 37% of each run, Pallas kernels for 0% -> 0%
where the time goes in v12:
time: 64.4 us; the launch traced here: 64.1 us
  matrix products  14.1 us (22%)
  starting transfers between devices  13.5 us (21%)
  local copies, waits for them, and re-layouts  13.4 us (21%)
  waiting for transfers between devices  9.73 us (15%)
  between operations  8.23 us (13%)
  other arithmetic  5.09 us (8%)
    ppermute x3, waiting for transfers between devices, shards(): lax.ppermute(resid_z, 'zq', [(j, (j + k) % group) for j in range(group)])  8.65 us
    unnamed x21, local copies, waits for them, and re-layouts  7.15 us
    dot_general x1, matrix products, shards(): jnp.einsum('sl,zsx->zlx', band_y, resid_y, preferred_element_type=jnp.flo...  4.18 us
    ppermute x1, starting transfers between devices, shards(): lax.ppermute(give_y, 'co', [(0, 1), (1, 0)]).astype(jnp.float32)  3.29 us
    ppermute x3, starting transfers between devices, shards(): lax.ppermute(resid_z, 'zq', [(j, (j + k) % group) for j in range(group)])  2.99 us
    ppermute x2, starting transfers between devices, double(): other = lax.ppermute(values, axis, [(0, 1), (1, 0)])  2.95 us
    ppermute x3, starting transfers between devices, shards(): got = lax.ppermute(sent, 'zq', [(j, (j + k) % group) for j in range(group)])  2.68 us
    convert_element_type x1, other arithmetic, shards(): coarse = volume.astype(jnp.bfloat16)  2.52 us
  transfers between devices with their start and end apart: 10, of which 3 were waited for; matrix products, arithmetic and copies ran while one was open for 37% of the time, Pallas kernels for 0%

profile of v12, /device:TPU:1, one launch (start us, length us, event | category | flops | bytes accessed | tf_op | source)
XLA Modules:
  0.0 64.1 jit_solution(12236322017280825756)
XLA Ops:
  0.0 1.4 %fusion.59 = (s32[1]{0:T(128)}, s32[1]{0:T(128)}, s32[1]{0:T(128)}, s32[1]{0:T(128)}) fusion(s32[25]{0:T(128)} %param.12, s32[]{:T(128)S(6)} %select_n.142, s32[25]{0:T(128)} %param.13), kind=kLoop, calls=%fused_computation.87 | loop fusion | bytes 36 | tf_op jit(solution)/shard_map/slice | solution.py:29
  6.1 2.5 %convert_element_type.76 = bf16[32,32,1024]{2,1,0:T(8,128)(2,1)S(1)} convert(f32[32,32,1024]{2,1,0:T(8,128)} %param.7) | non-fusion elementwise | flops 1048576 | bytes 6291456 | tf_op jit(solution)/shard_map/convert_element_type | solution.py:64
  10.3 3.3 %collective-permute-start = (bf16[16,16,1024]{2,1,0:T(8,128)(2,1)S(1)}, bf16[16,16,1024]{2,1,0:T(8,128)(2,1)}, u32[]{:S(2)}, u32[]{:S(2)}) collective-permute-start(bf16[16,16,1024]{2,1,0:T(8,128)(2,1)S(1)} %fusion.4), channel_id=1, source_target_pairs={{0,1},{1,0},{2,3},{3,2},{4,5},{5,4},{6,7},{7,6},{8,9},{9,8},{10,11... | collective-permute-start | bytes 1572872 | tf_op jit(solution)/shard_map/ppermute | solution.py:96
  15.6 2.5 %copy.16 = bf16[4,8,32,1024]{3,1,2,0:T(8,128)(2,1)} copy(bf16[4,8,32,1024]{3,2,1,0:T(8,128)(2,1)S(1)} %bitcast.62) | data formatting | bytes 4194304
  18.3 2.1 %convolution_convert_fusion = bf16[12,32768]{1,0:T(8,128)(2,1)S(1)} fusion(bf16[32,32768]{1,0:T(8,128)(2,1)} %bitcast.65, bf16[4,32]{1,0:T(4,128)(2,1)S(1)} %get-tuple-element.17, bf16[4,32]{1,0:T(4,128)(2,1)S(1)} %get-tuple-element.16, bf16[4,32]{1,0:T(4,128)(2,1)S(1)} %get-tuple-element.15), kind=kOutput, calls=%fused_computation | convolution fusion | flops 25561344 | bytes 2884352 | tf_op jit(solution)/shard_map/dot_general | solution.py:118
  20.4 1.0 %fusion.57 = (bf16[4,32768]{1,0:T(4,128)(2,1)}, bf16[4,32768]{1,0:T(4,128)(2,1)}, bf16[4,32768]{1,0:T(4,128)(2,1)}) fusion(bf16[12,32768]{1,0:T(8,128)(2,1)S(1)} %convolution_convert_fusion), kind=kLoop, calls=%fused_computation.85 | loop fusion | bytes 1572864 | tf_op jit(solution)/shard_map/slice | solution.py:120
  21.4 2.7 %collective-permute-start.6 = (bf16[4,32768]{1,0:T(4,128)(2,1)}, bf16[4,32768]{1,0:T(4,128)(2,1)}, u32[]{:S(2)}, u32[]{:S(2)}) collective-permute-start(bf16[4,32768]{1,0:T(4,128)(2,1)} %get-tuple-element.8), channel_id=1, source_target_pairs={{0,12},{4,0},{8,4},{12,8},{1,13},{5,1},{9,5},{13,9},{2,14},{6,2},{... | collective-permute-start | bytes 786440 | tf_op jit(solution)/shard_map/ppermute | solution.py:121
  24.5 1.0 %fusion.2 = bf16[25,16,128]{2,1,0:T(8,128)(2,1)S(1)} fusion(s32[25,128]{1,0:T(8,128)S(1)} %add_select_fusion, f32[25,16,128]{2,0,1:T(8,128)S(1)} %fusion.25), kind=kOutput, calls=%fused_computation.6 | convolution fusion | flops 79052800 | bytes 320000 | tf_op jit(solution)/shard_map/bsj,bjl->bsl/dot_general | solution.py:23
  25.6 1.0 %copy.10 = f32[1024,128]{0,1:T(8,128)} copy(f32[1024,128]{1,0:T(8,128)S(1)} %bitcast_convert_fusion) | data formatting | bytes 1048576 | tf_op jit(solution)/shard_map/convert_element_type | solution.py:72
  26.7 1.4 %convert_add_fusion = f32[16,16,1024]{2,1,0:T(8,128)S(1)} fusion(bf16[16,16,1024]{2,1,0:T(8,128)(2,1)} %collective-permute-done, bf16[16,32,1]{1,0,2:T(8,128)(2,1)S(1)} %fusion.38, bf16[32,32,1024]{2,1,0:T(8,128)(2,1)S(1)} %convert_element_type.76, s32[]{:T(128)S(6)} %select_n.130), kind=kOutput, calls=%fused_computation.24 | convolution fusion | flops 17301504 | bytes 2625540 | tf_op jit(solution)/shard_map/sl,zlx->zsx/dot_general | solution.py:84
  28.9 1.6 %collective-permute-start.1 = (bf16[8,16,1024]{2,1,0:T(8,128)(2,1)}, bf16[8,16,1024]{2,1,0:T(8,128)(2,1)}, u32[]{:S(2)}, u32[]{:S(2)}) collective-permute-start(bf16[8,16,1024]{2,1,0:T(8,128)(2,1)} %dynamic-slice_convert_fusion), channel_id=1, source_target_pairs={{0,2},{2,0},{1,3},{3,1},{4,6},{6,4},{5,7},{7,5},{8,10},{10,8},{9,1... | collective-permute-start | bytes 786440 | tf_op jit(solution)/shard_map/ppermute | solution.py:47
  30.5 1.5 %fusion.5 = bf16[1024,128]{0,1:T(8,128)(2,1)} fusion(f32[1024,128]{0,1:T(8,128)S(1)} %copy-done.2, bf16[1024,1024]{1,0:T(8,128)(2,1)S(1)} %bitcast.63, bf16[16,8,8,128]{3,2,1,0:T(8,128)(2,1)S(1)} %bitcast.67), kind=kOutput, calls=%fused_computation.12 | convolution fusion | flops 268697600 | bytes 3145728 | tf_op jit(solution)/shard_map/dot_general | solution.py:68
  32.0 0.9 %convert_bitcast_fusion = f32[1,4,32,1024]{3,2,1,0:T(8,128)} fusion(bf16[4,32,1024]{2,1,0:T(8,128)(2,1)S(1)} %copy-done.5), kind=kLoop, calls=%fused_computation.29 | loop fusion | flops 131072 | bytes 786432
  33.7 2.2 %copy.15 = f32[1,4,32,1024]{3,1,2,0:T(4,128)} copy(f32[1,4,32,1024]{3,2,1,0:T(8,128)} %convert_bitcast_fusion) | data formatting | bytes 1048576
  35.9 1.1 %copy.11 = bf16[1024,128]{1,0:T(8,128)(2,1)S(1)} copy(bf16[1024,128]{0,1:T(8,128)(2,1)} %fusion.5) | data formatting | bytes 524288 | tf_op jit(solution)/shard_map/convert_element_type | solution.py:73
  37.1 1.1 %subtract_convert_fusion.1 = bf16[8,16,1024]{2,1,0:T(8,128)(2,1)S(1)} fusion(bf16[8,16,1024]{2,1,0:T(8,128)(2,1)} %collective-permute-done.1, f32[16,16,1024]{2,1,0:T(8,128)S(1)} %convert_add_fusion, s32[]{:T(128)S(6)} %select_n.136, bf16[32,16,1024]{2,1,0:T(8,128)(2,1)} %param.9, s32[]{:T(128)S(6)} %select_n.129), kind=kLoop, calls=%fused_computation.31 | loop fusion | flops 655360 | bytes 1310728 | tf_op jit(solution)/shard_map/convert_element_type | solution.py:100
  39.0 1.9 %subtract_convert_fusion = bf16[4,32768]{1,0:T(4,128)(2,1)S(1)} fusion(f32[4,32768]{1,0:T(4,128)} %bitcast.69, bf16[4,32768]{1,0:T(4,128)(2,1)} %collective-permute-done.6, bf16[4,32768]{1,0:T(4,128)(2,1)} %collective-permute-done.5, bf16[4,32768]{1,0:T(4,128)(2,1)} %collective-permute-done.4, bf16[4,32]{1,0:T(4,128)(2,1)S(1)} %get-tuple-element.14, ...), kind=kOutput, calls=%fused_computation.30 | convolution fusion | flops 9437184 | bytes 3670272 | tf_op jit(solution)/shard_map/dot_general | solution.py:113
  41.8 1.4 %collective-permute-start.8 = (bf16[4,32768]{1,0:T(4,128)(2,1)S(1)}, bf16[4,32768]{1,0:T(4,128)(2,1)S(1)}, u32[]{:S(2)}, u32[]{:S(2)}) collective-permute-start(bf16[4,32768]{1,0:T(4,128)(2,1)S(1)} %subtract_convert_fusion), channel_id=1, source_target_pairs={{0,8},{4,12},{8,0},{12,4},{1,9},{5,13},{9,1},{13,5},{2,10},{6,14},... | collective-permute-start | bytes 786440 | tf_op jit(solution)/shard_map/ppermute | solution.py:128
  43.9 1.1 %collective-permute-done.2 = bf16[8,16,1024]{2,1,0:T(8,128)(2,1)S(1)} collective-permute-done((bf16[8,16,1024]{2,1,0:T(8,128)(2,1)S(1)}, bf16[8,16,1024]{2,1,0:T(8,128)(2,1)S(1)}, u32[]{:S(2)}, u32[]{:S(2)}) %collective-permute-start.2) | collective-permute-done | bytes 262176 | tf_op jit(solution)/shard_map/ppermute | solution.py:52
  45.1 2.1 %collective-permute-start.3 = (bf16[16,16,1024]{2,1,0:T(8,128)(2,1)S(1)}, bf16[16,16,1024]{2,1,0:T(8,128)(2,1)S(1)}, u32[]{:S(2)}, u32[]{:S(2)}) collective-permute-start(bf16[16,16,1024]{2,1,0:T(8,128)(2,1)S(1)} %pad_maximum_fusion), channel_id=1, source_target_pairs={{0,1},{1,0},{2,3},{3,2},{4,5},{5,4},{6,7},{7,6},{8,9},{9,8},{10,11... | collective-permute-start | bytes 1572872 | tf_op jit(solution)/shard_map/ppermute | solution.py:52
  47.9 1.0 %collective-permute-done.8 = bf16[4,32768]{1,0:T(4,128)(2,1)S(1)} collective-permute-done((bf16[4,32768]{1,0:T(4,128)(2,1)S(1)}, bf16[4,32768]{1,0:T(4,128)(2,1)S(1)}, u32[]{:S(2)}, u32[]{:S(2)}) %collective-permute-start.8) | collective-permute-done | bytes 262176 | tf_op jit(solution)/shard_map/ppermute | solution.py:128
  48.9 7.7 %collective-permute-done.7 = bf16[4,32768]{1,0:T(4,128)(2,1)S(1)} collective-permute-done((bf16[4,32768]{1,0:T(4,128)(2,1)S(1)}, bf16[4,32768]{1,0:T(4,128)(2,1)S(1)}, u32[]{:S(2)}, u32[]{:S(2)}) %collective-permute-start.7) | collective-permute-done | bytes 262176 | tf_op jit(solution)/shard_map/ppermute | solution.py:128
  57.3 2.4 %copy.17 = f32[4,8,32,1024]{3,2,1,0:T(8,128)S(1)} copy(f32[4,8,32,1024]{3,1,2,0:T(8,128)S(1)} %bitcast.64) | data formatting | bytes 8388608
  59.9 4.2 %fusion.1 = f32[32,32,1024]{2,1,0:T(8,128)} fusion(f32[32,32,1024]{2,1,0:T(8,128)S(1)} %copy-done, f32[4,8,32,1024]{3,2,1,0:T(8,128)S(1)} %copy.17, f32[32,32,1024]{2,1,0:T(8,128)S(1)} %fusion.61, bf16[16,32,1]{1,0,2:T(8,128)(2,1)S(1)} %fusion.38, bf16[16,16,1024]{2,1,0:T(8,128)(2,1)S(1)} %get-tuple-element.6, bf16[16,16,1024]{2,1,0:T(8,128)(2,1)S(1)} %get-tuple-element.5), kind=kOutput, calls=%fused_computation.3 | convolution fusion | flops 38273024 | bytes 17826816 | tf_op jit(solution)/shard_map/sl,zsx->zlx/dot_general | solution.py:103
  (48 shorter events, 6.8 us)
Async XLA Ops:
  6.1 3.8 %copy-start.6 = (f32[4,16,128]{2,1,0:T(8,128)S(1)}, f32[4,16,128]{2,1,0:T(8,128)}, u32[]{:S(2)}) copy-start(f32[4,16,128]{2,1,0:T(8,128)} %param.11) | copy-start | bytes 98308
  10.3 16.4 %collective-permute-start = (bf16[16,16,1024]{2,1,0:T(8,128)(2,1)S(1)}, bf16[16,16,1024]{2,1,0:T(8,128)(2,1)}, u32[]{:S(2)}, u32[]{:S(2)}) collective-permute-start(bf16[16,16,1024]{2,1,0:T(8,128)(2,1)S(1)} %fusion.4), channel_id=1, source_target_pairs={{0,1},{1,0},{2,3},{3,2},{4,5},{5,4},{6,7},{7,6},{8,9},{9,8},{10,11... | collective-permute-start | bytes 1572872 | tf_op jit(solution)/shard_map/ppermute | solution.py:96
  18.3 5.8 %copy-start.8 = (s32[25]{0:T(128)S(1)}, s32[25]{0:T(128)}, u32[]{:S(2)}) copy-start(s32[25]{0:T(128)} %param.13) | copy-start | bytes 304
  18.3 5.9 %copy-start.7 = (s32[25]{0:T(128)S(1)}, s32[25]{0:T(128)}, u32[]{:S(2)}) copy-start(s32[25]{0:T(128)} %param.12) | copy-start | bytes 304
  18.3 7.2 %copy-start.4 = (bf16[32,32,128]{2,1,0:T(8,128)(2,1)S(1)}, bf16[32,32,128]{2,1,0:T(8,128)(2,1)}, u32[]{:S(2)}) copy-start(bf16[32,32,128]{2,1,0:T(8,128)(2,1)} %param.8) | copy-start | bytes 786436
  21.4 17.6 %collective-permute-start.4 = (bf16[4,32768]{1,0:T(4,128)(2,1)}, bf16[4,32768]{1,0:T(4,128)(2,1)}, u32[]{:S(2)}, u32[]{:S(2)}) collective-permute-start(bf16[4,32768]{1,0:T(4,128)(2,1)} %get-tuple-element.7), channel_id=1, source_target_pairs={{0,4},{4,8},{8,12},{12,0},{1,5},{5,9},{9,13},{13,1},{2,6},{6,10},{... | collective-permute-start | bytes 786440 | tf_op jit(solution)/shard_map/ppermute | solution.py:121
  21.4 17.6 %collective-permute-start.6 = (bf16[4,32768]{1,0:T(4,128)(2,1)}, bf16[4,32768]{1,0:T(4,128)(2,1)}, u32[]{:S(2)}, u32[]{:S(2)}) collective-permute-start(bf16[4,32768]{1,0:T(4,128)(2,1)} %get-tuple-element.8), channel_id=1, source_target_pairs={{0,12},{4,0},{8,4},{12,8},{1,13},{5,1},{9,5},{13,9},{2,14},{6,2},{... | collective-permute-start | bytes 786440 | tf_op jit(solution)/shard_map/ppermute | solution.py:121
  24.1 14.9 %collective-permute-start.5 = (bf16[4,32768]{1,0:T(4,128)(2,1)}, bf16[4,32768]{1,0:T(4,128)(2,1)}, u32[]{:S(2)}, u32[]{:S(2)}) collective-permute-start(bf16[4,32768]{1,0:T(4,128)(2,1)} %get-tuple-element.9), channel_id=1, source_target_pairs={{0,8},{4,12},{8,0},{12,4},{1,9},{5,13},{9,1},{13,5},{2,10},{6,14},... | collective-permute-start | bytes 786440 | tf_op jit(solution)/shard_map/ppermute | solution.py:121
  26.6 3.9 %copy-start.2 = (f32[1024,128]{0,1:T(8,128)S(1)}, f32[1024,128]{0,1:T(8,128)}, u32[]{:S(2)}) copy-start(f32[1024,128]{0,1:T(8,128)} %copy.10) | copy-start | bytes 1572868
  28.1 3.9 %copy-start.5 = (bf16[4,32,1024]{2,1,0:T(8,128)(2,1)S(1)}, bf16[4,32,1024]{2,1,0:T(8,128)(2,1)}, u32[]{:S(2)}) copy-start(bf16[4,32,1024]{2,1,0:T(8,128)(2,1)} %param.10) | copy-start | bytes 786436
  28.9 8.2 %collective-permute-start.1 = (bf16[8,16,1024]{2,1,0:T(8,128)(2,1)}, bf16[8,16,1024]{2,1,0:T(8,128)(2,1)}, u32[]{:S(2)}, u32[]{:S(2)}) collective-permute-start(bf16[8,16,1024]{2,1,0:T(8,128)(2,1)} %dynamic-slice_convert_fusion), channel_id=1, source_target_pairs={{0,2},{2,0},{1,3},{3,1},{4,6},{6,4},{5,7},{7,5},{8,10},{10,8},{9,1... | collective-permute-start | bytes 786440 | tf_op jit(solution)/shard_map/ppermute | solution.py:47
  32.0 7.0 %copy-start.1 = (bf16[4,8,32,1024]{3,1,2,0:T(8,128)(2,1)S(1)}, bf16[4,8,32,1024]{3,1,2,0:T(8,128)(2,1)}, u32[]{:S(2)}) copy-start(bf16[4,8,32,1024]{3,1,2,0:T(8,128)(2,1)} %copy.16) | copy-start | bytes 6291460
  38.2 6.8 %collective-permute-start.2 = (bf16[8,16,1024]{2,1,0:T(8,128)(2,1)S(1)}, bf16[8,16,1024]{2,1,0:T(8,128)(2,1)S(1)}, u32[]{:S(2)}, u32[]{:S(2)}) collective-permute-start(bf16[8,16,1024]{2,1,0:T(8,128)(2,1)S(1)} %subtract_convert_fusion.1), channel_id=1, source_target_pairs={{0,2},{2,0},{1,3},{3,1},{4,6},{6,4},{5,7},{7,5},{8,10},{10,8},{9,1... | collective-permute-start | bytes 786440 | tf_op jit(solution)/shard_map/ppermute | solution.py:52
  39.0 8.2 %copy-start.3 = (bf16[128,1024,1]{1,0,2:T(8,128)(2,1)S(1)}, bf16[128,1024,1]{1,0,2:T(8,128)(2,1)}, u32[]{:S(2)}) copy-start(bf16[128,1024,1]{1,0,2:T(8,128)(2,1)} %reshape.82) | copy-start | bytes 786436
  40.9 7.0 %collective-permute-start.9 = (bf16[4,32768]{1,0:T(4,128)(2,1)S(1)}, bf16[4,32768]{1,0:T(4,128)(2,1)S(1)}, u32[]{:S(2)}, u32[]{:S(2)}) collective-permute-start(bf16[4,32768]{1,0:T(4,128)(2,1)S(1)} %subtract_convert_fusion), channel_id=1, source_target_pairs={{0,12},{4,0},{8,4},{12,8},{1,13},{5,1},{9,5},{13,9},{2,14},{6,2},{... | collective-permute-start | bytes 786440 | tf_op jit(solution)/shard_map/ppermute | solution.py:128
  41.8 7.1 %collective-permute-start.8 = (bf16[4,32768]{1,0:T(4,128)(2,1)S(1)}, bf16[4,32768]{1,0:T(4,128)(2,1)S(1)}, u32[]{:S(2)}, u32[]{:S(2)}) collective-permute-start(bf16[4,32768]{1,0:T(4,128)(2,1)S(1)} %subtract_convert_fusion), channel_id=1, source_target_pairs={{0,8},{4,12},{8,0},{12,4},{1,9},{5,13},{9,1},{13,5},{2,10},{6,14},... | collective-permute-start | bytes 786440 | tf_op jit(solution)/shard_map/ppermute | solution.py:128
  43.2 13.4 %collective-permute-start.7 = (bf16[4,32768]{1,0:T(4,128)(2,1)S(1)}, bf16[4,32768]{1,0:T(4,128)(2,1)S(1)}, u32[]{:S(2)}, u32[]{:S(2)}) collective-permute-start(bf16[4,32768]{1,0:T(4,128)(2,1)S(1)} %subtract_convert_fusion), channel_id=1, source_target_pairs={{0,4},{4,8},{8,12},{12,0},{1,5},{5,9},{9,13},{13,1},{2,6},{6,10},{... | collective-permute-start | bytes 786440 | tf_op jit(solution)/shard_map/ppermute | solution.py:128
  45.1 14.7 %collective-permute-start.3 = (bf16[16,16,1024]{2,1,0:T(8,128)(2,1)S(1)}, bf16[16,16,1024]{2,1,0:T(8,128)(2,1)S(1)}, u32[]{:S(2)}, u32[]{:S(2)}) collective-permute-start(bf16[16,16,1024]{2,1,0:T(8,128)(2,1)S(1)} %pad_maximum_fusion), channel_id=1, source_target_pairs={{0,1},{1,0},{2,3},{3,2},{4,5},{5,4},{6,7},{7,6},{8,9},{9,8},{10,11... | collective-permute-start | bytes 1572872 | tf_op jit(solution)/shard_map/ppermute | solution.py:52
  57.3 2.5 %copy-start = (f32[32,32,1024]{2,1,0:T(8,128)S(1)}, f32[32,32,1024]{2,1,0:T(8,128)}, u32[]{:S(2)}) copy-start(f32[32,32,1024]{2,1,0:T(8,128)} %param.7) | copy-start | bytes 12582916

commit v13 on v11

--- a/solution.py
+++ b/solution.py
@@ -22,6 +22,12 @@
     moving = (target[:, :, None] == columns[None, None, :]).astype(jnp.float32)
     shifted = jnp.einsum("bsj,bjl->bsl", picked, moving, precision=lax.Precision.HIGHEST)
     return shifted.astype(jnp.bfloat16)
+
+
+def spread(band, rows):
+    eye = jnp.eye(rows, dtype=band.dtype)
+    outer, inner = band.shape
+    return (band[:, None, :, None] * eye[None, :, None, :]).reshape(outer * rows, inner * rows)
 
 
 def banded_matrix(along):
@@ -101,19 +107,22 @@
     mat_z = lax.dynamic_index_in_dim(along_z, zb, 0, keepdims=False)
     band_z = lax.dynamic_slice_in_dim(mat_z, zq * planes, planes, 1)
     piece = SLICES // group
-    sheet = coarse.reshape(planes, rows_here * width)
+    sheet = coarse.reshape(planes * rows_here, width)
     own_rows = lax.dynamic_slice_in_dim(band_z, zq * piece, piece, 0)
-    fwd_z = jnp.dot(own_rows, sheet, preferred_element_type=jnp.float32)
+    fwd_z = jnp.dot(spread(own_rows, rows_here), sheet, preferred_element_type=jnp.float32)
     far_rows = jnp.concatenate(
         [lax.dynamic_slice_in_dim(band_z, ((zq + k) % group) * piece, piece, 0) for k in range(1, group)],
         0,
     )
-    far_z = jnp.dot(far_rows, sheet, preferred_element_type=jnp.float32).astype(jnp.bfloat16)
+    far_z = jnp.dot(
+        spread(far_rows, rows_here), sheet, preferred_element_type=jnp.float32
+    ).astype(jnp.bfloat16)
+    block = piece * rows_here
     for k in range(1, group):
-        sent = far_z[(k - 1) * piece : k * piece]
+        sent = far_z[(k - 1) * block : k * block]
         got = lax.ppermute(sent, "zq", [(j, (j + k) % group) for j in range(group)])
         fwd_z = fwd_z + got.astype(jnp.float32)
-    observed = slices_z.reshape(piece, rows_here * width).astype(jnp.float32)
+    observed = slices_z.reshape(block, width).astype(jnp.float32)
     resid_z = (observed - fwd_z).astype(jnp.bfloat16)
     pieces = [resid_z]
     rows = [own_rows]
@@ -121,10 +130,9 @@
         pieces.append(lax.ppermute(resid_z, "zq", [(j, (j + k) % group) for j in range(group)]))
         src = (zq - k + group) % group
         rows.append(lax.dynamic_slice_in_dim(band_z, src * piece, piece, 0))
-    corr_z = lax.dot_general(
-        jnp.concatenate(rows, 0),
+    corr_z = jnp.dot(
+        spread(jnp.concatenate(rows, 0).T, rows_here),
         jnp.concatenate(pieces, 0),
-        (((0,), (0,)), ((), ())),
         preferred_element_type=jnp.float32,
     ).reshape(planes, rows_here, width)
 

time: 57 us -> 67.1 us (1.18)
  waiting for transfers between devices: 10.3 us -> 16.3 us
  starting transfers between devices: 13.6 us -> 15.9 us
  other arithmetic: 5.59 us -> 7.65 us
  matrix products: 14.9 us -> 14.1 us
    mul x0 -> x6, local copies, waits for them, and re-layouts: none -> 6.34 us  [spread(): band[:, None, :, None] * eye[None, :, None, :]]
    unnamed x19 -> x20, local copies, waits for them, and re-layouts: 7.16 us -> 1.3 us
    dot_general x1, matrix products: 4.25 us -> 0.89 us  [shards(): jnp.einsum('sl,zsx->zlx', band_y, resid_y, preferred_element_type=jnp.flo...]
    ppermute x3, starting transfers between devices: 2.68 us -> 5.8 us  [shards(): got = lax.ppermute(sent, 'zq', [(j, (j + k) % group) for j in range(group)])]
    ppermute x2, waiting for transfers between devices: 1.01 us -> 3.5 us  [double(): other = lax.ppermute(values, axis, [(0, 1), (1, 0)])]
    ppermute x1, starting transfers between devices: 3.29 us -> 1.52 us  [shards(): lax.ppermute(give_y, 'co', [(0, 1), (1, 0)]).astype(jnp.float32)]
    dot_general x3, matrix products: 4.69 us -> 6.15 us  [the longest x1 3.47 us: shards(): jnp.dot(spread(jnp.concatenate(rows, 0).T, rows_here), jnp.concatenate(pi...]
    ppermute x1, waiting for transfers between devices: 0.01 us -> 1.33 us  [halve(): got = lax.ppermute(give.astype(jnp.bfloat16), axis, [(0, 1), (1, 0)])]
  transfers between devices with their start and end apart: 10 -> 10, of which waited for: 3 -> 5; matrix products, arithmetic and copies ran while one was open for 40% -> 27% of each run, Pallas kernels for 0% -> 0%
where the time goes in v13:
time: 67.1 us; the launch traced here: 66.8 us
  waiting for transfers between devices  16.3 us (24%)
  starting transfers between devices  15.9 us (24%)
  matrix products  14.1 us (21%)
  local copies, waits for them, and re-layouts  12.5 us (19%)
  other arithmetic  7.65 us (11%)
    ppermute x3, waiting for transfers between devices, shards(): lax.ppermute(resid_z, 'zq', [(j, (j + k) % group) for j in range(group)])  10.6 us
    mul x6, local copies, waits for them, and re-layouts, spread(): band[:, None, :, None] * eye[None, :, None, :]  6.34 us
    ppermute x3, starting transfers between devices, shards(): got = lax.ppermute(sent, 'zq', [(j, (j + k) % group) for j in range(group)])  5.8 us
    ppermute x3, starting transfers between devices, shards(): lax.ppermute(resid_z, 'zq', [(j, (j + k) % group) for j in range(group)])  3.52 us
    ppermute x2, waiting for transfers between devices, double(): other = lax.ppermute(values, axis, [(0, 1), (1, 0)])  3.5 us
    dot_general x1, matrix products, shards(): jnp.dot(spread(jnp.concatenate(rows, 0).T, rows_here), jnp.concatenate(pi...  3.47 us
    ppermute x2, starting transfers between devices, double(): other = lax.ppermute(values, axis, [(0, 1), (1, 0)])  3.46 us
    convert_element_type x1, other arithmetic, shards(): coarse = volume.astype(jnp.bfloat16)  2.58 us
  transfers between devices with their start and end apart: 10, of which 5 were waited for; matrix products, arithmetic and copies ran while one was open for 27% of the time, Pallas kernels for 0%

profile of v13, /device:TPU:1, one launch (start us, length us, event | category | flops | bytes accessed | tf_op | source)
XLA Modules:
  0.0 66.8 jit_solution(11372155895102390416)
XLA Ops:
  1.8 1.0 %fusion.7 = bf16[25,16,128]{2,1,0:T(8,128)(2,1)S(1)} fusion(s32[25,128]{1,0:T(8,128)S(1)} %add_select_fusion, f32[25,16,128]{2,0,1:T(8,128)S(1)} %fusion.30), kind=kOutput, calls=%fused_computation.14 | convolution fusion | flops 79104000 | bytes 320000 | tf_op jit(solution)/shard_map/bsj,bjl->bsl/dot_general | solution.py:23
  3.2 4.0 %mul.175 = bf16[384,1024]{1,0:T(8,128)(2,1)} reshape(bf16[12,32,32,32]{3,2,1,0:T(8,128)(2,1)S(1)} %broadcast_multiply_fusion) | data formatting | bytes 1572864 | tf_op jit(solution)/shard_map/mul | solution.py:30
  7.3 2.6 %convert_element_type.83 = bf16[32,32,1024]{2,1,0:T(8,128)(2,1)S(1)} convert(f32[32,32,1024]{2,1,0:T(8,128)} %param.7) | non-fusion elementwise | flops 1048576 | bytes 6291456 | tf_op jit(solution)/shard_map/convert_element_type | solution.py:64
  11.8 2.1 %collective-permute-start.4 = (bf16[128,1024]{1,0:T(8,128)(2,1)}, bf16[128,1024]{1,0:T(8,128)(2,1)}, u32[]{:S(2)}, u32[]{:S(2)}) collective-permute-start(bf16[128,1024]{1,0:T(8,128)(2,1)} %get-tuple-element.7), channel_id=1, source_target_pairs={{0,4},{4,8},{8,12},{12,0},{1,5},{5,9},{9,13},{13,1},{2,6},{6,10},{... | collective-permute-start | bytes 786440 | tf_op jit(solution)/shard_map/ppermute | solution.py:123
  13.9 2.6 %collective-permute-start.5 = (bf16[128,1024]{1,0:T(8,128)(2,1)}, bf16[128,1024]{1,0:T(8,128)(2,1)}, u32[]{:S(2)}, u32[]{:S(2)}) collective-permute-start(bf16[128,1024]{1,0:T(8,128)(2,1)} %get-tuple-element.9), channel_id=1, source_target_pairs={{0,8},{4,12},{8,0},{12,4},{1,9},{5,13},{9,1},{13,5},{2,10},{6,14},... | collective-permute-start | bytes 786440 | tf_op jit(solution)/shard_map/ppermute | solution.py:123
  16.5 1.1 %collective-permute-start.6 = (bf16[128,1024]{1,0:T(8,128)(2,1)}, bf16[128,1024]{1,0:T(8,128)(2,1)}, u32[]{:S(2)}, u32[]{:S(2)}) collective-permute-start(bf16[128,1024]{1,0:T(8,128)(2,1)} %get-tuple-element.8), channel_id=1, source_target_pairs={{0,12},{4,0},{8,4},{12,8},{1,13},{5,1},{9,5},{13,9},{2,14},{6,2},{... | collective-permute-start | bytes 786440 | tf_op jit(solution)/shard_map/ppermute | solution.py:123
  17.6 1.1 %fusion.5 = bf16[16,16,1024]{2,1,0:T(8,128)(2,1)} fusion(bf16[32,32,1024]{2,1,0:T(8,128)(2,1)S(1)} %convert_element_type.83, s32[]{:T(128)S(6)} %select_n.113, bf16[1,16,128]{2,1,0:T(8,128)(2,1)S(1)} %slice.25, s32[]{:T(128)S(6)} %select_n.112), kind=kOutput, calls=%fused_computation.12 | convolution fusion | flops 17039360 | bytes 1576968 | tf_op jit(solution)/shard_map/sl,zlx->zsx/dot_general | solution.py:89
  18.7 1.5 %collective-permute-start = (bf16[16,16,1024]{2,1,0:T(8,128)(2,1)}, bf16[16,16,1024]{2,1,0:T(8,128)(2,1)}, u32[]{:S(2)}, u32[]{:S(2)}) collective-permute-start(bf16[16,16,1024]{2,1,0:T(8,128)(2,1)} %fusion.5), channel_id=1, source_target_pairs={{0,1},{1,0},{2,3},{3,2},{4,5},{5,4},{6,7},{7,6},{8,9},{9,8},{10,11... | collective-permute-start | bytes 1572872 | tf_op jit(solution)/shard_map/ppermute | solution.py:95
  22.1 1.4 %convert_add_fusion = f32[16,16,1024]{2,1,0:T(8,128)S(1)} fusion(bf16[16,16,1024]{2,1,0:T(8,128)(2,1)} %collective-permute-done, bf16[32,32,1024]{2,1,0:T(8,128)(2,1)S(1)} %convert_element_type.83, s32[]{:T(128)S(6)} %select_n.111, bf16[1,16,128]{2,1,0:T(8,128)(2,1)S(1)} %slice.25, s32[]{:T(128)S(6)} %select_n.112), kind=kOutput, calls=%fused_computation.27 | convolution fusion | flops 17301504 | bytes 2625544 | tf_op jit(solution)/shard_map/sl,zlx->zsx/dot_general | solution.py:83
  25.2 1.6 %collective-permute-start.1 = (bf16[8,16,1024]{2,1,0:T(8,128)(2,1)}, bf16[8,16,1024]{2,1,0:T(8,128)(2,1)}, u32[]{:S(2)}, u32[]{:S(2)}) collective-permute-start(bf16[8,16,1024]{2,1,0:T(8,128)(2,1)} %dynamic-slice_convert_fusion), channel_id=1, source_target_pairs={{0,2},{2,0},{1,3},{3,1},{4,6},{6,4},{5,7},{7,5},{8,10},{10,8},{9,1... | collective-permute-start | bytes 786440 | tf_op jit(solution)/shard_map/ppermute | solution.py:45
  26.9 1.8 %mul.171 = bf16[128,1024]{1,0:T(8,128)(2,1)} reshape(bf16[4,32,32,32]{3,2,1,0:T(8,128)(2,1)S(1)} %broadcast_multiply_fusion.1) | data formatting | bytes 524288 | tf_op jit(solution)/shard_map/mul | solution.py:30
  29.1 2.0 %copy.11 = f32[1024,128]{0,1:T(8,128)} copy(f32[1024,128]{1,0:T(8,128)} %bitcast_convert_fusion) | data formatting | bytes 1048576 | tf_op jit(solution)/shard_map/convert_element_type | solution.py:72
  32.1 1.3 %collective-permute-done.1 = bf16[8,16,1024]{2,1,0:T(8,128)(2,1)} collective-permute-done((bf16[8,16,1024]{2,1,0:T(8,128)(2,1)}, bf16[8,16,1024]{2,1,0:T(8,128)(2,1)}, u32[]{:S(2)}, u32[]{:S(2)}) %collective-permute-start.1) | collective-permute-done | bytes 262176 | tf_op jit(solution)/shard_map/ppermute | solution.py:45
  33.4 1.8 %subtract_convert_fusion = bf16[8,16,1024]{2,1,0:T(8,128)(2,1)} fusion(bf16[8,16,1024]{2,1,0:T(8,128)(2,1)} %collective-permute-done.1, f32[16,16,1024]{2,1,0:T(8,128)S(1)} %copy-done.3, s32[]{:T(128)S(6)} %select_n.114, bf16[32,16,1024]{2,1,0:T(8,128)(2,1)} %param.9, s32[]{:T(128)S(6)} %select_n.110), kind=kLoop, calls=%fused_computation.37 | loop fusion | flops 655360 | bytes 1310728 | tf_op jit(solution)/shard_map/convert_element_type | solution.py:99
  35.2 1.3 %collective-permute-start.2 = (bf16[8,16,1024]{2,1,0:T(8,128)(2,1)}, bf16[8,16,1024]{2,1,0:T(8,128)(2,1)S(1)}, u32[]{:S(2)}, u32[]{:S(2)}) collective-permute-start(bf16[8,16,1024]{2,1,0:T(8,128)(2,1)} %subtract_convert_fusion), channel_id=1, source_target_pairs={{0,2},{2,0},{1,3},{3,1},{4,6},{6,4},{5,7},{7,5},{8,10},{10,8},{9,1... | collective-permute-start | bytes 786440 | tf_op jit(solution)/shard_map/ppermute | solution.py:50
  36.5 1.9 %fusion.6 = bf16[1024,128]{0,1:T(8,128)(2,1)S(1)} fusion(f32[1024,128]{0,1:T(8,128)} %copy.11, bf16[1024,1024]{1,0:T(8,128)(2,1)S(1)} %bitcast.71, bf16[16,8,8,128]{3,2,1,0:T(8,128)(2,1)S(1)} %bitcast.73), kind=kOutput, calls=%fused_computation.13 | convolution fusion | flops 268697600 | bytes 3145728 | tf_op jit(solution)/shard_map/dot_general | solution.py:68
  38.8 3.5 %collective-permute-done.2 = bf16[8,16,1024]{2,1,0:T(8,128)(2,1)S(1)} collective-permute-done((bf16[8,16,1024]{2,1,0:T(8,128)(2,1)}, bf16[8,16,1024]{2,1,0:T(8,128)(2,1)S(1)}, u32[]{:S(2)}, u32[]{:S(2)}) %collective-permute-start.2) | collective-permute-done | bytes 262176 | tf_op jit(solution)/shard_map/ppermute | solution.py:50
  42.3 1.0 %broadcast_select_fusion.3 = (bf16[8,16,1024]{2,1,0:T(8,128)(2,1)S(1)}, bf16[8,16,1024]{2,1,0:T(8,128)(2,1)S(1)}) fusion(bf16[8,16,1024]{2,1,0:T(8,128)(2,1)} %subtract_convert_fusion, bf16[8,16,1024]{2,1,0:T(8,128)(2,1)S(1)} %collective-permute-done.2, pred[]{:T(512)S(6)} %eq.71), kind=kLoop, calls=%fused_computation.45 | loop fusion | flops 262144 | bytes 1048577 | tf_op jit(solution)/shard_map/jit(_where)/select_n | solution.py:51
  43.3 2.2 %collective-permute-start.3 = (bf16[16,16,1024]{2,1,0:T(8,128)(2,1)S(1)}, bf16[16,16,1024]{2,1,0:T(8,128)(2,1)S(1)}, u32[]{:S(2)}, u32[]{:S(2)}) collective-permute-start(bf16[16,16,1024]{2,1,0:T(8,128)(2,1)S(1)} %pad_maximum_fusion), channel_id=1, source_target_pairs={{0,1},{1,0},{2,3},{3,2},{4,5},{5,4},{6,7},{7,6},{8,9},{9,8},{10,11... | collective-permute-start | bytes 1572872 | tf_op jit(solution)/shard_map/ppermute | solution.py:50
  46.5 1.7 %fusion.24 = bf16[128,1024]{1,0:T(8,128)(2,1)S(1)} fusion(bf16[128,1024]{1,0:T(8,128)(2,1)} %collective-permute-done.6, bf16[128,1024]{1,0:T(8,128)(2,1)} %collective-permute-done.5, bf16[128,1024]{1,0:T(8,128)(2,1)} %collective-permute-done.4, bf16[4,32,1024]{2,1,0:T(8,128)(2,1)S(1)} %copy-done.7, bf16[128,1024]{1,0:T(8,128)(2,1)S(1)} %copy-done.4, ...), kind=kOutput, calls=%fused_computation.33 | convolution fusion | flops 269615104 | bytes 3670016 | tf_op jit(solution)/shard_map/dot_general | solution.py:112
  48.7 1.1 %collective-permute-start.8 = (bf16[128,1024]{1,0:T(8,128)(2,1)S(1)}, bf16[128,1024]{1,0:T(8,128)(2,1)S(1)}, u32[]{:S(2)}, u32[]{:S(2)}) collective-permute-start(bf16[128,1024]{1,0:T(8,128)(2,1)S(1)} %fusion.24), channel_id=1, source_target_pairs={{0,8},{4,12},{8,0},{12,4},{1,9},{5,13},{9,1},{13,5},{2,10},{6,14},... | collective-permute-start | bytes 786440 | tf_op jit(solution)/shard_map/ppermute | solution.py:130
  49.8 2.0 %collective-permute-start.9 = (bf16[128,1024]{1,0:T(8,128)(2,1)S(1)}, bf16[128,1024]{1,0:T(8,128)(2,1)S(1)}, u32[]{:S(2)}, u32[]{:S(2)}) collective-permute-start(bf16[128,1024]{1,0:T(8,128)(2,1)S(1)} %fusion.24), channel_id=1, source_target_pairs={{0,12},{4,0},{8,4},{12,8},{1,13},{5,1},{9,5},{13,9},{2,14},{6,2},{... | collective-permute-start | bytes 786440 | tf_op jit(solution)/shard_map/ppermute | solution.py:130
  52.7 10.2 %collective-permute-done.7 = bf16[128,1024]{1,0:T(8,128)(2,1)S(1)} collective-permute-done((bf16[128,1024]{1,0:T(8,128)(2,1)S(1)}, bf16[128,1024]{1,0:T(8,128)(2,1)S(1)}, u32[]{:S(2)}, u32[]{:S(2)}) %collective-permute-start.7) | collective-permute-done | bytes 262176 | tf_op jit(solution)/shard_map/ppermute | solution.py:130
  63.3 3.5 %fusion.2 = f32[32,32,1024]{2,1,0:T(8,128)} fusion(f32[32,32,1024]{2,1,0:T(8,128)S(1)} %copy-done.1, f32[32,32,1024]{2,1,0:T(8,128)S(1)} %fusion.53, f32[32,1024,32]{1,2,0:T(8,128)S(1)} %fusion.8, bf16[128,1024]{1,0:T(8,128)(2,1)S(1)} %collective-permute-done.9, bf16[128,1024]{1,0:T(8,128)(2,1)S(1)} %collective-permute-done.8, ...), kind=kOutput, calls=%fused_computation.3 | convolution fusion | flops 1082654720 | bytes 17891328 | tf_op jit(solution)/shard_map/dot_general | solution.py:133
  (57 shorter events, 12.0 us)
Async XLA Ops:
  0.0 0.8 %copy-start = (f32[4,16,128]{2,1,0:T(8,128)S(1)}, f32[4,16,128]{2,1,0:T(8,128)}, u32[]{:S(2)}) copy-start(f32[4,16,128]{2,1,0:T(8,128)} %param.11) | copy-start | bytes 98308
  2.8 24.1 %copy-start.9 = (bf16[25,16,128]{2,1,0:T(8,128)(2,1)}, bf16[25,16,128]{2,1,0:T(8,128)(2,1)S(1)}, u32[]{:S(2)}) copy-start(bf16[25,16,128]{2,1,0:T(8,128)(2,1)S(1)} %fusion.7) | copy-start | bytes 307204
  7.3 2.6 %copy-start.6 = (bf16[384,1024]{1,0:T(8,128)(2,1)S(1)}, bf16[384,1024]{1,0:T(8,128)(2,1)}, u32[]{:S(2)}) copy-start(bf16[384,1024]{1,0:T(8,128)(2,1)} %mul.175) | copy-start | bytes 2359300
  10.9 9.4 %copy-start.8 = (bf16[32,32,128]{2,1,0:T(8,128)(2,1)S(1)}, bf16[32,32,128]{2,1,0:T(8,128)(2,1)}, u32[]{:S(2)}) copy-start(bf16[32,32,128]{2,1,0:T(8,128)(2,1)} %param.8) | copy-start | bytes 786436
  11.8 34.4 %collective-permute-start.4 = (bf16[128,1024]{1,0:T(8,128)(2,1)}, bf16[128,1024]{1,0:T(8,128)(2,1)}, u32[]{:S(2)}, u32[]{:S(2)}) collective-permute-start(bf16[128,1024]{1,0:T(8,128)(2,1)} %get-tuple-element.7), channel_id=1, source_target_pairs={{0,4},{4,8},{8,12},{12,0},{1,5},{5,9},{9,13},{13,1},{2,6},{6,10},{... | collective-permute-start | bytes 786440 | tf_op jit(solution)/shard_map/ppermute | solution.py:123
  13.9 32.3 %collective-permute-start.5 = (bf16[128,1024]{1,0:T(8,128)(2,1)}, bf16[128,1024]{1,0:T(8,128)(2,1)}, u32[]{:S(2)}, u32[]{:S(2)}) collective-permute-start(bf16[128,1024]{1,0:T(8,128)(2,1)} %get-tuple-element.9), channel_id=1, source_target_pairs={{0,8},{4,12},{8,0},{12,4},{1,9},{5,13},{9,1},{13,5},{2,10},{6,14},... | collective-permute-start | bytes 786440 | tf_op jit(solution)/shard_map/ppermute | solution.py:123
  16.5 29.7 %collective-permute-start.6 = (bf16[128,1024]{1,0:T(8,128)(2,1)}, bf16[128,1024]{1,0:T(8,128)(2,1)}, u32[]{:S(2)}, u32[]{:S(2)}) collective-permute-start(bf16[128,1024]{1,0:T(8,128)(2,1)} %get-tuple-element.8), channel_id=1, source_target_pairs={{0,12},{4,0},{8,4},{12,8},{1,13},{5,1},{9,5},{13,9},{2,14},{6,2},{... | collective-permute-start | bytes 786440 | tf_op jit(solution)/shard_map/ppermute | solution.py:123
  18.7 3.4 %collective-permute-start = (bf16[16,16,1024]{2,1,0:T(8,128)(2,1)}, bf16[16,16,1024]{2,1,0:T(8,128)(2,1)}, u32[]{:S(2)}, u32[]{:S(2)}) collective-permute-start(bf16[16,16,1024]{2,1,0:T(8,128)(2,1)} %fusion.5), channel_id=1, source_target_pairs={{0,1},{1,0},{2,3},{3,2},{4,5},{5,4},{6,7},{7,6},{8,9},{9,8},{10,11... | collective-permute-start | bytes 1572872 | tf_op jit(solution)/shard_map/ppermute | solution.py:95
  23.5 1.0 %copy-start.2 = (f32[16,16,1024]{2,1,0:T(8,128)}, f32[16,16,1024]{2,1,0:T(8,128)S(1)}, u32[]{:S(2)}) copy-start(f32[16,16,1024]{2,1,0:T(8,128)S(1)} %convert_add_fusion) | copy-start | bytes 3145732
  25.2 8.2 %collective-permute-start.1 = (bf16[8,16,1024]{2,1,0:T(8,128)(2,1)}, bf16[8,16,1024]{2,1,0:T(8,128)(2,1)}, u32[]{:S(2)}, u32[]{:S(2)}) collective-permute-start(bf16[8,16,1024]{2,1,0:T(8,128)(2,1)} %dynamic-slice_convert_fusion), channel_id=1, source_target_pairs={{0,2},{2,0},{1,3},{3,1},{4,6},{6,4},{5,7},{7,5},{8,10},{10,8},{9,1... | collective-permute-start | bytes 786440 | tf_op jit(solution)/shard_map/ppermute | solution.py:45
  26.9 4.3 %slice-start = ((bf16[25,16,128]{2,1,0:T(8,128)(2,1)}), bf16[8,16,128]{2,1,0:T(8,128)(2,1)S(1)}, s32[]{:S(2)}) async-start(bf16[25,16,128]{2,1,0:T(8,128)(2,1)} %copy-done.9), calls=%async_computation | async-start | bytes 65536 | tf_op jit(solution)/shard_map/slice | solution.py:61
  28.7 4.7 %copy-start.3 = (f32[16,16,1024]{2,1,0:T(8,128)S(1)}, f32[16,16,1024]{2,1,0:T(8,128)}, u32[]{:S(2)}) copy-start(f32[16,16,1024]{2,1,0:T(8,128)} %copy-done.2) | copy-start | bytes 3145732
  35.2 7.0 %collective-permute-start.2 = (bf16[8,16,1024]{2,1,0:T(8,128)(2,1)}, bf16[8,16,1024]{2,1,0:T(8,128)(2,1)S(1)}, u32[]{:S(2)}, u32[]{:S(2)}) collective-permute-start(bf16[8,16,1024]{2,1,0:T(8,128)(2,1)} %subtract_convert_fusion), channel_id=1, source_target_pairs={{0,2},{2,0},{1,3},{3,1},{4,6},{6,4},{5,7},{7,5},{8,10},{10,8},{9,1... | collective-permute-start | bytes 786440 | tf_op jit(solution)/shard_map/ppermute | solution.py:50
  38.4 7.1 %copy-start.5 = (bf16[128,1024,1]{1,0,2:T(8,128)(2,1)S(1)}, bf16[128,1024,1]{1,0,2:T(8,128)(2,1)}, u32[]{:S(2)}) copy-start(bf16[128,1024,1]{1,0,2:T(8,128)(2,1)} %reshape.131) | copy-start | bytes 786436
  43.3 8.4 %collective-permute-start.3 = (bf16[16,16,1024]{2,1,0:T(8,128)(2,1)S(1)}, bf16[16,16,1024]{2,1,0:T(8,128)(2,1)S(1)}, u32[]{:S(2)}, u32[]{:S(2)}) collective-permute-start(bf16[16,16,1024]{2,1,0:T(8,128)(2,1)S(1)} %pad_maximum_fusion), channel_id=1, source_target_pairs={{0,1},{1,0},{2,3},{3,2},{4,5},{5,4},{6,7},{7,6},{8,9},{9,8},{10,11... | collective-permute-start | bytes 1572872 | tf_op jit(solution)/shard_map/ppermute | solution.py:50
  45.5 1.0 %copy-start.4 = (bf16[128,1024]{1,0:T(8,128)(2,1)S(1)}, bf16[128,1024]{1,0:T(8,128)(2,1)}, u32[]{:S(2)}) copy-start(bf16[128,1024]{1,0:T(8,128)(2,1)} %mul.171) | copy-start | bytes 786436
  45.5 1.0 %copy-start.7 = (bf16[4,32,1024]{2,1,0:T(8,128)(2,1)S(1)}, bf16[4,32,1024]{2,1,0:T(8,128)(2,1)}, u32[]{:S(2)}) copy-start(bf16[4,32,1024]{2,1,0:T(8,128)(2,1)} %param.10) | copy-start | bytes 786436
  48.2 14.7 %collective-permute-start.7 = (bf16[128,1024]{1,0:T(8,128)(2,1)S(1)}, bf16[128,1024]{1,0:T(8,128)(2,1)S(1)}, u32[]{:S(2)}, u32[]{:S(2)}) collective-permute-start(bf16[128,1024]{1,0:T(8,128)(2,1)S(1)} %fusion.24), channel_id=1, source_target_pairs={{0,4},{4,8},{8,12},{12,0},{1,5},{5,9},{9,13},{13,1},{2,6},{6,10},{... | collective-permute-start | bytes 786440 | tf_op jit(solution)/shard_map/ppermute | solution.py:130
  48.7 14.3 %collective-permute-start.8 = (bf16[128,1024]{1,0:T(8,128)(2,1)S(1)}, bf16[128,1024]{1,0:T(8,128)(2,1)S(1)}, u32[]{:S(2)}, u32[]{:S(2)}) collective-permute-start(bf16[128,1024]{1,0:T(8,128)(2,1)S(1)} %fusion.24), channel_id=1, source_target_pairs={{0,8},{4,12},{8,0},{12,4},{1,9},{5,13},{9,1},{13,5},{2,10},{6,14},... | collective-permute-start | bytes 786440 | tf_op jit(solution)/shard_map/ppermute | solution.py:130
  49.8 13.5 %collective-permute-start.9 = (bf16[128,1024]{1,0:T(8,128)(2,1)S(1)}, bf16[128,1024]{1,0:T(8,128)(2,1)S(1)}, u32[]{:S(2)}, u32[]{:S(2)}) collective-permute-start(bf16[128,1024]{1,0:T(8,128)(2,1)S(1)} %fusion.24), channel_id=1, source_target_pairs={{0,12},{4,0},{8,4},{12,8},{1,13},{5,1},{9,5},{13,9},{2,14},{6,2},{... | collective-permute-start | bytes 786440 | tf_op jit(solution)/shard_map/ppermute | solution.py:130
  51.8 11.5 %copy-start.1 = (f32[32,32,1024]{2,1,0:T(8,128)S(1)}, f32[32,32,1024]{2,1,0:T(8,128)}, u32[]{:S(2)}) copy-start(f32[32,32,1024]{2,1,0:T(8,128)} %param.7) | copy-start | bytes 12582916

commit v14 on v11

--- a/solution.py
+++ b/solution.py
@@ -22,6 +22,12 @@
     moving = (target[:, :, None] == columns[None, None, :]).astype(jnp.float32)
     shifted = jnp.einsum("bsj,bjl->bsl", picked, moving, precision=lax.Precision.HIGHEST)
     return shifted.astype(jnp.bfloat16)
+
+
+def spread(band, rows):
+    eye = jnp.eye(rows, dtype=band.dtype)
+    outer, inner = band.shape
+    return (band[:, None, :, None] * eye[None, :, None, :]).reshape(outer * rows, inner * rows)
 
 
 def banded_matrix(along):
@@ -113,18 +119,17 @@
         sent = far_z[(k - 1) * piece : k * piece]
         got = lax.ppermute(sent, "zq", [(j, (j + k) % group) for j in range(group)])
         fwd_z = fwd_z + got.astype(jnp.float32)
-    observed = slices_z.reshape(piece, rows_here * width).astype(jnp.float32)
-    resid_z = (observed - fwd_z).astype(jnp.bfloat16)
+    fwd_z = fwd_z.reshape(slices_z.shape)
+    resid_z = (slices_z.astype(jnp.float32) - fwd_z).astype(jnp.bfloat16)
     pieces = [resid_z]
     rows = [own_rows]
     for k in range(1, group):
         pieces.append(lax.ppermute(resid_z, "zq", [(j, (j + k) % group) for j in range(group)]))
         src = (zq - k + group) % group
         rows.append(lax.dynamic_slice_in_dim(band_z, src * piece, piece, 0))
-    corr_z = lax.dot_general(
-        jnp.concatenate(rows, 0),
-        jnp.concatenate(pieces, 0),
-        (((0,), (0,)), ((), ())),
+    corr_z = jnp.dot(
+        spread(jnp.concatenate(rows, 0).T, rows_here),
+        jnp.concatenate(pieces, 0).reshape(SLICES * rows_here, width),
         preferred_element_type=jnp.float32,
     ).reshape(planes, rows_here, width)
 

time: 57 us -> 62.9 us (1.10)
  waiting for transfers between devices: 10.3 us -> 16.7 us
  local copies, waits for them, and re-layouts: 12 us -> 7.49 us
  starting transfers between devices: 13.6 us -> 16 us
  matrix products: 14.9 us -> 17.2 us
    unnamed x19 -> x11, local copies, waits for them, and re-layouts: 7.16 us -> 2.54 us
    dot_general x1, matrix products: 0.78 us -> 4.69 us  [shards(): jnp.dot(spread(jnp.concatenate(rows, 0).T, rows_here), jnp.concatenate(pi...]
    dot_general x1, matrix products: 4.25 us -> 0.89 us  [shards(): jnp.einsum('sl,zsx->zlx', band_y, resid_y, preferred_element_type=jnp.flo...]
    ppermute x3, starting transfers between devices: 2.68 us -> 5.8 us  [shards(): got = lax.ppermute(sent, 'zq', [(j, (j + k) % group) for j in range(group)])]
    ppermute x2, waiting for transfers between devices: 1.01 us -> 3.81 us  [double(): other = lax.ppermute(values, axis, [(0, 1), (1, 0)])]
    ppermute x1, waiting for transfers between devices: 0.01 us -> 1.83 us  [halve(): got = lax.ppermute(give.astype(jnp.bfloat16), axis, [(0, 1), (1, 0)])]
    ppermute x1, starting transfers between devices: 3.29 us -> 1.61 us  [shards(): lax.ppermute(give_y, 'co', [(0, 1), (1, 0)]).astype(jnp.float32)]
    ppermute x3, waiting for transfers between devices: 9.3 us -> 10.5 us  [shards(): lax.ppermute(resid_z, 'zq', [(j, (j + k) % group) for j in range(group)])]
  transfers between devices with their start and end apart: 10 -> 10, of which waited for: 3 -> 5; matrix products, arithmetic and copies ran while one was open for 40% -> 22% of each run, Pallas kernels for 0% -> 0%
where the time goes in v14:
time: 62.9 us; the launch traced here: 62.5 us
  matrix products  17.2 us (27%)
  waiting for transfers between devices  16.7 us (27%)
  starting transfers between devices  16 us (25%)
  local copies, waits for them, and re-layouts  7.49 us (12%)
  other arithmetic  5.03 us (8%)
    ppermute x3, waiting for transfers between devices, shards(): lax.ppermute(resid_z, 'zq', [(j, (j + k) % group) for j in range(group)])  10.5 us
    ppermute x3, starting transfers between devices, shards(): got = lax.ppermute(sent, 'zq', [(j, (j + k) % group) for j in range(group)])  5.8 us
    dot_general x1, matrix products, shards(): jnp.dot(spread(jnp.concatenate(rows, 0).T, rows_here), jnp.concatenate(pi...  4.69 us
    ppermute x2, waiting for transfers between devices, double(): other = lax.ppermute(values, axis, [(0, 1), (1, 0)])  3.81 us
    ppermute x3, starting transfers between devices, shards(): lax.ppermute(resid_z, 'zq', [(j, (j + k) % group) for j in range(group)])  3.59 us
    ppermute x2, starting transfers between devices, double(): other = lax.ppermute(values, axis, [(0, 1), (1, 0)])  3.4 us
    dot_general x1, matrix products, shards(): lax.dot_general(flat_coarse, banded_x, (((1,), (1,)), ((), ())), preferre...  2.59 us
    unnamed x11, local copies, waits for them, and re-layouts  2.54 us
  transfers between devices with their start and end apart: 10, of which 5 were waited for; matrix products, arithmetic and copies ran while one was open for 22% of the time, Pallas kernels for 0%

profile of v14, /device:TPU:1, one launch (start us, length us, event | category | flops | bytes accessed | tf_op | source)
XLA Modules:
  0.0 62.5 jit_solution(17381837709954814581)
XLA Ops:
  1.7 1.0 %fusion.12 = bf16[25,16,128]{2,1,0:T(8,128)(2,1)S(1)} fusion(s32[25,128]{1,0:T(8,128)S(1)} %add_select_fusion, f32[25,16,128]{2,0,1:T(8,128)S(1)} %fusion.32), kind=kOutput, calls=%fused_computation.17 | convolution fusion | flops 79104000 | bytes 320000 | tf_op jit(solution)/shard_map/bsj,bjl->bsl/dot_general | solution.py:23
  2.8 2.5 %convert_element_type.74 = bf16[32,32,1024]{2,1,0:T(8,128)(2,1)S(1)} convert(f32[32,32,1024]{2,1,0:T(8,128)} %param.7) | non-fusion elementwise | flops 1048576 | bytes 6291456 | tf_op jit(solution)/shard_map/convert_element_type | solution.py:64
  5.3 2.5 %copy.18 = bf16[4,8,32,1024]{3,1,2,0:T(8,128)(2,1)} copy(bf16[4,8,32,1024]{3,2,1,0:T(8,128)(2,1)S(1)} %bitcast.72) | data formatting | bytes 4194304
  7.9 2.0 %convolution_convert_fusion = bf16[12,32768]{1,0:T(8,128)(2,1)S(1)} fusion(bf16[32,32768]{1,0:T(8,128)(2,1)} %bitcast.74, bf16[4,32]{1,0:T(4,128)(2,1)S(1)} %get-tuple-element.15, bf16[4,32]{1,0:T(4,128)(2,1)S(1)} %get-tuple-element.14, bf16[4,32]{1,0:T(4,128)(2,1)S(1)} %get-tuple-element.13), kind=kOutput, calls=%fused_computation | convolution fusion | flops 25561344 | bytes 2884352 | tf_op jit(solution)/shard_map/dot_general | solution.py:117
  9.9 1.1 %fusion.60 = (bf16[4,32768]{1,0:T(4,128)(2,1)}, bf16[4,32768]{1,0:T(4,128)(2,1)}, bf16[4,32768]{1,0:T(4,128)(2,1)}) fusion(bf16[12,32768]{1,0:T(8,128)(2,1)S(1)} %convolution_convert_fusion), kind=kLoop, calls=%fused_computation.86 | loop fusion | bytes 1572864 | tf_op jit(solution)/shard_map/slice | solution.py:119
  11.0 2.1 %collective-permute-start.4 = (bf16[4,32768]{1,0:T(4,128)(2,1)}, bf16[4,32768]{1,0:T(4,128)(2,1)}, u32[]{:S(2)}, u32[]{:S(2)}) collective-permute-start(bf16[4,32768]{1,0:T(4,128)(2,1)} %get-tuple-element.5), channel_id=1, source_target_pairs={{0,4},{4,8},{8,12},{12,0},{1,5},{5,9},{9,13},{13,1},{2,6},{6,10},{... | collective-permute-start | bytes 786440 | tf_op jit(solution)/shard_map/ppermute | solution.py:120
  13.1 2.6 %collective-permute-start.5 = (bf16[4,32768]{1,0:T(4,128)(2,1)}, bf16[4,32768]{1,0:T(4,128)(2,1)}, u32[]{:S(2)}, u32[]{:S(2)}) collective-permute-start(bf16[4,32768]{1,0:T(4,128)(2,1)} %get-tuple-element.7), channel_id=1, source_target_pairs={{0,8},{4,12},{8,0},{12,4},{1,9},{5,13},{9,1},{13,5},{2,10},{6,14},... | collective-permute-start | bytes 786440 | tf_op jit(solution)/shard_map/ppermute | solution.py:120
  15.7 1.1 %collective-permute-start.6 = (bf16[4,32768]{1,0:T(4,128)(2,1)}, bf16[4,32768]{1,0:T(4,128)(2,1)}, u32[]{:S(2)}, u32[]{:S(2)}) collective-permute-start(bf16[4,32768]{1,0:T(4,128)(2,1)} %get-tuple-element.6), channel_id=1, source_target_pairs={{0,12},{4,0},{8,4},{12,8},{1,13},{5,1},{9,5},{13,9},{2,14},{6,2},{... | collective-permute-start | bytes 786440 | tf_op jit(solution)/shard_map/ppermute | solution.py:120
  17.1 1.6 %collective-permute-start = (bf16[16,16,1024]{2,1,0:T(8,128)(2,1)S(1)}, bf16[16,16,1024]{2,1,0:T(8,128)(2,1)}, u32[]{:S(2)}, u32[]{:S(2)}) collective-permute-start(bf16[16,16,1024]{2,1,0:T(8,128)(2,1)S(1)} %fusion.10), channel_id=1, source_target_pairs={{0,1},{1,0},{2,3},{3,2},{4,5},{5,4},{6,7},{7,6},{8,9},{9,8},{10,11... | collective-permute-start | bytes 1572872 | tf_op jit(solution)/shard_map/ppermute | solution.py:95
  20.4 1.4 %convert_add_fusion = f32[16,16,1024]{2,1,0:T(8,128)S(1)} fusion(bf16[16,16,1024]{2,1,0:T(8,128)(2,1)} %collective-permute-done, bf16[32,32,1024]{2,1,0:T(8,128)(2,1)S(1)} %convert_element_type.74, s32[]{:T(128)S(6)} %select_n.111, bf16[1,16,128]{2,1,0:T(8,128)(2,1)S(1)} %slice.25, s32[]{:T(128)S(6)} %select_n.112), kind=kOutput, calls=%fused_computation.29 | convolution fusion | flops 17301504 | bytes 2625544 | tf_op jit(solution)/shard_map/sl,zlx->zsx/dot_general | solution.py:83
  22.5 1.6 %collective-permute-start.1 = (bf16[8,16,1024]{2,1,0:T(8,128)(2,1)}, bf16[8,16,1024]{2,1,0:T(8,128)(2,1)}, u32[]{:S(2)}, u32[]{:S(2)}) collective-permute-start(bf16[8,16,1024]{2,1,0:T(8,128)(2,1)} %dynamic-slice_convert_fusion), channel_id=1, source_target_pairs={{0,2},{2,0},{1,3},{3,1},{4,6},{6,4},{5,7},{7,5},{8,10},{10,8},{9,1... | collective-permute-start | bytes 786440 | tf_op jit(solution)/shard_map/ppermute | solution.py:45
  24.2 2.6 %fusion.11 = bf16[1024,128]{0,1:T(8,128)(2,1)} fusion(f32[1024,128]{0,1:T(8,128)} %copy.11, bf16[1024,1024]{1,0:T(8,128)(2,1)S(1)} %bitcast.73, bf16[16,8,8,128]{3,2,1,0:T(8,128)(2,1)S(1)} %bitcast.76), kind=kOutput, calls=%fused_computation.16 | convolution fusion | flops 268697600 | bytes 3145728 | tf_op jit(solution)/shard_map/dot_general | solution.py:68
  27.7 1.1 %copy.12 = bf16[1024,128]{1,0:T(8,128)(2,1)S(1)} copy(bf16[1024,128]{0,1:T(8,128)(2,1)} %fusion.11) | data formatting | bytes 524288 | tf_op jit(solution)/shard_map/convert_element_type | solution.py:73
  28.8 1.8 %collective-permute-done.1 = bf16[8,16,1024]{2,1,0:T(8,128)(2,1)} collective-permute-done((bf16[8,16,1024]{2,1,0:T(8,128)(2,1)}, bf16[8,16,1024]{2,1,0:T(8,128)(2,1)}, u32[]{:S(2)}, u32[]{:S(2)}) %collective-permute-start.1) | collective-permute-done | bytes 262176 | tf_op jit(solution)/shard_map/ppermute | solution.py:45
  30.7 1.1 %subtract_convert_fusion = bf16[8,16,1024]{2,1,0:T(8,128)(2,1)S(1)} fusion(bf16[8,16,1024]{2,1,0:T(8,128)(2,1)} %collective-permute-done.1, f32[16,16,1024]{2,1,0:T(8,128)S(1)} %convert_add_fusion, s32[]{:T(128)S(6)} %select_n.114, bf16[32,16,1024]{2,1,0:T(8,128)(2,1)} %param.9, s32[]{:T(128)S(6)} %select_n.110), kind=kLoop, calls=%fused_computation.37 | loop fusion | flops 655360 | bytes 1310728 | tf_op jit(solution)/shard_map/convert_element_type | solution.py:99
  31.8 1.4 %collective-permute-start.2 = (bf16[8,16,1024]{2,1,0:T(8,128)(2,1)S(1)}, bf16[8,16,1024]{2,1,0:T(8,128)(2,1)S(1)}, u32[]{:S(2)}, u32[]{:S(2)}) collective-permute-start(bf16[8,16,1024]{2,1,0:T(8,128)(2,1)S(1)} %subtract_convert_fusion), channel_id=1, source_target_pairs={{0,2},{2,0},{1,3},{3,1},{4,6},{6,4},{5,7},{7,5},{8,10},{10,8},{9,1... | collective-permute-start | bytes 786440 | tf_op jit(solution)/shard_map/ppermute | solution.py:50
  33.2 1.7 %fusion.61 = f32[32,32,1024]{2,1,0:T(8,128)S(1)} fusion(bf16[32,32,128]{2,1,0:T(8,128)(2,1)S(1)} %bitcast.77, bf16[128,1024,1]{1,0,2:T(8,128)(2,1)} %reshape.107), kind=kOutput, calls=%fused_computation.87 | convolution fusion | flops 268435456 | bytes 4718592 | tf_op jit(solution)/shard_map/dot_general | solution.py:74
  34.9 3.8 %collective-permute-done.2 = bf16[8,16,1024]{2,1,0:T(8,128)(2,1)S(1)} collective-permute-done((bf16[8,16,1024]{2,1,0:T(8,128)(2,1)S(1)}, bf16[8,16,1024]{2,1,0:T(8,128)(2,1)S(1)}, u32[]{:S(2)}, u32[]{:S(2)}) %collective-permute-start.2) | collective-permute-done | bytes 262176 | tf_op jit(solution)/shard_map/ppermute | solution.py:50
  38.8 2.0 %collective-permute-start.3 = (bf16[16,16,1024]{2,1,0:T(8,128)(2,1)S(1)}, bf16[16,16,1024]{2,1,0:T(8,128)(2,1)S(1)}, u32[]{:S(2)}, u32[]{:S(2)}) collective-permute-start(bf16[16,16,1024]{2,1,0:T(8,128)(2,1)S(1)} %pad_maximum_fusion), channel_id=1, source_target_pairs={{0,1},{1,0},{2,3},{3,2},{4,5},{5,4},{6,7},{7,6},{8,9},{9,8},{10,11... | collective-permute-start | bytes 1572872 | tf_op jit(solution)/shard_map/ppermute | solution.py:50
  40.8 1.6 %convert_add_fusion.1 = f32[4,32768]{1,0:T(4,128)S(1)} fusion(bf16[4,32768]{1,0:T(4,128)(2,1)} %collective-permute-done.6, bf16[4,32768]{1,0:T(4,128)(2,1)} %collective-permute-done.5, bf16[4,32768]{1,0:T(4,128)(2,1)} %collective-permute-done.4, bf16[4,32]{1,0:T(4,128)(2,1)S(1)} %get-tuple-element.12, bf16[32,32768]{1,0:T(8,128)(2,1)S(1)} %bitcast.75), kind=kOutput, calls=%fused_computation.36 | convolution fusion | flops 9175040 | bytes 3408128 | tf_op jit(solution)/shard_map/dot_general | solution.py:112
  43.2 1.3 %collective-permute-start.8 = (bf16[4,32,1024]{2,1,0:T(8,128)(2,1)S(1)}, bf16[4,32,1024]{2,1,0:T(8,128)(2,1)S(1)}, u32[]{:S(2)}, u32[]{:S(2)}) collective-permute-start(bf16[4,32,1024]{2,1,0:T(8,128)(2,1)S(1)} %fusion.28), channel_id=1, source_target_pairs={{0,8},{4,12},{8,0},{12,4},{1,9},{5,13},{9,1},{13,5},{2,10},{6,14},... | collective-permute-start | bytes 786440 | tf_op jit(solution)/shard_map/ppermute | solution.py:127
  44.5 1.8 %collective-permute-start.9 = (bf16[4,32,1024]{2,1,0:T(8,128)(2,1)S(1)}, bf16[4,32,1024]{2,1,0:T(8,128)(2,1)S(1)}, u32[]{:S(2)}, u32[]{:S(2)}) collective-permute-start(bf16[4,32,1024]{2,1,0:T(8,128)(2,1)S(1)} %fusion.28), channel_id=1, source_target_pairs={{0,12},{4,0},{8,4},{12,8},{1,13},{5,1},{9,5},{13,9},{2,14},{6,2},{... | collective-permute-start | bytes 786440 | tf_op jit(solution)/shard_map/ppermute | solution.py:127
  47.3 10.2 %collective-permute-done.7 = bf16[4,32,1024]{2,1,0:T(8,128)(2,1)S(1)} collective-permute-done((bf16[4,32,1024]{2,1,0:T(8,128)(2,1)S(1)}, bf16[4,32,1024]{2,1,0:T(8,128)(2,1)S(1)}, u32[]{:S(2)}, u32[]{:S(2)}) %collective-permute-start.7) | collective-permute-done | bytes 262176 | tf_op jit(solution)/shard_map/ppermute | solution.py:127
  57.8 4.7 %fusion.1 = f32[32,32,1024]{2,1,0:T(8,128)} fusion(f32[32,32,1024]{2,1,0:T(8,128)S(1)} %copy-done.2, f32[32,32,1024]{2,1,0:T(8,128)S(1)} %fusion.61, f32[32,1024,32]{1,2,0:T(8,128)S(1)} %fusion.13, bf16[32,32]{1,0:T(8,128)(2,1)S(1)} %fusion.40, bf16[32,16]{1,0:T(8,128)(2,1)S(1)} %copy.13, bf16[4,32,1024]{2,1,0:T(8,128)(2,1)S(1)} %collective-permute-done.9, ...), kind=kOutput, calls=%fused_computation.3 | convolution fusion | flops 1080033280 | bytes 17828864 | tf_op jit(solution)/shard_map/dot_general | solution.py:130
  (39 shorter events, 7.7 us)
Async XLA Ops:
  0.0 0.8 %copy-start = (f32[4,16,128]{2,1,0:T(8,128)S(1)}, f32[4,16,128]{2,1,0:T(8,128)}, u32[]{:S(2)}) copy-start(f32[4,16,128]{2,1,0:T(8,128)} %param.11) | copy-start | bytes 98308
  7.8 10.9 %copy-start.3 = (bf16[32,32,128]{2,1,0:T(8,128)(2,1)S(1)}, bf16[32,32,128]{2,1,0:T(8,128)(2,1)}, u32[]{:S(2)}) copy-start(bf16[32,32,128]{2,1,0:T(8,128)(2,1)} %param.8) | copy-start | bytes 786436
  11.0 29.8 %collective-permute-start.4 = (bf16[4,32768]{1,0:T(4,128)(2,1)}, bf16[4,32768]{1,0:T(4,128)(2,1)}, u32[]{:S(2)}, u32[]{:S(2)}) collective-permute-start(bf16[4,32768]{1,0:T(4,128)(2,1)} %get-tuple-element.5), channel_id=1, source_target_pairs={{0,4},{4,8},{8,12},{12,0},{1,5},{5,9},{9,13},{13,1},{2,6},{6,10},{... | collective-permute-start | bytes 786440 | tf_op jit(solution)/shard_map/ppermute | solution.py:120
  13.1 27.7 %collective-permute-start.5 = (bf16[4,32768]{1,0:T(4,128)(2,1)}, bf16[4,32768]{1,0:T(4,128)(2,1)}, u32[]{:S(2)}, u32[]{:S(2)}) collective-permute-start(bf16[4,32768]{1,0:T(4,128)(2,1)} %get-tuple-element.7), channel_id=1, source_target_pairs={{0,8},{4,12},{8,0},{12,4},{1,9},{5,13},{9,1},{13,5},{2,10},{6,14},... | collective-permute-start | bytes 786440 | tf_op jit(solution)/shard_map/ppermute | solution.py:120
  15.7 25.1 %collective-permute-start.6 = (bf16[4,32768]{1,0:T(4,128)(2,1)}, bf16[4,32768]{1,0:T(4,128)(2,1)}, u32[]{:S(2)}, u32[]{:S(2)}) collective-permute-start(bf16[4,32768]{1,0:T(4,128)(2,1)} %get-tuple-element.6), channel_id=1, source_target_pairs={{0,12},{4,0},{8,4},{12,8},{1,13},{5,1},{9,5},{13,9},{2,14},{6,2},{... | collective-permute-start | bytes 786440 | tf_op jit(solution)/shard_map/ppermute | solution.py:120
  17.1 3.3 %collective-permute-start = (bf16[16,16,1024]{2,1,0:T(8,128)(2,1)S(1)}, bf16[16,16,1024]{2,1,0:T(8,128)(2,1)}, u32[]{:S(2)}, u32[]{:S(2)}) collective-permute-start(bf16[16,16,1024]{2,1,0:T(8,128)(2,1)S(1)} %fusion.10), channel_id=1, source_target_pairs={{0,1},{1,0},{2,3},{3,2},{4,5},{5,4},{6,7},{7,6},{8,9},{9,8},{10,11... | collective-permute-start | bytes 1572872 | tf_op jit(solution)/shard_map/ppermute | solution.py:95
  22.5 8.1 %collective-permute-start.1 = (bf16[8,16,1024]{2,1,0:T(8,128)(2,1)}, bf16[8,16,1024]{2,1,0:T(8,128)(2,1)}, u32[]{:S(2)}, u32[]{:S(2)}) collective-permute-start(bf16[8,16,1024]{2,1,0:T(8,128)(2,1)} %dynamic-slice_convert_fusion), channel_id=1, source_target_pairs={{0,2},{2,0},{1,3},{3,1},{4,6},{6,4},{5,7},{7,5},{8,10},{10,8},{9,1... | collective-permute-start | bytes 786440 | tf_op jit(solution)/shard_map/ppermute | solution.py:45
  28.8 12.0 %copy-start.1 = (bf16[4,8,32,1024]{3,1,2,0:T(8,128)(2,1)S(1)}, bf16[4,8,32,1024]{3,1,2,0:T(8,128)(2,1)}, u32[]{:S(2)}) copy-start(bf16[4,8,32,1024]{3,1,2,0:T(8,128)(2,1)} %copy.18) | copy-start | bytes 6291460
  31.8 6.9 %collective-permute-start.2 = (bf16[8,16,1024]{2,1,0:T(8,128)(2,1)S(1)}, bf16[8,16,1024]{2,1,0:T(8,128)(2,1)S(1)}, u32[]{:S(2)}, u32[]{:S(2)}) collective-permute-start(bf16[8,16,1024]{2,1,0:T(8,128)(2,1)S(1)} %subtract_convert_fusion), channel_id=1, source_target_pairs={{0,2},{2,0},{1,3},{3,1},{4,6},{6,4},{5,7},{7,5},{8,10},{10,8},{9,1... | collective-permute-start | bytes 786440 | tf_op jit(solution)/shard_map/ppermute | solution.py:50
  33.2 9.2 %copy-start.4 = (bf16[4,32,1024]{2,1,0:T(8,128)(2,1)S(1)}, bf16[4,32,1024]{2,1,0:T(8,128)(2,1)}, u32[]{:S(2)}) copy-start(bf16[4,32,1024]{2,1,0:T(8,128)(2,1)} %param.10) | copy-start | bytes 786436
  38.8 7.5 %collective-permute-start.3 = (bf16[16,16,1024]{2,1,0:T(8,128)(2,1)S(1)}, bf16[16,16,1024]{2,1,0:T(8,128)(2,1)S(1)}, u32[]{:S(2)}, u32[]{:S(2)}) collective-permute-start(bf16[16,16,1024]{2,1,0:T(8,128)(2,1)S(1)} %pad_maximum_fusion), channel_id=1, source_target_pairs={{0,1},{1,0},{2,3},{3,2},{4,5},{5,4},{6,7},{7,6},{8,9},{9,8},{10,11... | collective-permute-start | bytes 1572872 | tf_op jit(solution)/shard_map/ppermute | solution.py:50
  42.4 15.4 %copy-start.2 = (f32[32,32,1024]{2,1,0:T(8,128)S(1)}, f32[32,32,1024]{2,1,0:T(8,128)}, u32[]{:S(2)}) copy-start(f32[32,32,1024]{2,1,0:T(8,128)} %param.7) | copy-start | bytes 12582916
  42.7 14.7 %collective-permute-start.7 = (bf16[4,32,1024]{2,1,0:T(8,128)(2,1)S(1)}, bf16[4,32,1024]{2,1,0:T(8,128)(2,1)S(1)}, u32[]{:S(2)}, u32[]{:S(2)}) collective-permute-start(bf16[4,32,1024]{2,1,0:T(8,128)(2,1)S(1)} %fusion.28), channel_id=1, source_target_pairs={{0,4},{4,8},{8,12},{12,0},{1,5},{5,9},{9,13},{13,1},{2,6},{6,10},{... | collective-permute-start | bytes 786440 | tf_op jit(solution)/shard_map/ppermute | solution.py:127
  43.2 14.3 %collective-permute-start.8 = (bf16[4,32,1024]{2,1,0:T(8,128)(2,1)S(1)}, bf16[4,32,1024]{2,1,0:T(8,128)(2,1)S(1)}, u32[]{:S(2)}, u32[]{:S(2)}) collective-permute-start(bf16[4,32,1024]{2,1,0:T(8,128)(2,1)S(1)} %fusion.28), channel_id=1, source_target_pairs={{0,8},{4,12},{8,0},{12,4},{1,9},{5,13},{9,1},{13,5},{2,10},{6,14},... | collective-permute-start | bytes 786440 | tf_op jit(solution)/shard_map/ppermute | solution.py:127
  44.5 13.3 %collective-permute-start.9 = (bf16[4,32,1024]{2,1,0:T(8,128)(2,1)S(1)}, bf16[4,32,1024]{2,1,0:T(8,128)(2,1)S(1)}, u32[]{:S(2)}, u32[]{:S(2)}) collective-permute-start(bf16[4,32,1024]{2,1,0:T(8,128)(2,1)S(1)} %fusion.28), channel_id=1, source_target_pairs={{0,12},{4,0},{8,4},{12,8},{1,13},{5,1},{9,5},{13,9},{2,14},{6,2},{... | collective-permute-start | bytes 786440 | tf_op jit(solution)/shard_map/ppermute | solution.py:127

commit v15 on v11

--- a/solution.py
+++ b/solution.py
@@ -104,13 +104,15 @@
     sheet = coarse.reshape(planes, rows_here * width)
     own_rows = lax.dynamic_slice_in_dim(band_z, zq * piece, piece, 0)
     fwd_z = jnp.dot(own_rows, sheet, preferred_element_type=jnp.float32)
-    far_rows = jnp.concatenate(
+    far_rows = jnp.stack(
         [lax.dynamic_slice_in_dim(band_z, ((zq + k) % group) * piece, piece, 0) for k in range(1, group)],
         0,
     )
-    far_z = jnp.dot(far_rows, sheet, preferred_element_type=jnp.float32).astype(jnp.bfloat16)
+    far_z = jnp.einsum(
+        "ksl,lp->ksp", far_rows, sheet, preferred_element_type=jnp.float32
+    ).astype(jnp.bfloat16)
     for k in range(1, group):
-        sent = far_z[(k - 1) * piece : k * piece]
+        sent = far_z[k - 1]
         got = lax.ppermute(sent, "zq", [(j, (j + k) % group) for j in range(group)])
         fwd_z = fwd_z + got.astype(jnp.float32)
     observed = slices_z.reshape(piece, rows_here * width).astype(jnp.float32)

time: 57 us -> 59.4 us (1.042)
  local copies, waits for them, and re-layouts: 12 us -> 14.3 us
  matrix products: 14.9 us -> 15.6 us
    reshape x0 -> x1, local copies, waits for them, and re-layouts: none -> 2.33 us  [shards(): sheet = coarse.reshape(planes, rows_here * width)]
    squeeze x0 -> x1, local copies, waits for them, and re-layouts: none -> 1.07 us  [shards(): sent = far_z[k - 1]]
    slice x1 -> x0, local copies, waits for them, and re-layouts: 1.03 us -> none  [shards(): sent = far_z[(k - 1) * piece:k * piece]]
    ppermute x2, starting transfers between devices: 2.94 us -> 2.25 us  [double(): other = lax.ppermute(values, axis, [(0, 1), (1, 0)])]
    ppermute x3, starting transfers between devices: 3.06 us -> 3.71 us  [shards(): lax.ppermute(resid_z, 'zq', [(j, (j + k) % group) for j in range(group)])]
    dot_general x1, matrix products: 1.85 us -> 2.48 us  [shards(): fwd_z = jnp.dot(own_rows, sheet, preferred_element_type=jnp.float32)]
    ppermute x2, waiting for transfers between devices: 1.01 us -> 0.4 us  [double(): other = lax.ppermute(values, axis, [(0, 1), (1, 0)])]
    unnamed x19 -> x17, local copies, waits for them, and re-layouts: 7.16 us -> 7.17 us
  transfers between devices with their start and end apart: 10 -> 10, of which waited for: 3 -> 3; matrix products, arithmetic and copies ran while one was open for 40% -> 43% of each run, Pallas kernels for 0% -> 0%
where the time goes in v15:
time: 59.4 us; the launch traced here: 59.1 us
  matrix products  15.6 us (26%)
  local copies, waits for them, and re-layouts  14.3 us (24%)
  starting transfers between devices  13.5 us (23%)
  waiting for transfers between devices  9.75 us (16%)
  other arithmetic  5.58 us (9%)
    ppermute x3, waiting for transfers between devices, shards(): lax.ppermute(resid_z, 'zq', [(j, (j + k) % group) for j in range(group)])  9.33 us
    unnamed x17, local copies, waits for them, and re-layouts  7.17 us
    dot_general x1, matrix products, shards(): jnp.einsum('sl,zsx->zlx', band_y, resid_y, preferred_element_type=jnp.flo...  4.23 us
    ppermute x3, starting transfers between devices, shards(): lax.ppermute(resid_z, 'zq', [(j, (j + k) % group) for j in range(group)])  3.71 us
    ppermute x1, starting transfers between devices, shards(): lax.ppermute(give_y, 'co', [(0, 1), (1, 0)]).astype(jnp.float32)  3.29 us
    ppermute x3, starting transfers between devices, shards(): got = lax.ppermute(sent, 'zq', [(j, (j + k) % group) for j in range(group)])  2.68 us
    convert_element_type x1, other arithmetic, shards(): coarse = volume.astype(jnp.bfloat16)  2.56 us
    dot_general x1, matrix products, shards(): fwd_z = jnp.dot(own_rows, sheet, preferred_element_type=jnp.float32)  2.48 us
  transfers between devices with their start and end apart: 10, of which 3 were waited for; matrix products, arithmetic and copies ran while one was open for 43% of the time, Pallas kernels for 0%

profile of v15, /device:TPU:1, one launch (start us, length us, event | category | flops | bytes accessed | tf_op | source)
XLA Modules:
  0.0 59.1 jit_solution(3953438504679633749)
XLA Ops:
  0.8 1.0 %fusion.26 = f32[25,16,128]{2,0,1:T(8,128)S(1)} fusion(f32[4,16,128]{2,1,0:T(8,128)S(1)} %copy-done, s32[25]{0:T(128)} %param.12), kind=kOutput, calls=%fused_computation.46 | convolution fusion | flops 2457700 | bytes 237668 | tf_op jit(solution)/shard_map/bk,ksl->bsl/dot_general | solution.py:19
  1.7 1.0 %fusion.6 = bf16[25,16,128]{2,1,0:T(8,128)(2,1)S(1)} fusion(s32[25,128]{1,0:T(8,128)S(1)} %add_select_fusion, f32[25,16,128]{2,0,1:T(8,128)S(1)} %fusion.26), kind=kOutput, calls=%fused_computation.13 | convolution fusion | flops 79104000 | bytes 320000 | tf_op jit(solution)/shard_map/bsj,bjl->bsl/dot_general | solution.py:23
  2.8 2.6 %convert_element_type.70 = bf16[32,32,1024]{2,1,0:T(8,128)(2,1)S(1)} convert(f32[32,32,1024]{2,1,0:T(8,128)} %param.7) | non-fusion elementwise | flops 1048576 | bytes 6291456 | tf_op jit(solution)/shard_map/convert_element_type | solution.py:58
  5.7 3.3 %collective-permute-start = (bf16[16,16,1024]{2,1,0:T(8,128)(2,1)S(1)}, bf16[16,16,1024]{2,1,0:T(8,128)(2,1)}, u32[]{:S(2)}, u32[]{:S(2)}) collective-permute-start(bf16[16,16,1024]{2,1,0:T(8,128)(2,1)S(1)} %fusion.4), channel_id=1, source_target_pairs={{0,1},{1,0},{2,3},{3,2},{4,5},{5,4},{6,7},{7,6},{8,9},{9,8},{10,11... | collective-permute-start | bytes 1572872 | tf_op jit(solution)/shard_map/ppermute | solution.py:89
  9.0 2.3 %reshape.96 = bf16[32,32768,1]{1,0,2:T(8,128)(2,1)} reshape(bf16[32,32,1024]{2,1,0:T(8,128)(2,1)S(1)} %convert_element_type.70) | data formatting | bytes 4194304 | tf_op jit(solution)/shard_map/reshape | solution.py:104
  11.4 2.1 %convolution_convert_fusion = bf16[3,4,32768]{2,1,0:T(4,128)(2,1)S(1)} fusion(bf16[32,32768,1]{1,0,2:T(8,128)(2,1)} %reshape.96, bf16[1,4,32]{2,1,0:T(4,128)(2,1)S(1)} %get-tuple-element.15, bf16[1,4,32]{2,1,0:T(4,128)(2,1)S(1)} %get-tuple-element.14, bf16[1,4,32]{2,1,0:T(4,128)(2,1)S(1)} %get-tuple-element.13), kind=kOutput, calls=%fused_computation | convolution fusion | flops 25561344 | bytes 2884352 | tf_op jit(solution)/shard_map/ksl,lp->ksp/dot_general | solution.py:111
  13.6 1.1 %slice_bitcast_fusion.2 = (bf16[4,32768]{1,0:T(4,128)(2,1)}, bf16[4,32768]{1,0:T(4,128)(2,1)}, bf16[4,32768]{1,0:T(4,128)(2,1)}) fusion(bf16[3,4,32768]{2,1,0:T(4,128)(2,1)S(1)} %convolution_convert_fusion), kind=kLoop, calls=%fused_computation.40 | loop fusion | bytes 1572864 | tf_op jit(solution)/shard_map/squeeze | solution.py:115
  14.6 2.7 %collective-permute-start.6 = (bf16[4,32768]{1,0:T(4,128)(2,1)}, bf16[4,32768]{1,0:T(4,128)(2,1)}, u32[]{:S(2)}, u32[]{:S(2)}) collective-permute-start(bf16[4,32768]{1,0:T(4,128)(2,1)} %get-tuple-element.8), channel_id=1, source_target_pairs={{0,12},{4,0},{8,4},{12,8},{1,13},{5,1},{9,5},{13,9},{2,14},{6,2},{... | collective-permute-start | bytes 786440 | tf_op jit(solution)/shard_map/ppermute | solution.py:116
  17.4 1.0 %copy.10 = f32[1024,128]{0,1:T(8,128)} copy(f32[1024,128]{1,0:T(8,128)S(1)} %bitcast_convert_fusion) | data formatting | bytes 1048576 | tf_op jit(solution)/shard_map/convert_element_type | solution.py:66
  18.5 1.4 %convert_add_fusion = f32[16,16,1024]{2,1,0:T(8,128)S(1)} fusion(bf16[16,16,1024]{2,1,0:T(8,128)(2,1)} %collective-permute-done, bf16[32,32,1024]{2,1,0:T(8,128)(2,1)S(1)} %convert_element_type.70, s32[]{:T(128)S(6)} %select_n.111, bf16[1,16,128]{2,1,0:T(8,128)(2,1)S(1)} %slice.25, s32[]{:T(128)S(6)} %select_n.112), kind=kOutput, calls=%fused_computation.25 | convolution fusion | flops 17301504 | bytes 2625544 | tf_op jit(solution)/shard_map/sl,zlx->zsx/dot_general | solution.py:77
  20.7 1.6 %collective-permute-start.1 = (bf16[8,16,1024]{2,1,0:T(8,128)(2,1)}, bf16[8,16,1024]{2,1,0:T(8,128)(2,1)}, u32[]{:S(2)}, u32[]{:S(2)}) collective-permute-start(bf16[8,16,1024]{2,1,0:T(8,128)(2,1)} %dynamic-slice_convert_fusion), channel_id=1, source_target_pairs={{0,2},{2,0},{1,3},{3,1},{4,6},{6,4},{5,7},{7,5},{8,10},{10,8},{9,1... | collective-permute-start | bytes 786440 | tf_op jit(solution)/shard_map/ppermute | solution.py:39
  22.3 1.5 %fusion.5 = bf16[1024,128]{0,1:T(8,128)(2,1)} fusion(f32[1024,128]{0,1:T(8,128)S(1)} %copy-done.2, bf16[1024,1024]{1,0:T(8,128)(2,1)S(1)} %bitcast.68, bf16[16,8,8,128]{3,2,1,0:T(8,128)(2,1)S(1)} %bitcast.71), kind=kOutput, calls=%fused_computation.12 | convolution fusion | flops 268697600 | bytes 3145728 | tf_op jit(solution)/shard_map/dot_general | solution.py:62
  25.5 2.2 %copy.15 = f32[1,4,32,1024]{3,1,2,0:T(4,128)} copy(f32[1,4,32,1024]{3,2,1,0:T(8,128)} %convert_bitcast_fusion) | data formatting | bytes 1048576
  27.7 1.1 %copy.11 = bf16[1024,128]{1,0:T(8,128)(2,1)S(1)} copy(bf16[1024,128]{0,1:T(8,128)(2,1)} %fusion.5) | data formatting | bytes 524288 | tf_op jit(solution)/shard_map/convert_element_type | solution.py:67
  28.8 2.5 %copy.16 = bf16[4,8,32,1024]{3,1,2,0:T(8,128)(2,1)} copy(bf16[4,8,32,1024]{3,2,1,0:T(8,128)(2,1)S(1)} %bitcast.69) | data formatting | bytes 4194304
  31.3 1.1 %subtract_convert_fusion.1 = bf16[8,16,1024]{2,1,0:T(8,128)(2,1)S(1)} fusion(bf16[8,16,1024]{2,1,0:T(8,128)(2,1)} %collective-permute-done.1, f32[16,16,1024]{2,1,0:T(8,128)S(1)} %convert_add_fusion, s32[]{:T(128)S(6)} %select_n.114, bf16[32,16,1024]{2,1,0:T(8,128)(2,1)} %param.9, s32[]{:T(128)S(6)} %select_n.110), kind=kLoop, calls=%fused_computation.32 | loop fusion | flops 655360 | bytes 1310728 | tf_op jit(solution)/shard_map/convert_element_type | solution.py:93
  32.6 2.5 %subtract_convert_fusion = bf16[4,32768]{1,0:T(4,128)(2,1)S(1)} fusion(f32[4,32768]{1,0:T(4,128)} %bitcast.74, bf16[4,32768]{1,0:T(4,128)(2,1)} %collective-permute-done.6, bf16[4,32768]{1,0:T(4,128)(2,1)} %collective-permute-done.5, bf16[4,32768]{1,0:T(4,128)(2,1)} %collective-permute-done.4, bf16[4,32]{1,0:T(4,128)(2,1)S(1)} %get-tuple-element.12, ...), kind=kOutput, calls=%fused_computation.31 | convolution fusion | flops 9437184 | bytes 3670272 | tf_op jit(solution)/shard_map/dot_general | solution.py:106
  35.1 1.1 %collective-permute-start.9 = (bf16[4,32768]{1,0:T(4,128)(2,1)S(1)}, bf16[4,32768]{1,0:T(4,128)(2,1)S(1)}, u32[]{:S(2)}, u32[]{:S(2)}) collective-permute-start(bf16[4,32768]{1,0:T(4,128)(2,1)S(1)} %subtract_convert_fusion), channel_id=1, source_target_pairs={{0,12},{4,0},{8,4},{12,8},{1,13},{5,1},{9,5},{13,9},{2,14},{6,2},{... | collective-permute-start | bytes 786440 | tf_op jit(solution)/shard_map/ppermute | solution.py:123
  36.2 1.9 %collective-permute-start.8 = (bf16[4,32768]{1,0:T(4,128)(2,1)S(1)}, bf16[4,32768]{1,0:T(4,128)(2,1)S(1)}, u32[]{:S(2)}, u32[]{:S(2)}) collective-permute-start(bf16[4,32768]{1,0:T(4,128)(2,1)S(1)} %subtract_convert_fusion), channel_id=1, source_target_pairs={{0,8},{4,12},{8,0},{12,4},{1,9},{5,13},{9,1},{13,5},{2,10},{6,14},... | collective-permute-start | bytes 786440 | tf_op jit(solution)/shard_map/ppermute | solution.py:123
  39.3 2.2 %collective-permute-start.3 = (bf16[16,16,1024]{2,1,0:T(8,128)(2,1)S(1)}, bf16[16,16,1024]{2,1,0:T(8,128)(2,1)S(1)}, u32[]{:S(2)}, u32[]{:S(2)}) collective-permute-start(bf16[16,16,1024]{2,1,0:T(8,128)(2,1)S(1)} %pad_maximum_fusion), channel_id=1, source_target_pairs={{0,1},{1,0},{2,3},{3,2},{4,5},{5,4},{6,7},{7,6},{8,9},{9,8},{10,11... | collective-permute-start | bytes 1572872 | tf_op jit(solution)/shard_map/ppermute | solution.py:44
  42.2 1.9 %collective-permute-done.8 = bf16[4,32768]{1,0:T(4,128)(2,1)S(1)} collective-permute-done((bf16[4,32768]{1,0:T(4,128)(2,1)S(1)}, bf16[4,32768]{1,0:T(4,128)(2,1)S(1)}, u32[]{:S(2)}, u32[]{:S(2)}) %collective-permute-start.8) | collective-permute-done | bytes 262176 | tf_op jit(solution)/shard_map/ppermute | solution.py:123
  44.1 7.4 %collective-permute-done.7 = bf16[4,32768]{1,0:T(4,128)(2,1)S(1)} collective-permute-done((bf16[4,32768]{1,0:T(4,128)(2,1)S(1)}, bf16[4,32768]{1,0:T(4,128)(2,1)S(1)}, u32[]{:S(2)}, u32[]{:S(2)}) %collective-permute-start.7) | collective-permute-done | bytes 262176 | tf_op jit(solution)/shard_map/ppermute | solution.py:123
  52.3 2.4 %copy.17 = f32[4,8,32,1024]{3,2,1,0:T(8,128)S(1)} copy(f32[4,8,32,1024]{3,1,2,0:T(8,128)S(1)} %bitcast.70) | data formatting | bytes 8388608
  54.8 4.2 %fusion.1 = f32[32,32,1024]{2,1,0:T(8,128)} fusion(f32[32,32,1024]{2,1,0:T(8,128)S(1)} %copy-done.1, f32[4,8,32,1024]{3,2,1,0:T(8,128)S(1)} %copy.17, f32[32,32,1024]{2,1,0:T(8,128)S(1)} %fusion.60, bf16[16,16,1024]{2,1,0:T(8,128)(2,1)S(1)} %get-tuple-element.6, bf16[16,16,1024]{2,1,0:T(8,128)(2,1)S(1)} %get-tuple-element.5, ...), kind=kOutput, calls=%fused_computation.3 | convolution fusion | flops 38273024 | bytes 17829892 | tf_op jit(solution)/shard_map/sl,zsx->zlx/dot_general | solution.py:96
  (45 shorter events, 6.7 us)
Async XLA Ops:
  0.0 0.8 %copy-start = (f32[4,16,128]{2,1,0:T(8,128)S(1)}, f32[4,16,128]{2,1,0:T(8,128)}, u32[]{:S(2)}) copy-start(f32[4,16,128]{2,1,0:T(8,128)} %param.11) | copy-start | bytes 98308
  2.8 6.2 %copy-start.6 = (bf16[25,16,128]{2,1,0:T(8,128)(2,1)}, bf16[25,16,128]{2,1,0:T(8,128)(2,1)S(1)}, u32[]{:S(2)}) copy-start(bf16[25,16,128]{2,1,0:T(8,128)(2,1)S(1)} %fusion.6) | copy-start | bytes 307204
  5.7 12.8 %collective-permute-start = (bf16[16,16,1024]{2,1,0:T(8,128)(2,1)S(1)}, bf16[16,16,1024]{2,1,0:T(8,128)(2,1)}, u32[]{:S(2)}, u32[]{:S(2)}) collective-permute-start(bf16[16,16,1024]{2,1,0:T(8,128)(2,1)S(1)} %fusion.4), channel_id=1, source_target_pairs={{0,1},{1,0},{2,3},{3,2},{4,5},{5,4},{6,7},{7,6},{8,9},{9,8},{10,11... | collective-permute-start | bytes 1572872 | tf_op jit(solution)/shard_map/ppermute | solution.py:89
  9.0 2.3 %slice-start = ((bf16[25,16,128]{2,1,0:T(8,128)(2,1)}), bf16[16,16,128]{2,1,0:T(8,128)(2,1)S(1)}, s32[]{:S(2)}) async-start(bf16[25,16,128]{2,1,0:T(8,128)(2,1)} %copy-done.6), calls=%async_computation | async-start | bytes 131072 | tf_op jit(solution)/shard_map/slice | solution.py:57
  11.4 5.9 %copy-start.4 = (bf16[32,32,128]{2,1,0:T(8,128)(2,1)S(1)}, bf16[32,32,128]{2,1,0:T(8,128)(2,1)}, u32[]{:S(2)}) copy-start(bf16[32,32,128]{2,1,0:T(8,128)(2,1)} %param.8) | copy-start | bytes 786436
  13.6 4.8 %slice-start.1 = ((bf16[25,16,128]{2,1,0:T(8,128)(2,1)}), bf16[8,16,128]{2,1,0:T(8,128)(2,1)S(1)}, s32[]{:S(2)}) async-start(bf16[25,16,128]{2,1,0:T(8,128)(2,1)} %copy-done.6), calls=%async_computation.1 | async-start | bytes 65536 | tf_op jit(solution)/shard_map/slice | solution.py:55
  14.6 17.9 %collective-permute-start.4 = (bf16[4,32768]{1,0:T(4,128)(2,1)}, bf16[4,32768]{1,0:T(4,128)(2,1)}, u32[]{:S(2)}, u32[]{:S(2)}) collective-permute-start(bf16[4,32768]{1,0:T(4,128)(2,1)} %get-tuple-element.7), channel_id=1, source_target_pairs={{0,4},{4,8},{8,12},{12,0},{1,5},{5,9},{9,13},{13,1},{2,6},{6,10},{... | collective-permute-start | bytes 786440 | tf_op jit(solution)/shard_map/ppermute | solution.py:116
  14.6 17.9 %collective-permute-start.6 = (bf16[4,32768]{1,0:T(4,128)(2,1)}, bf16[4,32768]{1,0:T(4,128)(2,1)}, u32[]{:S(2)}, u32[]{:S(2)}) collective-permute-start(bf16[4,32768]{1,0:T(4,128)(2,1)} %get-tuple-element.8), channel_id=1, source_target_pairs={{0,12},{4,0},{8,4},{12,8},{1,13},{5,1},{9,5},{13,9},{2,14},{6,2},{... | collective-permute-start | bytes 786440 | tf_op jit(solution)/shard_map/ppermute | solution.py:116
  17.3 15.3 %collective-permute-start.5 = (bf16[4,32768]{1,0:T(4,128)(2,1)}, bf16[4,32768]{1,0:T(4,128)(2,1)}, u32[]{:S(2)}, u32[]{:S(2)}) collective-permute-start(bf16[4,32768]{1,0:T(4,128)(2,1)} %get-tuple-element.9), channel_id=1, source_target_pairs={{0,8},{4,12},{8,0},{12,4},{1,9},{5,13},{9,1},{13,5},{2,10},{6,14},... | collective-permute-start | bytes 786440 | tf_op jit(solution)/shard_map/ppermute | solution.py:116
  18.4 4.0 %copy-start.2 = (f32[1024,128]{0,1:T(8,128)S(1)}, f32[1024,128]{0,1:T(8,128)}, u32[]{:S(2)}) copy-start(f32[1024,128]{0,1:T(8,128)} %copy.10) | copy-start | bytes 1572868
  19.9 3.9 %copy-start.5 = (bf16[4,32,1024]{2,1,0:T(8,128)(2,1)S(1)}, bf16[4,32,1024]{2,1,0:T(8,128)(2,1)}, u32[]{:S(2)}) copy-start(bf16[4,32,1024]{2,1,0:T(8,128)(2,1)} %param.10) | copy-start | bytes 786436
  20.7 10.6 %collective-permute-start.1 = (bf16[8,16,1024]{2,1,0:T(8,128)(2,1)}, bf16[8,16,1024]{2,1,0:T(8,128)(2,1)}, u32[]{:S(2)}, u32[]{:S(2)}) collective-permute-start(bf16[8,16,1024]{2,1,0:T(8,128)(2,1)} %dynamic-slice_convert_fusion), channel_id=1, source_target_pairs={{0,2},{2,0},{1,3},{3,1},{4,6},{6,4},{5,7},{7,5},{8,10},{10,8},{9,1... | collective-permute-start | bytes 786440 | tf_op jit(solution)/shard_map/ppermute | solution.py:39
  32.5 6.7 %collective-permute-start.2 = (bf16[8,16,1024]{2,1,0:T(8,128)(2,1)S(1)}, bf16[8,16,1024]{2,1,0:T(8,128)(2,1)S(1)}, u32[]{:S(2)}, u32[]{:S(2)}) collective-permute-start(bf16[8,16,1024]{2,1,0:T(8,128)(2,1)S(1)} %subtract_convert_fusion.1), channel_id=1, source_target_pairs={{0,2},{2,0},{1,3},{3,1},{4,6},{6,4},{5,7},{7,5},{8,10},{10,8},{9,1... | collective-permute-start | bytes 786440 | tf_op jit(solution)/shard_map/ppermute | solution.py:44
  32.6 8.9 %copy-start.3 = (bf16[128,1024,1]{1,0,2:T(8,128)(2,1)S(1)}, bf16[128,1024,1]{1,0,2:T(8,128)(2,1)}, u32[]{:S(2)}) copy-start(bf16[128,1024,1]{1,0,2:T(8,128)(2,1)} %reshape.94) | copy-start | bytes 786436
  35.1 7.1 %collective-permute-start.9 = (bf16[4,32768]{1,0:T(4,128)(2,1)S(1)}, bf16[4,32768]{1,0:T(4,128)(2,1)S(1)}, u32[]{:S(2)}, u32[]{:S(2)}) collective-permute-start(bf16[4,32768]{1,0:T(4,128)(2,1)S(1)} %subtract_convert_fusion), channel_id=1, source_target_pairs={{0,12},{4,0},{8,4},{12,8},{1,13},{5,1},{9,5},{13,9},{2,14},{6,2},{... | collective-permute-start | bytes 786440 | tf_op jit(solution)/shard_map/ppermute | solution.py:123
  36.2 7.9 %collective-permute-start.8 = (bf16[4,32768]{1,0:T(4,128)(2,1)S(1)}, bf16[4,32768]{1,0:T(4,128)(2,1)S(1)}, u32[]{:S(2)}, u32[]{:S(2)}) collective-permute-start(bf16[4,32768]{1,0:T(4,128)(2,1)S(1)} %subtract_convert_fusion), channel_id=1, source_target_pairs={{0,8},{4,12},{8,0},{12,4},{1,9},{5,13},{9,1},{13,5},{2,10},{6,14},... | collective-permute-start | bytes 786440 | tf_op jit(solution)/shard_map/ppermute | solution.py:123
  38.0 13.5 %collective-permute-start.7 = (bf16[4,32768]{1,0:T(4,128)(2,1)S(1)}, bf16[4,32768]{1,0:T(4,128)(2,1)S(1)}, u32[]{:S(2)}, u32[]{:S(2)}) collective-permute-start(bf16[4,32768]{1,0:T(4,128)(2,1)S(1)} %subtract_convert_fusion), channel_id=1, source_target_pairs={{0,4},{4,8},{8,12},{12,0},{1,5},{5,9},{9,13},{13,1},{2,6},{6,10},{... | collective-permute-start | bytes 786440 | tf_op jit(solution)/shard_map/ppermute | solution.py:123
  39.3 15.4 %collective-permute-start.3 = (bf16[16,16,1024]{2,1,0:T(8,128)(2,1)S(1)}, bf16[16,16,1024]{2,1,0:T(8,128)(2,1)S(1)}, u32[]{:S(2)}, u32[]{:S(2)}) collective-permute-start(bf16[16,16,1024]{2,1,0:T(8,128)(2,1)S(1)} %pad_maximum_fusion), channel_id=1, source_target_pairs={{0,1},{1,0},{2,3},{3,2},{4,5},{5,4},{6,7},{7,6},{8,9},{9,8},{10,11... | collective-permute-start | bytes 1572872 | tf_op jit(solution)/shard_map/ppermute | solution.py:44
  52.3 2.5 %copy-start.1 = (f32[32,32,1024]{2,1,0:T(8,128)S(1)}, f32[32,32,1024]{2,1,0:T(8,128)}, u32[]{:S(2)}) copy-start(f32[32,32,1024]{2,1,0:T(8,128)} %param.7) | copy-start | bytes 12582916

commit v16 on v11

--- a/solution.py
+++ b/solution.py
@@ -109,7 +109,7 @@
         0,
     )
     far_z = jnp.dot(far_rows, sheet, preferred_element_type=jnp.float32).astype(jnp.bfloat16)
-    for k in range(1, group):
+    for k in sorted(range(1, group), key=lambda k: -min(k, group - k)):
         sent = far_z[(k - 1) * piece : k * piece]
         got = lax.ppermute(sent, "zq", [(j, (j + k) % group) for j in range(group)])
         fwd_z = fwd_z + got.astype(jnp.float32)
@@ -117,7 +117,7 @@
     resid_z = (observed - fwd_z).astype(jnp.bfloat16)
     pieces = [resid_z]
     rows = [own_rows]
-    for k in range(1, group):
+    for k in sorted(range(1, group), key=lambda k: -min(k, group - k)):
         pieces.append(lax.ppermute(resid_z, "zq", [(j, (j + k) % group) for j in range(group)]))
         src = (zq - k + group) % group
         rows.append(lax.dynamic_slice_in_dim(band_z, src * piece, piece, 0))

time: 57 us -> 56.8 us (level)
  the two profiles are of different devices: /device:TPU:1 before, /device:TPU:2 now
where the time goes in v16:
time: 56.8 us; the launch traced here: 56.5 us
  matrix products  14.9 us (26%)
  starting transfers between devices  12.9 us (23%)
  local copies, waits for them, and re-layouts  12 us (21%)
  waiting for transfers between devices  10.8 us (19%)
  other arithmetic  5.59 us (10%)
    ppermute x3, waiting for transfers between devices, shards(): lax.ppermute(resid_z, 'zq', [(j, (j + k) % group) for j in range(group)])  10.6 us
    unnamed x19, local copies, waits for them, and re-layouts  7.16 us
    ppermute x3, starting transfers between devices, shards(): got = lax.ppermute(sent, 'zq', [(j, (j + k) % group) for j in range(group)])  5.22 us
    dot_general x1, matrix products, shards(): jnp.einsum('sl,zsx->zlx', band_y, resid_y, preferred_element_type=jnp.flo...  4.24 us
    ppermute x3, starting transfers between devices, shards(): lax.ppermute(resid_z, 'zq', [(j, (j + k) % group) for j in range(group)])  3.91 us
    convert_element_type x1, other arithmetic, shards(): coarse = volume.astype(jnp.bfloat16)  2.56 us
    dot_general x1, matrix products, shards(): jnp.dot(far_rows, sheet, preferred_element_type=jnp.float32)  2.06 us
    ppermute x1, starting transfers between devices, halve(): got = lax.ppermute(give.astype(jnp.bfloat16), axis, [(0, 1), (1, 0)])  1.92 us
  transfers between devices with their start and end apart: 10, of which 3 were waited for; matrix products, arithmetic and copies ran while one was open for 40% of the time, Pallas kernels for 0%

profile of v16, /device:TPU:2, one launch (start us, length us, event | category | flops | bytes accessed | tf_op | source)
XLA Modules:
  0.0 56.5 jit_solution(727546036461756741)
XLA Ops:
  0.8 1.0 %fusion.26 = f32[25,16,128]{2,0,1:T(8,128)S(1)} fusion(f32[4,16,128]{2,1,0:T(8,128)S(1)} %copy-done, s32[25]{0:T(128)} %param.12), kind=kOutput, calls=%fused_computation.43 | convolution fusion | flops 2457700 | bytes 237668 | tf_op jit(solution)/shard_map/bk,ksl->bsl/dot_general | solution.py:19
  1.7 1.0 %fusion.6 = bf16[25,16,128]{2,1,0:T(8,128)(2,1)S(1)} fusion(s32[25,128]{1,0:T(8,128)S(1)} %add_select_fusion, f32[25,16,128]{2,0,1:T(8,128)S(1)} %fusion.26), kind=kOutput, calls=%fused_computation.13 | convolution fusion | flops 79104000 | bytes 320000 | tf_op jit(solution)/shard_map/bsj,bjl->bsl/dot_general | solution.py:23
  2.8 2.6 %convert_element_type.70 = bf16[32,32,1024]{2,1,0:T(8,128)(2,1)S(1)} convert(f32[32,32,1024]{2,1,0:T(8,128)} %param.7) | non-fusion elementwise | flops 1048576 | bytes 6291456 | tf_op jit(solution)/shard_map/convert_element_type | solution.py:58
  5.9 2.5 %copy.16 = bf16[4,8,32,1024]{3,1,2,0:T(8,128)(2,1)} copy(bf16[4,8,32,1024]{3,2,1,0:T(8,128)(2,1)S(1)} %bitcast.65) | data formatting | bytes 4194304
  8.5 2.1 %convolution_convert_fusion = bf16[12,32768]{1,0:T(8,128)(2,1)S(1)} fusion(bf16[32,32768]{1,0:T(8,128)(2,1)} %bitcast.68, bf16[4,32]{1,0:T(4,128)(2,1)S(1)} %get-tuple-element.14, bf16[4,32]{1,0:T(4,128)(2,1)S(1)} %get-tuple-element.15, bf16[4,32]{1,0:T(4,128)(2,1)S(1)} %get-tuple-element.13), kind=kOutput, calls=%fused_computation | convolution fusion | flops 25561344 | bytes 2884352 | tf_op jit(solution)/shard_map/dot_general | solution.py:111
  10.6 1.0 %fusion.60 = (bf16[4,32768]{1,0:T(4,128)(2,1)}, bf16[4,32768]{1,0:T(4,128)(2,1)}, bf16[4,32768]{1,0:T(4,128)(2,1)}) fusion(bf16[12,32768]{1,0:T(8,128)(2,1)S(1)} %convolution_convert_fusion), kind=kLoop, calls=%fused_computation.85 | loop fusion | bytes 1572864 | tf_op jit(solution)/shard_map/slice | solution.py:113
  11.6 3.2 %collective-permute-start.4 = (bf16[4,32768]{1,0:T(4,128)(2,1)}, bf16[4,32768]{1,0:T(4,128)(2,1)}, u32[]{:S(2)}, u32[]{:S(2)}) collective-permute-start(bf16[4,32768]{1,0:T(4,128)(2,1)} %get-tuple-element.7), channel_id=1, source_target_pairs={{0,8},{4,12},{8,0},{12,4},{1,9},{5,13},{9,1},{13,5},{2,10},{6,14},... | collective-permute-start | bytes 786440 | tf_op jit(solution)/shard_map/ppermute | solution.py:114
  14.8 1.0 %collective-permute-start.6 = (bf16[4,32768]{1,0:T(4,128)(2,1)}, bf16[4,32768]{1,0:T(4,128)(2,1)}, u32[]{:S(2)}, u32[]{:S(2)}) collective-permute-start(bf16[4,32768]{1,0:T(4,128)(2,1)} %get-tuple-element.8), channel_id=1, source_target_pairs={{0,12},{4,0},{8,4},{12,8},{1,13},{5,1},{9,5},{13,9},{2,14},{6,2},{... | collective-permute-start | bytes 786440 | tf_op jit(solution)/shard_map/ppermute | solution.py:114
  15.8 1.0 %collective-permute-start.5 = (bf16[4,32768]{1,0:T(4,128)(2,1)}, bf16[4,32768]{1,0:T(4,128)(2,1)}, u32[]{:S(2)}, u32[]{:S(2)}) collective-permute-start(bf16[4,32768]{1,0:T(4,128)(2,1)} %get-tuple-element.9), channel_id=1, source_target_pairs={{0,4},{4,8},{8,12},{12,0},{1,5},{5,9},{9,13},{13,1},{2,6},{6,10},{... | collective-permute-start | bytes 786440 | tf_op jit(solution)/shard_map/ppermute | solution.py:114
  16.9 1.0 %copy.10 = f32[1024,128]{0,1:T(8,128)} copy(f32[1024,128]{1,0:T(8,128)S(1)} %bitcast_convert_fusion) | data formatting | bytes 1048576 | tf_op jit(solution)/shard_map/convert_element_type | solution.py:66
  18.0 1.4 %convert_add_fusion = f32[16,16,1024]{2,1,0:T(8,128)S(1)} fusion(bf16[16,16,1024]{2,1,0:T(8,128)(2,1)} %collective-permute-done, bf16[32,32,1024]{2,1,0:T(8,128)(2,1)S(1)} %convert_element_type.70, s32[]{:T(128)S(6)} %select_n.111, bf16[1,16,128]{2,1,0:T(8,128)(2,1)S(1)} %slice.25, s32[]{:T(128)S(6)} %select_n.112), kind=kOutput, calls=%fused_computation.25 | convolution fusion | flops 17301504 | bytes 2625544 | tf_op jit(solution)/shard_map/sl,zlx->zsx/dot_general | solution.py:77
  20.2 1.9 %collective-permute-start.1 = (bf16[8,16,1024]{2,1,0:T(8,128)(2,1)}, bf16[8,16,1024]{2,1,0:T(8,128)(2,1)}, u32[]{:S(2)}, u32[]{:S(2)}) collective-permute-start(bf16[8,16,1024]{2,1,0:T(8,128)(2,1)} %dynamic-slice_convert_fusion), channel_id=1, source_target_pairs={{0,2},{2,0},{1,3},{3,1},{4,6},{6,4},{5,7},{7,5},{8,10},{10,8},{9,1... | collective-permute-start | bytes 786440 | tf_op jit(solution)/shard_map/ppermute | solution.py:39
  22.1 1.5 %fusion.5 = bf16[1024,128]{0,1:T(8,128)(2,1)} fusion(f32[1024,128]{0,1:T(8,128)S(1)} %copy-done.3, bf16[1024,1024]{1,0:T(8,128)(2,1)S(1)} %bitcast.66, bf16[16,8,8,128]{3,2,1,0:T(8,128)(2,1)S(1)} %bitcast.70), kind=kOutput, calls=%fused_computation.12 | convolution fusion | flops 268697600 | bytes 3145728 | tf_op jit(solution)/shard_map/dot_general | solution.py:62
  25.3 2.2 %copy.15 = f32[1,4,32,1024]{3,1,2,0:T(4,128)} copy(f32[1,4,32,1024]{3,2,1,0:T(8,128)} %convert_bitcast_fusion) | data formatting | bytes 1048576
  27.5 1.1 %copy.11 = bf16[1024,128]{1,0:T(8,128)(2,1)S(1)} copy(bf16[1024,128]{0,1:T(8,128)(2,1)} %fusion.5) | data formatting | bytes 524288 | tf_op jit(solution)/shard_map/convert_element_type | solution.py:67
  28.6 1.1 %subtract_convert_fusion.1 = bf16[8,16,1024]{2,1,0:T(8,128)(2,1)S(1)} fusion(bf16[8,16,1024]{2,1,0:T(8,128)(2,1)} %collective-permute-done.1, f32[16,16,1024]{2,1,0:T(8,128)S(1)} %convert_add_fusion, s32[]{:T(128)S(6)} %select_n.114, bf16[32,16,1024]{2,1,0:T(8,128)(2,1)} %param.9, s32[]{:T(128)S(6)} %select_n.110), kind=kLoop, calls=%fused_computation.32 | loop fusion | flops 655360 | bytes 1310728 | tf_op jit(solution)/shard_map/convert_element_type | solution.py:93
  29.8 1.6 %collective-permute-start.2 = (bf16[8,16,1024]{2,1,0:T(8,128)(2,1)S(1)}, bf16[8,16,1024]{2,1,0:T(8,128)(2,1)S(1)}, u32[]{:S(2)}, u32[]{:S(2)}) collective-permute-start(bf16[8,16,1024]{2,1,0:T(8,128)(2,1)S(1)} %subtract_convert_fusion.1), channel_id=1, source_target_pairs={{0,2},{2,0},{1,3},{3,1},{4,6},{6,4},{5,7},{7,5},{8,10},{10,8},{9,1... | collective-permute-start | bytes 786440 | tf_op jit(solution)/shard_map/ppermute | solution.py:44
  31.4 1.9 %subtract_convert_fusion = bf16[4,32768]{1,0:T(4,128)(2,1)S(1)} fusion(f32[4,32768]{1,0:T(4,128)} %bitcast.72, bf16[4,32768]{1,0:T(4,128)(2,1)} %collective-permute-done.6, bf16[4,32768]{1,0:T(4,128)(2,1)} %collective-permute-done.5, bf16[4,32768]{1,0:T(4,128)(2,1)} %collective-permute-done.4, bf16[4,32]{1,0:T(4,128)(2,1)S(1)} %get-tuple-element.12, ...), kind=kOutput, calls=%fused_computation.31 | convolution fusion | flops 9437184 | bytes 3670272 | tf_op jit(solution)/shard_map/dot_general | solution.py:106
  33.3 2.4 %collective-permute-start.9 = (bf16[4,32768]{1,0:T(4,128)(2,1)S(1)}, bf16[4,32768]{1,0:T(4,128)(2,1)S(1)}, u32[]{:S(2)}, u32[]{:S(2)}) collective-permute-start(bf16[4,32768]{1,0:T(4,128)(2,1)S(1)} %subtract_convert_fusion), channel_id=1, source_target_pairs={{0,12},{4,0},{8,4},{12,8},{1,13},{5,1},{9,5},{13,9},{2,14},{6,2},{... | collective-permute-start | bytes 786440 | tf_op jit(solution)/shard_map/ppermute | solution.py:121
  35.7 1.6 %collective-permute-start.7 = (bf16[4,32768]{1,0:T(4,128)(2,1)S(1)}, bf16[4,32768]{1,0:T(4,128)(2,1)S(1)}, u32[]{:S(2)}, u32[]{:S(2)}) collective-permute-start(bf16[4,32768]{1,0:T(4,128)(2,1)S(1)} %subtract_convert_fusion), channel_id=1, source_target_pairs={{0,8},{4,12},{8,0},{12,4},{1,9},{5,13},{9,1},{13,5},{2,10},{6,14},... | collective-permute-start | bytes 786440 | tf_op jit(solution)/shard_map/ppermute | solution.py:121
  38.3 7.2 %collective-permute-done.9 = bf16[4,32768]{1,0:T(4,128)(2,1)S(1)} collective-permute-done((bf16[4,32768]{1,0:T(4,128)(2,1)S(1)}, bf16[4,32768]{1,0:T(4,128)(2,1)S(1)}, u32[]{:S(2)}, u32[]{:S(2)}) %collective-permute-start.9) | collective-permute-done | bytes 262176 | tf_op jit(solution)/shard_map/ppermute | solution.py:121
  45.5 3.4 %collective-permute-done.8 = bf16[4,32768]{1,0:T(4,128)(2,1)S(1)} collective-permute-done((bf16[4,32768]{1,0:T(4,128)(2,1)S(1)}, bf16[4,32768]{1,0:T(4,128)(2,1)S(1)}, u32[]{:S(2)}, u32[]{:S(2)}) %collective-permute-start.8) | collective-permute-done | bytes 262176 | tf_op jit(solution)/shard_map/ppermute | solution.py:121
  49.7 2.4 %copy.17 = f32[4,8,32,1024]{3,2,1,0:T(8,128)S(1)} copy(f32[4,8,32,1024]{3,1,2,0:T(8,128)S(1)} %bitcast.67) | data formatting | bytes 8388608
  52.2 4.2 %fusion.1 = f32[32,32,1024]{2,1,0:T(8,128)} fusion(f32[32,32,1024]{2,1,0:T(8,128)S(1)} %copy-done.1, f32[4,8,32,1024]{3,2,1,0:T(8,128)S(1)} %copy.17, f32[32,32,1024]{2,1,0:T(8,128)S(1)} %fusion.61, bf16[16,16,1024]{2,1,0:T(8,128)(2,1)S(1)} %get-tuple-element.6, bf16[16,16,1024]{2,1,0:T(8,128)(2,1)S(1)} %get-tuple-element.5, ...), kind=kOutput, calls=%fused_computation.3 | convolution fusion | flops 38273024 | bytes 17829892 | tf_op jit(solution)/shard_map/sl,zsx->zlx/dot_general | solution.py:96
  (46 shorter events, 5.8 us)
Async XLA Ops:
  0.0 0.8 %copy-start = (f32[4,16,128]{2,1,0:T(8,128)S(1)}, f32[4,16,128]{2,1,0:T(8,128)}, u32[]{:S(2)}) copy-start(f32[4,16,128]{2,1,0:T(8,128)} %param.11) | copy-start | bytes 98308
  2.8 3.1 %copy-start.7 = (bf16[25,16,128]{2,1,0:T(8,128)(2,1)}, bf16[25,16,128]{2,1,0:T(8,128)(2,1)S(1)}, u32[]{:S(2)}) copy-start(bf16[25,16,128]{2,1,0:T(8,128)(2,1)S(1)} %fusion.6) | copy-start | bytes 307204
  5.7 12.3 %collective-permute-start = (bf16[16,16,1024]{2,1,0:T(8,128)(2,1)S(1)}, bf16[16,16,1024]{2,1,0:T(8,128)(2,1)}, u32[]{:S(2)}, u32[]{:S(2)}) collective-permute-start(bf16[16,16,1024]{2,1,0:T(8,128)(2,1)S(1)} %fusion.4), channel_id=1, source_target_pairs={{0,1},{1,0},{2,3},{3,2},{4,5},{5,4},{6,7},{7,6},{8,9},{9,8},{10,11... | collective-permute-start | bytes 1572872 | tf_op jit(solution)/shard_map/ppermute | solution.py:89
  5.9 2.5 %slice-start = ((bf16[25,16,128]{2,1,0:T(8,128)(2,1)}), bf16[16,16,128]{2,1,0:T(8,128)(2,1)S(1)}, s32[]{:S(2)}) async-start(bf16[25,16,128]{2,1,0:T(8,128)(2,1)} %copy-done.7), calls=%async_computation | async-start | bytes 131072 | tf_op jit(solution)/shard_map/slice | solution.py:57
  8.5 8.3 %copy-start.5 = (bf16[32,32,128]{2,1,0:T(8,128)(2,1)S(1)}, bf16[32,32,128]{2,1,0:T(8,128)(2,1)}, u32[]{:S(2)}) copy-start(bf16[32,32,128]{2,1,0:T(8,128)(2,1)} %param.8) | copy-start | bytes 786436
  10.5 7.3 %slice-start.1 = ((bf16[25,16,128]{2,1,0:T(8,128)(2,1)}), bf16[8,16,128]{2,1,0:T(8,128)(2,1)S(1)}, s32[]{:S(2)}) async-start(bf16[25,16,128]{2,1,0:T(8,128)(2,1)} %copy-done.7), calls=%async_computation.1 | async-start | bytes 65536 | tf_op jit(solution)/shard_map/slice | solution.py:55
  11.6 19.8 %collective-permute-start.4 = (bf16[4,32768]{1,0:T(4,128)(2,1)}, bf16[4,32768]{1,0:T(4,128)(2,1)}, u32[]{:S(2)}, u32[]{:S(2)}) collective-permute-start(bf16[4,32768]{1,0:T(4,128)(2,1)} %get-tuple-element.7), channel_id=1, source_target_pairs={{0,8},{4,12},{8,0},{12,4},{1,9},{5,13},{9,1},{13,5},{2,10},{6,14},... | collective-permute-start | bytes 786440 | tf_op jit(solution)/shard_map/ppermute | solution.py:114
  14.8 16.7 %collective-permute-start.6 = (bf16[4,32768]{1,0:T(4,128)(2,1)}, bf16[4,32768]{1,0:T(4,128)(2,1)}, u32[]{:S(2)}, u32[]{:S(2)}) collective-permute-start(bf16[4,32768]{1,0:T(4,128)(2,1)} %get-tuple-element.8), channel_id=1, source_target_pairs={{0,12},{4,0},{8,4},{12,8},{1,13},{5,1},{9,5},{13,9},{2,14},{6,2},{... | collective-permute-start | bytes 786440 | tf_op jit(solution)/shard_map/ppermute | solution.py:114
  15.8 15.6 %collective-permute-start.5 = (bf16[4,32768]{1,0:T(4,128)(2,1)}, bf16[4,32768]{1,0:T(4,128)(2,1)}, u32[]{:S(2)}, u32[]{:S(2)}) collective-permute-start(bf16[4,32768]{1,0:T(4,128)(2,1)} %get-tuple-element.9), channel_id=1, source_target_pairs={{0,4},{4,8},{8,12},{12,0},{1,5},{5,9},{9,13},{13,1},{2,6},{6,10},{... | collective-permute-start | bytes 786440 | tf_op jit(solution)/shard_map/ppermute | solution.py:114
  17.9 4.2 %copy-start.3 = (f32[1024,128]{0,1:T(8,128)S(1)}, f32[1024,128]{0,1:T(8,128)}, u32[]{:S(2)}) copy-start(f32[1024,128]{0,1:T(8,128)} %copy.10) | copy-start | bytes 1572868
  19.4 4.2 %copy-start.6 = (bf16[4,32,1024]{2,1,0:T(8,128)(2,1)S(1)}, bf16[4,32,1024]{2,1,0:T(8,128)(2,1)}, u32[]{:S(2)}) copy-start(bf16[4,32,1024]{2,1,0:T(8,128)(2,1)} %param.10) | copy-start | bytes 786436
  20.2 8.5 %collective-permute-start.1 = (bf16[8,16,1024]{2,1,0:T(8,128)(2,1)}, bf16[8,16,1024]{2,1,0:T(8,128)(2,1)}, u32[]{:S(2)}, u32[]{:S(2)}) collective-permute-start(bf16[8,16,1024]{2,1,0:T(8,128)(2,1)} %dynamic-slice_convert_fusion), channel_id=1, source_target_pairs={{0,2},{2,0},{1,3},{3,1},{4,6},{6,4},{5,7},{7,5},{8,10},{10,8},{9,1... | collective-permute-start | bytes 786440 | tf_op jit(solution)/shard_map/ppermute | solution.py:39
  23.6 7.8 %copy-start.2 = (bf16[4,8,32,1024]{3,1,2,0:T(8,128)(2,1)S(1)}, bf16[4,8,32,1024]{3,1,2,0:T(8,128)(2,1)}, u32[]{:S(2)}) copy-start(bf16[4,8,32,1024]{3,1,2,0:T(8,128)(2,1)} %copy.16) | copy-start | bytes 6291460
  29.8 7.6 %collective-permute-start.2 = (bf16[8,16,1024]{2,1,0:T(8,128)(2,1)S(1)}, bf16[8,16,1024]{2,1,0:T(8,128)(2,1)S(1)}, u32[]{:S(2)}, u32[]{:S(2)}) collective-permute-start(bf16[8,16,1024]{2,1,0:T(8,128)(2,1)S(1)} %subtract_convert_fusion.1), channel_id=1, source_target_pairs={{0,2},{2,0},{1,3},{3,1},{4,6},{6,4},{5,7},{7,5},{8,10},{10,8},{9,1... | collective-permute-start | bytes 786440 | tf_op jit(solution)/shard_map/ppermute | solution.py:44
  31.4 6.1 %copy-start.4 = (bf16[128,1024,1]{1,0,2:T(8,128)(2,1)S(1)}, bf16[128,1024,1]{1,0,2:T(8,128)(2,1)}, u32[]{:S(2)}) copy-start(bf16[128,1024,1]{1,0,2:T(8,128)(2,1)} %reshape.91) | copy-start | bytes 786436
  33.3 12.2 %collective-permute-start.9 = (bf16[4,32768]{1,0:T(4,128)(2,1)S(1)}, bf16[4,32768]{1,0:T(4,128)(2,1)S(1)}, u32[]{:S(2)}, u32[]{:S(2)}) collective-permute-start(bf16[4,32768]{1,0:T(4,128)(2,1)S(1)} %subtract_convert_fusion), channel_id=1, source_target_pairs={{0,12},{4,0},{8,4},{12,8},{1,13},{5,1},{9,5},{13,9},{2,14},{6,2},{... | collective-permute-start | bytes 786440 | tf_op jit(solution)/shard_map/ppermute | solution.py:121
  35.7 13.2 %collective-permute-start.8 = (bf16[4,32768]{1,0:T(4,128)(2,1)S(1)}, bf16[4,32768]{1,0:T(4,128)(2,1)S(1)}, u32[]{:S(2)}, u32[]{:S(2)}) collective-permute-start(bf16[4,32768]{1,0:T(4,128)(2,1)S(1)} %subtract_convert_fusion), channel_id=1, source_target_pairs={{0,4},{4,8},{8,12},{12,0},{1,5},{5,9},{9,13},{13,1},{2,6},{6,10},{... | collective-permute-start | bytes 786440 | tf_op jit(solution)/shard_map/ppermute | solution.py:121
  35.7 13.2 %collective-permute-start.7 = (bf16[4,32768]{1,0:T(4,128)(2,1)S(1)}, bf16[4,32768]{1,0:T(4,128)(2,1)S(1)}, u32[]{:S(2)}, u32[]{:S(2)}) collective-permute-start(bf16[4,32768]{1,0:T(4,128)(2,1)S(1)} %subtract_convert_fusion), channel_id=1, source_target_pairs={{0,8},{4,12},{8,0},{12,4},{1,9},{5,13},{9,1},{13,5},{2,10},{6,14},... | collective-permute-start | bytes 786440 | tf_op jit(solution)/shard_map/ppermute | solution.py:121
  37.5 14.6 %collective-permute-start.3 = (bf16[16,16,1024]{2,1,0:T(8,128)(2,1)S(1)}, bf16[16,16,1024]{2,1,0:T(8,128)(2,1)S(1)}, u32[]{:S(2)}, u32[]{:S(2)}) collective-permute-start(bf16[16,16,1024]{2,1,0:T(8,128)(2,1)S(1)} %pad_maximum_fusion), channel_id=1, source_target_pairs={{0,1},{1,0},{2,3},{3,2},{4,5},{5,4},{6,7},{7,6},{8,9},{9,8},{10,11... | collective-permute-start | bytes 1572872 | tf_op jit(solution)/shard_map/ppermute | solution.py:44
  49.7 2.5 %copy-start.1 = (f32[32,32,1024]{2,1,0:T(8,128)S(1)}, f32[32,32,1024]{2,1,0:T(8,128)}, u32[]{:S(2)}) copy-start(f32[32,32,1024]{2,1,0:T(8,128)} %param.7) | copy-start | bytes 12582916

commit v17 on v11

--- a/solution.py
+++ b/solution.py
@@ -128,7 +128,8 @@
         preferred_element_type=jnp.float32,
     ).reshape(planes, rows_here, width)
 
-    return volume + step_size * (corr_x + corr_y + corr_z)
+    base = lax.optimization_barrier(volume + step_size * corr_x)
+    return base + step_size * (corr_y + corr_z)
 
 
 def solution(mesh):

time: 57 us -> 56.2 us (0.986)
  matrix products: 14.9 us -> 14.2 us
    dot_general x1, matrix products: 4.25 us -> 3.38 us  [shards(): jnp.einsum('sl,zsx->zlx', band_y, resid_y, preferred_element_type=jnp.flo...]
where the time goes in v17:
time: 56.2 us; the launch traced here: 55.9 us
  matrix products  14.2 us (25%)
  starting transfers between devices  13.6 us (24%)
  local copies, waits for them, and re-layouts  12 us (21%)
  waiting for transfers between devices  10.3 us (18%)
  other arithmetic  5.59 us (10%)
    ppermute x3, waiting for transfers between devices, shards(): lax.ppermute(resid_z, 'zq', [(j, (j + k) % group) for j in range(group)])  9.4 us
    unnamed x19, local copies, waits for them, and re-layouts  7.16 us
    dot_general x1, matrix products, shards(): jnp.einsum('sl,zsx->zlx', band_y, resid_y, preferred_element_type=jnp.flo...  3.38 us
    ppermute x1, starting transfers between devices, shards(): lax.ppermute(give_y, 'co', [(0, 1), (1, 0)]).astype(jnp.float32)  3.29 us
    ppermute x3, starting transfers between devices, shards(): lax.ppermute(resid_z, 'zq', [(j, (j + k) % group) for j in range(group)])  3.06 us
    ppermute x2, starting transfers between devices, double(): other = lax.ppermute(values, axis, [(0, 1), (1, 0)])  2.94 us
    ppermute x3, starting transfers between devices, shards(): got = lax.ppermute(sent, 'zq', [(j, (j + k) % group) for j in range(group)])  2.68 us
    convert_element_type x1, other arithmetic, shards(): coarse = volume.astype(jnp.bfloat16)  2.56 us
  transfers between devices with their start and end apart: 10, of which 3 were waited for; matrix products, arithmetic and copies ran while one was open for 40% of the time, Pallas kernels for 0%

profile of v17, /device:TPU:1, one launch (start us, length us, event | category | flops | bytes accessed | tf_op | source)
XLA Modules:
  0.0 55.9 jit_solution(6923486566614026370)
XLA Ops:
  0.8 1.0 %fusion.26 = f32[25,16,128]{2,0,1:T(8,128)S(1)} fusion(f32[4,16,128]{2,1,0:T(8,128)S(1)} %copy-done, s32[25]{0:T(128)} %param.12), kind=kOutput, calls=%fused_computation.43 | convolution fusion | flops 2457700 | bytes 237668 | tf_op jit(solution)/shard_map/bk,ksl->bsl/dot_general | solution.py:19
  1.7 1.0 %fusion.6 = bf16[25,16,128]{2,1,0:T(8,128)(2,1)S(1)} fusion(s32[25,128]{1,0:T(8,128)S(1)} %add_select_fusion, f32[25,16,128]{2,0,1:T(8,128)S(1)} %fusion.26), kind=kOutput, calls=%fused_computation.13 | convolution fusion | flops 79104000 | bytes 320000 | tf_op jit(solution)/shard_map/bsj,bjl->bsl/dot_general | solution.py:23
  2.8 2.6 %convert_element_type.70 = bf16[32,32,1024]{2,1,0:T(8,128)(2,1)S(1)} convert(f32[32,32,1024]{2,1,0:T(8,128)} %param.7) | non-fusion elementwise | flops 1048576 | bytes 6291456 | tf_op jit(solution)/shard_map/convert_element_type | solution.py:58
  5.7 3.3 %collective-permute-start = (bf16[16,16,1024]{2,1,0:T(8,128)(2,1)S(1)}, bf16[16,16,1024]{2,1,0:T(8,128)(2,1)}, u32[]{:S(2)}, u32[]{:S(2)}) collective-permute-start(bf16[16,16,1024]{2,1,0:T(8,128)(2,1)S(1)} %fusion.4), channel_id=1, source_target_pairs={{0,1},{1,0},{2,3},{3,2},{4,5},{5,4},{6,7},{7,6},{8,9},{9,8},{10,11... | collective-permute-start | bytes 1572872 | tf_op jit(solution)/shard_map/ppermute | solution.py:89
  9.0 2.5 %copy.16 = bf16[4,8,32,1024]{3,1,2,0:T(8,128)(2,1)} copy(bf16[4,8,32,1024]{3,2,1,0:T(8,128)(2,1)S(1)} %bitcast.63) | data formatting | bytes 4194304
  11.6 2.1 %convolution_convert_fusion = bf16[12,32768]{1,0:T(8,128)(2,1)S(1)} fusion(bf16[32,32768]{1,0:T(8,128)(2,1)} %bitcast.66, bf16[4,32]{1,0:T(4,128)(2,1)S(1)} %get-tuple-element.15, bf16[4,32]{1,0:T(4,128)(2,1)S(1)} %get-tuple-element.14, bf16[4,32]{1,0:T(4,128)(2,1)S(1)} %get-tuple-element.13), kind=kOutput, calls=%fused_computation | convolution fusion | flops 25561344 | bytes 2884352 | tf_op jit(solution)/shard_map/dot_general | solution.py:111
  13.7 1.0 %fusion.60 = (bf16[4,32768]{1,0:T(4,128)(2,1)}, bf16[4,32768]{1,0:T(4,128)(2,1)}, bf16[4,32768]{1,0:T(4,128)(2,1)}) fusion(bf16[12,32768]{1,0:T(8,128)(2,1)S(1)} %convolution_convert_fusion), kind=kLoop, calls=%fused_computation.85 | loop fusion | bytes 1572864 | tf_op jit(solution)/shard_map/slice | solution.py:113
  14.7 2.7 %collective-permute-start.6 = (bf16[4,32768]{1,0:T(4,128)(2,1)}, bf16[4,32768]{1,0:T(4,128)(2,1)}, u32[]{:S(2)}, u32[]{:S(2)}) collective-permute-start(bf16[4,32768]{1,0:T(4,128)(2,1)} %get-tuple-element.8), channel_id=1, source_target_pairs={{0,12},{4,0},{8,4},{12,8},{1,13},{5,1},{9,5},{13,9},{2,14},{6,2},{... | collective-permute-start | bytes 786440 | tf_op jit(solution)/shard_map/ppermute | solution.py:114
  17.4 1.0 %copy.10 = f32[1024,128]{0,1:T(8,128)} copy(f32[1024,128]{1,0:T(8,128)S(1)} %bitcast_convert_fusion) | data formatting | bytes 1048576 | tf_op jit(solution)/shard_map/convert_element_type | solution.py:66
  18.5 1.4 %convert_add_fusion = f32[16,16,1024]{2,1,0:T(8,128)S(1)} fusion(bf16[16,16,1024]{2,1,0:T(8,128)(2,1)} %collective-permute-done, bf16[32,32,1024]{2,1,0:T(8,128)(2,1)S(1)} %convert_element_type.70, s32[]{:T(128)S(6)} %select_n.111, bf16[1,16,128]{2,1,0:T(8,128)(2,1)S(1)} %slice.25, s32[]{:T(128)S(6)} %select_n.112), kind=kOutput, calls=%fused_computation.25 | convolution fusion | flops 17301504 | bytes 2625544 | tf_op jit(solution)/shard_map/sl,zlx->zsx/dot_general | solution.py:77
  20.8 1.6 %collective-permute-start.1 = (bf16[8,16,1024]{2,1,0:T(8,128)(2,1)}, bf16[8,16,1024]{2,1,0:T(8,128)(2,1)}, u32[]{:S(2)}, u32[]{:S(2)}) collective-permute-start(bf16[8,16,1024]{2,1,0:T(8,128)(2,1)} %dynamic-slice_convert_fusion), channel_id=1, source_target_pairs={{0,2},{2,0},{1,3},{3,1},{4,6},{6,4},{5,7},{7,5},{8,10},{10,8},{9,1... | collective-permute-start | bytes 786440 | tf_op jit(solution)/shard_map/ppermute | solution.py:39
  22.4 1.5 %fusion.5 = bf16[1024,128]{0,1:T(8,128)(2,1)} fusion(f32[1024,128]{0,1:T(8,128)S(1)} %copy-done.3, bf16[1024,1024]{1,0:T(8,128)(2,1)S(1)} %bitcast.64, bf16[16,8,8,128]{3,2,1,0:T(8,128)(2,1)S(1)} %bitcast.68), kind=kOutput, calls=%fused_computation.12 | convolution fusion | flops 268697600 | bytes 3145728 | tf_op jit(solution)/shard_map/dot_general | solution.py:62
  25.6 2.2 %copy.15 = f32[1,4,32,1024]{3,1,2,0:T(4,128)} copy(f32[1,4,32,1024]{3,2,1,0:T(8,128)} %convert_bitcast_fusion) | data formatting | bytes 1048576
  27.8 1.1 %copy.11 = bf16[1024,128]{1,0:T(8,128)(2,1)S(1)} copy(bf16[1024,128]{0,1:T(8,128)(2,1)} %fusion.5) | data formatting | bytes 524288 | tf_op jit(solution)/shard_map/convert_element_type | solution.py:67
  28.9 1.1 %subtract_convert_fusion.1 = bf16[8,16,1024]{2,1,0:T(8,128)(2,1)S(1)} fusion(bf16[8,16,1024]{2,1,0:T(8,128)(2,1)} %collective-permute-done.1, f32[16,16,1024]{2,1,0:T(8,128)S(1)} %convert_add_fusion, s32[]{:T(128)S(6)} %select_n.114, bf16[32,16,1024]{2,1,0:T(8,128)(2,1)} %param.9, s32[]{:T(128)S(6)} %select_n.110), kind=kLoop, calls=%fused_computation.32 | loop fusion | flops 655360 | bytes 1310728 | tf_op jit(solution)/shard_map/convert_element_type | solution.py:93
  30.9 2.0 %subtract_convert_fusion = bf16[4,32768]{1,0:T(4,128)(2,1)S(1)} fusion(f32[4,32768]{1,0:T(4,128)} %bitcast.70, bf16[4,32768]{1,0:T(4,128)(2,1)} %collective-permute-done.6, bf16[4,32768]{1,0:T(4,128)(2,1)} %collective-permute-done.5, bf16[4,32768]{1,0:T(4,128)(2,1)} %collective-permute-done.4, bf16[4,32]{1,0:T(4,128)(2,1)S(1)} %get-tuple-element.12, ...), kind=kOutput, calls=%fused_computation.31 | convolution fusion | flops 9437184 | bytes 3670272 | tf_op jit(solution)/shard_map/dot_general | solution.py:106
  32.9 1.2 %collective-permute-start.9 = (bf16[4,32768]{1,0:T(4,128)(2,1)S(1)}, bf16[4,32768]{1,0:T(4,128)(2,1)S(1)}, u32[]{:S(2)}, u32[]{:S(2)}) collective-permute-start(bf16[4,32768]{1,0:T(4,128)(2,1)S(1)} %subtract_convert_fusion), channel_id=1, source_target_pairs={{0,12},{4,0},{8,4},{12,8},{1,13},{5,1},{9,5},{13,9},{2,14},{6,2},{... | collective-permute-start | bytes 786440 | tf_op jit(solution)/shard_map/ppermute | solution.py:121
  34.1 1.1 %collective-permute-start.8 = (bf16[4,32768]{1,0:T(4,128)(2,1)S(1)}, bf16[4,32768]{1,0:T(4,128)(2,1)S(1)}, u32[]{:S(2)}, u32[]{:S(2)}) collective-permute-start(bf16[4,32768]{1,0:T(4,128)(2,1)S(1)} %subtract_convert_fusion), channel_id=1, source_target_pairs={{0,8},{4,12},{8,0},{12,4},{1,9},{5,13},{9,1},{13,5},{2,10},{6,14},... | collective-permute-start | bytes 786440 | tf_op jit(solution)/shard_map/ppermute | solution.py:121
  35.9 0.9 %collective-permute-done.2 = bf16[8,16,1024]{2,1,0:T(8,128)(2,1)S(1)} collective-permute-done((bf16[8,16,1024]{2,1,0:T(8,128)(2,1)S(1)}, bf16[8,16,1024]{2,1,0:T(8,128)(2,1)S(1)}, u32[]{:S(2)}, u32[]{:S(2)}) %collective-permute-start.2) | collective-permute-done | bytes 262176 | tf_op jit(solution)/shard_map/ppermute | solution.py:44
  36.9 2.2 %collective-permute-start.3 = (bf16[16,16,1024]{2,1,0:T(8,128)(2,1)S(1)}, bf16[16,16,1024]{2,1,0:T(8,128)(2,1)S(1)}, u32[]{:S(2)}, u32[]{:S(2)}) collective-permute-start(bf16[16,16,1024]{2,1,0:T(8,128)(2,1)S(1)} %pad_maximum_fusion), channel_id=1, source_target_pairs={{0,1},{1,0},{2,3},{3,2},{4,5},{5,4},{6,7},{7,6},{8,9},{9,8},{10,11... | collective-permute-start | bytes 1572872 | tf_op jit(solution)/shard_map/ppermute | solution.py:44
  39.8 1.7 %collective-permute-done.8 = bf16[4,32768]{1,0:T(4,128)(2,1)S(1)} collective-permute-done((bf16[4,32768]{1,0:T(4,128)(2,1)S(1)}, bf16[4,32768]{1,0:T(4,128)(2,1)S(1)}, u32[]{:S(2)}, u32[]{:S(2)}) %collective-permute-start.8) | collective-permute-done | bytes 262176 | tf_op jit(solution)/shard_map/ppermute | solution.py:121
  41.5 7.7 %collective-permute-done.7 = bf16[4,32768]{1,0:T(4,128)(2,1)S(1)} collective-permute-done((bf16[4,32768]{1,0:T(4,128)(2,1)S(1)}, bf16[4,32768]{1,0:T(4,128)(2,1)S(1)}, u32[]{:S(2)}, u32[]{:S(2)}) %collective-permute-start.7) | collective-permute-done | bytes 262176 | tf_op jit(solution)/shard_map/ppermute | solution.py:121
  50.0 2.4 %copy.17 = f32[4,8,32,1024]{3,2,1,0:T(8,128)S(1)} copy(f32[4,8,32,1024]{3,1,2,0:T(8,128)S(1)} %bitcast.65) | data formatting | bytes 8388608
  52.5 3.4 %fusion.1 = f32[32,32,1024]{2,1,0:T(8,128)} fusion(f32[32,32,1024]{2,1,0:T(8,128)S(1)} %multiply_add_fusion, f32[4,8,32,1024]{3,2,1,0:T(8,128)S(1)} %copy.17, bf16[16,16,1024]{2,1,0:T(8,128)(2,1)S(1)} %get-tuple-element.6, bf16[16,16,1024]{2,1,0:T(8,128)(2,1)S(1)} %get-tuple-element.5, bf16[1,16,128]{2,1,0:T(8,128)(2,1)S(1)} %slice.25, s32[]{:T(128)S(6)} %select_n.112), kind=kOutput, calls=%fused_computation.3 | convolution fusion | flops 37224448 | bytes 13635588 | tf_op jit(solution)/shard_map/sl,zsx->zlx/dot_general | solution.py:96
  (46 shorter events, 7.1 us)
Async XLA Ops:
  0.0 0.8 %copy-start = (f32[4,16,128]{2,1,0:T(8,128)S(1)}, f32[4,16,128]{2,1,0:T(8,128)}, u32[]{:S(2)}) copy-start(f32[4,16,128]{2,1,0:T(8,128)} %param.11) | copy-start | bytes 98308
  2.8 6.2 %copy-start.7 = (bf16[25,16,128]{2,1,0:T(8,128)(2,1)}, bf16[25,16,128]{2,1,0:T(8,128)(2,1)S(1)}, u32[]{:S(2)}) copy-start(bf16[25,16,128]{2,1,0:T(8,128)(2,1)S(1)} %fusion.6) | copy-start | bytes 307204
  5.7 12.8 %collective-permute-start = (bf16[16,16,1024]{2,1,0:T(8,128)(2,1)S(1)}, bf16[16,16,1024]{2,1,0:T(8,128)(2,1)}, u32[]{:S(2)}, u32[]{:S(2)}) collective-permute-start(bf16[16,16,1024]{2,1,0:T(8,128)(2,1)S(1)} %fusion.4), channel_id=1, source_target_pairs={{0,1},{1,0},{2,3},{3,2},{4,5},{5,4},{6,7},{7,6},{8,9},{9,8},{10,11... | collective-permute-start | bytes 1572872 | tf_op jit(solution)/shard_map/ppermute | solution.py:89
  9.0 2.5 %slice-start = ((bf16[25,16,128]{2,1,0:T(8,128)(2,1)}), bf16[16,16,128]{2,1,0:T(8,128)(2,1)S(1)}, s32[]{:S(2)}) async-start(bf16[25,16,128]{2,1,0:T(8,128)(2,1)} %copy-done.7), calls=%async_computation | async-start | bytes 131072 | tf_op jit(solution)/shard_map/slice | solution.py:57
  11.6 5.8 %copy-start.5 = (bf16[32,32,128]{2,1,0:T(8,128)(2,1)S(1)}, bf16[32,32,128]{2,1,0:T(8,128)(2,1)}, u32[]{:S(2)}) copy-start(bf16[32,32,128]{2,1,0:T(8,128)(2,1)} %param.8) | copy-start | bytes 786436
  13.7 4.8 %slice-start.1 = ((bf16[25,16,128]{2,1,0:T(8,128)(2,1)}), bf16[8,16,128]{2,1,0:T(8,128)(2,1)S(1)}, s32[]{:S(2)}) async-start(bf16[25,16,128]{2,1,0:T(8,128)(2,1)} %copy-done.7), calls=%async_computation.1 | async-start | bytes 65536 | tf_op jit(solution)/shard_map/slice | solution.py:55
  14.7 16.2 %collective-permute-start.4 = (bf16[4,32768]{1,0:T(4,128)(2,1)}, bf16[4,32768]{1,0:T(4,128)(2,1)}, u32[]{:S(2)}, u32[]{:S(2)}) collective-permute-start(bf16[4,32768]{1,0:T(4,128)(2,1)} %get-tuple-element.7), channel_id=1, source_target_pairs={{0,4},{4,8},{8,12},{12,0},{1,5},{5,9},{9,13},{13,1},{2,6},{6,10},{... | collective-permute-start | bytes 786440 | tf_op jit(solution)/shard_map/ppermute | solution.py:114
  14.7 16.2 %collective-permute-start.6 = (bf16[4,32768]{1,0:T(4,128)(2,1)}, bf16[4,32768]{1,0:T(4,128)(2,1)}, u32[]{:S(2)}, u32[]{:S(2)}) collective-permute-start(bf16[4,32768]{1,0:T(4,128)(2,1)} %get-tuple-element.8), channel_id=1, source_target_pairs={{0,12},{4,0},{8,4},{12,8},{1,13},{5,1},{9,5},{13,9},{2,14},{6,2},{... | collective-permute-start | bytes 786440 | tf_op jit(solution)/shard_map/ppermute | solution.py:114
  17.4 13.5 %collective-permute-start.5 = (bf16[4,32768]{1,0:T(4,128)(2,1)}, bf16[4,32768]{1,0:T(4,128)(2,1)}, u32[]{:S(2)}, u32[]{:S(2)}) collective-permute-start(bf16[4,32768]{1,0:T(4,128)(2,1)} %get-tuple-element.9), channel_id=1, source_target_pairs={{0,8},{4,12},{8,0},{12,4},{1,9},{5,13},{9,1},{13,5},{2,10},{6,14},... | collective-permute-start | bytes 786440 | tf_op jit(solution)/shard_map/ppermute | solution.py:114
  18.4 3.9 %copy-start.3 = (f32[1024,128]{0,1:T(8,128)S(1)}, f32[1024,128]{0,1:T(8,128)}, u32[]{:S(2)}) copy-start(f32[1024,128]{0,1:T(8,128)} %copy.10) | copy-start | bytes 1572868
  20.0 3.9 %copy-start.6 = (bf16[4,32,1024]{2,1,0:T(8,128)(2,1)S(1)}, bf16[4,32,1024]{2,1,0:T(8,128)(2,1)}, u32[]{:S(2)}) copy-start(bf16[4,32,1024]{2,1,0:T(8,128)(2,1)} %param.10) | copy-start | bytes 786436
  20.8 8.2 %collective-permute-start.1 = (bf16[8,16,1024]{2,1,0:T(8,128)(2,1)}, bf16[8,16,1024]{2,1,0:T(8,128)(2,1)}, u32[]{:S(2)}, u32[]{:S(2)}) collective-permute-start(bf16[8,16,1024]{2,1,0:T(8,128)(2,1)} %dynamic-slice_convert_fusion), channel_id=1, source_target_pairs={{0,2},{2,0},{1,3},{3,1},{4,6},{6,4},{5,7},{7,5},{8,10},{10,8},{9,1... | collective-permute-start | bytes 786440 | tf_op jit(solution)/shard_map/ppermute | solution.py:39
  23.9 6.9 %copy-start.2 = (bf16[4,8,32,1024]{3,1,2,0:T(8,128)(2,1)S(1)}, bf16[4,8,32,1024]{3,1,2,0:T(8,128)(2,1)}, u32[]{:S(2)}) copy-start(bf16[4,8,32,1024]{3,1,2,0:T(8,128)(2,1)} %copy.16) | copy-start | bytes 6291460
  30.1 6.7 %collective-permute-start.2 = (bf16[8,16,1024]{2,1,0:T(8,128)(2,1)S(1)}, bf16[8,16,1024]{2,1,0:T(8,128)(2,1)S(1)}, u32[]{:S(2)}, u32[]{:S(2)}) collective-permute-start(bf16[8,16,1024]{2,1,0:T(8,128)(2,1)S(1)} %subtract_convert_fusion.1), channel_id=1, source_target_pairs={{0,2},{2,0},{1,3},{3,1},{4,6},{6,4},{5,7},{7,5},{8,10},{10,8},{9,1... | collective-permute-start | bytes 786440 | tf_op jit(solution)/shard_map/ppermute | solution.py:44
  30.9 8.2 %copy-start.1 = (f32[32,32,1024]{2,1,0:T(8,128)S(1)}, f32[32,32,1024]{2,1,0:T(8,128)}, u32[]{:S(2)}) copy-start(f32[32,32,1024]{2,1,0:T(8,128)} %param.7) | copy-start | bytes 12582916
  30.9 8.2 %copy-start.4 = (bf16[128,1024,1]{1,0,2:T(8,128)(2,1)S(1)}, bf16[128,1024,1]{1,0,2:T(8,128)(2,1)}, u32[]{:S(2)}) copy-start(bf16[128,1024,1]{1,0,2:T(8,128)(2,1)} %reshape.91) | copy-start | bytes 786436
  32.9 6.9 %collective-permute-start.9 = (bf16[4,32768]{1,0:T(4,128)(2,1)S(1)}, bf16[4,32768]{1,0:T(4,128)(2,1)S(1)}, u32[]{:S(2)}, u32[]{:S(2)}) collective-permute-start(bf16[4,32768]{1,0:T(4,128)(2,1)S(1)} %subtract_convert_fusion), channel_id=1, source_target_pairs={{0,12},{4,0},{8,4},{12,8},{1,13},{5,1},{9,5},{13,9},{2,14},{6,2},{... | collective-permute-start | bytes 786440 | tf_op jit(solution)/shard_map/ppermute | solution.py:121
  34.1 7.4 %collective-permute-start.8 = (bf16[4,32768]{1,0:T(4,128)(2,1)S(1)}, bf16[4,32768]{1,0:T(4,128)(2,1)S(1)}, u32[]{:S(2)}, u32[]{:S(2)}) collective-permute-start(bf16[4,32768]{1,0:T(4,128)(2,1)S(1)} %subtract_convert_fusion), channel_id=1, source_target_pairs={{0,8},{4,12},{8,0},{12,4},{1,9},{5,13},{9,1},{13,5},{2,10},{6,14},... | collective-permute-start | bytes 786440 | tf_op jit(solution)/shard_map/ppermute | solution.py:121
  35.1 14.0 %collective-permute-start.7 = (bf16[4,32768]{1,0:T(4,128)(2,1)S(1)}, bf16[4,32768]{1,0:T(4,128)(2,1)S(1)}, u32[]{:S(2)}, u32[]{:S(2)}) collective-permute-start(bf16[4,32768]{1,0:T(4,128)(2,1)S(1)} %subtract_convert_fusion), channel_id=1, source_target_pairs={{0,4},{4,8},{8,12},{12,0},{1,5},{5,9},{9,13},{13,1},{2,6},{6,10},{... | collective-permute-start | bytes 786440 | tf_op jit(solution)/shard_map/ppermute | solution.py:121
  36.9 15.5 %collective-permute-start.3 = (bf16[16,16,1024]{2,1,0:T(8,128)(2,1)S(1)}, bf16[16,16,1024]{2,1,0:T(8,128)(2,1)S(1)}, u32[]{:S(2)}, u32[]{:S(2)}) collective-permute-start(bf16[16,16,1024]{2,1,0:T(8,128)(2,1)S(1)} %pad_maximum_fusion), channel_id=1, source_target_pairs={{0,1},{1,0},{2,3},{3,2},{4,5},{5,4},{6,7},{7,6},{8,9},{9,8},{10,11... | collective-permute-start | bytes 1572872 | tf_op jit(solution)/shard_map/ppermute | solution.py:44

commit v18 on v16

--- a/solution.py
+++ b/solution.py
@@ -128,7 +128,8 @@
         preferred_element_type=jnp.float32,
     ).reshape(planes, rows_here, width)
 
-    return volume + step_size * (corr_x + corr_y + corr_z)
+    base = lax.optimization_barrier(volume + step_size * corr_x)
+    return base + step_size * (corr_y + corr_z)
 
 
 def solution(mesh):

time: 56.8 us -> 56 us (0.986)
  the two profiles are of different devices: /device:TPU:2 before, /device:TPU:4 now
where the time goes in v18:
time: 56 us; the launch traced here: 55.7 us
  matrix products  14.2 us (25%)
  starting transfers between devices  12.9 us (23%)
  local copies, waits for them, and re-layouts  12 us (21%)
  waiting for transfers between devices  10.7 us (19%)
  other arithmetic  5.59 us (10%)
    ppermute x3, waiting for transfers between devices, shards(): lax.ppermute(resid_z, 'zq', [(j, (j + k) % group) for j in range(group)])  10.7 us
    unnamed x19, local copies, waits for them, and re-layouts  7.16 us
    ppermute x3, starting transfers between devices, shards(): got = lax.ppermute(sent, 'zq', [(j, (j + k) % group) for j in range(group)])  5.22 us
    ppermute x3, starting transfers between devices, shards(): lax.ppermute(resid_z, 'zq', [(j, (j + k) % group) for j in range(group)])  3.9 us
    dot_general x1, matrix products, shards(): jnp.einsum('sl,zsx->zlx', band_y, resid_y, preferred_element_type=jnp.flo...  3.38 us
    convert_element_type x1, other arithmetic, shards(): coarse = volume.astype(jnp.bfloat16)  2.56 us
    dot_general x1, matrix products, shards(): jnp.dot(far_rows, sheet, preferred_element_type=jnp.float32)  2.06 us
    dot_general x1, matrix products, shards(): fwd_z = jnp.dot(own_rows, sheet, preferred_element_type=jnp.float32)  1.96 us
  transfers between devices with their start and end apart: 10, of which 2 were waited for; matrix products, arithmetic and copies ran while one was open for 41% of the time, Pallas kernels for 0%

profile of v18, /device:TPU:4, one launch (start us, length us, event | category | flops | bytes accessed | tf_op | source)
XLA Modules:
  0.0 55.7 jit_solution(5135251035069282475)
XLA Ops:
  0.8 1.0 %fusion.26 = f32[25,16,128]{2,0,1:T(8,128)S(1)} fusion(f32[4,16,128]{2,1,0:T(8,128)S(1)} %copy-done, s32[25]{0:T(128)} %param.12), kind=kOutput, calls=%fused_computation.43 | convolution fusion | flops 2457700 | bytes 237668 | tf_op jit(solution)/shard_map/bk,ksl->bsl/dot_general | solution.py:19
  1.7 1.0 %fusion.6 = bf16[25,16,128]{2,1,0:T(8,128)(2,1)S(1)} fusion(s32[25,128]{1,0:T(8,128)S(1)} %add_select_fusion, f32[25,16,128]{2,0,1:T(8,128)S(1)} %fusion.26), kind=kOutput, calls=%fused_computation.13 | convolution fusion | flops 79104000 | bytes 320000 | tf_op jit(solution)/shard_map/bsj,bjl->bsl/dot_general | solution.py:23
  2.8 2.6 %convert_element_type.70 = bf16[32,32,1024]{2,1,0:T(8,128)(2,1)S(1)} convert(f32[32,32,1024]{2,1,0:T(8,128)} %param.7) | non-fusion elementwise | flops 1048576 | bytes 6291456 | tf_op jit(solution)/shard_map/convert_element_type | solution.py:58
  5.9 2.5 %copy.16 = bf16[4,8,32,1024]{3,1,2,0:T(8,128)(2,1)} copy(bf16[4,8,32,1024]{3,2,1,0:T(8,128)(2,1)S(1)} %bitcast.63) | data formatting | bytes 4194304
  8.5 2.1 %convolution_convert_fusion = bf16[12,32768]{1,0:T(8,128)(2,1)S(1)} fusion(bf16[32,32768]{1,0:T(8,128)(2,1)} %bitcast.66, bf16[4,32]{1,0:T(4,128)(2,1)S(1)} %get-tuple-element.14, bf16[4,32]{1,0:T(4,128)(2,1)S(1)} %get-tuple-element.15, bf16[4,32]{1,0:T(4,128)(2,1)S(1)} %get-tuple-element.13), kind=kOutput, calls=%fused_computation | convolution fusion | flops 25561344 | bytes 2884352 | tf_op jit(solution)/shard_map/dot_general | solution.py:111
  10.6 1.0 %fusion.60 = (bf16[4,32768]{1,0:T(4,128)(2,1)}, bf16[4,32768]{1,0:T(4,128)(2,1)}, bf16[4,32768]{1,0:T(4,128)(2,1)}) fusion(bf16[12,32768]{1,0:T(8,128)(2,1)S(1)} %convolution_convert_fusion), kind=kLoop, calls=%fused_computation.85 | loop fusion | bytes 1572864 | tf_op jit(solution)/shard_map/slice | solution.py:113
  11.6 3.2 %collective-permute-start.4 = (bf16[4,32768]{1,0:T(4,128)(2,1)}, bf16[4,32768]{1,0:T(4,128)(2,1)}, u32[]{:S(2)}, u32[]{:S(2)}) collective-permute-start(bf16[4,32768]{1,0:T(4,128)(2,1)} %get-tuple-element.7), channel_id=1, source_target_pairs={{0,8},{4,12},{8,0},{12,4},{1,9},{5,13},{9,1},{13,5},{2,10},{6,14},... | collective-permute-start | bytes 786440 | tf_op jit(solution)/shard_map/ppermute | solution.py:114
  14.8 1.1 %collective-permute-start.6 = (bf16[4,32768]{1,0:T(4,128)(2,1)}, bf16[4,32768]{1,0:T(4,128)(2,1)}, u32[]{:S(2)}, u32[]{:S(2)}) collective-permute-start(bf16[4,32768]{1,0:T(4,128)(2,1)} %get-tuple-element.8), channel_id=1, source_target_pairs={{0,12},{4,0},{8,4},{12,8},{1,13},{5,1},{9,5},{13,9},{2,14},{6,2},{... | collective-permute-start | bytes 786440 | tf_op jit(solution)/shard_map/ppermute | solution.py:114
  15.8 1.0 %collective-permute-start.5 = (bf16[4,32768]{1,0:T(4,128)(2,1)}, bf16[4,32768]{1,0:T(4,128)(2,1)}, u32[]{:S(2)}, u32[]{:S(2)}) collective-permute-start(bf16[4,32768]{1,0:T(4,128)(2,1)} %get-tuple-element.9), channel_id=1, source_target_pairs={{0,4},{4,8},{8,12},{12,0},{1,5},{5,9},{9,13},{13,1},{2,6},{6,10},{... | collective-permute-start | bytes 786440 | tf_op jit(solution)/shard_map/ppermute | solution.py:114
  16.9 1.0 %copy.10 = f32[1024,128]{0,1:T(8,128)} copy(f32[1024,128]{1,0:T(8,128)S(1)} %bitcast_convert_fusion) | data formatting | bytes 1048576 | tf_op jit(solution)/shard_map/convert_element_type | solution.py:66
  18.0 1.4 %convert_add_fusion = f32[16,16,1024]{2,1,0:T(8,128)S(1)} fusion(bf16[16,16,1024]{2,1,0:T(8,128)(2,1)} %collective-permute-done, bf16[32,32,1024]{2,1,0:T(8,128)(2,1)S(1)} %convert_element_type.70, s32[]{:T(128)S(6)} %select_n.111, bf16[1,16,128]{2,1,0:T(8,128)(2,1)S(1)} %slice.25, s32[]{:T(128)S(6)} %select_n.112), kind=kOutput, calls=%fused_computation.25 | convolution fusion | flops 17301504 | bytes 2625544 | tf_op jit(solution)/shard_map/sl,zlx->zsx/dot_general | solution.py:77
  20.2 1.9 %collective-permute-start.1 = (bf16[8,16,1024]{2,1,0:T(8,128)(2,1)}, bf16[8,16,1024]{2,1,0:T(8,128)(2,1)}, u32[]{:S(2)}, u32[]{:S(2)}) collective-permute-start(bf16[8,16,1024]{2,1,0:T(8,128)(2,1)} %dynamic-slice_convert_fusion), channel_id=1, source_target_pairs={{0,2},{2,0},{1,3},{3,1},{4,6},{6,4},{5,7},{7,5},{8,10},{10,8},{9,1... | collective-permute-start | bytes 786440 | tf_op jit(solution)/shard_map/ppermute | solution.py:39
  22.1 1.5 %fusion.5 = bf16[1024,128]{0,1:T(8,128)(2,1)} fusion(f32[1024,128]{0,1:T(8,128)S(1)} %copy-done.3, bf16[1024,1024]{1,0:T(8,128)(2,1)S(1)} %bitcast.64, bf16[16,8,8,128]{3,2,1,0:T(8,128)(2,1)S(1)} %bitcast.68), kind=kOutput, calls=%fused_computation.12 | convolution fusion | flops 268697600 | bytes 3145728 | tf_op jit(solution)/shard_map/dot_general | solution.py:62
  25.3 2.2 %copy.15 = f32[1,4,32,1024]{3,1,2,0:T(4,128)} copy(f32[1,4,32,1024]{3,2,1,0:T(8,128)} %convert_bitcast_fusion) | data formatting | bytes 1048576
  27.5 1.1 %copy.11 = bf16[1024,128]{1,0:T(8,128)(2,1)S(1)} copy(bf16[1024,128]{0,1:T(8,128)(2,1)} %fusion.5) | data formatting | bytes 524288 | tf_op jit(solution)/shard_map/convert_element_type | solution.py:67
  28.6 1.1 %subtract_convert_fusion.1 = bf16[8,16,1024]{2,1,0:T(8,128)(2,1)S(1)} fusion(bf16[8,16,1024]{2,1,0:T(8,128)(2,1)} %collective-permute-done.1, f32[16,16,1024]{2,1,0:T(8,128)S(1)} %convert_add_fusion, s32[]{:T(128)S(6)} %select_n.114, bf16[32,16,1024]{2,1,0:T(8,128)(2,1)} %param.9, s32[]{:T(128)S(6)} %select_n.110), kind=kLoop, calls=%fused_computation.32 | loop fusion | flops 655360 | bytes 1310728 | tf_op jit(solution)/shard_map/convert_element_type | solution.py:93
  29.8 1.6 %collective-permute-start.2 = (bf16[8,16,1024]{2,1,0:T(8,128)(2,1)S(1)}, bf16[8,16,1024]{2,1,0:T(8,128)(2,1)S(1)}, u32[]{:S(2)}, u32[]{:S(2)}) collective-permute-start(bf16[8,16,1024]{2,1,0:T(8,128)(2,1)S(1)} %subtract_convert_fusion.1), channel_id=1, source_target_pairs={{0,2},{2,0},{1,3},{3,1},{4,6},{6,4},{5,7},{7,5},{8,10},{10,8},{9,1... | collective-permute-start | bytes 786440 | tf_op jit(solution)/shard_map/ppermute | solution.py:44
  31.5 2.0 %subtract_convert_fusion = bf16[4,32768]{1,0:T(4,128)(2,1)S(1)} fusion(f32[4,32768]{1,0:T(4,128)} %bitcast.70, bf16[4,32768]{1,0:T(4,128)(2,1)} %collective-permute-done.6, bf16[4,32768]{1,0:T(4,128)(2,1)} %collective-permute-done.5, bf16[4,32768]{1,0:T(4,128)(2,1)} %collective-permute-done.4, bf16[4,32]{1,0:T(4,128)(2,1)S(1)} %get-tuple-element.12, ...), kind=kOutput, calls=%fused_computation.31 | convolution fusion | flops 9437184 | bytes 3670272 | tf_op jit(solution)/shard_map/dot_general | solution.py:106
  33.4 2.3 %collective-permute-start.9 = (bf16[4,32768]{1,0:T(4,128)(2,1)S(1)}, bf16[4,32768]{1,0:T(4,128)(2,1)S(1)}, u32[]{:S(2)}, u32[]{:S(2)}) collective-permute-start(bf16[4,32768]{1,0:T(4,128)(2,1)S(1)} %subtract_convert_fusion), channel_id=1, source_target_pairs={{0,12},{4,0},{8,4},{12,8},{1,13},{5,1},{9,5},{13,9},{2,14},{6,2},{... | collective-permute-start | bytes 786440 | tf_op jit(solution)/shard_map/ppermute | solution.py:121
  35.8 1.6 %collective-permute-start.7 = (bf16[4,32768]{1,0:T(4,128)(2,1)S(1)}, bf16[4,32768]{1,0:T(4,128)(2,1)S(1)}, u32[]{:S(2)}, u32[]{:S(2)}) collective-permute-start(bf16[4,32768]{1,0:T(4,128)(2,1)S(1)} %subtract_convert_fusion), channel_id=1, source_target_pairs={{0,8},{4,12},{8,0},{12,4},{1,9},{5,13},{9,1},{13,5},{2,10},{6,14},... | collective-permute-start | bytes 786440 | tf_op jit(solution)/shard_map/ppermute | solution.py:121
  38.3 7.3 %collective-permute-done.9 = bf16[4,32768]{1,0:T(4,128)(2,1)S(1)} collective-permute-done((bf16[4,32768]{1,0:T(4,128)(2,1)S(1)}, bf16[4,32768]{1,0:T(4,128)(2,1)S(1)}, u32[]{:S(2)}, u32[]{:S(2)}) %collective-permute-start.9) | collective-permute-done | bytes 262176 | tf_op jit(solution)/shard_map/ppermute | solution.py:121
  45.6 3.4 %collective-permute-done.8 = bf16[4,32768]{1,0:T(4,128)(2,1)S(1)} collective-permute-done((bf16[4,32768]{1,0:T(4,128)(2,1)S(1)}, bf16[4,32768]{1,0:T(4,128)(2,1)S(1)}, u32[]{:S(2)}, u32[]{:S(2)}) %collective-permute-start.8) | collective-permute-done | bytes 262176 | tf_op jit(solution)/shard_map/ppermute | solution.py:121
  49.8 2.4 %copy.17 = f32[4,8,32,1024]{3,2,1,0:T(8,128)S(1)} copy(f32[4,8,32,1024]{3,1,2,0:T(8,128)S(1)} %bitcast.65) | data formatting | bytes 8388608
  52.3 3.4 %fusion.1 = f32[32,32,1024]{2,1,0:T(8,128)} fusion(f32[32,32,1024]{2,1,0:T(8,128)S(1)} %multiply_add_fusion, f32[4,8,32,1024]{3,2,1,0:T(8,128)S(1)} %copy.17, bf16[16,16,1024]{2,1,0:T(8,128)(2,1)S(1)} %get-tuple-element.6, bf16[16,16,1024]{2,1,0:T(8,128)(2,1)S(1)} %get-tuple-element.5, bf16[1,16,128]{2,1,0:T(8,128)(2,1)S(1)} %slice.25, s32[]{:T(128)S(6)} %select_n.112), kind=kOutput, calls=%fused_computation.3 | convolution fusion | flops 37224448 | bytes 13635588 | tf_op jit(solution)/shard_map/sl,zsx->zlx/dot_general | solution.py:96
  (46 shorter events, 5.7 us)
Async XLA Ops:
  0.0 0.8 %copy-start = (f32[4,16,128]{2,1,0:T(8,128)S(1)}, f32[4,16,128]{2,1,0:T(8,128)}, u32[]{:S(2)}) copy-start(f32[4,16,128]{2,1,0:T(8,128)} %param.11) | copy-start | bytes 98308
  2.8 3.1 %copy-start.7 = (bf16[25,16,128]{2,1,0:T(8,128)(2,1)}, bf16[25,16,128]{2,1,0:T(8,128)(2,1)S(1)}, u32[]{:S(2)}) copy-start(bf16[25,16,128]{2,1,0:T(8,128)(2,1)S(1)} %fusion.6) | copy-start | bytes 307204
  5.7 12.3 %collective-permute-start = (bf16[16,16,1024]{2,1,0:T(8,128)(2,1)S(1)}, bf16[16,16,1024]{2,1,0:T(8,128)(2,1)}, u32[]{:S(2)}, u32[]{:S(2)}) collective-permute-start(bf16[16,16,1024]{2,1,0:T(8,128)(2,1)S(1)} %fusion.4), channel_id=1, source_target_pairs={{0,1},{1,0},{2,3},{3,2},{4,5},{5,4},{6,7},{7,6},{8,9},{9,8},{10,11... | collective-permute-start | bytes 1572872 | tf_op jit(solution)/shard_map/ppermute | solution.py:89
  5.9 2.5 %slice-start = ((bf16[25,16,128]{2,1,0:T(8,128)(2,1)}), bf16[16,16,128]{2,1,0:T(8,128)(2,1)S(1)}, s32[]{:S(2)}) async-start(bf16[25,16,128]{2,1,0:T(8,128)(2,1)} %copy-done.7), calls=%async_computation | async-start | bytes 131072 | tf_op jit(solution)/shard_map/slice | solution.py:57
  8.5 8.3 %copy-start.5 = (bf16[32,32,128]{2,1,0:T(8,128)(2,1)S(1)}, bf16[32,32,128]{2,1,0:T(8,128)(2,1)}, u32[]{:S(2)}) copy-start(bf16[32,32,128]{2,1,0:T(8,128)(2,1)} %param.8) | copy-start | bytes 786436
  10.5 7.3 %slice-start.1 = ((bf16[25,16,128]{2,1,0:T(8,128)(2,1)}), bf16[8,16,128]{2,1,0:T(8,128)(2,1)S(1)}, s32[]{:S(2)}) async-start(bf16[25,16,128]{2,1,0:T(8,128)(2,1)} %copy-done.7), calls=%async_computation.1 | async-start | bytes 65536 | tf_op jit(solution)/shard_map/slice | solution.py:55
  11.6 19.8 %collective-permute-start.4 = (bf16[4,32768]{1,0:T(4,128)(2,1)}, bf16[4,32768]{1,0:T(4,128)(2,1)}, u32[]{:S(2)}, u32[]{:S(2)}) collective-permute-start(bf16[4,32768]{1,0:T(4,128)(2,1)} %get-tuple-element.7), channel_id=1, source_target_pairs={{0,8},{4,12},{8,0},{12,4},{1,9},{5,13},{9,1},{13,5},{2,10},{6,14},... | collective-permute-start | bytes 786440 | tf_op jit(solution)/shard_map/ppermute | solution.py:114
  14.8 16.7 %collective-permute-start.6 = (bf16[4,32768]{1,0:T(4,128)(2,1)}, bf16[4,32768]{1,0:T(4,128)(2,1)}, u32[]{:S(2)}, u32[]{:S(2)}) collective-permute-start(bf16[4,32768]{1,0:T(4,128)(2,1)} %get-tuple-element.8), channel_id=1, source_target_pairs={{0,12},{4,0},{8,4},{12,8},{1,13},{5,1},{9,5},{13,9},{2,14},{6,2},{... | collective-permute-start | bytes 786440 | tf_op jit(solution)/shard_map/ppermute | solution.py:114
  15.8 15.6 %collective-permute-start.5 = (bf16[4,32768]{1,0:T(4,128)(2,1)}, bf16[4,32768]{1,0:T(4,128)(2,1)}, u32[]{:S(2)}, u32[]{:S(2)}) collective-permute-start(bf16[4,32768]{1,0:T(4,128)(2,1)} %get-tuple-element.9), channel_id=1, source_target_pairs={{0,4},{4,8},{8,12},{12,0},{1,5},{5,9},{9,13},{13,1},{2,6},{6,10},{... | collective-permute-start | bytes 786440 | tf_op jit(solution)/shard_map/ppermute | solution.py:114
  17.9 4.2 %copy-start.3 = (f32[1024,128]{0,1:T(8,128)S(1)}, f32[1024,128]{0,1:T(8,128)}, u32[]{:S(2)}) copy-start(f32[1024,128]{0,1:T(8,128)} %copy.10) | copy-start | bytes 1572868
  19.4 4.2 %copy-start.6 = (bf16[4,32,1024]{2,1,0:T(8,128)(2,1)S(1)}, bf16[4,32,1024]{2,1,0:T(8,128)(2,1)}, u32[]{:S(2)}) copy-start(bf16[4,32,1024]{2,1,0:T(8,128)(2,1)} %param.10) | copy-start | bytes 786436
  20.2 8.4 %collective-permute-start.1 = (bf16[8,16,1024]{2,1,0:T(8,128)(2,1)}, bf16[8,16,1024]{2,1,0:T(8,128)(2,1)}, u32[]{:S(2)}, u32[]{:S(2)}) collective-permute-start(bf16[8,16,1024]{2,1,0:T(8,128)(2,1)} %dynamic-slice_convert_fusion), channel_id=1, source_target_pairs={{0,2},{2,0},{1,3},{3,1},{4,6},{6,4},{5,7},{7,5},{8,10},{10,8},{9,1... | collective-permute-start | bytes 786440 | tf_op jit(solution)/shard_map/ppermute | solution.py:39
  23.6 7.8 %copy-start.2 = (bf16[4,8,32,1024]{3,1,2,0:T(8,128)(2,1)S(1)}, bf16[4,8,32,1024]{3,1,2,0:T(8,128)(2,1)}, u32[]{:S(2)}) copy-start(bf16[4,8,32,1024]{3,1,2,0:T(8,128)(2,1)} %copy.16) | copy-start | bytes 6291460
  29.8 7.6 %collective-permute-start.2 = (bf16[8,16,1024]{2,1,0:T(8,128)(2,1)S(1)}, bf16[8,16,1024]{2,1,0:T(8,128)(2,1)S(1)}, u32[]{:S(2)}, u32[]{:S(2)}) collective-permute-start(bf16[8,16,1024]{2,1,0:T(8,128)(2,1)S(1)} %subtract_convert_fusion.1), channel_id=1, source_target_pairs={{0,2},{2,0},{1,3},{3,1},{4,6},{6,4},{5,7},{7,5},{8,10},{10,8},{9,1... | collective-permute-start | bytes 786440 | tf_op jit(solution)/shard_map/ppermute | solution.py:44
  31.4 6.1 %copy-start.1 = (f32[32,32,1024]{2,1,0:T(8,128)S(1)}, f32[32,32,1024]{2,1,0:T(8,128)}, u32[]{:S(2)}) copy-start(f32[32,32,1024]{2,1,0:T(8,128)} %param.7) | copy-start | bytes 12582916
  31.5 6.1 %copy-start.4 = (bf16[128,1024,1]{1,0,2:T(8,128)(2,1)S(1)}, bf16[128,1024,1]{1,0,2:T(8,128)(2,1)}, u32[]{:S(2)}) copy-start(bf16[128,1024,1]{1,0,2:T(8,128)(2,1)} %reshape.91) | copy-start | bytes 786436
  33.4 12.2 %collective-permute-start.9 = (bf16[4,32768]{1,0:T(4,128)(2,1)S(1)}, bf16[4,32768]{1,0:T(4,128)(2,1)S(1)}, u32[]{:S(2)}, u32[]{:S(2)}) collective-permute-start(bf16[4,32768]{1,0:T(4,128)(2,1)S(1)} %subtract_convert_fusion), channel_id=1, source_target_pairs={{0,12},{4,0},{8,4},{12,8},{1,13},{5,1},{9,5},{13,9},{2,14},{6,2},{... | collective-permute-start | bytes 786440 | tf_op jit(solution)/shard_map/ppermute | solution.py:121
  35.8 13.2 %collective-permute-start.8 = (bf16[4,32768]{1,0:T(4,128)(2,1)S(1)}, bf16[4,32768]{1,0:T(4,128)(2,1)S(1)}, u32[]{:S(2)}, u32[]{:S(2)}) collective-permute-start(bf16[4,32768]{1,0:T(4,128)(2,1)S(1)} %subtract_convert_fusion), channel_id=1, source_target_pairs={{0,4},{4,8},{8,12},{12,0},{1,5},{5,9},{9,13},{13,1},{2,6},{6,10},{... | collective-permute-start | bytes 786440 | tf_op jit(solution)/shard_map/ppermute | solution.py:121
  35.8 13.2 %collective-permute-start.7 = (bf16[4,32768]{1,0:T(4,128)(2,1)S(1)}, bf16[4,32768]{1,0:T(4,128)(2,1)S(1)}, u32[]{:S(2)}, u32[]{:S(2)}) collective-permute-start(bf16[4,32768]{1,0:T(4,128)(2,1)S(1)} %subtract_convert_fusion), channel_id=1, source_target_pairs={{0,8},{4,12},{8,0},{12,4},{1,9},{5,13},{9,1},{13,5},{2,10},{6,14},... | collective-permute-start | bytes 786440 | tf_op jit(solution)/shard_map/ppermute | solution.py:121
  37.5 14.8 %collective-permute-start.3 = (bf16[16,16,1024]{2,1,0:T(8,128)(2,1)S(1)}, bf16[16,16,1024]{2,1,0:T(8,128)(2,1)S(1)}, u32[]{:S(2)}, u32[]{:S(2)}) collective-permute-start(bf16[16,16,1024]{2,1,0:T(8,128)(2,1)S(1)} %pad_maximum_fusion), channel_id=1, source_target_pairs={{0,1},{1,0},{2,3},{3,2},{4,5},{5,4},{6,7},{7,6},{8,9},{9,8},{10,11... | collective-permute-start | bytes 1572872 | tf_op jit(solution)/shard_map/ppermute | solution.py:44
